TPU v7x, 32 devices: a whole 2x2x4 slice. The times are simulated.
32 devices in a mesh: dp: 8 (over z, y), feat: 4 (over x, core).
Axes of the slice: x: 2, y: 2, z: 4, core: 2. Of those that a mesh axis runs over, the one named last changes fastest.
Arguments:
- activations: bfloat16 [16384, 2048], P('feat', 'dp'), may hold values from -6 to 6
- cotangent: bfloat16 [16384, 2048], P('feat', 'dp'), may hold values from -6 to 6
- r_mix: bfloat16 [64, 256, 256], P('feat', 'dp'), may hold values from -0.375 to 0.375
- l_mix: bfloat16 [256, 4096], P('feat', 'dp'), may hold values from -0.75 to 0.75
Outputs:
- grad_x: bfloat16 [16384, 2048], P('feat', 'dp')
- grad_r: float32 [64, 256, 256], P('feat', 'dp')
- grad_l: float32 [256, 4096], P('feat', 'dp')
All inputs are finite; a program needn't handle non-finite values.
Results may differ from a plain program's by a relative error of at most 0.0055.
Values may be sent and summed in bfloat16 or wider, within the bound.
No kernel may reach another device: no remote copies, remote signals or barrier semaphores. Data moves between devices by JAX's collectives and lax.ppermute only.
A program may use at most 64 MiB of HBM per device.

v0:
```python
import math

import jax
import jax.numpy as jnp
from jax import lax
from jax.sharding import PartitionSpec as P

BLOCKS = 64
WIDTH = 256


def gelu_tanh(values):
    return jax.nn.gelu(values, approximate=True)


def slope_of(pre_act, upstream):
    _, pullback = jax.vjp(gelu_tanh, pre_act)
    return pullback(upstream.astype(jnp.float32))[0].astype(jnp.bfloat16)


def body(activations, cotangent, r_mix, l_mix):
    tok_count = activations.shape[1]
    local_blocks = activations.shape[0] // WIDTH
    grad_scale = 1.0 / math.sqrt(tok_count * lax.axis_size("dp"))
    r_whole, l_whole = (
        lax.all_gather(r_mix, "dp", axis=1, tiled=True),
        lax.all_gather(l_mix, "dp", axis=1, tiled=True),
    )
    local_cols = l_whole.shape[0]
    l_blocks = l_whole.reshape(local_cols, BLOCKS, BLOCKS)
    x_blocks = activations.reshape(local_blocks, WIDTH, tok_count)
    g_blocks = cotangent.reshape(local_blocks, WIDTH, tok_count)
    mixed_rows = jnp.einsum(
        "bit,bio->bot", x_blocks, r_whole, preferred_element_type=jnp.float32
    ).astype(jnp.bfloat16)
    outgoing = (mixed_rows,)
    parts = (lax.all_to_all(outgoing[0], "feat", split_axis=1, concat_axis=0, tiled=True),)
    columns = parts[0]
    pre_act = jnp.einsum("bst,sbc->cst", columns, l_blocks, preferred_element_type=jnp.float32)
    arrived = (columns, pre_act) + tuple(parts[1:])
    columns = arrived[0]
    pre_act = arrived[1]
    pre_rows = lax.all_to_all(pre_act, "feat", split_axis=0, concat_axis=1, tiled=True)
    slope_rows = slope_of(pre_rows, g_blocks)
    slope_cols = lax.all_to_all(slope_rows, "feat", split_axis=1, concat_axis=0, tiled=True)
    back_cols = jnp.einsum(
        "cst,sbc->bst", slope_cols, l_blocks, preferred_element_type=jnp.float32
    ).astype(jnp.bfloat16)
    l_term = jnp.einsum("bst,cst->sbc", columns, slope_cols, preferred_element_type=jnp.float32)
    l_term = l_term.reshape(local_cols, BLOCKS * BLOCKS) * grad_scale
    back_rows = lax.all_to_all(back_cols, "feat", split_axis=0, concat_axis=1, tiled=True)
    back_rows, through_r = (
        back_rows,
        jnp.einsum("bot,bio->bit", back_rows, r_whole, preferred_element_type=jnp.float32),
    )
    grad_x = (
        (g_blocks.astype(jnp.float32) + through_r)
        .astype(jnp.bfloat16)
        .reshape(local_blocks * WIDTH, tok_count)
    )
    r_term = (
        jnp.einsum("bit,bot->bio", x_blocks, back_rows, preferred_element_type=jnp.float32)
        * grad_scale
    )
    grad_l, grad_r = (
        lax.psum_scatter(l_term, "dp", scatter_dimension=1, tiled=True),
        lax.psum_scatter(r_term, "dp", scatter_dimension=1, tiled=True),
    )
    return (grad_x, grad_r, grad_l)


def solution(mesh):
    placed = (P("feat", "dp"), P("feat", "dp"), P("feat", "dp", None), P("feat", "dp"))
    return jax.shard_map(
        body,
        mesh=mesh,
        in_specs=placed,
        out_specs=(P("feat", "dp"), P("feat", "dp", None), P("feat", "dp")),
        check_vma=False,
    )
```

profile of v0, /device:TPU:0, one launch (start us, length us, event | category | flops | bytes accessed | tf_op | source)
XLA Modules:
  0.0 399.9 jit_solution(9625601833998472881)
XLA Ops:
  7.9 54.3 %all-gather.2.cloned.1.call-done = bf16[16,256,256]{2,1,0:T(8,128)(2,1)} async-done(((bf16[16,32,256]{2,1,0:T(8,128)(2,1)}), bf16[16,256,256]{2,1,0:T(8,128)(2,1)}) %all-gather.2.cloned.1.call-update) | async-done | bytes 2097168 | tf_op jit(solution)/shard_map/all_gather | solution.py:26
  62.2 2.4 convolution_convert_fusion
  64.6 2.5 copy.19
  67.1 4.6 %all-to-all-start = ((bf16[16,256,256]{2,0,1:T(8,128)(2,1)}), bf16[16,256,256]{2,0,1:T(8,128)(2,1)}, u32[]{:S(2)}, u32[]{:S(2)}) async-start(bf16[16,256,256]{2,0,1:T(8,128)(2,1)} %copy.19), calls=%async_computation | async-start | bytes 4194304 | tf_op jit(solution)/shard_map/all_to_all | solution.py:37
  71.7 33.3 %all_gather.7 = bf16[64,4096]{1,0:T(8,128)(2,1)} all-gather(bf16[64,512]{1,0:T(8,128)(2,1)S(1)} %copy-done.5), channel_id=1, replica_groups=mesh['dp'=8,'feat'=4] {'dp'}, dimensions={1}, use_global_device_ids=true | all-gather | bytes 589824 | tf_op jit(solution)/shard_map/all_gather | solution.py:27
  105.0 2.1 reshape.22
  107.1 1.8 copy.20
  109.0 1.3 copy-done.1
  111.0 2.4 copy.22
  113.5 51.1 %all_to_all.72 = f32[64,64,256]{2,1,0:T(8,128)S(1)} all-to-all(f32[64,64,256]{2,1,0:T(8,128)S(1)} %copy.22), channel_id=1, replica_groups=mesh['dp'=8,'feat'=4] {'feat'}, dimensions={0} | all-to-all | bytes 8388608 | tf_op jit(solution)/shard_map/all_to_all | solution.py:43
  166.1 3.3 fusion.6
  169.5 1.2 copy.24
  170.6 28.2 %all_to_all.73 = bf16[16,256,256]{2,0,1:T(8,128)(2,1)S(1)} all-to-all(bf16[16,256,256]{2,0,1:T(8,128)(2,1)S(1)} %copy.24), channel_id=1, replica_groups=mesh['dp'=8,'feat'=4] {'feat'}, dimensions={1} | all-to-all | bytes 4194304 | tf_op jit(solution)/shard_map/all_to_all | solution.py:45
  200.4 1.2 copy.26
  201.6 28.2 %all_to_all.74 = bf16[64,64,256]{2,1,0:T(8,128)(2,1)S(1)} all-to-all(bf16[64,64,256]{2,1,0:T(8,128)(2,1)S(1)} %copy.26), channel_id=1, replica_groups=mesh['dp'=8,'feat'=4] {'feat'}, dimensions={0} | all-to-all | bytes 4194304 | tf_op jit(solution)/shard_map/all_to_all | solution.py:51
  230.0 1.3 copy-done.3
  231.4 2.7 multiply_bitcast_fusion
  234.1 5.5 %copy.28 = f32[16,256,256]{2,0,1:T(8,128)} copy(f32[16,256,256]{1,2,0:T(8,128)} %multiply_bitcast_fusion) | data formatting | bytes 8388608 | tf_op jit(solution)/shard_map/mul | solution.py:62
  239.6 4.2 %convolution_multiply_fusion = f32[64,64,64]{2,1,0:T(8,128)} fusion(bf16[64,64,256]{2,0,1:T(8,128)(2,1)} %bitcast.50, bf16[64,64,256]{2,0,1:T(8,128)(2,1)} %bitcast.52), kind=kOutput, calls=%fused_computation.20 | convolution fusion | flops 134479872 | bytes 5242880 | tf_op jit(solution)/shard_map/bst,cst->sbc/dot_general | solution.py:49
  243.9 3.1 mul.78
  247.0 4.9 %fusion.10 = bf16[16,256,256]{2,1,0:T(8,128)(2,1)} fusion(bf16[16,256,256]{2,1,0:T(8,128)(2,1)} %bitcast.58, bf16[16,256,256]{2,1,0:T(8,128)(2,1)} %all-gather.2.cloned.1.call-done, bf16[16,256,256]{2,1,0:T(8,128)(2,1)} %bitcast.54), kind=kOutput, calls=%fused_computation.15 | convolution fusion | flops 540016640 | bytes 8388608 | tf_op jit(solution)/shard_map/bot,bio->bit/dot_general | solution.py:54
  251.9 73.5 %reduce-scatter.3.cloned.1.call-done = f32[16,32,256]{2,0,1:T(8,128)} async-done(((f32[16,256,256]{2,0,1:T(8,128)}), f32[16,32,256]{2,0,1:T(8,128)}) %reduce-scatter.3.cloned.1.call-update) | async-done | bytes 524304 | tf_op jit(solution)/shard_map/reduce_scatter | solution.py:67
  325.4 2.1 copy.29
  327.6 65.8 %reduce-scatter.5.cloned.1.call-done = f32[64,512]{1,0:T(8,128)} async-done(((f32[64,4096]{1,0:T(8,128)}), f32[64,512]{1,0:T(8,128)}) %reduce-scatter.5.cloned.1.call-update) | async-done | bytes 131088 | tf_op jit(solution)/shard_map/reduce_scatter | solution.py:66
  (22 shorter events, 5.0 us)
Async XLA Ops:
  7.2 55.0 %copy-start = (bf16[4096,256]{1,0:T(8,128)(2,1)S(1)}, bf16[4096,256]{1,0:T(8,128)(2,1)}, u32[]{:S(2)}) copy-start(bf16[4096,256]{1,0:T(8,128)(2,1)} %param.4) | copy-start | bytes 6291460
  7.2 55.0 %all-gather.2.cloned.1.call-start = ((), (), s32[]{:S(2)}) async-start(), calls=%async_computation.6 | async-start | bytes 2359296 | tf_op jit(solution)/shard_map/all_gather | solution.py:26
  67.1 4.6 %copy-start.5 = (bf16[64,512]{1,0:T(8,128)(2,1)S(1)}, bf16[64,512]{1,0:T(8,128)(2,1)}, u32[]{:S(2)}) copy-start(bf16[64,512]{1,0:T(8,128)(2,1)} %param.7) | copy-start | bytes 196612
  67.1 40.0 %all-to-all-start = ((bf16[16,256,256]{2,0,1:T(8,128)(2,1)}), bf16[16,256,256]{2,0,1:T(8,128)(2,1)}, u32[]{:S(2)}, u32[]{:S(2)}) async-start(bf16[16,256,256]{2,0,1:T(8,128)(2,1)} %copy.19), calls=%async_computation | async-start | bytes 4194304 | tf_op jit(solution)/shard_map/all_to_all | solution.py:37
  71.6 253.8 %reduce-scatter.3.cloned.1.call-start = ((), (), s32[]{:S(2)}) async-start(), calls=%async_computation.7 | async-start | bytes 4718592 | tf_op jit(solution)/shard_map/reduce_scatter | solution.py:67
  109.0 1.3 copy-start.1
  164.6 1.6 copy-start.4
  199.1 1.3 copy-start.2
  230.0 1.3 copy-start.3
  239.6 153.8 %reduce-scatter.5.cloned.1.call-start = ((), (), s32[]{:S(2)}) async-start(), calls=%async_computation.8 | async-start | bytes 1179648 | tf_op jit(solution)/shard_map/reduce_scatter | solution.py:66
Sparse Core Ops, SparseCore 0:
  10.2 51.9 all-gather.1
  239.7 85.6 reduce-scatter.2
  329.8 63.5 reduce-scatter.4
where the time goes:
time: 401 us; the launch traced here: 400 us
  waiting for transfers between devices  194 us (48%)
  blocking collectives  141 us (35%)
  local copies, waits for them, and re-layouts  27.3 us (7%)
  matrix products  15.7 us (4%)
  between operations  13.9 us (3%)
  starting transfers between devices  4.69 us (1%)
    reduce_scatter x1, waiting for transfers between devices, body(): lax.psum_scatter(r_term, 'dp', scatter_dimension=1, tiled=True)  73.5 us
    reduce_scatter x1, waiting for transfers between devices, body(): lax.psum_scatter(l_term, 'dp', scatter_dimension=1, tiled=True)  65.8 us
    all_gather x1, waiting for transfers between devices, body(): lax.all_gather(r_mix, 'dp', axis=1, tiled=True)  54.3 us
    all_to_all x1, blocking collectives, body(): lax.all_to_all(pre_act, 'feat', split_axis=0, concat_axis=1, tiled=True)  51.1 us
    all_gather x1, blocking collectives, body(): lax.all_gather(l_mix, 'dp', axis=1, tiled=True)  33.3 us
    all_to_all x1, blocking collectives, body(): lax.all_to_all(slope_rows, 'feat', split_axis=1, concat_axis=0, tiled=True)  28.2 us
    all_to_all x1, blocking collectives, body(): lax.all_to_all(back_cols, 'feat', split_axis=0, concat_axis=1, tiled=True)  28.2 us
  transfers between devices with their start and end apart: 4, of which 3 were waited for; matrix products, arithmetic and copies ran while one was open for 4% of the time, Pallas kernels for 0%

commit v1 on v0

v1 whole, which is shorter than its diff:
```python
import math

import jax
import jax.numpy as jnp
from jax import lax
from jax.sharding import PartitionSpec as P

BLOCKS = 64
WIDTH = 256


def gelu_tanh(values):
    return jax.nn.gelu(values, approximate=True)


def slope_of(pre_act, upstream):
    _, pullback = jax.vjp(gelu_tanh, pre_act)
    return pullback(upstream.astype(jnp.float32))[0].astype(jnp.bfloat16)


def body(activations, cotangent, r_mix, l_mix):
    tok_count = activations.shape[1]
    local_blocks = activations.shape[0] // WIDTH
    grad_scale = 1.0 / math.sqrt(tok_count * lax.axis_size("dp"))
    x_blocks = activations.reshape(local_blocks, WIDTH, tok_count)
    g_blocks = cotangent.reshape(local_blocks, WIDTH, tok_count)
    g_cols = lax.all_to_all(g_blocks, "feat", split_axis=1, concat_axis=0, tiled=True)
    r_lead = jnp.transpose(r_mix, (1, 0, 2))
    r_whole = lax.all_gather(r_lead, "dp", axis=0, tiled=True)
    local_cols = l_mix.shape[0]
    l_lead = jnp.transpose(l_mix.reshape(local_cols, -1, BLOCKS), (1, 0, 2))
    l_blocks = lax.all_gather(l_lead, "dp", axis=0, tiled=True)
    mixed_rows = jnp.einsum(
        "bit,ibo->bot", x_blocks, r_whole, preferred_element_type=jnp.float32
    ).astype(jnp.bfloat16)
    columns = lax.all_to_all(mixed_rows, "feat", split_axis=1, concat_axis=0, tiled=True)
    pre_act = jnp.einsum("bst,bsc->cst", columns, l_blocks, preferred_element_type=jnp.float32)
    slope_cols = slope_of(pre_act, g_cols)
    back_cols = jnp.einsum(
        "cst,bsc->bst", slope_cols, l_blocks, preferred_element_type=jnp.float32
    ).astype(jnp.bfloat16)
    l_term = jnp.einsum("bst,cst->bsc", columns, slope_cols, preferred_element_type=jnp.float32)
    l_term = l_term * grad_scale
    grad_l = lax.psum_scatter(l_term, "dp", scatter_dimension=0, tiled=True)
    grad_l = jnp.transpose(grad_l, (1, 0, 2)).reshape(local_cols, -1)
    back_rows = lax.all_to_all(back_cols, "feat", split_axis=0, concat_axis=1, tiled=True)
    through_r = jnp.einsum("bot,ibo->bit", back_rows, r_whole, preferred_element_type=jnp.float32)
    grad_x = (
        (g_blocks.astype(jnp.float32) + through_r)
        .astype(jnp.bfloat16)
        .reshape(local_blocks * WIDTH, tok_count)
    )
    r_term = (
        jnp.einsum("bit,bot->ibo", x_blocks, back_rows, preferred_element_type=jnp.float32)
        * grad_scale
    )
    grad_r = lax.psum_scatter(r_term, "dp", scatter_dimension=0, tiled=True)
    grad_r = jnp.transpose(grad_r, (1, 0, 2))
    return (grad_x, grad_r, grad_l)


def solution(mesh):
    placed = (P("feat", "dp"), P("feat", "dp"), P("feat", "dp", None), P("feat", "dp"))
    return jax.shard_map(
        body,
        mesh=mesh,
        in_specs=placed,
        out_specs=(P("feat", "dp"), P("feat", "dp", None), P("feat", "dp")),
        check_vma=False,
    )
```

time: 401 us -> 286 us (0.71)
  blocking collectives: 141 us -> 58.3 us
  waiting for transfers between devices: 194 us -> 155 us
  starting transfers between devices: 4.69 us -> 9.16 us
    all_to_all x2 -> x0, blocking collectives: 79.2 us -> none  [the longest x1 51.1 us: body(): lax.all_to_all(pre_act, 'feat', split_axis=0, concat_axis=1, tiled=True)]
    reduce_scatter x2, waiting for transfers between devices: 139 us -> 108 us  [the longest x1 88.7 us: body(): grad_r = lax.psum_scatter(r_term, 'dp', scatter_dimension=0, tiled=True)]
    all_gather x1, waiting for transfers between devices: 54.3 us -> 45.7 us  [body(): r_whole = lax.all_gather(r_lead, 'dp', axis=0, tiled=True)]
    all_to_all x1 -> x2, starting transfers between devices: 4.57 us -> 9.04 us  [the longest x1 4.59 us: body(): lax.all_to_all(mixed_rows, 'feat', split_axis=1, concat_axis=0, tiled=True)]
  transfers between devices with their start and end apart: 4 -> 5, of which waited for: 3 -> 3; matrix products, arithmetic and copies ran while one was open for 4% -> 11% of each run, Pallas kernels for 0% -> 0%
where the time goes in v1:
time: 286 us; the launch traced here: 285 us
  waiting for transfers between devices  155 us (54%)
  blocking collectives  58.3 us (20%)
  local copies, waits for them, and re-layouts  31.1 us (11%)
  matrix products  18 us (6%)
  between operations  13.8 us (5%)
  starting transfers between devices  9.16 us (3%)
    reduce_scatter x1, waiting for transfers between devices, body(): grad_r = lax.psum_scatter(r_term, 'dp', scatter_dimension=0, tiled=True)  88.7 us
    all_gather x1, waiting for transfers between devices, body(): r_whole = lax.all_gather(r_lead, 'dp', axis=0, tiled=True)  45.7 us
    all_gather x1, blocking collectives, body(): l_blocks = lax.all_gather(l_lead, 'dp', axis=0, tiled=True)  29.9 us
    all_to_all x1, blocking collectives, body(): lax.all_to_all(back_cols, 'feat', split_axis=0, concat_axis=1, tiled=True)  28.5 us
    reduce_scatter x1, waiting for transfers between devices, body(): grad_l = lax.psum_scatter(l_term, 'dp', scatter_dimension=0, tiled=True)  19.6 us
  transfers between devices with their start and end apart: 5, of which 3 were waited for; matrix products, arithmetic and copies ran while one was open for 11% of the time, Pallas kernels for 0%

profile of v1, /device:TPU:0, one launch (start us, length us, event | category | flops | bytes accessed | tf_op | source)
XLA Modules:
  0.0 285.1 jit_solution(15059337977617921921)
XLA Ops:
  7.9 4.1 %copy.16 = bf16[16,256,256]{2,0,1:T(8,128)(2,1)} copy(bf16[16,256,256]{2,1,0:T(8,128)(2,1)} %bitcast.69) | data formatting | bytes 4194304 | tf_op jit(solution)/shard_map/reshape | solution.py:26
  12.0 4.5 %all-to-all-start = ((bf16[16,256,256]{2,0,1:T(8,128)(2,1)}), bf16[16,256,256]{2,0,1:T(8,128)(2,1)}, u32[]{:S(2)}, u32[]{:S(2)}) async-start(bf16[16,256,256]{2,0,1:T(8,128)(2,1)} %copy.16), calls=%async_computation | async-start | bytes 4194304 | tf_op jit(solution)/shard_map/all_to_all | solution.py:27
  16.5 45.7 %all-gather.2.cloned.1.call-done = bf16[256,16,256]{2,0,1:T(8,128)(2,1)} async-done(((bf16[32,16,256]{2,0,1:T(8,128)(2,1)}), bf16[256,16,256]{2,0,1:T(8,128)(2,1)}) %all-gather.2.cloned.1.call-update) | async-done | bytes 2097168 | tf_op jit(solution)/shard_map/all_gather | solution.py:29
  62.2 2.4 convolution_convert_fusion
  64.6 2.5 copy.18
  67.1 4.6 %all-to-all-start.1 = ((bf16[16,256,256]{2,0,1:T(8,128)(2,1)}), bf16[16,256,256]{2,0,1:T(8,128)(2,1)}, u32[]{:S(2)}, u32[]{:S(2)}) async-start(bf16[16,256,256]{2,0,1:T(8,128)(2,1)} %copy.18), calls=%async_computation.1 | async-start | bytes 4194304 | tf_op jit(solution)/shard_map/all_to_all | solution.py:36
  71.8 29.9 %all_gather.7 = bf16[64,64,64]{2,0,1:T(8,128)(2,1)S(1)} all-gather(bf16[8,64,64]{2,0,1:T(8,128)(2,1)S(1)} %bitcast.72), channel_id=1, replica_groups=mesh['dp'=8,'feat'=4] {'dp'}, dimensions={0}, use_global_device_ids=true | all-gather | bytes 589824 | tf_op jit(solution)/shard_map/all_gather | solution.py:32
  101.7 4.1 %copy.17 = f32[16,4,64,256]{3,0,1,2:T(8,128)} copy(bf16[16,4,64,256]{3,0,2,1:T(8,128)(2,1)} %bitcast.24) | data formatting | bytes 6291456 | tf_op jit(solution)/shard_map/convert_element_type | solution.py:18
  105.9 2.0 copy.19
  108.7 3.7 %fusion.6 = bf16[64,64,256]{2,0,1:T(8,128)(2,1)S(1)} fusion(f32[16,4,64,256]{3,0,1,2:T(8,128)S(1)} %copy-done.3, bf16[64,64,256]{2,0,1:T(8,128)(2,1)S(1)} %bitcast.66, bf16[64,64,64]{2,0,1:T(8,128)(2,1)S(1)} %all_gather.7), kind=kOutput, calls=%fused_computation.8 | convolution fusion | flops 155189248 | bytes 8912896 | tf_op jit(solution)/shard_map/bst,bsc->cst/dot_general | solution.py:37
  112.4 1.3 copy-done.2
  113.7 2.0 multiply_bitcast_fusion.1
  115.7 3.8 %copy.23 = f32[64,64,64]{2,1,0:T(8,128)} copy(f32[64,64,64]{0,2,1:T(8,128)} %multiply_bitcast_fusion.1) | data formatting | bytes 2097152 | tf_op jit(solution)/shard_map/mul | solution.py:43
  119.6 2.3 convert_bitcast_fusion
  121.9 1.2 copy.20
  123.1 28.5 %all_to_all.45 = bf16[64,64,256]{2,1,0:T(8,128)(2,1)S(1)} all-to-all(bf16[64,64,256]{2,1,0:T(8,128)(2,1)S(1)} %copy.20), channel_id=1, replica_groups=mesh['dp'=8,'feat'=4] {'feat'}, dimensions={0} | all-to-all | bytes 4194304 | tf_op jit(solution)/shard_map/all_to_all | solution.py:46
  151.8 1.3 copy-done.1
  153.2 2.7 multiply_bitcast_fusion
  155.9 5.5 %copy.22 = f32[256,16,256]{2,1,0:T(8,128)} copy(f32[256,16,256]{0,2,1:T(8,128)} %multiply_bitcast_fusion) | data formatting | bytes 8388608 | tf_op jit(solution)/shard_map/mul | solution.py:54
  161.4 4.9 %fusion.7 = bf16[16,256,256]{2,1,0:T(8,128)(2,1)} fusion(bf16[16,256,256]{2,1,0:T(8,128)(2,1)} %bitcast.70, bf16[256,16,256]{2,0,1:T(8,128)(2,1)} %all-gather.2.cloned.1.call-done, bf16[16,256,256]{2,1,0:T(8,128)(2,1)} %bitcast.65), kind=kOutput, calls=%fused_computation.10 | convolution fusion | flops 540016640 | bytes 8388608 | tf_op jit(solution)/shard_map/bot,ibo->bit/dot_general | solution.py:47
  166.3 19.6 %reduce-scatter.5.cloned.1.call-done = f32[8,64,64]{2,1,0:T(8,128)} async-done(((f32[64,64,64]{2,1,0:T(8,128)}), f32[8,64,64]{2,1,0:T(8,128)}) %reduce-scatter.5.cloned.1.call-update) | async-done | bytes 131088 | tf_op jit(solution)/shard_map/reduce_scatter | solution.py:44
  185.9 1.1 copy.24
  187.8 88.7 %reduce-scatter.3.cloned.1.call-done = f32[32,16,256]{2,1,0:T(8,128)} async-done(((f32[256,16,256]{2,1,0:T(8,128)}), f32[32,16,256]{2,1,0:T(8,128)}) %reduce-scatter.3.cloned.1.call-update) | async-done | bytes 524304 | tf_op jit(solution)/shard_map/reduce_scatter | solution.py:57
  276.5 2.1 copy.25
  (19 shorter events, 2.8 us)
Async XLA Ops:
  7.2 55.0 %copy-start = (bf16[4096,256]{1,0:T(8,128)(2,1)S(1)}, bf16[4096,256]{1,0:T(8,128)(2,1)}, u32[]{:S(2)}) copy-start(bf16[4096,256]{1,0:T(8,128)(2,1)} %param.4) | copy-start | bytes 6291460
  7.2 55.0 %all-gather.2.cloned.1.call-start = ((), (), s32[]{:S(2)}) async-start(), calls=%async_computation.5 | async-start | bytes 2359296 | tf_op jit(solution)/shard_map/all_gather | solution.py:29
  12.0 55.1 %all-to-all-start = ((bf16[16,256,256]{2,0,1:T(8,128)(2,1)}), bf16[16,256,256]{2,0,1:T(8,128)(2,1)}, u32[]{:S(2)}, u32[]{:S(2)}) async-start(bf16[16,256,256]{2,0,1:T(8,128)(2,1)} %copy.16), calls=%async_computation | async-start | bytes 4194304 | tf_op jit(solution)/shard_map/all_to_all | solution.py:27
  67.0 4.7 %copy-start.4 = (bf16[64,512]{1,0:T(8,128)(2,1)S(1)}, bf16[64,512]{1,0:T(8,128)(2,1)}, u32[]{:S(2)}) copy-start(bf16[64,512]{1,0:T(8,128)(2,1)} %param.7) | copy-start | bytes 196612
  67.1 38.8 %all-to-all-start.1 = ((bf16[16,256,256]{2,0,1:T(8,128)(2,1)}), bf16[16,256,256]{2,0,1:T(8,128)(2,1)}, u32[]{:S(2)}, u32[]{:S(2)}) async-start(bf16[16,256,256]{2,0,1:T(8,128)(2,1)} %copy.18), calls=%async_computation.1 | async-start | bytes 4194304 | tf_op jit(solution)/shard_map/all_to_all | solution.py:36
  71.6 114.3 %reduce-scatter.5.cloned.1.call-start = ((), (), s32[]{:S(2)}) async-start(), calls=%async_computation.7 | async-start | bytes 2359296 | tf_op jit(solution)/shard_map/reduce_scatter | solution.py:44
  105.9 2.8 copy-start.3
  112.4 1.3 copy-start.2
  119.6 156.9 %reduce-scatter.3.cloned.1.call-start = ((), (), s32[]{:S(2)}) async-start(), calls=%async_computation.6 | async-start | bytes 4718592 | tf_op jit(solution)/shard_map/reduce_scatter | solution.py:57
  151.8 1.3 copy-start.1
Sparse Core Ops, SparseCore 0:
  10.2 51.9 all-gather.1
  119.7 66.1 reduce-scatter.4
  189.5 86.8 reduce-scatter.2

commit v2 on v1

v2 whole, which is shorter than its diff:
```python
import math

import jax
import jax.numpy as jnp
import numpy as np
from jax import lax
from jax.sharding import PartitionSpec as P

BLOCKS = 64
WIDTH = 256


def gelu_tanh(values):
    return jax.nn.gelu(values, approximate=True)


def slope_of(pre_act, upstream):
    _, pullback = jax.vjp(gelu_tanh, pre_act)
    return pullback(upstream.astype(jnp.float32))[0].astype(jnp.bfloat16)


def ring_of(mesh):
    row = mesh.devices[(slice(None),) + (0,) * (mesh.devices.ndim - 1)]
    size = len(row)
    try:
        spots = [tuple(d.coords) for d in row]
    except AttributeError:
        return list(range(size))
    near = [
        [j for j in range(size) if sum(abs(a - b) for a, b in zip(spots[i], spots[j])) == 1]
        for i in range(size)
    ]
    path, seen, budget = [0], {0}, [20000]

    def grow():
        budget[0] -= 1
        if budget[0] < 0:
            return False
        if len(path) == size:
            return 0 in near[path[-1]] or size <= 2
        here = path[-1]
        for nxt in sorted(near[here], key=lambda j: len([k for k in near[j] if k not in seen])):
            if nxt in seen:
                continue
            path.append(nxt)
            seen.add(nxt)
            if grow():
                return True
            path.pop()
            seen.discard(nxt)
        return False

    return list(path) if grow() else list(range(size))


def ring_reduce_scatter(parts, ring):
    n = len(ring)
    order = jnp.asarray(np.array(ring, np.int32))
    place = jnp.asarray(np.argsort(np.array(ring)).astype(np.int32))
    here = place[lax.axis_index("dp")]
    half = parts.shape[1] // 2
    halves = (parts[:, :half], parts[:, half:])
    forward = [(ring[p], ring[(p + 1) % n]) for p in range(n)]
    backward = [(ring[p], ring[(p - 1) % n]) for p in range(n)]
    totals = []
    for way, pairs, src in ((1, forward, halves[0]), (-1, backward, halves[1])):
        acc = None
        for step in range(n):
            owner = order[(here - way * (1 + step)) % n]
            mine = lax.dynamic_index_in_dim(src, owner, axis=0, keepdims=False)
            acc = mine if acc is None else acc + mine
            if step < n - 1:
                acc = lax.ppermute(acc, "dp", pairs)
        totals.append(acc)
    return jnp.concatenate(totals, axis=0)


def body(ring, activations, cotangent, r_mix, l_mix):
    tok_count = activations.shape[1]
    local_blocks = activations.shape[0] // WIDTH
    n_dp = lax.axis_size("dp")
    grad_scale = 1.0 / math.sqrt(tok_count * n_dp)
    x_blocks = activations.reshape(local_blocks, WIDTH, tok_count)
    g_blocks = cotangent.reshape(local_blocks, WIDTH, tok_count)
    g_cols = lax.all_to_all(g_blocks, "feat", split_axis=1, concat_axis=0, tiled=True)
    local_cols = l_mix.shape[0]
    rows_r = r_mix.shape[1]
    r_flat = r_mix.reshape(1, -1)
    packed = jnp.concatenate([r_flat, l_mix.reshape(1, -1)], axis=1)
    packed = lax.all_gather(packed, "dp", axis=0, tiled=True)
    r_size = r_flat.shape[1]
    r_whole = packed[:, :r_size].reshape(n_dp, local_blocks, rows_r, WIDTH)
    r_whole = jnp.transpose(r_whole, (1, 0, 2, 3)).reshape(local_blocks, n_dp * rows_r, WIDTH)
    l_whole = packed[:, r_size:].reshape(n_dp, local_cols, -1, BLOCKS)
    l_blocks = jnp.transpose(l_whole, (0, 2, 1, 3)).reshape(-1, local_cols, BLOCKS)
    mixed_rows = jnp.einsum(
        "bit,bio->bot", x_blocks, r_whole, preferred_element_type=jnp.float32
    ).astype(jnp.bfloat16)
    columns = lax.all_to_all(mixed_rows, "feat", split_axis=1, concat_axis=0, tiled=True)
    pre_act = jnp.einsum("bst,bsc->cst", columns, l_blocks, preferred_element_type=jnp.float32)
    slope_cols = slope_of(pre_act, g_cols)
    back_cols = jnp.einsum(
        "cst,bsc->sbt", slope_cols, l_blocks, preferred_element_type=jnp.float32
    ).astype(jnp.bfloat16)
    l_term = jnp.einsum("bst,cst->bsc", columns, slope_cols, preferred_element_type=jnp.float32)
    l_term = (l_term * grad_scale).reshape(n_dp, -1, local_cols, BLOCKS)
    grad_l = ring_reduce_scatter(l_term, ring)
    grad_l = jnp.transpose(grad_l, (1, 0, 2)).reshape(local_cols, -1)
    back_rows = lax.all_to_all(back_cols, "feat", split_axis=1, concat_axis=0, tiled=True)
    through_r = jnp.einsum("obt,bio->bit", back_rows, r_whole, preferred_element_type=jnp.float32)
    grad_x = (
        (g_blocks.astype(jnp.float32) + through_r)
        .astype(jnp.bfloat16)
        .reshape(local_blocks * WIDTH, tok_count)
    )
    r_term = (
        jnp.einsum("bit,obt->ibo", x_blocks, back_rows, preferred_element_type=jnp.float32)
        * grad_scale
    ).reshape(n_dp, rows_r, local_blocks, WIDTH)
    grad_r = ring_reduce_scatter(r_term, ring)
    grad_r = jnp.transpose(grad_r, (1, 0, 2))
    return (grad_x, grad_r, grad_l)


def solution(mesh):
    ring = ring_of(mesh)
    placed = (P("feat", "dp"), P("feat", "dp"), P("feat", "dp", None), P("feat", "dp"))
    return jax.shard_map(
        lambda *args: body(ring, *args),
        mesh=mesh,
        in_specs=placed,
        out_specs=(P("feat", "dp"), P("feat", "dp", None), P("feat", "dp")),
        check_vma=False,
    )
```

time: 286 us -> 301 us (1.052)
  blocking collectives: 58.3 us -> 0 us
  between operations: 13.8 us -> 55.1 us
  starting transfers between devices: 9.16 us -> 46.6 us
  waiting for transfers between devices: 155 us -> 122 us
  other arithmetic: 0 us -> 16.3 us
  local copies, waits for them, and re-layouts: 31.1 us -> 44.2 us
  matrix products: 18 us -> 14.8 us
    reduce_scatter x2 -> x0, waiting for transfers between devices: 108 us -> none  [the longest x1 88.7 us: body(): grad_r = lax.psum_scatter(r_term, 'dp', scatter_dimension=0, tiled=True)]
    ppermute x0 -> x28, waiting for transfers between devices: none -> 41.8 us  [ring_reduce_scatter(): acc = lax.ppermute(acc, 'dp', pairs)]
    all_gather x1, waiting for transfers between devices: 45.7 us -> 80.6 us  [body(): packed = lax.all_gather(packed, 'dp', axis=0, tiled=True)]
    ppermute x0 -> x28, starting transfers between devices: none -> 32.9 us  [ring_reduce_scatter(): acc = lax.ppermute(acc, 'dp', pairs)]
    all_gather x1 -> x0, blocking collectives: 29.9 us -> none  [body(): l_blocks = lax.all_gather(l_lead, 'dp', axis=0, tiled=True)]
    all_to_all x1 -> x0, blocking collectives: 28.5 us -> none  [body(): lax.all_to_all(back_cols, 'feat', split_axis=0, concat_axis=1, tiled=True)]
    add x0 -> x28, other arithmetic: none -> 11.8 us  [ring_reduce_scatter(): acc = mine if acc is None else acc + mine]
    mul x2 -> x1, local copies, waits for them, and re-layouts: 9.33 us -> 3.81 us  [body(): l_term = (l_term * grad_scale).reshape(n_dp, -1, local_cols, BLOCKS)]
  transfers between devices with their start and end apart: 5 -> 32, of which waited for: 3 -> 13; matrix products, arithmetic and copies ran while one was open for 11% -> 15% of each run, Pallas kernels for 0% -> 0%
where the time goes in v2:
time: 301 us; the launch traced here: 299 us
  waiting for transfers between devices  122 us (41%)
  between operations  55.1 us (18%)
  starting transfers between devices  46.6 us (15%)
  local copies, waits for them, and re-layouts  44.2 us (15%)
  other arithmetic  16.3 us (5%)
  matrix products  14.8 us (5%)
    all_gather x1, waiting for transfers between devices, body(): packed = lax.all_gather(packed, 'dp', axis=0, tiled=True)  80.6 us
    ppermute x28, waiting for transfers between devices, ring_reduce_scatter(): acc = lax.ppermute(acc, 'dp', pairs)  41.8 us
    ppermute x28, starting transfers between devices, ring_reduce_scatter(): acc = lax.ppermute(acc, 'dp', pairs)  32.9 us
    add x28, other arithmetic, ring_reduce_scatter(): acc = mine if acc is None else acc + mine  11.8 us
    unnamed x20, local copies, waits for them, and re-layouts  10.3 us
  transfers between devices with their start and end apart: 32, of which 13 were waited for; matrix products, arithmetic and copies ran while one was open for 15% of the time, Pallas kernels for 0%

profile of v2, /device:TPU:0, one launch (start us, length us, event | category | flops | bytes accessed | tf_op | source)
XLA Modules:
  0.0 299.4 jit_solution(11265219353165768789)
XLA Ops:
  9.4 3.6 %maximum_bitcast_fusion = bf16[1,1,163840]{2,1,0:T(2,128)(2,1)} fusion(bf16[1,32768]{1,0:T(2,128)(2,1)S(1)} %bitcast.189, bf16[1,131072]{1,0:T(2,128)(2,1)S(1)} %reshape.111), kind=kLoop, calls=%fused_computation.22 | loop fusion | flops 655360 | bytes 655360
  13.0 4.1 %copy.37 = bf16[16,256,256]{2,0,1:T(8,128)(2,1)} copy(bf16[16,256,256]{2,1,0:T(8,128)(2,1)} %bitcast.183) | data formatting | bytes 4194304 | tf_op jit(solution)/shard_map/reshape | solution.py:84
  17.1 4.5 %all-to-all-start = ((bf16[16,256,256]{2,0,1:T(8,128)(2,1)}), bf16[16,256,256]{2,0,1:T(8,128)(2,1)}, u32[]{:S(2)}, u32[]{:S(2)}) async-start(bf16[16,256,256]{2,0,1:T(8,128)(2,1)} %copy.37), calls=%async_computation | async-start | bytes 4194304 | tf_op jit(solution)/shard_map/all_to_all | solution.py:85
  21.6 80.6 %all-gather.3.cloned.1.call-done = bf16[8,1,163840]{2,1,0:T(2,128)(2,1)} async-done(((bf16[1,1,163840]{2,1,0:T(2,128)(2,1)}), bf16[8,1,163840]{2,1,0:T(2,128)(2,1)}) %all-gather.3.cloned.1.call-update) | async-done | bytes 2621456 | tf_op jit(solution)/shard_map/all_gather | solution.py:90
  102.1 5.8 %copy.58 = bf16[8,1,163840]{2,0,1:T(8,128)(2,1)S(1)} copy(bf16[8,1,163840]{2,1,0:T(2,128)(2,1)} %all-gather.3.cloned.1.call-done) | data formatting | bytes 5242880
  114.0 4.8 %all-to-all-start.1 = ((bf16[16,256,256]{2,0,1:T(8,128)(2,1)}), bf16[16,256,256]{2,0,1:T(8,128)(2,1)}, u32[]{:S(2)}, u32[]{:S(2)}) async-start(bf16[16,256,256]{2,0,1:T(8,128)(2,1)} %copy.40), calls=%async_computation.1 | async-start | bytes 4194304 | tf_op jit(solution)/shard_map/all_to_all | solution.py:99
  160.8 4.2 %copy.38 = f32[16,4,64,256]{3,0,1,2:T(8,128)} copy(bf16[16,4,64,256]{3,0,2,1:T(8,128)(2,1)} %bitcast.92) | data formatting | bytes 6291456 | tf_op jit(solution)/shard_map/convert_element_type | solution.py:19
  172.4 5.1 %fusion.6 = bf16[64,64,256]{2,0,1:T(8,128)(2,1)S(1)} fusion(f32[16,4,64,256]{3,0,1,2:T(8,128)S(1)} %copy-done.6, bf16[64,64,256]{2,0,1:T(8,128)(2,1)S(1)} %bitcast.179, bf16[64,64,64]{2,1,0:T(8,128)(2,1)S(1)} %bitcast.185), kind=kOutput, calls=%fused_computation.8 | convolution fusion | flops 155189248 | bytes 8912896 | tf_op jit(solution)/shard_map/bst,bsc->cst/dot_general | solution.py:100
  183.4 3.8 %copy.46 = f32[64,64,64]{2,1,0:T(8,128)} copy(f32[64,64,64]{0,2,1:T(8,128)} %multiply_bitcast_fusion) | data formatting | bytes 2097152 | tf_op jit(solution)/shard_map/mul | solution.py:106
  187.2 2.7 fusion.13
  189.9 4.5 %all-to-all-start.2 = ((bf16[64,64,256]{2,0,1:T(8,128)(2,1)}), bf16[64,64,256]{2,0,1:T(8,128)(2,1)}, u32[]{:S(2)}, u32[]{:S(2)}) async-start(bf16[64,64,256]{2,0,1:T(8,128)(2,1)} %copy.44), calls=%async_computation.2 | async-start | bytes 4194304 | tf_op jit(solution)/shard_map/all_to_all | solution.py:109
  197.4 3.8 %collective-permute-done.21 = f32[4,64,64]{2,1,0:T(8,128)S(1)} collective-permute-done((f32[4,64,64]{2,1,0:T(8,128)S(1)}, f32[4,64,64]{2,1,0:T(8,128)S(1)}, u32[]{:S(2)}, u32[]{:S(2)}) %collective-permute-start.21) | collective-permute-done | bytes 65568 | tf_op jit(solution)/shard_map/ppermute | solution.py:73
  204.3 3.1 %collective-permute-done.22 = f32[4,64,64]{2,1,0:T(8,128)S(1)} collective-permute-done((f32[4,64,64]{2,1,0:T(8,128)S(1)}, f32[4,64,64]{2,1,0:T(8,128)S(1)}, u32[]{:S(2)}, u32[]{:S(2)}) %collective-permute-start.22) | collective-permute-done | bytes 65568 | tf_op jit(solution)/shard_map/ppermute | solution.py:73
  210.4 2.9 collective-permute-done.23
  216.4 2.9 collective-permute-done.24
  222.3 2.9 collective-permute-done.25
  237.7 2.6 collective-permute-start.8
  243.5 3.2 %collective-permute-done.8 = f32[16,16,256]{2,0,1:T(8,128)S(1)} collective-permute-done((f32[16,16,256]{2,0,1:T(8,128)S(1)}, f32[16,16,256]{2,0,1:T(8,128)S(1)}, u32[]{:S(2)}, u32[]{:S(2)}) %collective-permute-start.8) | collective-permute-done | bytes 262176 | tf_op jit(solution)/shard_map/ppermute | solution.py:73
  251.0 4.7 %collective-permute-done.9 = f32[16,16,256]{2,0,1:T(8,128)S(1)} collective-permute-done((f32[16,16,256]{2,0,1:T(8,128)S(1)}, f32[16,16,256]{2,0,1:T(8,128)S(1)}, u32[]{:S(2)}, u32[]{:S(2)}) %collective-permute-start.9) | collective-permute-done | bytes 262176 | tf_op jit(solution)/shard_map/ppermute | solution.py:73
  255.8 2.5 collective-permute-start.10
  259.4 5.3 %collective-permute-done.10 = f32[16,16,256]{2,0,1:T(8,128)S(1)} collective-permute-done((f32[16,16,256]{2,0,1:T(8,128)S(1)}, f32[16,16,256]{2,0,1:T(8,128)S(1)}, u32[]{:S(2)}, u32[]{:S(2)}) %collective-permute-start.10) | collective-permute-done | bytes 262176 | tf_op jit(solution)/shard_map/ppermute | solution.py:73
  266.9 5.8 %collective-permute-done.11 = f32[16,16,256]{2,0,1:T(8,128)S(1)} collective-permute-done((f32[16,16,256]{2,0,1:T(8,128)S(1)}, f32[16,16,256]{2,0,1:T(8,128)S(1)}, u32[]{:S(2)}, u32[]{:S(2)}) %collective-permute-start.11) | collective-permute-done | bytes 262176 | tf_op jit(solution)/shard_map/ppermute | solution.py:73
  275.9 4.9 %collective-permute-done.12 = f32[16,16,256]{2,0,1:T(8,128)S(1)} collective-permute-done((f32[16,16,256]{2,0,1:T(8,128)S(1)}, f32[16,16,256]{2,0,1:T(8,128)S(1)}, u32[]{:S(2)}, u32[]{:S(2)}) %collective-permute-start.12) | collective-permute-done | bytes 262176 | tf_op jit(solution)/shard_map/ppermute | solution.py:73
  284.9 4.9 %add_convert_fusion = bf16[16,256,256]{2,1,0:T(8,128)(2,1)} fusion(bf16[16,256,256]{2,1,0:T(8,128)(2,1)} %bitcast.184, bf16[16,256,256]{2,1,0:T(8,128)(2,1)} %bitcast.173, bf16[256,16,256]{2,0,1:T(8,128)(2,1)} %bitcast.175), kind=kOutput, calls=%fused_computation.14 | convolution fusion | flops 540016640 | bytes 8388608 | tf_op jit(solution)/shard_map/obt,bio->bit/dot_general | solution.py:110
  (121 shorter events, 71.5 us)
Async XLA Ops:
  7.2 94.9 %all-gather.3.cloned.1.call-start = ((), (), s32[]{:S(2)}) async-start(), calls=%async_computation.3 | async-start | bytes 5898240 | tf_op jit(solution)/shard_map/all_gather | solution.py:90
  17.1 96.9 %all-to-all-start = ((bf16[16,256,256]{2,0,1:T(8,128)(2,1)}), bf16[16,256,256]{2,0,1:T(8,128)(2,1)}, u32[]{:S(2)}, u32[]{:S(2)}) async-start(bf16[16,256,256]{2,0,1:T(8,128)(2,1)} %copy.37), calls=%async_computation | async-start | bytes 4194304 | tf_op jit(solution)/shard_map/all_to_all | solution.py:85
  114.0 55.6 %all-to-all-start.1 = ((bf16[16,256,256]{2,0,1:T(8,128)(2,1)}), bf16[16,256,256]{2,0,1:T(8,128)(2,1)}, u32[]{:S(2)}, u32[]{:S(2)}) async-start(bf16[16,256,256]{2,0,1:T(8,128)(2,1)} %copy.40), calls=%async_computation.1 | async-start | bytes 4194304 | tf_op jit(solution)/shard_map/all_to_all | solution.py:99
  189.9 36.7 %all-to-all-start.2 = ((bf16[64,64,256]{2,0,1:T(8,128)(2,1)}), bf16[64,64,256]{2,0,1:T(8,128)(2,1)}, u32[]{:S(2)}, u32[]{:S(2)}) async-start(bf16[64,64,256]{2,0,1:T(8,128)(2,1)} %copy.44), calls=%async_computation.2 | async-start | bytes 4194304 | tf_op jit(solution)/shard_map/all_to_all | solution.py:109
  195.7 6.8 %collective-permute-start.14 = (f32[4,64,64]{2,1,0:T(8,128)S(1)}, f32[4,64,64]{2,1,0:T(8,128)S(1)}, u32[]{:S(2)}, u32[]{:S(2)}) collective-permute-start(f32[4,64,64]{2,1,0:T(8,128)S(1)} %dynamic-slice_bitcast_fusion.3), channel_id=1, source_target_pairs={{0,4},{4,12},{12,20},{20,28},{28,24},{24,16},{16,8},{8,0},{1,5},{5... | collective-permute-start | bytes 196616 | tf_op jit(solution)/shard_map/ppermute | solution.py:73
  220.6 12.0 %collective-permute-start.18 = (f32[4,64,64]{2,1,0:T(8,128)S(1)}, f32[4,64,64]{2,1,0:T(8,128)}, u32[]{:S(2)}, u32[]{:S(2)}) collective-permute-start(f32[4,64,64]{2,1,0:T(8,128)S(1)} %bitcast_add_fusion.24), channel_id=1, source_target_pairs={{0,4},{4,12},{12,20},{20,28},{28,24},{24,16},{16,8},{8,0},{1,5},{5... | collective-permute-start | bytes 196616 | tf_op jit(solution)/shard_map/ppermute | solution.py:73
  226.1 14.3 %collective-permute-start.26 = (f32[4,64,64]{2,1,0:T(8,128)S(1)}, f32[4,64,64]{2,1,0:T(8,128)S(1)}, u32[]{:S(2)}, u32[]{:S(2)}) collective-permute-start(f32[4,64,64]{2,1,0:T(8,128)S(1)} %bitcast_add_fusion.16), channel_id=1, source_target_pairs={{0,8},{4,0},{12,4},{20,12},{28,20},{24,28},{16,24},{8,16},{1,9},{5... | collective-permute-start | bytes 196616 | tf_op jit(solution)/shard_map/ppermute | solution.py:73
  230.5 7.2 %collective-permute-start.7 = (f32[16,16,256]{2,0,1:T(8,128)S(1)}, f32[16,16,256]{2,0,1:T(8,128)S(1)}, u32[]{:S(2)}, u32[]{:S(2)}) collective-permute-start(f32[16,16,256]{2,0,1:T(8,128)S(1)} %dynamic-slice_bitcast_fusion), channel_id=1, source_target_pairs={{0,8},{4,0},{12,4},{20,12},{28,20},{24,28},{16,24},{8,16},{1,9},{5... | collective-permute-start | bytes 786440 | tf_op jit(solution)/shard_map/ppermute | solution.py:73
  232.2 8.2 %collective-permute-start = (f32[16,16,256]{2,0,1:T(8,128)S(1)}, f32[16,16,256]{2,0,1:T(8,128)S(1)}, u32[]{:S(2)}, u32[]{:S(2)}) collective-permute-start(f32[16,16,256]{2,0,1:T(8,128)S(1)} %dynamic-slice_bitcast_fusion.1), channel_id=1, source_target_pairs={{0,4},{4,12},{12,20},{20,28},{28,24},{24,16},{16,8},{8,0},{1,5},{5... | collective-permute-start | bytes 786440 | tf_op jit(solution)/shard_map/ppermute | solution.py:73
  233.5 15.9 %collective-permute-start.19 = (f32[4,64,64]{2,1,0:T(8,128)S(1)}, f32[4,64,64]{2,1,0:T(8,128)S(1)}, u32[]{:S(2)}, u32[]{:S(2)}) collective-permute-start(f32[4,64,64]{2,1,0:T(8,128)S(1)} %bitcast_add_fusion.23), channel_id=1, source_target_pairs={{0,4},{4,12},{12,20},{20,28},{28,24},{24,16},{16,8},{8,0},{1,5},{5... | collective-permute-start | bytes 196616 | tf_op jit(solution)/shard_map/ppermute | solution.py:73
  237.7 9.0 %collective-permute-start.8 = (f32[16,16,256]{2,0,1:T(8,128)S(1)}, f32[16,16,256]{2,0,1:T(8,128)S(1)}, u32[]{:S(2)}, u32[]{:S(2)}) collective-permute-start(f32[16,16,256]{2,0,1:T(8,128)S(1)} %bitcast_add_fusion.6), channel_id=1, source_target_pairs={{0,8},{4,0},{12,4},{20,12},{28,20},{24,28},{16,24},{8,16},{1,9},{5... | collective-permute-start | bytes 786440 | tf_op jit(solution)/shard_map/ppermute | solution.py:73
  240.4 8.9 %collective-permute-start.1 = (f32[16,16,256]{2,0,1:T(8,128)S(1)}, f32[16,16,256]{2,0,1:T(8,128)S(1)}, u32[]{:S(2)}, u32[]{:S(2)}) collective-permute-start(f32[16,16,256]{2,0,1:T(8,128)S(1)} %bitcast_add_fusion.13), channel_id=1, source_target_pairs={{0,4},{4,12},{12,20},{20,28},{28,24},{24,16},{16,8},{8,0},{1,5},{5... | collective-permute-start | bytes 786440 | tf_op jit(solution)/shard_map/ppermute | solution.py:73
  241.4 17.0 %collective-permute-start.27 = (f32[4,64,64]{2,1,0:T(8,128)S(1)}, f32[4,64,64]{2,1,0:T(8,128)S(1)}, u32[]{:S(2)}, u32[]{:S(2)}) collective-permute-start(f32[4,64,64]{2,1,0:T(8,128)S(1)} %bitcast_add_fusion.15), channel_id=1, source_target_pairs={{0,8},{4,0},{12,4},{20,12},{28,20},{24,28},{16,24},{8,16},{1,9},{5... | collective-permute-start | bytes 196616 | tf_op jit(solution)/shard_map/ppermute | solution.py:73
  246.8 9.0 %collective-permute-start.9 = (f32[16,16,256]{2,0,1:T(8,128)S(1)}, f32[16,16,256]{2,0,1:T(8,128)S(1)}, u32[]{:S(2)}, u32[]{:S(2)}) collective-permute-start(f32[16,16,256]{2,0,1:T(8,128)S(1)} %bitcast_add_fusion.5), channel_id=1, source_target_pairs={{0,8},{4,0},{12,4},{20,12},{28,20},{24,28},{16,24},{8,16},{1,9},{5... | collective-permute-start | bytes 786440 | tf_op jit(solution)/shard_map/ppermute | solution.py:73
  249.3 9.0 %collective-permute-start.2 = (f32[16,16,256]{2,0,1:T(8,128)S(1)}, f32[16,16,256]{2,0,1:T(8,128)S(1)}, u32[]{:S(2)}, u32[]{:S(2)}) collective-permute-start(f32[16,16,256]{2,0,1:T(8,128)S(1)} %bitcast_add_fusion.12), channel_id=1, source_target_pairs={{0,4},{4,12},{12,20},{20,28},{28,24},{24,16},{16,8},{8,0},{1,5},{5... | collective-permute-start | bytes 786440 | tf_op jit(solution)/shard_map/ppermute | solution.py:73
  249.4 17.5 %collective-permute-start.20 = (f32[4,64,64]{2,1,0:T(8,128)S(1)}, f32[4,64,64]{2,1,0:T(8,128)S(1)}, u32[]{:S(2)}, u32[]{:S(2)}) collective-permute-start(f32[4,64,64]{2,1,0:T(8,128)S(1)} %bitcast_add_fusion.22), channel_id=1, source_target_pairs={{0,4},{4,12},{12,20},{20,28},{28,24},{24,16},{16,8},{8,0},{1,5},{5... | collective-permute-start | bytes 196616 | tf_op jit(solution)/shard_map/ppermute | solution.py:73
  255.8 8.9 %collective-permute-start.10 = (f32[16,16,256]{2,0,1:T(8,128)S(1)}, f32[16,16,256]{2,0,1:T(8,128)S(1)}, u32[]{:S(2)}, u32[]{:S(2)}) collective-permute-start(f32[16,16,256]{2,0,1:T(8,128)S(1)} %bitcast_add_fusion.4), channel_id=1, source_target_pairs={{0,8},{4,0},{12,4},{20,12},{28,20},{24,28},{16,24},{8,16},{1,9},{5... | collective-permute-start | bytes 786440 | tf_op jit(solution)/shard_map/ppermute | solution.py:73
  258.3 8.1 %collective-permute-start.3 = (f32[16,16,256]{2,0,1:T(8,128)S(1)}, f32[16,16,256]{2,0,1:T(8,128)S(1)}, u32[]{:S(2)}, u32[]{:S(2)}) collective-permute-start(f32[16,16,256]{2,0,1:T(8,128)S(1)} %bitcast_add_fusion.11), channel_id=1, source_target_pairs={{0,4},{4,12},{12,20},{20,28},{28,24},{24,16},{16,8},{8,0},{1,5},{5... | collective-permute-start | bytes 786440 | tf_op jit(solution)/shard_map/ppermute | solution.py:73
  264.7 8.0 %collective-permute-start.11 = (f32[16,16,256]{2,0,1:T(8,128)S(1)}, f32[16,16,256]{2,0,1:T(8,128)S(1)}, u32[]{:S(2)}, u32[]{:S(2)}) collective-permute-start(f32[16,16,256]{2,0,1:T(8,128)S(1)} %bitcast_add_fusion.3), channel_id=1, source_target_pairs={{0,8},{4,0},{12,4},{20,12},{28,20},{24,28},{16,24},{8,16},{1,9},{5... | collective-permute-start | bytes 786440 | tf_op jit(solution)/shard_map/ppermute | solution.py:73
  266.5 7.3 %collective-permute-start.4 = (f32[16,16,256]{2,0,1:T(8,128)S(1)}, f32[16,16,256]{2,0,1:T(8,128)S(1)}, u32[]{:S(2)}, u32[]{:S(2)}) collective-permute-start(f32[16,16,256]{2,0,1:T(8,128)S(1)} %bitcast_add_fusion.10), channel_id=1, source_target_pairs={{0,4},{4,12},{12,20},{20,28},{28,24},{24,16},{16,8},{8,0},{1,5},{5... | collective-permute-start | bytes 786440 | tf_op jit(solution)/shard_map/ppermute | solution.py:73
  272.7 8.0 %collective-permute-start.12 = (f32[16,16,256]{2,0,1:T(8,128)S(1)}, f32[16,16,256]{2,0,1:T(8,128)S(1)}, u32[]{:S(2)}, u32[]{:S(2)}) collective-permute-start(f32[16,16,256]{2,0,1:T(8,128)S(1)} %bitcast_add_fusion.2), channel_id=1, source_target_pairs={{0,8},{4,0},{12,4},{20,12},{28,20},{24,28},{16,24},{8,16},{1,9},{5... | collective-permute-start | bytes 786440 | tf_op jit(solution)/shard_map/ppermute | solution.py:73
  273.8 8.3 %collective-permute-start.5 = (f32[16,16,256]{2,0,1:T(8,128)S(1)}, f32[16,16,256]{2,0,1:T(8,128)S(1)}, u32[]{:S(2)}, u32[]{:S(2)}) collective-permute-start(f32[16,16,256]{2,0,1:T(8,128)S(1)} %bitcast_add_fusion.9), channel_id=1, source_target_pairs={{0,4},{4,12},{12,20},{20,28},{28,24},{24,16},{16,8},{8,0},{1,5},{5... | collective-permute-start | bytes 786440 | tf_op jit(solution)/shard_map/ppermute | solution.py:73
  281.7 8.0 %collective-permute-start.13 = (f32[16,16,256]{2,0,1:T(8,128)S(1)}, f32[16,16,256]{2,0,1:T(8,128)S(1)}, u32[]{:S(2)}, u32[]{:S(2)}) collective-permute-start(f32[16,16,256]{2,0,1:T(8,128)S(1)} %bitcast_add_fusion.1), channel_id=1, source_target_pairs={{0,8},{4,0},{12,4},{20,12},{28,20},{24,28},{16,24},{8,16},{1,9},{5... | collective-permute-start | bytes 786440 | tf_op jit(solution)/shard_map/ppermute | solution.py:73
  283.1 7.7 %collective-permute-start.6 = (f32[16,16,256]{2,0,1:T(8,128)S(1)}, f32[16,16,256]{2,0,1:T(8,128)S(1)}, u32[]{:S(2)}, u32[]{:S(2)}) collective-permute-start(f32[16,16,256]{2,0,1:T(8,128)S(1)} %bitcast_add_fusion.8), channel_id=1, source_target_pairs={{0,4},{4,12},{12,20},{20,28},{28,24},{24,16},{16,8},{8,0},{1,5},{5... | collective-permute-start | bytes 786440 | tf_op jit(solution)/shard_map/ppermute | solution.py:73
  (17 other events, 260.7 us)
Sparse Core Ops, SparseCore 0:
  13.1 88.9 all-gather.2

commit v3 on v2

--- a/solution.py
+++ b/solution.py
@@ -85,16 +85,15 @@
     g_cols = lax.all_to_all(g_blocks, "feat", split_axis=1, concat_axis=0, tiled=True)
     local_cols = l_mix.shape[0]
     rows_r = r_mix.shape[1]
-    r_flat = r_mix.reshape(1, -1)
-    packed = jnp.concatenate([r_flat, l_mix.reshape(1, -1)], axis=1)
+    r_lead = jnp.transpose(r_mix, (1, 0, 2)).reshape(-1, WIDTH)
+    l_lead = jnp.transpose(l_mix.reshape(local_cols, -1, BLOCKS), (1, 0, 2)).reshape(-1, WIDTH)
+    r_size = r_lead.shape[0]
+    packed = jnp.concatenate([r_lead, l_lead], axis=0)[None]
     packed = lax.all_gather(packed, "dp", axis=0, tiled=True)
-    r_size = r_flat.shape[1]
-    r_whole = packed[:, :r_size].reshape(n_dp, local_blocks, rows_r, WIDTH)
-    r_whole = jnp.transpose(r_whole, (1, 0, 2, 3)).reshape(local_blocks, n_dp * rows_r, WIDTH)
-    l_whole = packed[:, r_size:].reshape(n_dp, local_cols, -1, BLOCKS)
-    l_blocks = jnp.transpose(l_whole, (0, 2, 1, 3)).reshape(-1, local_cols, BLOCKS)
+    r_whole = packed[:, :r_size].reshape(n_dp * rows_r, local_blocks, WIDTH)
+    l_blocks = packed[:, r_size:].reshape(-1, local_cols, BLOCKS)
     mixed_rows = jnp.einsum(
-        "bit,bio->bot", x_blocks, r_whole, preferred_element_type=jnp.float32
+        "bit,ibo->bot", x_blocks, r_whole, preferred_element_type=jnp.float32
     ).astype(jnp.bfloat16)
     columns = lax.all_to_all(mixed_rows, "feat", split_axis=1, concat_axis=0, tiled=True)
     pre_act = jnp.einsum("bst,bsc->cst", columns, l_blocks, preferred_element_type=jnp.float32)
@@ -107,7 +106,7 @@
     grad_l = ring_reduce_scatter(l_term, ring)
     grad_l = jnp.transpose(grad_l, (1, 0, 2)).reshape(local_cols, -1)
     back_rows = lax.all_to_all(back_cols, "feat", split_axis=1, concat_axis=0, tiled=True)
-    through_r = jnp.einsum("obt,bio->bit", back_rows, r_whole, preferred_element_type=jnp.float32)
+    through_r = jnp.einsum("obt,ibo->bit", back_rows, r_whole, preferred_element_type=jnp.float32)
     grad_x = (
         (g_blocks.astype(jnp.float32) + through_r)
         .astype(jnp.bfloat16)

time: 301 us -> 261 us (0.87)
  waiting for transfers between devices: 122 us -> 96.8 us
  local copies, waits for them, and re-layouts: 44.2 us -> 36.5 us
  starting transfers between devices: 46.6 us -> 41.2 us
    all_gather x1, waiting for transfers between devices: 80.6 us -> 49.2 us  [body(): packed = lax.all_gather(packed, 'dp', axis=0, tiled=True)]
    unnamed x20 -> x17, local copies, waits for them, and re-layouts: 10.3 us -> 2.48 us
    ppermute x28, waiting for transfers between devices: 41.8 us -> 47.6 us  [ring_reduce_scatter(): acc = lax.ppermute(acc, 'dp', pairs)]
    ppermute x28, starting transfers between devices: 32.9 us -> 27.5 us  [ring_reduce_scatter(): acc = lax.ppermute(acc, 'dp', pairs)]
    unnamed x1 -> x0, other arithmetic: 3.62 us -> none
  transfers between devices with their start and end apart: 32 -> 32, of which waited for: 13 -> 16; matrix products, arithmetic and copies ran while one was open for 15% -> 15% of each run, Pallas kernels for 0% -> 0%
where the time goes in v3:
time: 261 us; the launch traced here: 259 us
  waiting for transfers between devices  96.8 us (37%)
  between operations  55.3 us (21%)
  starting transfers between devices  41.2 us (16%)
  local copies, waits for them, and re-layouts  36.5 us (14%)
  matrix products  15.8 us (6%)
  other arithmetic  13.4 us (5%)
    all_gather x1, waiting for transfers between devices, body(): packed = lax.all_gather(packed, 'dp', axis=0, tiled=True)  49.2 us
    ppermute x28, waiting for transfers between devices, ring_reduce_scatter(): acc = lax.ppermute(acc, 'dp', pairs)  47.6 us
    ppermute x28, starting transfers between devices, ring_reduce_scatter(): acc = lax.ppermute(acc, 'dp', pairs)  27.5 us
    add x28, other arithmetic, ring_reduce_scatter(): acc = mine if acc is None else acc + mine  11.8 us
  transfers between devices with their start and end apart: 32, of which 16 were waited for; matrix products, arithmetic and copies ran while one was open for 15% of the time, Pallas kernels for 0%

profile of v3, /device:TPU:0, one launch (start us, length us, event | category | flops | bytes accessed | tf_op | source)
XLA Modules:
  0.0 259.0 jit_solution(213690872126595535)
XLA Ops:
  10.4 4.1 %copy.39 = bf16[16,256,256]{2,0,1:T(8,128)(2,1)} copy(bf16[16,256,256]{2,1,0:T(8,128)(2,1)} %bitcast.168) | data formatting | bytes 4194304 | tf_op jit(solution)/shard_map/reshape | solution.py:84
  14.5 4.5 %all-to-all-start = ((bf16[16,256,256]{2,0,1:T(8,128)(2,1)}), bf16[16,256,256]{2,0,1:T(8,128)(2,1)}, u32[]{:S(2)}, u32[]{:S(2)}) async-start(bf16[16,256,256]{2,0,1:T(8,128)(2,1)} %copy.39), calls=%async_computation | async-start | bytes 4194304 | tf_op jit(solution)/shard_map/all_to_all | solution.py:85
  18.9 49.2 %all-gather.3.cloned.1.call-done = bf16[5120,256]{1,0:T(8,128)(2,1)} async-done(((bf16[640,256]{1,0:T(8,128)(2,1)}), bf16[5120,256]{1,0:T(8,128)(2,1)}) %all-gather.3.cloned.1.call-update) | async-done | bytes 2621456 | tf_op jit(solution)/shard_map/all_gather | solution.py:92
  71.4 2.5 copy.42
  73.9 4.8 %all-to-all-start.1 = ((bf16[16,256,256]{2,0,1:T(8,128)(2,1)}), bf16[16,256,256]{2,0,1:T(8,128)(2,1)}, u32[]{:S(2)}, u32[]{:S(2)}) async-start(bf16[16,256,256]{2,0,1:T(8,128)(2,1)} %copy.42), calls=%async_computation.1 | async-start | bytes 4194304 | tf_op jit(solution)/shard_map/all_to_all | solution.py:98
  121.0 4.2 %copy.40 = f32[16,4,64,256]{3,0,1,2:T(8,128)} copy(bf16[16,4,64,256]{3,0,2,1:T(8,128)(2,1)} %bitcast.93) | data formatting | bytes 6291456 | tf_op jit(solution)/shard_map/convert_element_type | solution.py:19
  131.4 5.1 %fusion.6 = bf16[64,64,256]{2,0,1:T(8,128)(2,1)S(1)} fusion(f32[16,4,64,256]{3,0,1,2:T(8,128)S(1)} %copy-done.5, bf16[64,64,256]{2,0,1:T(8,128)(2,1)S(1)} %bitcast.165, bf16[64,64,64]{2,1,0:T(8,128)(2,1)S(1)} %reshape.112), kind=kOutput, calls=%fused_computation.8 | convolution fusion | flops 155189248 | bytes 8912896 | tf_op jit(solution)/shard_map/bst,bsc->cst/dot_general | solution.py:99
  139.9 2.5 copy.46
  142.4 3.8 %copy.49 = f32[64,64,64]{2,1,0:T(8,128)} copy(f32[64,64,64]{0,2,1:T(8,128)} %multiply_bitcast_fusion) | data formatting | bytes 2097152 | tf_op jit(solution)/shard_map/mul | solution.py:105
  146.2 2.7 %fusion.15 = (f32[8,4,64,64]{3,2,1,0:T(8,128)S(1)}, f32[8,4,64,64]{3,2,1,0:T(8,128)}) fusion(f32[8,8,64,64]{3,2,1,0:T(8,128)} %bitcast.167), kind=kLoop, calls=%fused_computation.60 | loop fusion | bytes 2097152 | tf_op jit(solution)/shard_map/slice | solution.py:62
  148.9 4.5 %all-to-all-start.2 = ((bf16[64,64,256]{2,0,1:T(8,128)(2,1)}), bf16[64,64,256]{2,0,1:T(8,128)(2,1)}, u32[]{:S(2)}, u32[]{:S(2)}) async-start(bf16[64,64,256]{2,0,1:T(8,128)(2,1)} %copy.46), calls=%async_computation.2 | async-start | bytes 4194304 | tf_op jit(solution)/shard_map/all_to_all | solution.py:108
  156.4 3.8 %collective-permute-done.21 = f32[4,64,64]{2,1,0:T(8,128)S(1)} collective-permute-done((f32[4,64,64]{2,1,0:T(8,128)S(1)}, f32[4,64,64]{2,1,0:T(8,128)S(1)}, u32[]{:S(2)}, u32[]{:S(2)}) %collective-permute-start.21) | collective-permute-done | bytes 65568 | tf_op jit(solution)/shard_map/ppermute | solution.py:73
  163.2 3.1 %collective-permute-done.22 = f32[4,64,64]{2,1,0:T(8,128)S(1)} collective-permute-done((f32[4,64,64]{2,1,0:T(8,128)S(1)}, f32[4,64,64]{2,1,0:T(8,128)S(1)}, u32[]{:S(2)}, u32[]{:S(2)}) %collective-permute-start.22) | collective-permute-done | bytes 65568 | tf_op jit(solution)/shard_map/ppermute | solution.py:73
  169.4 2.9 %collective-permute-done.23 = f32[4,64,64]{2,1,0:T(8,128)S(1)} collective-permute-done((f32[4,64,64]{2,1,0:T(8,128)S(1)}, f32[4,64,64]{2,1,0:T(8,128)S(1)}, u32[]{:S(2)}, u32[]{:S(2)}) %collective-permute-start.23) | collective-permute-done | bytes 65568 | tf_op jit(solution)/shard_map/ppermute | solution.py:73
  175.3 2.9 %collective-permute-done.24 = f32[4,64,64]{2,1,0:T(8,128)S(1)} collective-permute-done((f32[4,64,64]{2,1,0:T(8,128)S(1)}, f32[4,64,64]{2,1,0:T(8,128)S(1)}, u32[]{:S(2)}, u32[]{:S(2)}) %collective-permute-start.24) | collective-permute-done | bytes 65568 | tf_op jit(solution)/shard_map/ppermute | solution.py:73
  181.3 2.9 %collective-permute-done.25 = f32[4,64,64]{2,1,0:T(8,128)S(1)} collective-permute-done((f32[4,64,64]{2,1,0:T(8,128)S(1)}, f32[4,64,64]{2,1,0:T(8,128)S(1)}, u32[]{:S(2)}, u32[]{:S(2)}) %collective-permute-start.25) | collective-permute-done | bytes 65568 | tf_op jit(solution)/shard_map/ppermute | solution.py:73
  194.2 4.2 %collective-permute-done.7 = f32[16,16,256]{2,0,1:T(8,128)S(1)} collective-permute-done((f32[16,16,256]{2,0,1:T(8,128)S(1)}, f32[16,16,256]{2,0,1:T(8,128)S(1)}, u32[]{:S(2)}, u32[]{:S(2)}) %collective-permute-start.7) | collective-permute-done | bytes 262176 | tf_op jit(solution)/shard_map/ppermute | solution.py:73
  202.4 4.9 %collective-permute-done.8 = f32[16,16,256]{2,0,1:T(8,128)S(1)} collective-permute-done((f32[16,16,256]{2,0,1:T(8,128)S(1)}, f32[16,16,256]{2,0,1:T(8,128)S(1)}, u32[]{:S(2)}, u32[]{:S(2)}) %collective-permute-start.8) | collective-permute-done | bytes 262176 | tf_op jit(solution)/shard_map/ppermute | solution.py:73
  207.4 2.3 collective-permute-start.2
  210.3 6.2 %collective-permute-done.9 = f32[16,16,256]{2,0,1:T(8,128)S(1)} collective-permute-done((f32[16,16,256]{2,0,1:T(8,128)S(1)}, f32[16,16,256]{2,0,1:T(8,128)S(1)}, u32[]{:S(2)}, u32[]{:S(2)}) %collective-permute-start.9) | collective-permute-done | bytes 262176 | tf_op jit(solution)/shard_map/ppermute | solution.py:73
  219.7 5.3 %collective-permute-done.10 = f32[16,16,256]{2,0,1:T(8,128)S(1)} collective-permute-done((f32[16,16,256]{2,0,1:T(8,128)S(1)}, f32[16,16,256]{2,0,1:T(8,128)S(1)}, u32[]{:S(2)}, u32[]{:S(2)}) %collective-permute-start.10) | collective-permute-done | bytes 262176 | tf_op jit(solution)/shard_map/ppermute | solution.py:73
  227.2 5.3 %collective-permute-done.11 = f32[16,16,256]{2,0,1:T(8,128)S(1)} collective-permute-done((f32[16,16,256]{2,0,1:T(8,128)S(1)}, f32[16,16,256]{2,0,1:T(8,128)S(1)}, u32[]{:S(2)}, u32[]{:S(2)}) %collective-permute-start.11) | collective-permute-done | bytes 262176 | tf_op jit(solution)/shard_map/ppermute | solution.py:73
  235.7 4.4 %collective-permute-done.12 = f32[16,16,256]{2,0,1:T(8,128)S(1)} collective-permute-done((f32[16,16,256]{2,0,1:T(8,128)S(1)}, f32[16,16,256]{2,0,1:T(8,128)S(1)}, u32[]{:S(2)}, u32[]{:S(2)}) %collective-permute-start.12) | collective-permute-done | bytes 262176 | tf_op jit(solution)/shard_map/ppermute | solution.py:73
  244.2 5.1 %add_convert_fusion = bf16[16,256,256]{2,1,0:T(8,128)(2,1)} fusion(bf16[16,256,256]{2,1,0:T(8,128)(2,1)} %bitcast.169, bf16[256,16,256]{2,0,1:T(8,128)(2,1)} %bitcast.163, bf16[256,16,256]{2,1,0:T(8,128)(2,1)} %bitcast.161), kind=kOutput, calls=%fused_computation.14 | convolution fusion | flops 540016640 | bytes 8388608 | tf_op jit(solution)/shard_map/obt,ibo->bit/dot_general | solution.py:109
  (118 shorter events, 62.8 us)
Async XLA Ops:
  7.2 61.0 %all-gather.3.cloned.1.call-start = ((), (), s32[]{:S(2)}) async-start(), calls=%async_computation.3 | async-start | bytes 2949120 | tf_op jit(solution)/shard_map/all_gather | solution.py:92
  14.5 59.4 %all-to-all-start = ((bf16[16,256,256]{2,0,1:T(8,128)(2,1)}), bf16[16,256,256]{2,0,1:T(8,128)(2,1)}, u32[]{:S(2)}, u32[]{:S(2)}) async-start(bf16[16,256,256]{2,0,1:T(8,128)(2,1)} %copy.39), calls=%async_computation | async-start | bytes 4194304 | tf_op jit(solution)/shard_map/all_to_all | solution.py:85
  73.9 54.7 %all-to-all-start.1 = ((bf16[16,256,256]{2,0,1:T(8,128)(2,1)}), bf16[16,256,256]{2,0,1:T(8,128)(2,1)}, u32[]{:S(2)}, u32[]{:S(2)}) async-start(bf16[16,256,256]{2,0,1:T(8,128)(2,1)} %copy.42), calls=%async_computation.1 | async-start | bytes 4194304 | tf_op jit(solution)/shard_map/all_to_all | solution.py:98
  148.9 37.8 %all-to-all-start.2 = ((bf16[64,64,256]{2,0,1:T(8,128)(2,1)}), bf16[64,64,256]{2,0,1:T(8,128)(2,1)}, u32[]{:S(2)}, u32[]{:S(2)}) async-start(bf16[64,64,256]{2,0,1:T(8,128)(2,1)} %copy.46), calls=%async_computation.2 | async-start | bytes 4194304 | tf_op jit(solution)/shard_map/all_to_all | solution.py:108
  155.8 6.8 %collective-permute-start.14 = (f32[4,64,64]{2,1,0:T(8,128)S(1)}, f32[4,64,64]{2,1,0:T(8,128)S(1)}, u32[]{:S(2)}, u32[]{:S(2)}) collective-permute-start(f32[4,64,64]{2,1,0:T(8,128)S(1)} %dynamic-slice_bitcast_fusion.3), channel_id=1, source_target_pairs={{0,4},{4,12},{12,20},{20,28},{28,24},{24,16},{16,8},{8,0},{1,5},{5... | collective-permute-start | bytes 196616 | tf_op jit(solution)/shard_map/ppermute | solution.py:73
  180.7 12.0 %collective-permute-start.18 = (f32[4,64,64]{2,1,0:T(8,128)S(1)}, f32[4,64,64]{2,1,0:T(8,128)}, u32[]{:S(2)}, u32[]{:S(2)}) collective-permute-start(f32[4,64,64]{2,1,0:T(8,128)S(1)} %bitcast_add_fusion.24), channel_id=1, source_target_pairs={{0,4},{4,12},{12,20},{20,28},{28,24},{24,16},{16,8},{8,0},{1,5},{5... | collective-permute-start | bytes 196616 | tf_op jit(solution)/shard_map/ppermute | solution.py:73
  185.1 15.8 %collective-permute-start.26 = (f32[4,64,64]{2,1,0:T(8,128)S(1)}, f32[4,64,64]{2,1,0:T(8,128)S(1)}, u32[]{:S(2)}, u32[]{:S(2)}) collective-permute-start(f32[4,64,64]{2,1,0:T(8,128)S(1)} %bitcast_add_fusion.16), channel_id=1, source_target_pairs={{0,8},{4,0},{12,4},{20,12},{28,20},{24,28},{16,24},{8,16},{1,9},{5... | collective-permute-start | bytes 196616 | tf_op jit(solution)/shard_map/ppermute | solution.py:73
  190.5 7.9 %collective-permute-start.7 = (f32[16,16,256]{2,0,1:T(8,128)S(1)}, f32[16,16,256]{2,0,1:T(8,128)S(1)}, u32[]{:S(2)}, u32[]{:S(2)}) collective-permute-start(f32[16,16,256]{2,0,1:T(8,128)S(1)} %dynamic-slice_bitcast_fusion), channel_id=1, source_target_pairs={{0,8},{4,0},{12,4},{20,12},{28,20},{24,28},{16,24},{8,16},{1,9},{5... | collective-permute-start | bytes 786440 | tf_op jit(solution)/shard_map/ppermute | solution.py:73
  191.6 7.6 %collective-permute-start = (f32[16,16,256]{2,0,1:T(8,128)S(1)}, f32[16,16,256]{2,0,1:T(8,128)S(1)}, u32[]{:S(2)}, u32[]{:S(2)}) collective-permute-start(f32[16,16,256]{2,0,1:T(8,128)S(1)} %dynamic-slice_bitcast_fusion.1), channel_id=1, source_target_pairs={{0,4},{4,12},{12,20},{20,28},{28,24},{24,16},{16,8},{8,0},{1,5},{5... | collective-permute-start | bytes 786440 | tf_op jit(solution)/shard_map/ppermute | solution.py:73
  193.6 16.1 %collective-permute-start.19 = (f32[4,64,64]{2,1,0:T(8,128)S(1)}, f32[4,64,64]{2,1,0:T(8,128)S(1)}, u32[]{:S(2)}, u32[]{:S(2)}) collective-permute-start(f32[4,64,64]{2,1,0:T(8,128)S(1)} %bitcast_add_fusion.23), channel_id=1, source_target_pairs={{0,4},{4,12},{12,20},{20,28},{28,24},{24,16},{16,8},{8,0},{1,5},{5... | collective-permute-start | bytes 196616 | tf_op jit(solution)/shard_map/ppermute | solution.py:73
  198.5 8.8 %collective-permute-start.8 = (f32[16,16,256]{2,0,1:T(8,128)S(1)}, f32[16,16,256]{2,0,1:T(8,128)S(1)}, u32[]{:S(2)}, u32[]{:S(2)}) collective-permute-start(f32[16,16,256]{2,0,1:T(8,128)S(1)} %bitcast_add_fusion.6), channel_id=1, source_target_pairs={{0,8},{4,0},{12,4},{20,12},{28,20},{24,28},{16,24},{8,16},{1,9},{5... | collective-permute-start | bytes 786440 | tf_op jit(solution)/shard_map/ppermute | solution.py:73
  199.3 8.1 %collective-permute-start.1 = (f32[16,16,256]{2,0,1:T(8,128)S(1)}, f32[16,16,256]{2,0,1:T(8,128)S(1)}, u32[]{:S(2)}, u32[]{:S(2)}) collective-permute-start(f32[16,16,256]{2,0,1:T(8,128)S(1)} %bitcast_add_fusion.13), channel_id=1, source_target_pairs={{0,4},{4,12},{12,20},{20,28},{28,24},{24,16},{16,8},{8,0},{1,5},{5... | collective-permute-start | bytes 786440 | tf_op jit(solution)/shard_map/ppermute | solution.py:73
  201.8 16.9 %collective-permute-start.27 = (f32[4,64,64]{2,1,0:T(8,128)S(1)}, f32[4,64,64]{2,1,0:T(8,128)S(1)}, u32[]{:S(2)}, u32[]{:S(2)}) collective-permute-start(f32[4,64,64]{2,1,0:T(8,128)S(1)} %bitcast_add_fusion.15), channel_id=1, source_target_pairs={{0,8},{4,0},{12,4},{20,12},{28,20},{24,28},{16,24},{8,16},{1,9},{5... | collective-permute-start | bytes 196616 | tf_op jit(solution)/shard_map/ppermute | solution.py:73
  207.3 9.2 %collective-permute-start.9 = (f32[16,16,256]{2,0,1:T(8,128)S(1)}, f32[16,16,256]{2,0,1:T(8,128)S(1)}, u32[]{:S(2)}, u32[]{:S(2)}) collective-permute-start(f32[16,16,256]{2,0,1:T(8,128)S(1)} %bitcast_add_fusion.5), channel_id=1, source_target_pairs={{0,8},{4,0},{12,4},{20,12},{28,20},{24,28},{16,24},{8,16},{1,9},{5... | collective-permute-start | bytes 786440 | tf_op jit(solution)/shard_map/ppermute | solution.py:73
  207.4 9.2 %collective-permute-start.2 = (f32[16,16,256]{2,0,1:T(8,128)S(1)}, f32[16,16,256]{2,0,1:T(8,128)S(1)}, u32[]{:S(2)}, u32[]{:S(2)}) collective-permute-start(f32[16,16,256]{2,0,1:T(8,128)S(1)} %bitcast_add_fusion.12), channel_id=1, source_target_pairs={{0,4},{4,12},{12,20},{20,28},{28,24},{24,16},{16,8},{8,0},{1,5},{5... | collective-permute-start | bytes 786440 | tf_op jit(solution)/shard_map/ppermute | solution.py:73
  209.7 17.4 %collective-permute-start.20 = (f32[4,64,64]{2,1,0:T(8,128)S(1)}, f32[4,64,64]{2,1,0:T(8,128)S(1)}, u32[]{:S(2)}, u32[]{:S(2)}) collective-permute-start(f32[4,64,64]{2,1,0:T(8,128)S(1)} %bitcast_add_fusion.22), channel_id=1, source_target_pairs={{0,4},{4,12},{12,20},{20,28},{28,24},{24,16},{16,8},{8,0},{1,5},{5... | collective-permute-start | bytes 196616 | tf_op jit(solution)/shard_map/ppermute | solution.py:73
  216.6 8.4 %collective-permute-start.10 = (f32[16,16,256]{2,0,1:T(8,128)S(1)}, f32[16,16,256]{2,0,1:T(8,128)S(1)}, u32[]{:S(2)}, u32[]{:S(2)}) collective-permute-start(f32[16,16,256]{2,0,1:T(8,128)S(1)} %bitcast_add_fusion.4), channel_id=1, source_target_pairs={{0,8},{4,0},{12,4},{20,12},{28,20},{24,28},{16,24},{8,16},{1,9},{5... | collective-permute-start | bytes 786440 | tf_op jit(solution)/shard_map/ppermute | solution.py:73
  216.7 9.1 %collective-permute-start.3 = (f32[16,16,256]{2,0,1:T(8,128)S(1)}, f32[16,16,256]{2,0,1:T(8,128)S(1)}, u32[]{:S(2)}, u32[]{:S(2)}) collective-permute-start(f32[16,16,256]{2,0,1:T(8,128)S(1)} %bitcast_add_fusion.11), channel_id=1, source_target_pairs={{0,4},{4,12},{12,20},{20,28},{28,24},{24,16},{16,8},{8,0},{1,5},{5... | collective-permute-start | bytes 786440 | tf_op jit(solution)/shard_map/ppermute | solution.py:73
  225.0 7.5 %collective-permute-start.11 = (f32[16,16,256]{2,0,1:T(8,128)S(1)}, f32[16,16,256]{2,0,1:T(8,128)S(1)}, u32[]{:S(2)}, u32[]{:S(2)}) collective-permute-start(f32[16,16,256]{2,0,1:T(8,128)S(1)} %bitcast_add_fusion.3), channel_id=1, source_target_pairs={{0,8},{4,0},{12,4},{20,12},{28,20},{24,28},{16,24},{8,16},{1,9},{5... | collective-permute-start | bytes 786440 | tf_op jit(solution)/shard_map/ppermute | solution.py:73
  225.8 8.2 %collective-permute-start.4 = (f32[16,16,256]{2,0,1:T(8,128)S(1)}, f32[16,16,256]{2,0,1:T(8,128)S(1)}, u32[]{:S(2)}, u32[]{:S(2)}) collective-permute-start(f32[16,16,256]{2,0,1:T(8,128)S(1)} %bitcast_add_fusion.10), channel_id=1, source_target_pairs={{0,4},{4,12},{12,20},{20,28},{28,24},{24,16},{16,8},{8,0},{1,5},{5... | collective-permute-start | bytes 786440 | tf_op jit(solution)/shard_map/ppermute | solution.py:73
  232.6 7.6 %collective-permute-start.12 = (f32[16,16,256]{2,0,1:T(8,128)S(1)}, f32[16,16,256]{2,0,1:T(8,128)S(1)}, u32[]{:S(2)}, u32[]{:S(2)}) collective-permute-start(f32[16,16,256]{2,0,1:T(8,128)S(1)} %bitcast_add_fusion.2), channel_id=1, source_target_pairs={{0,8},{4,0},{12,4},{20,12},{28,20},{24,28},{16,24},{8,16},{1,9},{5... | collective-permute-start | bytes 786440 | tf_op jit(solution)/shard_map/ppermute | solution.py:73
  234.0 8.3 %collective-permute-start.5 = (f32[16,16,256]{2,0,1:T(8,128)S(1)}, f32[16,16,256]{2,0,1:T(8,128)S(1)}, u32[]{:S(2)}, u32[]{:S(2)}) collective-permute-start(f32[16,16,256]{2,0,1:T(8,128)S(1)} %bitcast_add_fusion.9), channel_id=1, source_target_pairs={{0,4},{4,12},{12,20},{20,28},{28,24},{24,16},{16,8},{8,0},{1,5},{5... | collective-permute-start | bytes 786440 | tf_op jit(solution)/shard_map/ppermute | solution.py:73
  241.1 8.3 %collective-permute-start.13 = (f32[16,16,256]{2,0,1:T(8,128)S(1)}, f32[16,16,256]{2,0,1:T(8,128)S(1)}, u32[]{:S(2)}, u32[]{:S(2)}) collective-permute-start(f32[16,16,256]{2,0,1:T(8,128)S(1)} %bitcast_add_fusion.1), channel_id=1, source_target_pairs={{0,8},{4,0},{12,4},{20,12},{28,20},{24,28},{16,24},{8,16},{1,9},{5... | collective-permute-start | bytes 786440 | tf_op jit(solution)/shard_map/ppermute | solution.py:73
  243.3 7.0 %collective-permute-start.6 = (f32[16,16,256]{2,0,1:T(8,128)S(1)}, f32[16,16,256]{2,0,1:T(8,128)S(1)}, u32[]{:S(2)}, u32[]{:S(2)}) collective-permute-start(f32[16,16,256]{2,0,1:T(8,128)S(1)} %bitcast_add_fusion.8), channel_id=1, source_target_pairs={{0,4},{4,12},{12,20},{20,28},{28,24},{24,16},{16,8},{8,0},{1,5},{5... | collective-permute-start | bytes 786440 | tf_op jit(solution)/shard_map/ppermute | solution.py:73
  (16 other events, 219.0 us)
Sparse Core Ops, SparseCore 0:
  10.8 57.3 all-gather.2

commit v4 on v3

--- a/solution.py
+++ b/solution.py
@@ -82,7 +82,10 @@
     grad_scale = 1.0 / math.sqrt(tok_count * n_dp)
     x_blocks = activations.reshape(local_blocks, WIDTH, tok_count)
     g_blocks = cotangent.reshape(local_blocks, WIDTH, tok_count)
-    g_cols = lax.all_to_all(g_blocks, "feat", split_axis=1, concat_axis=0, tiled=True)
+    n_feat = lax.axis_size("feat")
+    g_out = jnp.transpose(g_blocks.reshape(local_blocks, n_feat, -1, tok_count), (1, 0, 2, 3))
+    g_cols = lax.all_to_all(g_out, "feat", split_axis=0, concat_axis=0, tiled=True)
+    g_cols = g_cols.reshape(-1, WIDTH // n_feat, tok_count)
     local_cols = l_mix.shape[0]
     rows_r = r_mix.shape[1]
     r_lead = jnp.transpose(r_mix, (1, 0, 2)).reshape(-1, WIDTH)
@@ -92,28 +95,31 @@
     packed = lax.all_gather(packed, "dp", axis=0, tiled=True)
     r_whole = packed[:, :r_size].reshape(n_dp * rows_r, local_blocks, WIDTH)
     l_blocks = packed[:, r_size:].reshape(-1, local_cols, BLOCKS)
-    mixed_rows = jnp.einsum(
-        "bit,ibo->bot", x_blocks, r_whole, preferred_element_type=jnp.float32
+    r_split = r_whole.reshape(n_dp * rows_r, local_blocks, n_feat, -1)
+    mixed_out = jnp.einsum(
+        "bit,ibqs->qbst", x_blocks, r_split, preferred_element_type=jnp.float32
     ).astype(jnp.bfloat16)
-    columns = lax.all_to_all(mixed_rows, "feat", split_axis=1, concat_axis=0, tiled=True)
+    columns = lax.all_to_all(mixed_out, "feat", split_axis=0, concat_axis=0, tiled=True)
+    columns = columns.reshape(-1, WIDTH // n_feat, tok_count)
     pre_act = jnp.einsum("bst,bsc->cst", columns, l_blocks, preferred_element_type=jnp.float32)
     slope_cols = slope_of(pre_act, g_cols)
     back_cols = jnp.einsum(
-        "cst,bsc->sbt", slope_cols, l_blocks, preferred_element_type=jnp.float32
+        "cst,bsc->bst", slope_cols, l_blocks, preferred_element_type=jnp.float32
     ).astype(jnp.bfloat16)
     l_term = jnp.einsum("bst,cst->bsc", columns, slope_cols, preferred_element_type=jnp.float32)
     l_term = (l_term * grad_scale).reshape(n_dp, -1, local_cols, BLOCKS)
     grad_l = ring_reduce_scatter(l_term, ring)
     grad_l = jnp.transpose(grad_l, (1, 0, 2)).reshape(local_cols, -1)
-    back_rows = lax.all_to_all(back_cols, "feat", split_axis=1, concat_axis=0, tiled=True)
-    through_r = jnp.einsum("obt,ibo->bit", back_rows, r_whole, preferred_element_type=jnp.float32)
+    back_out = back_cols.reshape(n_feat, local_blocks, -1, tok_count)
+    back_rows = lax.all_to_all(back_out, "feat", split_axis=0, concat_axis=0, tiled=True)
+    through_r = jnp.einsum("qbst,ibqs->bit", back_rows, r_split, preferred_element_type=jnp.float32)
     grad_x = (
         (g_blocks.astype(jnp.float32) + through_r)
         .astype(jnp.bfloat16)
         .reshape(local_blocks * WIDTH, tok_count)
     )
     r_term = (
-        jnp.einsum("bit,obt->ibo", x_blocks, back_rows, preferred_element_type=jnp.float32)
+        jnp.einsum("bit,qbst->ibqs", x_blocks, back_rows, preferred_element_type=jnp.float32)
         * grad_scale
     ).reshape(n_dp, rows_r, local_blocks, WIDTH)
     grad_r = ring_reduce_scatter(r_term, ring)

time: 261 us -> 295 us (1.13)
  local copies, waits for them, and re-layouts: 36.5 us -> 66.5 us
  matrix products: 15.8 us -> 24.5 us
  waiting for transfers between devices: 96.8 us -> 91.1 us
    another operation x0 -> x2, local copies, waits for them, and re-layouts: none -> 14.2 us  [body(): r_split = r_whole.reshape(n_dp * rows_r, local_blocks, n_feat, -1)]
    mul x0 -> x1, local copies, waits for them, and re-layouts: none -> 8.74 us  [body(): jnp.einsum('bit,qbst->ibqs', x_blocks, back_rows, preferred_element_type=...]
    reshape x1 -> x2, local copies, waits for them, and re-layouts: 4.09 us -> 11.1 us  [the longest x1 8.58 us: body(): r_term = (jnp.einsum('bit,qbst->ibqs', x_blocks, back_rows, preferred_ele...]
    ppermute x28, waiting for transfers between devices: 47.6 us -> 41.9 us  [ring_reduce_scatter(): acc = lax.ppermute(acc, 'dp', pairs)]
    dot_general x4, matrix products: 8.7 us -> 13 us  [the longest x1 5.06 us: body(): jnp.einsum('qbst,ibqs->bit', back_rows, r_split, preferred_element_type=j...]
    transpose x0 -> x1, local copies, waits for them, and re-layouts: none -> 4.1 us  [body(): jnp.transpose(g_blocks.reshape(local_blocks, n_feat, -1, tok_count), (1,...]
    all_to_all x2 -> x0, local copies, waits for them, and re-layouts: 3.86 us -> none  [the longest x1 2.03 us: body(): lax.all_to_all(mixed_rows, 'feat', split_axis=1, concat_axis=0, tiled=True)]
    convert_element_type x2 -> x1, local copies, waits for them, and re-layouts: 5.01 us -> 1.46 us  [body(): mixed_out = jnp.einsum('bit,ibqs->qbst', x_blocks, r_split, preferred_ele...]
  transfers between devices with their start and end apart: 32 -> 32, of which waited for: 16 -> 17; matrix products, arithmetic and copies ran while one was open for 15% -> 26% of each run, Pallas kernels for 0% -> 0%
where the time goes in v4:
time: 295 us; the launch traced here: 293 us
  waiting for transfers between devices  91.1 us (31%)
  local copies, waits for them, and re-layouts  66.5 us (23%)
  between operations  54.7 us (19%)
  starting transfers between devices  43.2 us (15%)
  matrix products  24.5 us (8%)
  other arithmetic  12.6 us (4%)
    all_gather x1, waiting for transfers between devices, body(): packed = lax.all_gather(packed, 'dp', axis=0, tiled=True)  49.2 us
    ppermute x28, waiting for transfers between devices, ring_reduce_scatter(): acc = lax.ppermute(acc, 'dp', pairs)  41.9 us
    ppermute x28, starting transfers between devices, ring_reduce_scatter(): acc = lax.ppermute(acc, 'dp', pairs)  29.5 us
    another operation x2, local copies, waits for them, and re-layouts, body(): r_split = r_whole.reshape(n_dp * rows_r, local_blocks, n_feat, -1)  14.2 us
    add x28, other arithmetic, ring_reduce_scatter(): acc = mine if acc is None else acc + mine  11.8 us
    mul x1, local copies, waits for them, and re-layouts, body(): jnp.einsum('bit,qbst->ibqs', x_blocks, back_rows, preferred_element_type=...  8.74 us
    reshape x1, local copies, waits for them, and re-layouts, body(): r_term = (jnp.einsum('bit,qbst->ibqs', x_blocks, back_rows, preferred_ele...  8.58 us
    dot_general x1, matrix products, body(): jnp.einsum('bst,bsc->cst', columns, l_blocks, preferred_element_type=jnp....  7 us
  transfers between devices with their start and end apart: 32, of which 17 were waited for; matrix products, arithmetic and copies ran while one was open for 26% of the time, Pallas kernels for 0%

profile of v4, /device:TPU:0, one launch (start us, length us, event | category | flops | bytes accessed | tf_op | source)
XLA Modules:
  0.0 292.8 jit_solution(17096070395247927859)
XLA Ops:
  10.4 4.1 %copy.77 = bf16[4,16,64,256]{3,1,2,0:T(8,128)(2,1)} copy(bf16[4,16,64,256]{3,2,0,1:T(8,128)(2,1)} %bitcast.165) | data formatting | bytes 4194304 | tf_op jit(solution)/shard_map/transpose | solution.py:86
  14.5 4.4 %all-to-all-start = ((bf16[4,16,64,256]{3,1,2,0:T(8,128)(2,1)}), bf16[4,16,64,256]{3,1,2,0:T(8,128)(2,1)}, u32[]{:S(2)}, u32[]{:S(2)}) async-start(bf16[4,16,64,256]{3,1,2,0:T(8,128)(2,1)} %copy.77), calls=%async_computation | async-start | bytes 4194304 | tf_op jit(solution)/shard_map/all_to_all | solution.py:87
  18.9 49.2 %all-gather.3.cloned.1.call-done = bf16[5120,256]{1,0:T(8,128)(2,1)} async-done(((bf16[640,256]{1,0:T(8,128)(2,1)}), bf16[5120,256]{1,0:T(8,128)(2,1)}) %all-gather.3.cloned.1.call-update) | async-done | bytes 2621456 | tf_op jit(solution)/shard_map/all_gather | solution.py:95
  68.2 3.0 %slice.24 = bf16[8,512,256]{2,1,0:T(8,128)(2,1)} slice(bf16[8,640,256]{2,1,0:T(8,128)(2,1)} %bitcast.163), slice={[0:8], [0:512], [0:256]} | slice | bytes 4194304 | tf_op jit(solution)/shard_map/slice | solution.py:96
  71.2 7.1 %reshape_reshape.6 = bf16[256,16,4,64]{3,2,1,0:T(4,128)(2,1)} reshape(bf16[8,512,256]{2,1,0:T(8,128)(2,1)} %slice.24) | data formatting | bytes 4194304 | tf_op jit(solution)/shard_map/reshape;reshape | solution.py:98
  78.3 7.2 %copy.85 = bf16[256,16,4,64]{0,3,2,1:T(8,128)(2,1)} copy(bf16[256,16,4,64]{3,2,1,0:T(4,128)(2,1)} %reshape_reshape.6) | data formatting | bytes 4194304 | tf_op jit(solution)/shard_map/reshape;reshape | solution.py:98
  89.2 4.8 %all-to-all-start.1 = ((bf16[4,16,64,256]{3,2,1,0:T(8,128)(2,1)}), bf16[4,16,64,256]{3,2,1,0:T(8,128)(2,1)}, u32[]{:S(2)}, u32[]{:S(2)}) async-start(bf16[4,16,64,256]{3,2,1,0:T(8,128)(2,1)} %copy.80), calls=%async_computation.1 | async-start | bytes 4194304 | tf_op jit(solution)/shard_map/all_to_all | solution.py:102
  135.8 4.2 %copy.78 = f32[4,16,64,256]{3,1,0,2:T(8,128)} copy(bf16[4,16,64,256]{3,1,2,0:T(8,128)(2,1)} %all-to-all-done) | data formatting | bytes 6291456 | tf_op jit(solution)/shard_map/convert_element_type | solution.py:19
  143.5 7.0 %fusion.6 = bf16[64,64,256]{2,0,1:T(8,128)(2,1)S(1)} fusion(f32[4,16,64,256]{3,1,0,2:T(8,128)} %copy.78, bf16[64,64,256]{2,1,0:T(8,128)(2,1)} %bitcast.12, bf16[64,64,64]{2,1,0:T(8,128)(2,1)S(1)} %reshape.112), kind=kOutput, calls=%fused_computation.8 | convolution fusion | flops 155189248 | bytes 8912896 | tf_op jit(solution)/shard_map/bst,bsc->cst/dot_general | solution.py:104
  150.5 4.5 %multiply_bitcast_fusion.1 = f32[64,64,64]{0,2,1:T(8,128)} fusion(bf16[64,64,256]{2,0,1:T(8,128)(2,1)S(1)} %fusion.6, bf16[64,64,256]{2,1,0:T(8,128)(2,1)} %bitcast.12), kind=kOutput, calls=%fused_computation.17 | convolution fusion | flops 134479872 | bytes 5242880 | tf_op jit(solution)/shard_map/bst,cst->bsc/dot_general | solution.py:109
  158.8 3.8 %copy.90 = f32[64,64,64]{2,1,0:T(8,128)} copy(f32[64,64,64]{0,2,1:T(8,128)} %multiply_bitcast_fusion.1) | data formatting | bytes 2097152 | tf_op jit(solution)/shard_map/mul | solution.py:110
  165.3 4.5 %all-to-all-start.2 = ((bf16[4,16,64,256]{3,2,1,0:T(8,128)(2,1)}), bf16[4,16,64,256]{3,2,1,0:T(8,128)(2,1)}, u32[]{:S(2)}, u32[]{:S(2)}) async-start(bf16[4,16,64,256]{3,2,1,0:T(8,128)(2,1)} %copy.84), calls=%async_computation.2 | async-start | bytes 4194304 | tf_op jit(solution)/shard_map/all_to_all | solution.py:114
  172.9 3.8 %collective-permute-done.21 = f32[4,64,64]{2,1,0:T(8,128)S(1)} collective-permute-done((f32[4,64,64]{2,1,0:T(8,128)S(1)}, f32[4,64,64]{2,1,0:T(8,128)S(1)}, u32[]{:S(2)}, u32[]{:S(2)}) %collective-permute-start.21) | collective-permute-done | bytes 65568 | tf_op jit(solution)/shard_map/ppermute | solution.py:73
  179.7 3.1 %collective-permute-done.22 = f32[4,64,64]{2,1,0:T(8,128)S(1)} collective-permute-done((f32[4,64,64]{2,1,0:T(8,128)S(1)}, f32[4,64,64]{2,1,0:T(8,128)S(1)}, u32[]{:S(2)}, u32[]{:S(2)}) %collective-permute-start.22) | collective-permute-done | bytes 65568 | tf_op jit(solution)/shard_map/ppermute | solution.py:73
  203.3 4.4 %multiply_bitcast_fusion = f32[256,16,4,64]{0,3,2,1:T(8,128)} fusion(bf16[16,256,256,1]{2,1,3,0:T(8,128)(2,1)S(1)} %bitcast.160, bf16[4,16,64,256]{3,2,1,0:T(8,128)(2,1)} %all-to-all-done.2), kind=kOutput, calls=%fused_computation.16 | convolution fusion | flops 537919488 | bytes 8388608 | tf_op jit(solution)/shard_map/bit,qbst->ibqs/dot_general | solution.py:122
  207.7 8.7 %copy.88 = f32[256,16,4,64]{3,2,1,0:T(4,128)} copy(f32[256,16,4,64]{0,3,2,1:T(8,128)} %multiply_bitcast_fusion) | data formatting | bytes 8388608 | tf_op jit(solution)/shard_map/mul | solution.py:122
  216.4 8.6 %reshape.117 = f32[8,32,16,256]{3,2,1,0:T(8,128)} reshape(f32[256,16,4,64]{3,2,1,0:T(4,128)} %copy.88) | data formatting | bytes 8388608 | tf_op jit(solution)/shard_map/reshape | solution.py:124
  231.7 5.2 %collective-permute-done.7 = f32[16,16,256]{2,1,0:T(8,128)S(1)} collective-permute-done((f32[16,16,256]{2,1,0:T(8,128)S(1)}, f32[16,16,256]{2,1,0:T(8,128)S(1)}, u32[]{:S(2)}, u32[]{:S(2)}) %collective-permute-start.7) | collective-permute-done | bytes 262176 | tf_op jit(solution)/shard_map/ppermute | solution.py:73
  241.2 4.4 %collective-permute-done.8 = f32[16,16,256]{2,1,0:T(8,128)S(1)} collective-permute-done((f32[16,16,256]{2,1,0:T(8,128)S(1)}, f32[16,16,256]{2,1,0:T(8,128)S(1)}, u32[]{:S(2)}, u32[]{:S(2)}) %collective-permute-start.8) | collective-permute-done | bytes 262176 | tf_op jit(solution)/shard_map/ppermute | solution.py:73
  249.1 4.5 %collective-permute-done.9 = f32[16,16,256]{2,1,0:T(8,128)S(1)} collective-permute-done((f32[16,16,256]{2,1,0:T(8,128)S(1)}, f32[16,16,256]{2,1,0:T(8,128)S(1)}, u32[]{:S(2)}, u32[]{:S(2)}) %collective-permute-start.9) | collective-permute-done | bytes 262176 | tf_op jit(solution)/shard_map/ppermute | solution.py:73
  256.9 3.8 %collective-permute-done.10 = f32[16,16,256]{2,1,0:T(8,128)S(1)} collective-permute-done((f32[16,16,256]{2,1,0:T(8,128)S(1)}, f32[16,16,256]{2,1,0:T(8,128)S(1)}, u32[]{:S(2)}, u32[]{:S(2)}) %collective-permute-start.10) | collective-permute-done | bytes 262176 | tf_op jit(solution)/shard_map/ppermute | solution.py:73
  263.0 4.2 %collective-permute-done.11 = f32[16,16,256]{2,1,0:T(8,128)S(1)} collective-permute-done((f32[16,16,256]{2,1,0:T(8,128)S(1)}, f32[16,16,256]{2,1,0:T(8,128)S(1)}, u32[]{:S(2)}, u32[]{:S(2)}) %collective-permute-start.11) | collective-permute-done | bytes 262176 | tf_op jit(solution)/shard_map/ppermute | solution.py:73
  270.4 3.2 %collective-permute-done.12 = f32[16,16,256]{2,1,0:T(8,128)S(1)} collective-permute-done((f32[16,16,256]{2,1,0:T(8,128)S(1)}, f32[16,16,256]{2,1,0:T(8,128)S(1)}, u32[]{:S(2)}, u32[]{:S(2)}) %collective-permute-start.12) | collective-permute-done | bytes 262176 | tf_op jit(solution)/shard_map/ppermute | solution.py:73
  277.7 5.1 %fusion.7 = bf16[16,256,256]{2,1,0:T(8,128)(2,1)} fusion(bf16[16,256,256]{2,1,0:T(8,128)(2,1)} %bitcast.166, bf16[256,16,4,64]{0,3,2,1:T(8,128)(2,1)} %copy.85, bf16[4,16,64,256]{3,2,1,0:T(8,128)(2,1)} %all-to-all-done.2), kind=kOutput, calls=%fused_computation.10 | convolution fusion | flops 540016640 | bytes 8388608 | tf_op jit(solution)/shard_map/qbst,ibqs->bit/dot_general | solution.py:115
  (115 shorter events, 75.4 us)
Async XLA Ops:
  7.2 61.0 %all-gather.3.cloned.1.call-start = ((), (), s32[]{:S(2)}) async-start(), calls=%async_computation.3 | async-start | bytes 2949120 | tf_op jit(solution)/shard_map/all_gather | solution.py:95
  14.5 74.7 %all-to-all-start = ((bf16[4,16,64,256]{3,1,2,0:T(8,128)(2,1)}), bf16[4,16,64,256]{3,1,2,0:T(8,128)(2,1)}, u32[]{:S(2)}, u32[]{:S(2)}) async-start(bf16[4,16,64,256]{3,1,2,0:T(8,128)(2,1)} %copy.77), calls=%async_computation | async-start | bytes 4194304 | tf_op jit(solution)/shard_map/all_to_all | solution.py:87
  89.2 54.2 %all-to-all-start.1 = ((bf16[4,16,64,256]{3,2,1,0:T(8,128)(2,1)}), bf16[4,16,64,256]{3,2,1,0:T(8,128)(2,1)}, u32[]{:S(2)}, u32[]{:S(2)}) async-start(bf16[4,16,64,256]{3,2,1,0:T(8,128)(2,1)} %copy.80), calls=%async_computation.1 | async-start | bytes 4194304 | tf_op jit(solution)/shard_map/all_to_all | solution.py:102
  165.3 38.0 %all-to-all-start.2 = ((bf16[4,16,64,256]{3,2,1,0:T(8,128)(2,1)}), bf16[4,16,64,256]{3,2,1,0:T(8,128)(2,1)}, u32[]{:S(2)}, u32[]{:S(2)}) async-start(bf16[4,16,64,256]{3,2,1,0:T(8,128)(2,1)} %copy.84), calls=%async_computation.2 | async-start | bytes 4194304 | tf_op jit(solution)/shard_map/all_to_all | solution.py:114
  172.3 6.8 %collective-permute-start.14 = (f32[4,64,64]{2,1,0:T(8,128)S(1)}, f32[4,64,64]{2,1,0:T(8,128)S(1)}, u32[]{:S(2)}, u32[]{:S(2)}) collective-permute-start(f32[4,64,64]{2,1,0:T(8,128)S(1)} %dynamic-slice_bitcast_fusion.3), channel_id=1, source_target_pairs={{0,4},{4,12},{12,20},{20,28},{28,24},{24,16},{16,8},{8,0},{1,5},{5... | collective-permute-start | bytes 196616 | tf_op jit(solution)/shard_map/ppermute | solution.py:73
  197.2 33.0 %collective-permute-start.18 = (f32[4,64,64]{2,1,0:T(8,128)S(1)}, f32[4,64,64]{2,1,0:T(8,128)}, u32[]{:S(2)}, u32[]{:S(2)}) collective-permute-start(f32[4,64,64]{2,1,0:T(8,128)S(1)} %bitcast_add_fusion.24), channel_id=1, source_target_pairs={{0,4},{4,12},{12,20},{20,28},{28,24},{24,16},{16,8},{8,0},{1,5},{5... | collective-permute-start | bytes 196616 | tf_op jit(solution)/shard_map/ppermute | solution.py:73
  201.6 37.7 %collective-permute-start.26 = (f32[4,64,64]{2,1,0:T(8,128)S(1)}, f32[4,64,64]{2,1,0:T(8,128)S(1)}, u32[]{:S(2)}, u32[]{:S(2)}) collective-permute-start(f32[4,64,64]{2,1,0:T(8,128)S(1)} %bitcast_add_fusion.16), channel_id=1, source_target_pairs={{0,8},{4,0},{12,4},{20,12},{28,20},{24,28},{16,24},{8,16},{1,9},{5... | collective-permute-start | bytes 196616 | tf_op jit(solution)/shard_map/ppermute | solution.py:73
  228.0 8.9 %collective-permute-start.7 = (f32[16,16,256]{2,1,0:T(8,128)S(1)}, f32[16,16,256]{2,1,0:T(8,128)S(1)}, u32[]{:S(2)}, u32[]{:S(2)}) collective-permute-start(f32[16,16,256]{2,1,0:T(8,128)S(1)} %dynamic-slice_bitcast_fusion), channel_id=1, source_target_pairs={{0,8},{4,0},{12,4},{20,12},{28,20},{24,28},{16,24},{8,16},{1,9},{5... | collective-permute-start | bytes 786440 | tf_op jit(solution)/shard_map/ppermute | solution.py:73
  229.1 9.1 %collective-permute-start = (f32[16,16,256]{2,1,0:T(8,128)S(1)}, f32[16,16,256]{2,1,0:T(8,128)S(1)}, u32[]{:S(2)}, u32[]{:S(2)}) collective-permute-start(f32[16,16,256]{2,1,0:T(8,128)S(1)} %dynamic-slice_bitcast_fusion.1), channel_id=1, source_target_pairs={{0,4},{4,12},{12,20},{20,28},{28,24},{24,16},{16,8},{8,0},{1,5},{5... | collective-permute-start | bytes 786440 | tf_op jit(solution)/shard_map/ppermute | solution.py:73
  231.1 17.4 %collective-permute-start.19 = (f32[4,64,64]{2,1,0:T(8,128)S(1)}, f32[4,64,64]{2,1,0:T(8,128)S(1)}, u32[]{:S(2)}, u32[]{:S(2)}) collective-permute-start(f32[4,64,64]{2,1,0:T(8,128)S(1)} %bitcast_add_fusion.23), channel_id=1, source_target_pairs={{0,4},{4,12},{12,20},{20,28},{28,24},{24,16},{16,8},{8,0},{1,5},{5... | collective-permute-start | bytes 196616 | tf_op jit(solution)/shard_map/ppermute | solution.py:73
  236.9 8.7 %collective-permute-start.8 = (f32[16,16,256]{2,1,0:T(8,128)S(1)}, f32[16,16,256]{2,1,0:T(8,128)S(1)}, u32[]{:S(2)}, u32[]{:S(2)}) collective-permute-start(f32[16,16,256]{2,1,0:T(8,128)S(1)} %bitcast_add_fusion.6), channel_id=1, source_target_pairs={{0,8},{4,0},{12,4},{20,12},{28,20},{24,28},{16,24},{8,16},{1,9},{5... | collective-permute-start | bytes 786440 | tf_op jit(solution)/shard_map/ppermute | solution.py:73
  238.2 9.2 %collective-permute-start.1 = (f32[16,16,256]{2,1,0:T(8,128)S(1)}, f32[16,16,256]{2,1,0:T(8,128)S(1)}, u32[]{:S(2)}, u32[]{:S(2)}) collective-permute-start(f32[16,16,256]{2,1,0:T(8,128)S(1)} %bitcast_add_fusion.13), channel_id=1, source_target_pairs={{0,4},{4,12},{12,20},{20,28},{28,24},{24,16},{16,8},{8,0},{1,5},{5... | collective-permute-start | bytes 786440 | tf_op jit(solution)/shard_map/ppermute | solution.py:73
  240.2 15.8 %collective-permute-start.27 = (f32[4,64,64]{2,1,0:T(8,128)S(1)}, f32[4,64,64]{2,1,0:T(8,128)S(1)}, u32[]{:S(2)}, u32[]{:S(2)}) collective-permute-start(f32[4,64,64]{2,1,0:T(8,128)S(1)} %bitcast_add_fusion.15), channel_id=1, source_target_pairs={{0,8},{4,0},{12,4},{20,12},{28,20},{24,28},{16,24},{8,16},{1,9},{5... | collective-permute-start | bytes 196616 | tf_op jit(solution)/shard_map/ppermute | solution.py:73
  245.7 7.9 %collective-permute-start.9 = (f32[16,16,256]{2,1,0:T(8,128)S(1)}, f32[16,16,256]{2,1,0:T(8,128)S(1)}, u32[]{:S(2)}, u32[]{:S(2)}) collective-permute-start(f32[16,16,256]{2,1,0:T(8,128)S(1)} %bitcast_add_fusion.5), channel_id=1, source_target_pairs={{0,8},{4,0},{12,4},{20,12},{28,20},{24,28},{16,24},{8,16},{1,9},{5... | collective-permute-start | bytes 786440 | tf_op jit(solution)/shard_map/ppermute | solution.py:73
  247.4 7.4 %collective-permute-start.2 = (f32[16,16,256]{2,1,0:T(8,128)S(1)}, f32[16,16,256]{2,1,0:T(8,128)S(1)}, u32[]{:S(2)}, u32[]{:S(2)}) collective-permute-start(f32[16,16,256]{2,1,0:T(8,128)S(1)} %bitcast_add_fusion.12), channel_id=1, source_target_pairs={{0,4},{4,12},{12,20},{20,28},{28,24},{24,16},{16,8},{8,0},{1,5},{5... | collective-permute-start | bytes 786440 | tf_op jit(solution)/shard_map/ppermute | solution.py:73
  248.5 14.5 %collective-permute-start.20 = (f32[4,64,64]{2,1,0:T(8,128)S(1)}, f32[4,64,64]{2,1,0:T(8,128)S(1)}, u32[]{:S(2)}, u32[]{:S(2)}) collective-permute-start(f32[4,64,64]{2,1,0:T(8,128)S(1)} %bitcast_add_fusion.22), channel_id=1, source_target_pairs={{0,4},{4,12},{12,20},{20,28},{28,24},{24,16},{16,8},{8,0},{1,5},{5... | collective-permute-start | bytes 196616 | tf_op jit(solution)/shard_map/ppermute | solution.py:73
  253.7 7.0 %collective-permute-start.10 = (f32[16,16,256]{2,1,0:T(8,128)S(1)}, f32[16,16,256]{2,1,0:T(8,128)S(1)}, u32[]{:S(2)}, u32[]{:S(2)}) collective-permute-start(f32[16,16,256]{2,1,0:T(8,128)S(1)} %bitcast_add_fusion.4), channel_id=1, source_target_pairs={{0,8},{4,0},{12,4},{20,12},{28,20},{24,28},{16,24},{8,16},{1,9},{5... | collective-permute-start | bytes 786440 | tf_op jit(solution)/shard_map/ppermute | solution.py:73
  254.9 7.0 %collective-permute-start.3 = (f32[16,16,256]{2,1,0:T(8,128)S(1)}, f32[16,16,256]{2,1,0:T(8,128)S(1)}, u32[]{:S(2)}, u32[]{:S(2)}) collective-permute-start(f32[16,16,256]{2,1,0:T(8,128)S(1)} %bitcast_add_fusion.11), channel_id=1, source_target_pairs={{0,4},{4,12},{12,20},{20,28},{28,24},{24,16},{16,8},{8,0},{1,5},{5... | collective-permute-start | bytes 786440 | tf_op jit(solution)/shard_map/ppermute | solution.py:73
  260.7 6.4 %collective-permute-start.11 = (f32[16,16,256]{2,1,0:T(8,128)S(1)}, f32[16,16,256]{2,1,0:T(8,128)S(1)}, u32[]{:S(2)}, u32[]{:S(2)}) collective-permute-start(f32[16,16,256]{2,1,0:T(8,128)S(1)} %bitcast_add_fusion.3), channel_id=1, source_target_pairs={{0,8},{4,0},{12,4},{20,12},{28,20},{24,28},{16,24},{8,16},{1,9},{5... | collective-permute-start | bytes 786440 | tf_op jit(solution)/shard_map/ppermute | solution.py:73
  261.9 6.4 %collective-permute-start.4 = (f32[16,16,256]{2,1,0:T(8,128)S(1)}, f32[16,16,256]{2,1,0:T(8,128)S(1)}, u32[]{:S(2)}, u32[]{:S(2)}) collective-permute-start(f32[16,16,256]{2,1,0:T(8,128)S(1)} %bitcast_add_fusion.10), channel_id=1, source_target_pairs={{0,4},{4,12},{12,20},{20,28},{28,24},{24,16},{16,8},{8,0},{1,5},{5... | collective-permute-start | bytes 786440 | tf_op jit(solution)/shard_map/ppermute | solution.py:73
  267.2 6.4 %collective-permute-start.12 = (f32[16,16,256]{2,1,0:T(8,128)S(1)}, f32[16,16,256]{2,1,0:T(8,128)S(1)}, u32[]{:S(2)}, u32[]{:S(2)}) collective-permute-start(f32[16,16,256]{2,1,0:T(8,128)S(1)} %bitcast_add_fusion.2), channel_id=1, source_target_pairs={{0,8},{4,0},{12,4},{20,12},{28,20},{24,28},{16,24},{8,16},{1,9},{5... | collective-permute-start | bytes 786440 | tf_op jit(solution)/shard_map/ppermute | solution.py:73
  268.4 7.3 %collective-permute-start.5 = (f32[16,16,256]{2,1,0:T(8,128)S(1)}, f32[16,16,256]{2,1,0:T(8,128)S(1)}, u32[]{:S(2)}, u32[]{:S(2)}) collective-permute-start(f32[16,16,256]{2,1,0:T(8,128)S(1)} %bitcast_add_fusion.9), channel_id=1, source_target_pairs={{0,4},{4,12},{12,20},{20,28},{28,24},{24,16},{16,8},{8,0},{1,5},{5... | collective-permute-start | bytes 786440 | tf_op jit(solution)/shard_map/ppermute | solution.py:73
  274.6 8.2 %collective-permute-start.13 = (f32[16,16,256]{2,1,0:T(8,128)S(1)}, f32[16,16,256]{2,1,0:T(8,128)S(1)}, u32[]{:S(2)}, u32[]{:S(2)}) collective-permute-start(f32[16,16,256]{2,1,0:T(8,128)S(1)} %bitcast_add_fusion.1), channel_id=1, source_target_pairs={{0,8},{4,0},{12,4},{20,12},{28,20},{24,28},{16,24},{8,16},{1,9},{5... | collective-permute-start | bytes 786440 | tf_op jit(solution)/shard_map/ppermute | solution.py:73
  276.6 7.2 %collective-permute-start.6 = (f32[16,16,256]{2,1,0:T(8,128)S(1)}, f32[16,16,256]{2,1,0:T(8,128)S(1)}, u32[]{:S(2)}, u32[]{:S(2)}) collective-permute-start(f32[16,16,256]{2,1,0:T(8,128)S(1)} %bitcast_add_fusion.8), channel_id=1, source_target_pairs={{0,4},{4,12},{12,20},{20,28},{28,24},{24,16},{16,8},{8,0},{1,5},{5... | collective-permute-start | bytes 786440 | tf_op jit(solution)/shard_map/ppermute | solution.py:73
  (13 other events, 222.9 us)
Sparse Core Ops, SparseCore 0:
  10.8 57.3 all-gather.2

commit v5 on v3

--- a/solution.py
+++ b/solution.py
@@ -75,6 +75,27 @@
     return jnp.concatenate(totals, axis=0)
 
 
+def ring_all_gather(piece, ring):
+    n = len(ring)
+    order = jnp.asarray(np.array(ring, np.int32))
+    place = jnp.asarray(np.argsort(np.array(ring)).astype(np.int32))
+    me = lax.axis_index("dp")
+    here = place[me]
+    half = piece.shape[0] // 2
+    forward = [(ring[p], ring[(p + 1) % n]) for p in range(n)]
+    backward = [(ring[p], ring[(p - 1) % n]) for p in range(n)]
+    outs = []
+    for way, pairs, src in ((1, forward, piece[:half]), (-1, backward, piece[half:])):
+        held = lax.dynamic_update_index_in_dim(jnp.zeros((n,) + src.shape, src.dtype), src, me, 0)
+        cur = src
+        for step in range(n - 1):
+            cur = lax.ppermute(cur, "dp", pairs)
+            owner = order[(here - way * (1 + step)) % n]
+            held = lax.dynamic_update_index_in_dim(held, cur, owner, 0)
+        outs.append(held)
+    return jnp.concatenate(outs, axis=1)
+
+
 def body(ring, activations, cotangent, r_mix, l_mix):
     tok_count = activations.shape[1]
     local_blocks = activations.shape[0] // WIDTH
@@ -88,8 +109,8 @@
     r_lead = jnp.transpose(r_mix, (1, 0, 2)).reshape(-1, WIDTH)
     l_lead = jnp.transpose(l_mix.reshape(local_cols, -1, BLOCKS), (1, 0, 2)).reshape(-1, WIDTH)
     r_size = r_lead.shape[0]
-    packed = jnp.concatenate([r_lead, l_lead], axis=0)[None]
-    packed = lax.all_gather(packed, "dp", axis=0, tiled=True)
+    packed = jnp.concatenate([r_lead, l_lead], axis=0)
+    packed = ring_all_gather(packed, ring)
     r_whole = packed[:, :r_size].reshape(n_dp * rows_r, local_blocks, WIDTH)
     l_blocks = packed[:, r_size:].reshape(-1, local_cols, BLOCKS)
     mixed_rows = jnp.einsum(

time: 261 us -> 255 us (0.977)
  starting transfers between devices: 41.2 us -> 62 us
  waiting for transfers between devices: 96.8 us -> 80.8 us
  between operations: 55.3 us -> 42.5 us
    all_gather x1 -> x0, waiting for transfers between devices: 49.2 us -> none  [body(): packed = lax.all_gather(packed, 'dp', axis=0, tiled=True)]
    ppermute x0 -> x14, waiting for transfers between devices: none -> 23.9 us  [ring_all_gather(): cur = lax.ppermute(cur, 'dp', pairs)]
    ppermute x0 -> x14, starting transfers between devices: none -> 15.4 us  [ring_all_gather(): cur = lax.ppermute(cur, 'dp', pairs)]
    all_to_all x1, waiting for transfers between devices: 0.01 us -> 14.9 us  [body(): lax.all_to_all(mixed_rows, 'feat', split_axis=1, concat_axis=0, tiled=True)]
    ppermute x28, waiting for transfers between devices: 47.6 us -> 41.9 us  [ring_reduce_scatter(): acc = lax.ppermute(acc, 'dp', pairs)]
    ppermute x28, starting transfers between devices: 27.5 us -> 32.8 us  [ring_reduce_scatter(): acc = lax.ppermute(acc, 'dp', pairs)]
    dynamic_update_slice x0 -> x15, local copies, waits for them, and re-layouts: none -> 3.03 us  [the longest x14 2.09 us: ring_all_gather(): held = lax.dynamic_update_index_in_dim(held, cur, owner, 0)]
  transfers between devices with their start and end apart: 32 -> 45, of which waited for: 16 -> 19; matrix products, arithmetic and copies ran while one was open for 15% -> 17% of each run, Pallas kernels for 0% -> 0%
where the time goes in v5:
time: 255 us; the launch traced here: 253 us
  waiting for transfers between devices  80.8 us (32%)
  starting transfers between devices  62 us (24%)
  between operations  42.5 us (17%)
  local copies, waits for them, and re-layouts  37.8 us (15%)
  matrix products  15.8 us (6%)
  other arithmetic  14.4 us (6%)
    ppermute x28, waiting for transfers between devices, ring_reduce_scatter(): acc = lax.ppermute(acc, 'dp', pairs)  41.9 us
    ppermute x28, starting transfers between devices, ring_reduce_scatter(): acc = lax.ppermute(acc, 'dp', pairs)  32.8 us
    ppermute x14, waiting for transfers between devices, ring_all_gather(): cur = lax.ppermute(cur, 'dp', pairs)  23.9 us
    ppermute x14, starting transfers between devices, ring_all_gather(): cur = lax.ppermute(cur, 'dp', pairs)  15.4 us
    all_to_all x1, waiting for transfers between devices, body(): lax.all_to_all(mixed_rows, 'feat', split_axis=1, concat_axis=0, tiled=True)  14.9 us
    add x28, other arithmetic, ring_reduce_scatter(): acc = mine if acc is None else acc + mine  11.8 us
    dot_general x1, matrix products, body(): jnp.einsum('obt,ibo->bit', back_rows, r_whole, preferred_element_type=jnp...  5.13 us
  transfers between devices with their start and end apart: 45, of which 19 were waited for; matrix products, arithmetic and copies ran while one was open for 17% of the time, Pallas kernels for 0%

profile of v5, /device:TPU:0, one launch (start us, length us, event | category | flops | bytes accessed | tf_op | source)
XLA Modules:
  0.0 253.3 jit_solution(4524213871127338325)
XLA Ops:
  2.6 3.0 %collective-permute-start = (bf16[320,256]{1,0:T(8,128)(2,1)}, bf16[320,256]{1,0:T(8,128)(2,1)}, u32[]{:S(2)}, u32[]{:S(2)}) collective-permute-start(bf16[320,256]{1,0:T(8,128)(2,1)} %bitcast.3), channel_id=1, source_target_pairs={{0,4},{4,12},{12,20},{20,28},{28,24},{24,16},{16,8},{8,0},{1,5},{5... | collective-permute-start | bytes 491528 | tf_op jit(solution)/shard_map/ppermute | solution.py:92
  8.5 4.1 %copy.41 = bf16[16,256,256]{2,0,1:T(8,128)(2,1)} copy(bf16[16,256,256]{2,1,0:T(8,128)(2,1)} %bitcast.203) | data formatting | bytes 4194304 | tf_op jit(solution)/shard_map/reshape | solution.py:105
  12.6 4.6 %all-to-all-start = ((bf16[16,256,256]{2,0,1:T(8,128)(2,1)}), bf16[16,256,256]{2,0,1:T(8,128)(2,1)}, u32[]{:S(2)}, u32[]{:S(2)}) async-start(bf16[16,256,256]{2,0,1:T(8,128)(2,1)} %copy.41), calls=%async_computation | async-start | bytes 4194304 | tf_op jit(solution)/shard_map/all_to_all | solution.py:106
  61.0 3.0 %collective-permute-done.1 = bf16[320,256]{1,0:T(8,128)(2,1)S(1)} collective-permute-done((bf16[320,256]{1,0:T(8,128)(2,1)}, bf16[320,256]{1,0:T(8,128)(2,1)S(1)}, u32[]{:S(2)}, u32[]{:S(2)}) %collective-permute-start.1) | collective-permute-done | bytes 163872 | tf_op jit(solution)/shard_map/ppermute | solution.py:92
  66.1 3.9 %collective-permute-done.2 = bf16[320,256]{1,0:T(8,128)(2,1)S(1)} collective-permute-done((bf16[320,256]{1,0:T(8,128)(2,1)S(1)}, bf16[320,256]{1,0:T(8,128)(2,1)S(1)}, u32[]{:S(2)}, u32[]{:S(2)}) %collective-permute-start.2) | collective-permute-done | bytes 163872 | tf_op jit(solution)/shard_map/ppermute | solution.py:92
  72.1 3.2 %collective-permute-done.3 = bf16[320,256]{1,0:T(8,128)(2,1)S(1)} collective-permute-done((bf16[320,256]{1,0:T(8,128)(2,1)S(1)}, bf16[320,256]{1,0:T(8,128)(2,1)S(1)}, u32[]{:S(2)}, u32[]{:S(2)}) %collective-permute-start.3) | collective-permute-done | bytes 163872 | tf_op jit(solution)/shard_map/ppermute | solution.py:92
  77.4 3.9 %collective-permute-done.4 = bf16[320,256]{1,0:T(8,128)(2,1)S(1)} collective-permute-done((bf16[320,256]{1,0:T(8,128)(2,1)S(1)}, bf16[320,256]{1,0:T(8,128)(2,1)S(1)}, u32[]{:S(2)}, u32[]{:S(2)}) %collective-permute-start.4) | collective-permute-done | bytes 163872 | tf_op jit(solution)/shard_map/ppermute | solution.py:92
  83.4 4.8 %collective-permute-done.5 = bf16[320,256]{1,0:T(8,128)(2,1)S(1)} collective-permute-done((bf16[320,256]{1,0:T(8,128)(2,1)S(1)}, bf16[320,256]{1,0:T(8,128)(2,1)S(1)}, u32[]{:S(2)}, u32[]{:S(2)}) %collective-permute-start.5) | collective-permute-done | bytes 163872 | tf_op jit(solution)/shard_map/ppermute | solution.py:92
  90.4 5.0 %collective-permute-done.13 = bf16[320,256]{1,0:T(8,128)(2,1)S(1)} collective-permute-done((bf16[320,256]{1,0:T(8,128)(2,1)S(1)}, bf16[320,256]{1,0:T(8,128)(2,1)S(1)}, u32[]{:S(2)}, u32[]{:S(2)}) %collective-permute-start.13) | collective-permute-done | bytes 163872 | tf_op jit(solution)/shard_map/ppermute | solution.py:92
  99.8 4.6 %all-to-all-start.1 = ((bf16[16,256,256]{2,0,1:T(8,128)(2,1)}), bf16[16,256,256]{2,0,1:T(8,128)(2,1)}, u32[]{:S(2)}, u32[]{:S(2)}) async-start(bf16[16,256,256]{2,0,1:T(8,128)(2,1)} %copy.44), calls=%async_computation.1 | async-start | bytes 4194304 | tf_op jit(solution)/shard_map/all_to_all | solution.py:119
  110.9 4.2 %copy.42 = f32[16,4,64,256]{3,0,1,2:T(8,128)} copy(bf16[16,4,64,256]{3,0,2,1:T(8,128)(2,1)} %bitcast.109) | data formatting | bytes 6291456 | tf_op jit(solution)/shard_map/convert_element_type | solution.py:19
  115.1 14.9 %all-to-all-done.1 = bf16[16,256,256]{2,0,1:T(8,128)(2,1)} async-done(((bf16[16,256,256]{2,0,1:T(8,128)(2,1)}), bf16[16,256,256]{2,0,1:T(8,128)(2,1)}, u32[]{:S(2)}, u32[]{:S(2)}) %all-to-all-start.1) | async-done | bytes 2097184 | tf_op jit(solution)/shard_map/all_to_all | solution.py:119
  132.8 5.1 %fusion.6 = bf16[64,64,256]{2,0,1:T(8,128)(2,1)S(1)} fusion(f32[16,4,64,256]{3,0,1,2:T(8,128)S(1)} %copy-done.5, bf16[64,64,256]{2,0,1:T(8,128)(2,1)S(1)} %bitcast.200, bf16[64,64,64]{2,1,0:T(8,128)(2,1)S(1)} %reshape.142), kind=kOutput, calls=%fused_computation.8 | convolution fusion | flops 155189248 | bytes 8912896 | tf_op jit(solution)/shard_map/bst,bsc->cst/dot_general | solution.py:120
  143.8 3.8 %copy.51 = f32[64,64,64]{2,1,0:T(8,128)} copy(f32[64,64,64]{0,2,1:T(8,128)} %multiply_bitcast_fusion) | data formatting | bytes 2097152 | tf_op jit(solution)/shard_map/mul | solution.py:126
  150.3 4.5 %all-to-all-start.2 = ((bf16[64,64,256]{2,0,1:T(8,128)(2,1)}), bf16[64,64,256]{2,0,1:T(8,128)(2,1)}, u32[]{:S(2)}, u32[]{:S(2)}) async-start(bf16[64,64,256]{2,0,1:T(8,128)(2,1)} %copy.48), calls=%async_computation.2 | async-start | bytes 4194304 | tf_op jit(solution)/shard_map/all_to_all | solution.py:129
  157.8 3.8 %collective-permute-done.35 = f32[4,64,64]{2,1,0:T(8,128)S(1)} collective-permute-done((f32[4,64,64]{2,1,0:T(8,128)S(1)}, f32[4,64,64]{2,1,0:T(8,128)S(1)}, u32[]{:S(2)}, u32[]{:S(2)}) %collective-permute-start.35) | collective-permute-done | bytes 65568 | tf_op jit(solution)/shard_map/ppermute | solution.py:73
  164.7 3.1 %collective-permute-done.36 = f32[4,64,64]{2,1,0:T(8,128)S(1)} collective-permute-done((f32[4,64,64]{2,1,0:T(8,128)S(1)}, f32[4,64,64]{2,1,0:T(8,128)S(1)}, u32[]{:S(2)}, u32[]{:S(2)}) %collective-permute-start.36) | collective-permute-done | bytes 65568 | tf_op jit(solution)/shard_map/ppermute | solution.py:73
  182.7 2.9 %collective-permute-done.39 = f32[4,64,64]{2,1,0:T(8,128)S(1)} collective-permute-done((f32[4,64,64]{2,1,0:T(8,128)S(1)}, f32[4,64,64]{2,1,0:T(8,128)S(1)}, u32[]{:S(2)}, u32[]{:S(2)}) %collective-permute-start.39) | collective-permute-done | bytes 65568 | tf_op jit(solution)/shard_map/ppermute | solution.py:73
  203.8 3.0 %collective-permute-done.22 = f32[16,16,256]{2,0,1:T(8,128)S(1)} collective-permute-done((f32[16,16,256]{2,0,1:T(8,128)S(1)}, f32[16,16,256]{2,0,1:T(8,128)S(1)}, u32[]{:S(2)}, u32[]{:S(2)}) %collective-permute-start.22) | collective-permute-done | bytes 262176 | tf_op jit(solution)/shard_map/ppermute | solution.py:73
  210.4 5.4 %collective-permute-done.23 = f32[16,16,256]{2,0,1:T(8,128)S(1)} collective-permute-done((f32[16,16,256]{2,0,1:T(8,128)S(1)}, f32[16,16,256]{2,0,1:T(8,128)S(1)}, u32[]{:S(2)}, u32[]{:S(2)}) %collective-permute-start.23) | collective-permute-done | bytes 262176 | tf_op jit(solution)/shard_map/ppermute | solution.py:73
  219.6 4.9 %collective-permute-done.24 = f32[16,16,256]{2,0,1:T(8,128)S(1)} collective-permute-done((f32[16,16,256]{2,0,1:T(8,128)S(1)}, f32[16,16,256]{2,0,1:T(8,128)S(1)}, u32[]{:S(2)}, u32[]{:S(2)}) %collective-permute-start.24) | collective-permute-done | bytes 262176 | tf_op jit(solution)/shard_map/ppermute | solution.py:73
  227.2 5.1 %collective-permute-done.25 = f32[16,16,256]{2,0,1:T(8,128)S(1)} collective-permute-done((f32[16,16,256]{2,0,1:T(8,128)S(1)}, f32[16,16,256]{2,0,1:T(8,128)S(1)}, u32[]{:S(2)}, u32[]{:S(2)}) %collective-permute-start.25) | collective-permute-done | bytes 262176 | tf_op jit(solution)/shard_map/ppermute | solution.py:73
  235.9 5.3 %collective-permute-done.26 = f32[16,16,256]{2,0,1:T(8,128)S(1)} collective-permute-done((f32[16,16,256]{2,0,1:T(8,128)S(1)}, f32[16,16,256]{2,0,1:T(8,128)S(1)}, u32[]{:S(2)}, u32[]{:S(2)}) %collective-permute-start.26) | collective-permute-done | bytes 262176 | tf_op jit(solution)/shard_map/ppermute | solution.py:73
  245.3 5.1 %add_convert_fusion = bf16[16,256,256]{2,1,0:T(8,128)(2,1)} fusion(bf16[16,256,256]{2,1,0:T(8,128)(2,1)} %bitcast.204, bf16[256,16,256]{2,0,1:T(8,128)(2,1)} %bitcast.198, bf16[256,16,256]{2,1,0:T(8,128)(2,1)} %bitcast.196), kind=kOutput, calls=%fused_computation.14 | convolution fusion | flops 540016640 | bytes 8388608 | tf_op jit(solution)/shard_map/obt,ibo->bit/dot_general | solution.py:130
  (163 shorter events, 99.7 us)
Async XLA Ops:
  2.6 54.3 %collective-permute-start = (bf16[320,256]{1,0:T(8,128)(2,1)}, bf16[320,256]{1,0:T(8,128)(2,1)}, u32[]{:S(2)}, u32[]{:S(2)}) collective-permute-start(bf16[320,256]{1,0:T(8,128)(2,1)} %bitcast.3), channel_id=1, source_target_pairs={{0,4},{4,12},{12,20},{20,28},{28,24},{24,16},{16,8},{8,0},{1,5},{5... | collective-permute-start | bytes 491528 | tf_op jit(solution)/shard_map/ppermute | solution.py:92
  8.5 50.5 %collective-permute-start.7 = (bf16[320,256]{1,0:T(8,128)(2,1)}, bf16[320,256]{1,0:T(8,128)(2,1)}, u32[]{:S(2)}, u32[]{:S(2)}) collective-permute-start(bf16[320,256]{1,0:T(8,128)(2,1)} %get-tuple-element.4), channel_id=1, source_target_pairs={{0,8},{4,0},{12,4},{20,12},{28,20},{24,28},{16,24},{8,16},{1,9},{5... | collective-permute-start | bytes 491528 | tf_op jit(solution)/shard_map/ppermute | solution.py:92
  12.6 87.2 %all-to-all-start = ((bf16[16,256,256]{2,0,1:T(8,128)(2,1)}), bf16[16,256,256]{2,0,1:T(8,128)(2,1)}, u32[]{:S(2)}, u32[]{:S(2)}) async-start(bf16[16,256,256]{2,0,1:T(8,128)(2,1)} %copy.41), calls=%async_computation | async-start | bytes 4194304 | tf_op jit(solution)/shard_map/all_to_all | solution.py:106
  99.8 30.2 %all-to-all-start.1 = ((bf16[16,256,256]{2,0,1:T(8,128)(2,1)}), bf16[16,256,256]{2,0,1:T(8,128)(2,1)}, u32[]{:S(2)}, u32[]{:S(2)}) async-start(bf16[16,256,256]{2,0,1:T(8,128)(2,1)} %copy.44), calls=%async_computation.1 | async-start | bytes 4194304 | tf_op jit(solution)/shard_map/all_to_all | solution.py:119
  150.3 36.6 %all-to-all-start.2 = ((bf16[64,64,256]{2,0,1:T(8,128)(2,1)}), bf16[64,64,256]{2,0,1:T(8,128)(2,1)}, u32[]{:S(2)}, u32[]{:S(2)}) async-start(bf16[64,64,256]{2,0,1:T(8,128)(2,1)} %copy.48), calls=%async_computation.2 | async-start | bytes 4194304 | tf_op jit(solution)/shard_map/all_to_all | solution.py:129
  180.9 12.0 %collective-permute-start.32 = (f32[4,64,64]{2,1,0:T(8,128)S(1)}, f32[4,64,64]{2,1,0:T(8,128)}, u32[]{:S(2)}, u32[]{:S(2)}) collective-permute-start(f32[4,64,64]{2,1,0:T(8,128)S(1)} %bitcast_add_fusion.24), channel_id=1, source_target_pairs={{0,4},{4,12},{12,20},{20,28},{28,24},{24,16},{16,8},{8,0},{1,5},{5... | collective-permute-start | bytes 196616 | tf_op jit(solution)/shard_map/ppermute | solution.py:73
  186.5 14.2 %collective-permute-start.40 = (f32[4,64,64]{2,1,0:T(8,128)S(1)}, f32[4,64,64]{2,1,0:T(8,128)S(1)}, u32[]{:S(2)}, u32[]{:S(2)}) collective-permute-start(f32[4,64,64]{2,1,0:T(8,128)S(1)} %bitcast_add_fusion.16), channel_id=1, source_target_pairs={{0,8},{4,0},{12,4},{20,12},{28,20},{24,28},{16,24},{8,16},{1,9},{5... | collective-permute-start | bytes 196616 | tf_op jit(solution)/shard_map/ppermute | solution.py:73
  190.8 7.3 %collective-permute-start.21 = (f32[16,16,256]{2,0,1:T(8,128)S(1)}, f32[16,16,256]{2,0,1:T(8,128)S(1)}, u32[]{:S(2)}, u32[]{:S(2)}) collective-permute-start(f32[16,16,256]{2,0,1:T(8,128)S(1)} %dynamic-slice_bitcast_fusion), channel_id=1, source_target_pairs={{0,8},{4,0},{12,4},{20,12},{28,20},{24,28},{16,24},{8,16},{1,9},{5... | collective-permute-start | bytes 786440 | tf_op jit(solution)/shard_map/ppermute | solution.py:73
  192.4 8.3 %collective-permute-start.14 = (f32[16,16,256]{2,0,1:T(8,128)S(1)}, f32[16,16,256]{2,0,1:T(8,128)S(1)}, u32[]{:S(2)}, u32[]{:S(2)}) collective-permute-start(f32[16,16,256]{2,0,1:T(8,128)S(1)} %dynamic-slice_bitcast_fusion.1), channel_id=1, source_target_pairs={{0,4},{4,12},{12,20},{20,28},{28,24},{24,16},{16,8},{8,0},{1,5},{5... | collective-permute-start | bytes 786440 | tf_op jit(solution)/shard_map/ppermute | solution.py:73
  193.8 15.6 %collective-permute-start.33 = (f32[4,64,64]{2,1,0:T(8,128)S(1)}, f32[4,64,64]{2,1,0:T(8,128)S(1)}, u32[]{:S(2)}, u32[]{:S(2)}) collective-permute-start(f32[4,64,64]{2,1,0:T(8,128)S(1)} %bitcast_add_fusion.23), channel_id=1, source_target_pairs={{0,4},{4,12},{12,20},{20,28},{28,24},{24,16},{16,8},{8,0},{1,5},{5... | collective-permute-start | bytes 196616 | tf_op jit(solution)/shard_map/ppermute | solution.py:73
  198.1 8.6 %collective-permute-start.22 = (f32[16,16,256]{2,0,1:T(8,128)S(1)}, f32[16,16,256]{2,0,1:T(8,128)S(1)}, u32[]{:S(2)}, u32[]{:S(2)}) collective-permute-start(f32[16,16,256]{2,0,1:T(8,128)S(1)} %bitcast_add_fusion.6), channel_id=1, source_target_pairs={{0,8},{4,0},{12,4},{20,12},{28,20},{24,28},{16,24},{8,16},{1,9},{5... | collective-permute-start | bytes 786440 | tf_op jit(solution)/shard_map/ppermute | solution.py:73
  200.7 8.7 %collective-permute-start.15 = (f32[16,16,256]{2,0,1:T(8,128)S(1)}, f32[16,16,256]{2,0,1:T(8,128)S(1)}, u32[]{:S(2)}, u32[]{:S(2)}) collective-permute-start(f32[16,16,256]{2,0,1:T(8,128)S(1)} %bitcast_add_fusion.13), channel_id=1, source_target_pairs={{0,4},{4,12},{12,20},{20,28},{28,24},{24,16},{16,8},{8,0},{1,5},{5... | collective-permute-start | bytes 786440 | tf_op jit(solution)/shard_map/ppermute | solution.py:73
  201.7 17.0 %collective-permute-start.41 = (f32[4,64,64]{2,1,0:T(8,128)S(1)}, f32[4,64,64]{2,1,0:T(8,128)S(1)}, u32[]{:S(2)}, u32[]{:S(2)}) collective-permute-start(f32[4,64,64]{2,1,0:T(8,128)S(1)} %bitcast_add_fusion.15), channel_id=1, source_target_pairs={{0,8},{4,0},{12,4},{20,12},{28,20},{24,28},{16,24},{8,16},{1,9},{5... | collective-permute-start | bytes 196616 | tf_op jit(solution)/shard_map/ppermute | solution.py:73
  206.8 9.0 %collective-permute-start.23 = (f32[16,16,256]{2,0,1:T(8,128)S(1)}, f32[16,16,256]{2,0,1:T(8,128)S(1)}, u32[]{:S(2)}, u32[]{:S(2)}) collective-permute-start(f32[16,16,256]{2,0,1:T(8,128)S(1)} %bitcast_add_fusion.5), channel_id=1, source_target_pairs={{0,8},{4,0},{12,4},{20,12},{28,20},{24,28},{16,24},{8,16},{1,9},{5... | collective-permute-start | bytes 786440 | tf_op jit(solution)/shard_map/ppermute | solution.py:73
  209.4 9.0 %collective-permute-start.16 = (f32[16,16,256]{2,0,1:T(8,128)S(1)}, f32[16,16,256]{2,0,1:T(8,128)S(1)}, u32[]{:S(2)}, u32[]{:S(2)}) collective-permute-start(f32[16,16,256]{2,0,1:T(8,128)S(1)} %bitcast_add_fusion.12), channel_id=1, source_target_pairs={{0,4},{4,12},{12,20},{20,28},{28,24},{24,16},{16,8},{8,0},{1,5},{5... | collective-permute-start | bytes 786440 | tf_op jit(solution)/shard_map/ppermute | solution.py:73
  209.5 17.7 %collective-permute-start.34 = (f32[4,64,64]{2,1,0:T(8,128)S(1)}, f32[4,64,64]{2,1,0:T(8,128)S(1)}, u32[]{:S(2)}, u32[]{:S(2)}) collective-permute-start(f32[4,64,64]{2,1,0:T(8,128)S(1)} %bitcast_add_fusion.22), channel_id=1, source_target_pairs={{0,4},{4,12},{12,20},{20,28},{28,24},{24,16},{16,8},{8,0},{1,5},{5... | collective-permute-start | bytes 196616 | tf_op jit(solution)/shard_map/ppermute | solution.py:73
  215.9 8.6 %collective-permute-start.24 = (f32[16,16,256]{2,0,1:T(8,128)S(1)}, f32[16,16,256]{2,0,1:T(8,128)S(1)}, u32[]{:S(2)}, u32[]{:S(2)}) collective-permute-start(f32[16,16,256]{2,0,1:T(8,128)S(1)} %bitcast_add_fusion.4), channel_id=1, source_target_pairs={{0,8},{4,0},{12,4},{20,12},{28,20},{24,28},{16,24},{8,16},{1,9},{5... | collective-permute-start | bytes 786440 | tf_op jit(solution)/shard_map/ppermute | solution.py:73
  218.4 8.1 %collective-permute-start.17 = (f32[16,16,256]{2,0,1:T(8,128)S(1)}, f32[16,16,256]{2,0,1:T(8,128)S(1)}, u32[]{:S(2)}, u32[]{:S(2)}) collective-permute-start(f32[16,16,256]{2,0,1:T(8,128)S(1)} %bitcast_add_fusion.11), channel_id=1, source_target_pairs={{0,4},{4,12},{12,20},{20,28},{28,24},{24,16},{16,8},{8,0},{1,5},{5... | collective-permute-start | bytes 786440 | tf_op jit(solution)/shard_map/ppermute | solution.py:73
  224.5 7.8 %collective-permute-start.25 = (f32[16,16,256]{2,0,1:T(8,128)S(1)}, f32[16,16,256]{2,0,1:T(8,128)S(1)}, u32[]{:S(2)}, u32[]{:S(2)}) collective-permute-start(f32[16,16,256]{2,0,1:T(8,128)S(1)} %bitcast_add_fusion.3), channel_id=1, source_target_pairs={{0,8},{4,0},{12,4},{20,12},{28,20},{24,28},{16,24},{8,16},{1,9},{5... | collective-permute-start | bytes 786440 | tf_op jit(solution)/shard_map/ppermute | solution.py:73
  226.6 7.3 %collective-permute-start.18 = (f32[16,16,256]{2,0,1:T(8,128)S(1)}, f32[16,16,256]{2,0,1:T(8,128)S(1)}, u32[]{:S(2)}, u32[]{:S(2)}) collective-permute-start(f32[16,16,256]{2,0,1:T(8,128)S(1)} %bitcast_add_fusion.10), channel_id=1, source_target_pairs={{0,4},{4,12},{12,20},{20,28},{28,24},{24,16},{16,8},{8,0},{1,5},{5... | collective-permute-start | bytes 786440 | tf_op jit(solution)/shard_map/ppermute | solution.py:73
  232.4 8.9 %collective-permute-start.26 = (f32[16,16,256]{2,0,1:T(8,128)S(1)}, f32[16,16,256]{2,0,1:T(8,128)S(1)}, u32[]{:S(2)}, u32[]{:S(2)}) collective-permute-start(f32[16,16,256]{2,0,1:T(8,128)S(1)} %bitcast_add_fusion.2), channel_id=1, source_target_pairs={{0,8},{4,0},{12,4},{20,12},{28,20},{24,28},{16,24},{8,16},{1,9},{5... | collective-permute-start | bytes 786440 | tf_op jit(solution)/shard_map/ppermute | solution.py:73
  233.9 8.3 %collective-permute-start.19 = (f32[16,16,256]{2,0,1:T(8,128)S(1)}, f32[16,16,256]{2,0,1:T(8,128)S(1)}, u32[]{:S(2)}, u32[]{:S(2)}) collective-permute-start(f32[16,16,256]{2,0,1:T(8,128)S(1)} %bitcast_add_fusion.9), channel_id=1, source_target_pairs={{0,4},{4,12},{12,20},{20,28},{28,24},{24,16},{16,8},{8,0},{1,5},{5... | collective-permute-start | bytes 786440 | tf_op jit(solution)/shard_map/ppermute | solution.py:73
  242.2 8.3 %collective-permute-start.27 = (f32[16,16,256]{2,0,1:T(8,128)S(1)}, f32[16,16,256]{2,0,1:T(8,128)S(1)}, u32[]{:S(2)}, u32[]{:S(2)}) collective-permute-start(f32[16,16,256]{2,0,1:T(8,128)S(1)} %bitcast_add_fusion.1), channel_id=1, source_target_pairs={{0,8},{4,0},{12,4},{20,12},{28,20},{24,28},{16,24},{8,16},{1,9},{5... | collective-permute-start | bytes 786440 | tf_op jit(solution)/shard_map/ppermute | solution.py:73
  243.3 8.2 %collective-permute-start.20 = (f32[16,16,256]{2,0,1:T(8,128)S(1)}, f32[16,16,256]{2,0,1:T(8,128)S(1)}, u32[]{:S(2)}, u32[]{:S(2)}) collective-permute-start(f32[16,16,256]{2,0,1:T(8,128)S(1)} %bitcast_add_fusion.8), channel_id=1, source_target_pairs={{0,4},{4,12},{12,20},{20,28},{28,24},{24,16},{16,8},{8,0},{1,5},{5... | collective-permute-start | bytes 786440 | tf_op jit(solution)/shard_map/ppermute | solution.py:73
  (30 other events, 336.9 us)

commit v6 on v5

--- a/solution.py
+++ b/solution.py
@@ -103,7 +103,6 @@
     grad_scale = 1.0 / math.sqrt(tok_count * n_dp)
     x_blocks = activations.reshape(local_blocks, WIDTH, tok_count)
     g_blocks = cotangent.reshape(local_blocks, WIDTH, tok_count)
-    g_cols = lax.all_to_all(g_blocks, "feat", split_axis=1, concat_axis=0, tiled=True)
     local_cols = l_mix.shape[0]
     rows_r = r_mix.shape[1]
     r_lead = jnp.transpose(r_mix, (1, 0, 2)).reshape(-1, WIDTH)
@@ -117,6 +116,8 @@
         "bit,ibo->bot", x_blocks, r_whole, preferred_element_type=jnp.float32
     ).astype(jnp.bfloat16)
     columns = lax.all_to_all(mixed_rows, "feat", split_axis=1, concat_axis=0, tiled=True)
+    g_late, columns = lax.optimization_barrier((g_blocks, columns))
+    g_cols = lax.all_to_all(g_late, "feat", split_axis=1, concat_axis=0, tiled=True)
     pre_act = jnp.einsum("bst,bsc->cst", columns, l_blocks, preferred_element_type=jnp.float32)
     slope_cols = slope_of(pre_act, g_cols)
     back_cols = jnp.einsum(

time: 255 us -> 276 us (1.082)
  blocking collectives: 0 us -> 28.3 us
  local copies, waits for them, and re-layouts: 37.8 us -> 32.5 us
  starting transfers between devices: 62 us -> 58.1 us
  waiting for transfers between devices: 80.8 us -> 84 us
    all_to_all x0 -> x1, blocking collectives: none -> 28.3 us  [body(): lax.all_to_all(mixed_rows, 'feat', split_axis=1, concat_axis=0, tiled=True)]
    all_to_all x2 -> x1, starting transfers between devices: 9.21 us -> 4.63 us  [body(): lax.all_to_all(g_late, 'feat', split_axis=1, concat_axis=0, tiled=True)]
    all_to_all x2 -> x1, waiting for transfers between devices: 14.9 us -> 19.3 us  [body(): lax.all_to_all(g_late, 'feat', split_axis=1, concat_axis=0, tiled=True)]
    reshape x1 -> x0, local copies, waits for them, and re-layouts: 4.08 us -> none  [body(): g_blocks = cotangent.reshape(local_blocks, WIDTH, tok_count)]
  transfers between devices with their start and end apart: 45 -> 44, of which waited for: 19 -> 21; matrix products, arithmetic and copies ran while one was open for 17% -> 11% of each run, Pallas kernels for 0% -> 0%
where the time goes in v6:
time: 276 us; the launch traced here: 275 us
  waiting for transfers between devices  84 us (30%)
  starting transfers between devices  58.1 us (21%)
  between operations  41.5 us (15%)
  local copies, waits for them, and re-layouts  32.5 us (12%)
  blocking collectives  28.3 us (10%)
  matrix products  15.8 us (6%)
  other arithmetic  14.4 us (5%)
    ppermute x28, waiting for transfers between devices, ring_reduce_scatter(): acc = lax.ppermute(acc, 'dp', pairs)  41.9 us
    ppermute x28, starting transfers between devices, ring_reduce_scatter(): acc = lax.ppermute(acc, 'dp', pairs)  33.1 us
    all_to_all x1, blocking collectives, body(): lax.all_to_all(mixed_rows, 'feat', split_axis=1, concat_axis=0, tiled=True)  28.3 us
    ppermute x14, waiting for transfers between devices, ring_all_gather(): cur = lax.ppermute(cur, 'dp', pairs)  22.7 us
    all_to_all x1, waiting for transfers between devices, body(): lax.all_to_all(g_late, 'feat', split_axis=1, concat_axis=0, tiled=True)  19.3 us
    ppermute x14, starting transfers between devices, ring_all_gather(): cur = lax.ppermute(cur, 'dp', pairs)  15.9 us
    add x28, other arithmetic, ring_reduce_scatter(): acc = mine if acc is None else acc + mine  11.8 us
  transfers between devices with their start and end apart: 44, of which 21 were waited for; matrix products, arithmetic and copies ran while one was open for 11% of the time, Pallas kernels for 0%

profile of v6, /device:TPU:0, one launch (start us, length us, event | category | flops | bytes accessed | tf_op | source)
XLA Modules:
  0.0 274.6 jit_solution(12772609567938099964)
XLA Ops:
  2.6 3.0 %collective-permute-start = (bf16[320,256]{1,0:T(8,128)(2,1)}, bf16[320,256]{1,0:T(8,128)(2,1)}, u32[]{:S(2)}, u32[]{:S(2)}) collective-permute-start(bf16[320,256]{1,0:T(8,128)(2,1)} %bitcast.3), channel_id=1, source_target_pairs={{0,4},{4,12},{12,20},{20,28},{28,24},{24,16},{16,8},{8,0},{1,5},{5... | collective-permute-start | bytes 491528 | tf_op jit(solution)/shard_map/ppermute | solution.py:92
  55.4 3.2 %collective-permute-done.2 = bf16[320,256]{1,0:T(8,128)(2,1)S(1)} collective-permute-done((bf16[320,256]{1,0:T(8,128)(2,1)S(1)}, bf16[320,256]{1,0:T(8,128)(2,1)S(1)}, u32[]{:S(2)}, u32[]{:S(2)}) %collective-permute-start.2) | collective-permute-done | bytes 163872 | tf_op jit(solution)/shard_map/ppermute | solution.py:92
  60.9 4.3 %collective-permute-done.3 = bf16[320,256]{1,0:T(8,128)(2,1)S(1)} collective-permute-done((bf16[320,256]{1,0:T(8,128)(2,1)S(1)}, bf16[320,256]{1,0:T(8,128)(2,1)S(1)}, u32[]{:S(2)}, u32[]{:S(2)}) %collective-permute-start.3) | collective-permute-done | bytes 163872 | tf_op jit(solution)/shard_map/ppermute | solution.py:92
  67.9 4.4 %collective-permute-done.4 = bf16[320,256]{1,0:T(8,128)(2,1)S(1)} collective-permute-done((bf16[320,256]{1,0:T(8,128)(2,1)S(1)}, bf16[320,256]{1,0:T(8,128)(2,1)S(1)}, u32[]{:S(2)}, u32[]{:S(2)}) %collective-permute-start.4) | collective-permute-done | bytes 163872 | tf_op jit(solution)/shard_map/ppermute | solution.py:92
  74.4 3.6 %collective-permute-done.5 = bf16[320,256]{1,0:T(8,128)(2,1)S(1)} collective-permute-done((bf16[320,256]{1,0:T(8,128)(2,1)S(1)}, bf16[320,256]{1,0:T(8,128)(2,1)S(1)}, u32[]{:S(2)}, u32[]{:S(2)}) %collective-permute-start.5) | collective-permute-done | bytes 163872 | tf_op jit(solution)/shard_map/ppermute | solution.py:92
  80.1 5.1 %collective-permute-done.13 = bf16[320,256]{1,0:T(8,128)(2,1)S(1)} collective-permute-done((bf16[320,256]{1,0:T(8,128)(2,1)S(1)}, bf16[320,256]{1,0:T(8,128)(2,1)S(1)}, u32[]{:S(2)}, u32[]{:S(2)}) %collective-permute-start.13) | collective-permute-done | bytes 163872 | tf_op jit(solution)/shard_map/ppermute | solution.py:92
  88.1 28.3 %all_to_all.45 = bf16[16,256,256]{2,0,1:T(8,128)(2,1)S(1)} all-to-all(bf16[16,256,256]{2,0,1:T(8,128)(2,1)S(1)} %copy.42), channel_id=1, replica_groups=mesh['dp'=8,'feat'=4] {'feat'}, dimensions={1} | all-to-all | bytes 4194304 | tf_op jit(solution)/shard_map/all_to_all | solution.py:118
  121.3 4.6 %all-to-all-start.1 = ((bf16[16,256,256]{2,0,1:T(8,128)(2,1)}), bf16[16,256,256]{2,0,1:T(8,128)(2,1)}, u32[]{:S(2)}, u32[]{:S(2)}) async-start(bf16[16,256,256]{2,0,1:T(8,128)(2,1)} %copy.44), calls=%async_computation.1 | async-start | bytes 4194304 | tf_op jit(solution)/shard_map/all_to_all | solution.py:120
  132.2 19.3 %all-to-all-done.1 = bf16[16,256,256]{2,0,1:T(8,128)(2,1)} async-done(((bf16[16,256,256]{2,0,1:T(8,128)(2,1)}), bf16[16,256,256]{2,0,1:T(8,128)(2,1)}, u32[]{:S(2)}, u32[]{:S(2)}) %all-to-all-start.1) | async-done | bytes 2097184 | tf_op jit(solution)/shard_map/all_to_all | solution.py:120
  153.8 5.1 %fusion.6 = bf16[64,64,256]{2,0,1:T(8,128)(2,1)S(1)} fusion(f32[16,4,64,256]{3,0,1,2:T(8,128)S(1)} %copy.45, bf16[64,64,256]{2,0,1:T(8,128)(2,1)S(1)} %bitcast.200, bf16[64,64,64]{2,1,0:T(8,128)(2,1)S(1)} %reshape.142), kind=kOutput, calls=%fused_computation.8 | convolution fusion | flops 155189248 | bytes 8912896 | tf_op jit(solution)/shard_map/bst,bsc->cst/dot_general | solution.py:121
  164.8 3.8 %copy.51 = f32[64,64,64]{2,1,0:T(8,128)} copy(f32[64,64,64]{0,2,1:T(8,128)} %multiply_bitcast_fusion) | data formatting | bytes 2097152 | tf_op jit(solution)/shard_map/mul | solution.py:127
  171.3 4.4 %all-to-all-start.2 = ((bf16[64,64,256]{2,0,1:T(8,128)(2,1)}), bf16[64,64,256]{2,0,1:T(8,128)(2,1)}, u32[]{:S(2)}, u32[]{:S(2)}) async-start(bf16[64,64,256]{2,0,1:T(8,128)(2,1)} %copy.48), calls=%async_computation.2 | async-start | bytes 4194304 | tf_op jit(solution)/shard_map/all_to_all | solution.py:130
  178.9 3.8 %collective-permute-done.35 = f32[4,64,64]{2,1,0:T(8,128)S(1)} collective-permute-done((f32[4,64,64]{2,1,0:T(8,128)S(1)}, f32[4,64,64]{2,1,0:T(8,128)S(1)}, u32[]{:S(2)}, u32[]{:S(2)}) %collective-permute-start.35) | collective-permute-done | bytes 65568 | tf_op jit(solution)/shard_map/ppermute | solution.py:73
  185.7 3.1 %collective-permute-done.36 = f32[4,64,64]{2,1,0:T(8,128)S(1)} collective-permute-done((f32[4,64,64]{2,1,0:T(8,128)S(1)}, f32[4,64,64]{2,1,0:T(8,128)S(1)}, u32[]{:S(2)}, u32[]{:S(2)}) %collective-permute-start.36) | collective-permute-done | bytes 65568 | tf_op jit(solution)/shard_map/ppermute | solution.py:73
  191.8 2.9 %collective-permute-done.37 = f32[4,64,64]{2,1,0:T(8,128)S(1)} collective-permute-done((f32[4,64,64]{2,1,0:T(8,128)S(1)}, f32[4,64,64]{2,1,0:T(8,128)S(1)}, u32[]{:S(2)}, u32[]{:S(2)}) %collective-permute-start.37) | collective-permute-done | bytes 65568 | tf_op jit(solution)/shard_map/ppermute | solution.py:73
  197.8 2.9 %collective-permute-done.38 = f32[4,64,64]{2,1,0:T(8,128)S(1)} collective-permute-done((f32[4,64,64]{2,1,0:T(8,128)S(1)}, f32[4,64,64]{2,1,0:T(8,128)S(1)}, u32[]{:S(2)}, u32[]{:S(2)}) %collective-permute-start.38) | collective-permute-done | bytes 65568 | tf_op jit(solution)/shard_map/ppermute | solution.py:73
  203.7 2.9 %collective-permute-done.39 = f32[4,64,64]{2,1,0:T(8,128)S(1)} collective-permute-done((f32[4,64,64]{2,1,0:T(8,128)S(1)}, f32[4,64,64]{2,1,0:T(8,128)S(1)}, u32[]{:S(2)}, u32[]{:S(2)}) %collective-permute-start.39) | collective-permute-done | bytes 65568 | tf_op jit(solution)/shard_map/ppermute | solution.py:73
  216.7 2.7 collective-permute-done.21
  224.7 3.0 %collective-permute-done.22 = f32[16,16,256]{2,0,1:T(8,128)S(1)} collective-permute-done((f32[16,16,256]{2,0,1:T(8,128)S(1)}, f32[16,16,256]{2,0,1:T(8,128)S(1)}, u32[]{:S(2)}, u32[]{:S(2)}) %collective-permute-start.22) | collective-permute-done | bytes 262176 | tf_op jit(solution)/shard_map/ppermute | solution.py:73
  231.5 5.0 %collective-permute-done.23 = f32[16,16,256]{2,0,1:T(8,128)S(1)} collective-permute-done((f32[16,16,256]{2,0,1:T(8,128)S(1)}, f32[16,16,256]{2,0,1:T(8,128)S(1)}, u32[]{:S(2)}, u32[]{:S(2)}) %collective-permute-start.23) | collective-permute-done | bytes 262176 | tf_op jit(solution)/shard_map/ppermute | solution.py:73
  240.3 5.1 %collective-permute-done.24 = f32[16,16,256]{2,0,1:T(8,128)S(1)} collective-permute-done((f32[16,16,256]{2,0,1:T(8,128)S(1)}, f32[16,16,256]{2,0,1:T(8,128)S(1)}, u32[]{:S(2)}, u32[]{:S(2)}) %collective-permute-start.24) | collective-permute-done | bytes 262176 | tf_op jit(solution)/shard_map/ppermute | solution.py:73
  248.4 5.1 %collective-permute-done.25 = f32[16,16,256]{2,0,1:T(8,128)S(1)} collective-permute-done((f32[16,16,256]{2,0,1:T(8,128)S(1)}, f32[16,16,256]{2,0,1:T(8,128)S(1)}, u32[]{:S(2)}, u32[]{:S(2)}) %collective-permute-start.25) | collective-permute-done | bytes 262176 | tf_op jit(solution)/shard_map/ppermute | solution.py:73
  257.6 4.9 %collective-permute-done.26 = f32[16,16,256]{2,0,1:T(8,128)S(1)} collective-permute-done((f32[16,16,256]{2,0,1:T(8,128)S(1)}, f32[16,16,256]{2,0,1:T(8,128)S(1)}, u32[]{:S(2)}, u32[]{:S(2)}) %collective-permute-start.26) | collective-permute-done | bytes 262176 | tf_op jit(solution)/shard_map/ppermute | solution.py:73
  266.6 5.1 %add_convert_fusion = bf16[16,256,256]{2,1,0:T(8,128)(2,1)} fusion(bf16[16,256,256]{2,1,0:T(8,128)(2,1)} %bitcast.204, bf16[256,16,256]{2,0,1:T(8,128)(2,1)} %bitcast.198, bf16[256,16,256]{2,1,0:T(8,128)(2,1)} %bitcast.196), kind=kOutput, calls=%fused_computation.14 | convolution fusion | flops 540016640 | bytes 8388608 | tf_op jit(solution)/shard_map/obt,ibo->bit/dot_general | solution.py:131
  (164 shorter events, 97.3 us)
Async XLA Ops:
  2.6 44.8 %collective-permute-start = (bf16[320,256]{1,0:T(8,128)(2,1)}, bf16[320,256]{1,0:T(8,128)(2,1)}, u32[]{:S(2)}, u32[]{:S(2)}) collective-permute-start(bf16[320,256]{1,0:T(8,128)(2,1)} %bitcast.3), channel_id=1, source_target_pairs={{0,4},{4,12},{12,20},{20,28},{28,24},{24,16},{16,8},{8,0},{1,5},{5... | collective-permute-start | bytes 491528 | tf_op jit(solution)/shard_map/ppermute | solution.py:92
  8.5 41.0 %collective-permute-start.7 = (bf16[320,256]{1,0:T(8,128)(2,1)}, bf16[320,256]{1,0:T(8,128)(2,1)}, u32[]{:S(2)}, u32[]{:S(2)}) collective-permute-start(bf16[320,256]{1,0:T(8,128)(2,1)} %get-tuple-element.8), channel_id=1, source_target_pairs={{0,8},{4,0},{12,4},{20,12},{28,20},{24,28},{16,24},{8,16},{1,9},{5... | collective-permute-start | bytes 491528 | tf_op jit(solution)/shard_map/ppermute | solution.py:92
  78.0 7.2 %collective-permute-start.6 = (bf16[320,256]{1,0:T(8,128)(2,1)S(1)}, bf16[320,256]{1,0:T(8,128)(2,1)S(1)}, u32[]{:S(2)}, u32[]{:S(2)}) collective-permute-start(bf16[320,256]{1,0:T(8,128)(2,1)S(1)} %collective-permute-done.5), channel_id=1, source_target_pairs={{0,4},{4,12},{12,20},{20,28},{28,24},{24,16},{16,8},{8,0},{1,5},{5... | collective-permute-start | bytes 491528 | tf_op jit(solution)/shard_map/ppermute | solution.py:92
  121.3 30.2 %all-to-all-start.1 = ((bf16[16,256,256]{2,0,1:T(8,128)(2,1)}), bf16[16,256,256]{2,0,1:T(8,128)(2,1)}, u32[]{:S(2)}, u32[]{:S(2)}) async-start(bf16[16,256,256]{2,0,1:T(8,128)(2,1)} %copy.44), calls=%async_computation.1 | async-start | bytes 4194304 | tf_op jit(solution)/shard_map/all_to_all | solution.py:120
  171.3 36.8 %all-to-all-start.2 = ((bf16[64,64,256]{2,0,1:T(8,128)(2,1)}), bf16[64,64,256]{2,0,1:T(8,128)(2,1)}, u32[]{:S(2)}, u32[]{:S(2)}) async-start(bf16[64,64,256]{2,0,1:T(8,128)(2,1)} %copy.48), calls=%async_computation.2 | async-start | bytes 4194304 | tf_op jit(solution)/shard_map/all_to_all | solution.py:130
  202.2 12.0 %collective-permute-start.32 = (f32[4,64,64]{2,1,0:T(8,128)S(1)}, f32[4,64,64]{2,1,0:T(8,128)}, u32[]{:S(2)}, u32[]{:S(2)}) collective-permute-start(f32[4,64,64]{2,1,0:T(8,128)S(1)} %bitcast_add_fusion.24), channel_id=1, source_target_pairs={{0,4},{4,12},{12,20},{20,28},{28,24},{24,16},{16,8},{8,0},{1,5},{5... | collective-permute-start | bytes 196616 | tf_op jit(solution)/shard_map/ppermute | solution.py:73
  207.6 14.3 %collective-permute-start.40 = (f32[4,64,64]{2,1,0:T(8,128)S(1)}, f32[4,64,64]{2,1,0:T(8,128)S(1)}, u32[]{:S(2)}, u32[]{:S(2)}) collective-permute-start(f32[4,64,64]{2,1,0:T(8,128)S(1)} %bitcast_add_fusion.16), channel_id=1, source_target_pairs={{0,8},{4,0},{12,4},{20,12},{28,20},{24,28},{16,24},{8,16},{1,9},{5... | collective-permute-start | bytes 196616 | tf_op jit(solution)/shard_map/ppermute | solution.py:73
  212.0 7.4 %collective-permute-start.21 = (f32[16,16,256]{2,0,1:T(8,128)S(1)}, f32[16,16,256]{2,0,1:T(8,128)S(1)}, u32[]{:S(2)}, u32[]{:S(2)}) collective-permute-start(f32[16,16,256]{2,0,1:T(8,128)S(1)} %dynamic-slice_bitcast_fusion), channel_id=1, source_target_pairs={{0,8},{4,0},{12,4},{20,12},{28,20},{24,28},{16,24},{8,16},{1,9},{5... | collective-permute-start | bytes 786440 | tf_op jit(solution)/shard_map/ppermute | solution.py:73
  213.5 8.1 %collective-permute-start.14 = (f32[16,16,256]{2,0,1:T(8,128)S(1)}, f32[16,16,256]{2,0,1:T(8,128)S(1)}, u32[]{:S(2)}, u32[]{:S(2)}) collective-permute-start(f32[16,16,256]{2,0,1:T(8,128)S(1)} %dynamic-slice_bitcast_fusion.1), channel_id=1, source_target_pairs={{0,4},{4,12},{12,20},{20,28},{28,24},{24,16},{16,8},{8,0},{1,5},{5... | collective-permute-start | bytes 786440 | tf_op jit(solution)/shard_map/ppermute | solution.py:73
  215.1 15.0 %collective-permute-start.33 = (f32[4,64,64]{2,1,0:T(8,128)S(1)}, f32[4,64,64]{2,1,0:T(8,128)S(1)}, u32[]{:S(2)}, u32[]{:S(2)}) collective-permute-start(f32[4,64,64]{2,1,0:T(8,128)S(1)} %bitcast_add_fusion.23), channel_id=1, source_target_pairs={{0,4},{4,12},{12,20},{20,28},{28,24},{24,16},{16,8},{8,0},{1,5},{5... | collective-permute-start | bytes 196616 | tf_op jit(solution)/shard_map/ppermute | solution.py:73
  219.5 8.2 %collective-permute-start.22 = (f32[16,16,256]{2,0,1:T(8,128)S(1)}, f32[16,16,256]{2,0,1:T(8,128)S(1)}, u32[]{:S(2)}, u32[]{:S(2)}) collective-permute-start(f32[16,16,256]{2,0,1:T(8,128)S(1)} %bitcast_add_fusion.6), channel_id=1, source_target_pairs={{0,8},{4,0},{12,4},{20,12},{28,20},{24,28},{16,24},{8,16},{1,9},{5... | collective-permute-start | bytes 786440 | tf_op jit(solution)/shard_map/ppermute | solution.py:73
  221.6 8.4 %collective-permute-start.15 = (f32[16,16,256]{2,0,1:T(8,128)S(1)}, f32[16,16,256]{2,0,1:T(8,128)S(1)}, u32[]{:S(2)}, u32[]{:S(2)}) collective-permute-start(f32[16,16,256]{2,0,1:T(8,128)S(1)} %bitcast_add_fusion.13), channel_id=1, source_target_pairs={{0,4},{4,12},{12,20},{20,28},{28,24},{24,16},{16,8},{8,0},{1,5},{5... | collective-permute-start | bytes 786440 | tf_op jit(solution)/shard_map/ppermute | solution.py:73
  222.8 16.5 %collective-permute-start.41 = (f32[4,64,64]{2,1,0:T(8,128)S(1)}, f32[4,64,64]{2,1,0:T(8,128)S(1)}, u32[]{:S(2)}, u32[]{:S(2)}) collective-permute-start(f32[4,64,64]{2,1,0:T(8,128)S(1)} %bitcast_add_fusion.15), channel_id=1, source_target_pairs={{0,8},{4,0},{12,4},{20,12},{28,20},{24,28},{16,24},{8,16},{1,9},{5... | collective-permute-start | bytes 196616 | tf_op jit(solution)/shard_map/ppermute | solution.py:73
  227.7 8.8 %collective-permute-start.23 = (f32[16,16,256]{2,0,1:T(8,128)S(1)}, f32[16,16,256]{2,0,1:T(8,128)S(1)}, u32[]{:S(2)}, u32[]{:S(2)}) collective-permute-start(f32[16,16,256]{2,0,1:T(8,128)S(1)} %bitcast_add_fusion.5), channel_id=1, source_target_pairs={{0,8},{4,0},{12,4},{20,12},{28,20},{24,28},{16,24},{8,16},{1,9},{5... | collective-permute-start | bytes 786440 | tf_op jit(solution)/shard_map/ppermute | solution.py:73
  230.1 9.2 %collective-permute-start.16 = (f32[16,16,256]{2,0,1:T(8,128)S(1)}, f32[16,16,256]{2,0,1:T(8,128)S(1)}, u32[]{:S(2)}, u32[]{:S(2)}) collective-permute-start(f32[16,16,256]{2,0,1:T(8,128)S(1)} %bitcast_add_fusion.12), channel_id=1, source_target_pairs={{0,4},{4,12},{12,20},{20,28},{28,24},{24,16},{16,8},{8,0},{1,5},{5... | collective-permute-start | bytes 786440 | tf_op jit(solution)/shard_map/ppermute | solution.py:73
  230.2 18.2 %collective-permute-start.34 = (f32[4,64,64]{2,1,0:T(8,128)S(1)}, f32[4,64,64]{2,1,0:T(8,128)S(1)}, u32[]{:S(2)}, u32[]{:S(2)}) collective-permute-start(f32[4,64,64]{2,1,0:T(8,128)S(1)} %bitcast_add_fusion.22), channel_id=1, source_target_pairs={{0,4},{4,12},{12,20},{20,28},{28,24},{24,16},{16,8},{8,0},{1,5},{5... | collective-permute-start | bytes 196616 | tf_op jit(solution)/shard_map/ppermute | solution.py:73
  236.5 8.9 %collective-permute-start.24 = (f32[16,16,256]{2,0,1:T(8,128)S(1)}, f32[16,16,256]{2,0,1:T(8,128)S(1)}, u32[]{:S(2)}, u32[]{:S(2)}) collective-permute-start(f32[16,16,256]{2,0,1:T(8,128)S(1)} %bitcast_add_fusion.4), channel_id=1, source_target_pairs={{0,8},{4,0},{12,4},{20,12},{28,20},{24,28},{16,24},{8,16},{1,9},{5... | collective-permute-start | bytes 786440 | tf_op jit(solution)/shard_map/ppermute | solution.py:73
  239.3 8.4 %collective-permute-start.17 = (f32[16,16,256]{2,0,1:T(8,128)S(1)}, f32[16,16,256]{2,0,1:T(8,128)S(1)}, u32[]{:S(2)}, u32[]{:S(2)}) collective-permute-start(f32[16,16,256]{2,0,1:T(8,128)S(1)} %bitcast_add_fusion.11), channel_id=1, source_target_pairs={{0,4},{4,12},{12,20},{20,28},{28,24},{24,16},{16,8},{8,0},{1,5},{5... | collective-permute-start | bytes 786440 | tf_op jit(solution)/shard_map/ppermute | solution.py:73
  245.4 8.1 %collective-permute-start.25 = (f32[16,16,256]{2,0,1:T(8,128)S(1)}, f32[16,16,256]{2,0,1:T(8,128)S(1)}, u32[]{:S(2)}, u32[]{:S(2)}) collective-permute-start(f32[16,16,256]{2,0,1:T(8,128)S(1)} %bitcast_add_fusion.3), channel_id=1, source_target_pairs={{0,8},{4,0},{12,4},{20,12},{28,20},{24,28},{16,24},{8,16},{1,9},{5... | collective-permute-start | bytes 786440 | tf_op jit(solution)/shard_map/ppermute | solution.py:73
  247.8 7.8 %collective-permute-start.18 = (f32[16,16,256]{2,0,1:T(8,128)S(1)}, f32[16,16,256]{2,0,1:T(8,128)S(1)}, u32[]{:S(2)}, u32[]{:S(2)}) collective-permute-start(f32[16,16,256]{2,0,1:T(8,128)S(1)} %bitcast_add_fusion.10), channel_id=1, source_target_pairs={{0,4},{4,12},{12,20},{20,28},{28,24},{24,16},{16,8},{8,0},{1,5},{5... | collective-permute-start | bytes 786440 | tf_op jit(solution)/shard_map/ppermute | solution.py:73
  253.6 8.9 %collective-permute-start.26 = (f32[16,16,256]{2,0,1:T(8,128)S(1)}, f32[16,16,256]{2,0,1:T(8,128)S(1)}, u32[]{:S(2)}, u32[]{:S(2)}) collective-permute-start(f32[16,16,256]{2,0,1:T(8,128)S(1)} %bitcast_add_fusion.2), channel_id=1, source_target_pairs={{0,8},{4,0},{12,4},{20,12},{28,20},{24,28},{16,24},{8,16},{1,9},{5... | collective-permute-start | bytes 786440 | tf_op jit(solution)/shard_map/ppermute | solution.py:73
  255.6 8.8 %collective-permute-start.19 = (f32[16,16,256]{2,0,1:T(8,128)S(1)}, f32[16,16,256]{2,0,1:T(8,128)S(1)}, u32[]{:S(2)}, u32[]{:S(2)}) collective-permute-start(f32[16,16,256]{2,0,1:T(8,128)S(1)} %bitcast_add_fusion.9), channel_id=1, source_target_pairs={{0,4},{4,12},{12,20},{20,28},{28,24},{24,16},{16,8},{8,0},{1,5},{5... | collective-permute-start | bytes 786440 | tf_op jit(solution)/shard_map/ppermute | solution.py:73
  263.5 8.3 %collective-permute-start.27 = (f32[16,16,256]{2,0,1:T(8,128)S(1)}, f32[16,16,256]{2,0,1:T(8,128)S(1)}, u32[]{:S(2)}, u32[]{:S(2)}) collective-permute-start(f32[16,16,256]{2,0,1:T(8,128)S(1)} %bitcast_add_fusion.1), channel_id=1, source_target_pairs={{0,8},{4,0},{12,4},{20,12},{28,20},{24,28},{16,24},{8,16},{1,9},{5... | collective-permute-start | bytes 786440 | tf_op jit(solution)/shard_map/ppermute | solution.py:73
  265.4 7.4 %collective-permute-start.20 = (f32[16,16,256]{2,0,1:T(8,128)S(1)}, f32[16,16,256]{2,0,1:T(8,128)S(1)}, u32[]{:S(2)}, u32[]{:S(2)}) collective-permute-start(f32[16,16,256]{2,0,1:T(8,128)S(1)} %bitcast_add_fusion.8), channel_id=1, source_target_pairs={{0,4},{4,12},{12,20},{20,28},{28,24},{24,16},{16,8},{8,0},{1,5},{5... | collective-permute-start | bytes 786440 | tf_op jit(solution)/shard_map/ppermute | solution.py:73
  (30 other events, 326.7 us)

commit v7 on v5

--- a/solution.py
+++ b/solution.py
@@ -81,20 +81,17 @@
     place = jnp.asarray(np.argsort(np.array(ring)).astype(np.int32))
     me = lax.axis_index("dp")
     here = place[me]
-    half = piece.shape[0] // 2
     forward = [(ring[p], ring[(p + 1) % n]) for p in range(n)]
     backward = [(ring[p], ring[(p - 1) % n]) for p in range(n)]
-    outs = []
-    for way, pairs, src in ((1, forward, piece[:half]), (-1, backward, piece[half:])):
-        held = lax.dynamic_update_index_in_dim(jnp.zeros((n,) + src.shape, src.dtype), src, me, 0)
-        cur = src
-        for step in range(n - 1):
+    held = lax.dynamic_update_index_in_dim(jnp.zeros((n,) + piece.shape, piece.dtype), piece, me, 0)
+    ahead = n // 2
+    for way, pairs, hops in ((1, forward, ahead), (-1, backward, n - 1 - ahead)):
+        cur = piece
+        for step in range(hops):
             cur = lax.ppermute(cur, "dp", pairs)
             owner = order[(here - way * (1 + step)) % n]
             held = lax.dynamic_update_index_in_dim(held, cur, owner, 0)
-        outs.append(held)
-    return jnp.concatenate(outs, axis=1)
-
+    return held
 
 def body(ring, activations, cotangent, r_mix, l_mix):
     tok_count = activations.shape[1]

time: 255 us -> 229 us (0.90)
  waiting for transfers between devices: 80.8 us -> 68.4 us
  starting transfers between devices: 62 us -> 51.9 us
    all_to_all x1, waiting for transfers between devices: 14.9 us -> 1.3 us  [body(): lax.all_to_all(mixed_rows, 'feat', split_axis=1, concat_axis=0, tiled=True)]
    ppermute x14 -> x7, starting transfers between devices: 15.4 us -> 8.93 us  [ring_all_gather(): cur = lax.ppermute(cur, 'dp', pairs)]
    ppermute x28, starting transfers between devices: 32.8 us -> 29.3 us  [ring_reduce_scatter(): acc = lax.ppermute(acc, 'dp', pairs)]
    ppermute x28, waiting for transfers between devices: 41.9 us -> 45.3 us  [ring_reduce_scatter(): acc = lax.ppermute(acc, 'dp', pairs)]
    ppermute x14 -> x7, waiting for transfers between devices: 23.9 us -> 21.8 us  [ring_all_gather(): cur = lax.ppermute(cur, 'dp', pairs)]
  transfers between devices with their start and end apart: 45 -> 38, of which waited for: 19 -> 16; matrix products, arithmetic and copies ran while one was open for 17% -> 17% of each run, Pallas kernels for 0% -> 0%
where the time goes in v7:
time: 229 us; the launch traced here: 228 us
  waiting for transfers between devices  68.4 us (30%)
  starting transfers between devices  51.9 us (23%)
  between operations  41.5 us (18%)
  local copies, waits for them, and re-layouts  37.7 us (16%)
  matrix products  15.8 us (7%)
  other arithmetic  12.7 us (6%)
    ppermute x28, waiting for transfers between devices, ring_reduce_scatter(): acc = lax.ppermute(acc, 'dp', pairs)  45.3 us
    ppermute x28, starting transfers between devices, ring_reduce_scatter(): acc = lax.ppermute(acc, 'dp', pairs)  29.3 us
    ppermute x7, waiting for transfers between devices, ring_all_gather(): cur = lax.ppermute(cur, 'dp', pairs)  21.8 us
    add x28, other arithmetic, ring_reduce_scatter(): acc = mine if acc is None else acc + mine  11.8 us
    ppermute x7, starting transfers between devices, ring_all_gather(): cur = lax.ppermute(cur, 'dp', pairs)  8.93 us
    dot_general x1, matrix products, body(): jnp.einsum('obt,ibo->bit', back_rows, r_whole, preferred_element_type=jnp...  5.13 us
    dot_general x1, matrix products, body(): jnp.einsum('bst,bsc->cst', columns, l_blocks, preferred_element_type=jnp....  5.07 us
    all_to_all x1, starting transfers between devices, body(): lax.all_to_all(mixed_rows, 'feat', split_axis=1, concat_axis=0, tiled=True)  4.65 us
  transfers between devices with their start and end apart: 38, of which 16 were waited for; matrix products, arithmetic and copies ran while one was open for 17% of the time, Pallas kernels for 0%

profile of v7, /device:TPU:0, one launch (start us, length us, event | category | flops | bytes accessed | tf_op | source)
XLA Modules:
  0.0 228.0 jit_solution(13052850072499111885)
XLA Ops:
  3.1 3.0 %collective-permute-start = (bf16[640,256]{1,0:T(8,128)(2,1)S(1)}, bf16[640,256]{1,0:T(8,128)(2,1)}, u32[]{:S(2)}, u32[]{:S(2)}) collective-permute-start(bf16[640,256]{1,0:T(8,128)(2,1)S(1)} %pad_maximum_fusion), channel_id=1, source_target_pairs={{0,4},{4,12},{12,20},{20,28},{28,24},{24,16},{16,8},{8,0},{1,5},{5... | collective-permute-start | bytes 983048 | tf_op jit(solution)/shard_map/ppermute | solution.py:91
  6.2 7.7 %collective-permute-done = bf16[640,256]{1,0:T(8,128)(2,1)} collective-permute-done((bf16[640,256]{1,0:T(8,128)(2,1)S(1)}, bf16[640,256]{1,0:T(8,128)(2,1)}, u32[]{:S(2)}, u32[]{:S(2)}) %collective-permute-start) | collective-permute-done | bytes 327712 | tf_op jit(solution)/shard_map/ppermute | solution.py:91
  15.7 4.1 %copy.41 = bf16[16,256,256]{2,0,1:T(8,128)(2,1)} copy(bf16[16,256,256]{2,1,0:T(8,128)(2,1)} %bitcast.183) | data formatting | bytes 4194304 | tf_op jit(solution)/shard_map/reshape | solution.py:102
  19.8 4.6 %all-to-all-start = ((bf16[16,256,256]{2,0,1:T(8,128)(2,1)}), bf16[16,256,256]{2,0,1:T(8,128)(2,1)}, u32[]{:S(2)}, u32[]{:S(2)}) async-start(bf16[16,256,256]{2,0,1:T(8,128)(2,1)} %copy.41), calls=%async_computation | async-start | bytes 4194304 | tf_op jit(solution)/shard_map/all_to_all | solution.py:103
  52.9 6.8 %collective-permute-done.5 = bf16[640,256]{1,0:T(8,128)(2,1)S(1)} collective-permute-done((bf16[640,256]{1,0:T(8,128)(2,1)S(1)}, bf16[640,256]{1,0:T(8,128)(2,1)S(1)}, u32[]{:S(2)}, u32[]{:S(2)}) %collective-permute-start.5) | collective-permute-done | bytes 327712 | tf_op jit(solution)/shard_map/ppermute | solution.py:91
  61.8 7.2 %collective-permute-done.3 = bf16[640,256]{1,0:T(8,128)(2,1)S(1)} collective-permute-done((bf16[640,256]{1,0:T(8,128)(2,1)S(1)}, bf16[640,256]{1,0:T(8,128)(2,1)S(1)}, u32[]{:S(2)}, u32[]{:S(2)}) %collective-permute-start.3) | collective-permute-done | bytes 327712 | tf_op jit(solution)/shard_map/ppermute | solution.py:91
  74.8 4.6 %all-to-all-start.1 = ((bf16[16,256,256]{2,0,1:T(8,128)(2,1)}), bf16[16,256,256]{2,0,1:T(8,128)(2,1)}, u32[]{:S(2)}, u32[]{:S(2)}) async-start(bf16[16,256,256]{2,0,1:T(8,128)(2,1)} %copy.44), calls=%async_computation.1 | async-start | bytes 4194304 | tf_op jit(solution)/shard_map/all_to_all | solution.py:116
  99.5 4.2 %copy.42 = f32[16,4,64,256]{3,0,1,2:T(8,128)} copy(bf16[16,4,64,256]{3,0,2,1:T(8,128)(2,1)} %bitcast.100) | data formatting | bytes 6291456 | tf_op jit(solution)/shard_map/convert_element_type | solution.py:19
  107.8 5.1 %fusion.6 = bf16[64,64,256]{2,0,1:T(8,128)(2,1)S(1)} fusion(f32[16,4,64,256]{3,0,1,2:T(8,128)S(1)} %copy-done.6, bf16[64,64,256]{2,0,1:T(8,128)(2,1)S(1)} %bitcast.180, bf16[64,64,64]{2,1,0:T(8,128)(2,1)S(1)} %reshape.126), kind=kOutput, calls=%fused_computation.8 | convolution fusion | flops 155189248 | bytes 8912896 | tf_op jit(solution)/shard_map/bst,bsc->cst/dot_general | solution.py:117
  118.7 3.8 %copy.51 = f32[64,64,64]{2,1,0:T(8,128)} copy(f32[64,64,64]{0,2,1:T(8,128)} %multiply_bitcast_fusion) | data formatting | bytes 2097152 | tf_op jit(solution)/shard_map/mul | solution.py:123
  122.6 2.7 %fusion.15 = (f32[8,4,64,64]{3,2,1,0:T(8,128)S(1)}, f32[8,4,64,64]{3,2,1,0:T(8,128)}) fusion(f32[8,8,64,64]{3,2,1,0:T(8,128)} %bitcast.182), kind=kLoop, calls=%fused_computation.68 | loop fusion | bytes 2097152 | tf_op jit(solution)/shard_map/slice | solution.py:62
  125.2 4.4 %all-to-all-start.2 = ((bf16[64,64,256]{2,0,1:T(8,128)(2,1)}), bf16[64,64,256]{2,0,1:T(8,128)(2,1)}, u32[]{:S(2)}, u32[]{:S(2)}) async-start(bf16[64,64,256]{2,0,1:T(8,128)(2,1)} %copy.48), calls=%async_computation.2 | async-start | bytes 4194304 | tf_op jit(solution)/shard_map/all_to_all | solution.py:126
  132.8 3.8 %collective-permute-done.28 = f32[4,64,64]{2,1,0:T(8,128)S(1)} collective-permute-done((f32[4,64,64]{2,1,0:T(8,128)S(1)}, f32[4,64,64]{2,1,0:T(8,128)S(1)}, u32[]{:S(2)}, u32[]{:S(2)}) %collective-permute-start.28) | collective-permute-done | bytes 65568 | tf_op jit(solution)/shard_map/ppermute | solution.py:73
  139.6 3.1 %collective-permute-done.29 = f32[4,64,64]{2,1,0:T(8,128)S(1)} collective-permute-done((f32[4,64,64]{2,1,0:T(8,128)S(1)}, f32[4,64,64]{2,1,0:T(8,128)S(1)}, u32[]{:S(2)}, u32[]{:S(2)}) %collective-permute-start.29) | collective-permute-done | bytes 65568 | tf_op jit(solution)/shard_map/ppermute | solution.py:73
  145.8 2.9 %collective-permute-done.30 = f32[4,64,64]{2,1,0:T(8,128)S(1)} collective-permute-done((f32[4,64,64]{2,1,0:T(8,128)S(1)}, f32[4,64,64]{2,1,0:T(8,128)S(1)}, u32[]{:S(2)}, u32[]{:S(2)}) %collective-permute-start.30) | collective-permute-done | bytes 65568 | tf_op jit(solution)/shard_map/ppermute | solution.py:73
  151.7 2.9 %collective-permute-done.31 = f32[4,64,64]{2,1,0:T(8,128)S(1)} collective-permute-done((f32[4,64,64]{2,1,0:T(8,128)S(1)}, f32[4,64,64]{2,1,0:T(8,128)S(1)}, u32[]{:S(2)}, u32[]{:S(2)}) %collective-permute-start.31) | collective-permute-done | bytes 65568 | tf_op jit(solution)/shard_map/ppermute | solution.py:73
  157.7 2.9 %collective-permute-done.32 = f32[4,64,64]{2,1,0:T(8,128)S(1)} collective-permute-done((f32[4,64,64]{2,1,0:T(8,128)S(1)}, f32[4,64,64]{2,1,0:T(8,128)S(1)}, u32[]{:S(2)}, u32[]{:S(2)}) %collective-permute-start.32) | collective-permute-done | bytes 65568 | tf_op jit(solution)/shard_map/ppermute | solution.py:73
  170.6 4.7 %collective-permute-done.14 = f32[16,16,256]{2,0,1:T(8,128)S(1)} collective-permute-done((f32[16,16,256]{2,0,1:T(8,128)S(1)}, f32[16,16,256]{2,0,1:T(8,128)S(1)}, u32[]{:S(2)}, u32[]{:S(2)}) %collective-permute-start.14) | collective-permute-done | bytes 262176 | tf_op jit(solution)/shard_map/ppermute | solution.py:73
  180.2 4.2 %collective-permute-done.15 = f32[16,16,256]{2,0,1:T(8,128)S(1)} collective-permute-done((f32[16,16,256]{2,0,1:T(8,128)S(1)}, f32[16,16,256]{2,0,1:T(8,128)S(1)}, u32[]{:S(2)}, u32[]{:S(2)}) %collective-permute-start.15) | collective-permute-done | bytes 262176 | tf_op jit(solution)/shard_map/ppermute | solution.py:73
  186.7 6.5 %collective-permute-done.16 = f32[16,16,256]{2,0,1:T(8,128)S(1)} collective-permute-done((f32[16,16,256]{2,0,1:T(8,128)S(1)}, f32[16,16,256]{2,0,1:T(8,128)S(1)}, u32[]{:S(2)}, u32[]{:S(2)}) %collective-permute-start.16) | collective-permute-done | bytes 262176 | tf_op jit(solution)/shard_map/ppermute | solution.py:73
  196.4 4.9 %collective-permute-done.17 = f32[16,16,256]{2,0,1:T(8,128)S(1)} collective-permute-done((f32[16,16,256]{2,0,1:T(8,128)S(1)}, f32[16,16,256]{2,0,1:T(8,128)S(1)}, u32[]{:S(2)}, u32[]{:S(2)}) %collective-permute-start.17) | collective-permute-done | bytes 262176 | tf_op jit(solution)/shard_map/ppermute | solution.py:73
  203.5 4.9 %collective-permute-done.18 = f32[16,16,256]{2,0,1:T(8,128)S(1)} collective-permute-done((f32[16,16,256]{2,0,1:T(8,128)S(1)}, f32[16,16,256]{2,0,1:T(8,128)S(1)}, u32[]{:S(2)}, u32[]{:S(2)}) %collective-permute-start.18) | collective-permute-done | bytes 262176 | tf_op jit(solution)/shard_map/ppermute | solution.py:73
  211.7 4.2 %collective-permute-done.19 = f32[16,16,256]{2,0,1:T(8,128)S(1)} collective-permute-done((f32[16,16,256]{2,0,1:T(8,128)S(1)}, f32[16,16,256]{2,0,1:T(8,128)S(1)}, u32[]{:S(2)}, u32[]{:S(2)}) %collective-permute-start.19) | collective-permute-done | bytes 262176 | tf_op jit(solution)/shard_map/ppermute | solution.py:73
  220.0 5.1 %add_convert_fusion = bf16[16,256,256]{2,1,0:T(8,128)(2,1)} fusion(bf16[16,256,256]{2,1,0:T(8,128)(2,1)} %bitcast.184, bf16[256,16,256]{2,0,1:T(8,128)(2,1)} %bitcast.178, bf16[256,16,256]{2,1,0:T(8,128)(2,1)} %bitcast.176), kind=kOutput, calls=%fused_computation.14 | convolution fusion | flops 540016640 | bytes 8388608 | tf_op jit(solution)/shard_map/obt,ibo->bit/dot_general | solution.py:127
  (140 shorter events, 78.1 us)
Async XLA Ops:
  3.1 10.9 %collective-permute-start = (bf16[640,256]{1,0:T(8,128)(2,1)S(1)}, bf16[640,256]{1,0:T(8,128)(2,1)}, u32[]{:S(2)}, u32[]{:S(2)}) collective-permute-start(bf16[640,256]{1,0:T(8,128)(2,1)S(1)} %pad_maximum_fusion), channel_id=1, source_target_pairs={{0,4},{4,12},{12,20},{20,28},{28,24},{24,16},{16,8},{8,0},{1,5},{5... | collective-permute-start | bytes 983048 | tf_op jit(solution)/shard_map/ppermute | solution.py:91
  6.1 43.4 %collective-permute-start.4 = (bf16[640,256]{1,0:T(8,128)(2,1)S(1)}, bf16[640,256]{1,0:T(8,128)(2,1)S(1)}, u32[]{:S(2)}, u32[]{:S(2)}) collective-permute-start(bf16[640,256]{1,0:T(8,128)(2,1)S(1)} %pad_maximum_fusion), channel_id=1, source_target_pairs={{0,8},{4,0},{12,4},{20,12},{28,20},{24,28},{16,24},{8,16},{1,9},{5... | collective-permute-start | bytes 983048 | tf_op jit(solution)/shard_map/ppermute | solution.py:91
  14.0 36.0 %collective-permute-start.1 = (bf16[640,256]{1,0:T(8,128)(2,1)}, bf16[640,256]{1,0:T(8,128)(2,1)S(1)}, u32[]{:S(2)}, u32[]{:S(2)}) collective-permute-start(bf16[640,256]{1,0:T(8,128)(2,1)} %collective-permute-done), channel_id=1, source_target_pairs={{0,4},{4,12},{12,20},{20,28},{28,24},{24,16},{16,8},{8,0},{1,5},{5... | collective-permute-start | bytes 983048 | tf_op jit(solution)/shard_map/ppermute | solution.py:91
  19.8 55.0 %all-to-all-start = ((bf16[16,256,256]{2,0,1:T(8,128)(2,1)}), bf16[16,256,256]{2,0,1:T(8,128)(2,1)}, u32[]{:S(2)}, u32[]{:S(2)}) async-start(bf16[16,256,256]{2,0,1:T(8,128)(2,1)} %copy.41), calls=%async_computation | async-start | bytes 4194304 | tf_op jit(solution)/shard_map/all_to_all | solution.py:103
  49.6 10.1 %collective-permute-start.5 = (bf16[640,256]{1,0:T(8,128)(2,1)S(1)}, bf16[640,256]{1,0:T(8,128)(2,1)S(1)}, u32[]{:S(2)}, u32[]{:S(2)}) collective-permute-start(bf16[640,256]{1,0:T(8,128)(2,1)S(1)} %collective-permute-done.4), channel_id=1, source_target_pairs={{0,8},{4,0},{12,4},{20,12},{28,20},{24,28},{16,24},{8,16},{1,9},{5... | collective-permute-start | bytes 983048 | tf_op jit(solution)/shard_map/ppermute | solution.py:91
  50.0 10.1 %collective-permute-start.2 = (bf16[640,256]{1,0:T(8,128)(2,1)S(1)}, bf16[640,256]{1,0:T(8,128)(2,1)S(1)}, u32[]{:S(2)}, u32[]{:S(2)}) collective-permute-start(bf16[640,256]{1,0:T(8,128)(2,1)S(1)} %collective-permute-done.1), channel_id=1, source_target_pairs={{0,4},{4,12},{12,20},{20,28},{28,24},{24,16},{16,8},{8,0},{1,5},{5... | collective-permute-start | bytes 983048 | tf_op jit(solution)/shard_map/ppermute | solution.py:91
  59.7 9.4 %collective-permute-start.6 = (bf16[640,256]{1,0:T(8,128)(2,1)S(1)}, bf16[640,256]{1,0:T(8,128)(2,1)S(1)}, u32[]{:S(2)}, u32[]{:S(2)}) collective-permute-start(bf16[640,256]{1,0:T(8,128)(2,1)S(1)} %collective-permute-done.5), channel_id=1, source_target_pairs={{0,8},{4,0},{12,4},{20,12},{28,20},{24,28},{16,24},{8,16},{1,9},{5... | collective-permute-start | bytes 983048 | tf_op jit(solution)/shard_map/ppermute | solution.py:91
  60.0 9.0 %collective-permute-start.3 = (bf16[640,256]{1,0:T(8,128)(2,1)S(1)}, bf16[640,256]{1,0:T(8,128)(2,1)S(1)}, u32[]{:S(2)}, u32[]{:S(2)}) collective-permute-start(bf16[640,256]{1,0:T(8,128)(2,1)S(1)} %collective-permute-done.2), channel_id=1, source_target_pairs={{0,4},{4,12},{12,20},{20,28},{28,24},{24,16},{16,8},{8,0},{1,5},{5... | collective-permute-start | bytes 983048 | tf_op jit(solution)/shard_map/ppermute | solution.py:91
  74.8 30.2 %all-to-all-start.1 = ((bf16[16,256,256]{2,0,1:T(8,128)(2,1)}), bf16[16,256,256]{2,0,1:T(8,128)(2,1)}, u32[]{:S(2)}, u32[]{:S(2)}) async-start(bf16[16,256,256]{2,0,1:T(8,128)(2,1)} %copy.44), calls=%async_computation.1 | async-start | bytes 4194304 | tf_op jit(solution)/shard_map/all_to_all | solution.py:116
  125.2 38.0 %all-to-all-start.2 = ((bf16[64,64,256]{2,0,1:T(8,128)(2,1)}), bf16[64,64,256]{2,0,1:T(8,128)(2,1)}, u32[]{:S(2)}, u32[]{:S(2)}) async-start(bf16[64,64,256]{2,0,1:T(8,128)(2,1)} %copy.48), calls=%async_computation.2 | async-start | bytes 4194304 | tf_op jit(solution)/shard_map/all_to_all | solution.py:126
  157.3 12.0 %collective-permute-start.25 = (f32[4,64,64]{2,1,0:T(8,128)S(1)}, f32[4,64,64]{2,1,0:T(8,128)}, u32[]{:S(2)}, u32[]{:S(2)}) collective-permute-start(f32[4,64,64]{2,1,0:T(8,128)S(1)} %bitcast_add_fusion.24), channel_id=1, source_target_pairs={{0,4},{4,12},{12,20},{20,28},{28,24},{24,16},{16,8},{8,0},{1,5},{5... | collective-permute-start | bytes 196616 | tf_op jit(solution)/shard_map/ppermute | solution.py:73
  161.5 16.3 %collective-permute-start.33 = (f32[4,64,64]{2,1,0:T(8,128)S(1)}, f32[4,64,64]{2,1,0:T(8,128)S(1)}, u32[]{:S(2)}, u32[]{:S(2)}) collective-permute-start(f32[4,64,64]{2,1,0:T(8,128)S(1)} %bitcast_add_fusion.16), channel_id=1, source_target_pairs={{0,8},{4,0},{12,4},{20,12},{28,20},{24,28},{16,24},{8,16},{1,9},{5... | collective-permute-start | bytes 196616 | tf_op jit(solution)/shard_map/ppermute | solution.py:73
  167.2 8.2 %collective-permute-start.14 = (f32[16,16,256]{2,0,1:T(8,128)S(1)}, f32[16,16,256]{2,0,1:T(8,128)S(1)}, u32[]{:S(2)}, u32[]{:S(2)}) collective-permute-start(f32[16,16,256]{2,0,1:T(8,128)S(1)} %dynamic-slice_bitcast_fusion), channel_id=1, source_target_pairs={{0,8},{4,0},{12,4},{20,12},{28,20},{24,28},{16,24},{8,16},{1,9},{5... | collective-permute-start | bytes 786440 | tf_op jit(solution)/shard_map/ppermute | solution.py:73
  168.8 8.3 %collective-permute-start.7 = (f32[16,16,256]{2,0,1:T(8,128)S(1)}, f32[16,16,256]{2,0,1:T(8,128)S(1)}, u32[]{:S(2)}, u32[]{:S(2)}) collective-permute-start(f32[16,16,256]{2,0,1:T(8,128)S(1)} %dynamic-slice_bitcast_fusion.1), channel_id=1, source_target_pairs={{0,4},{4,12},{12,20},{20,28},{28,24},{24,16},{16,8},{8,0},{1,5},{5... | collective-permute-start | bytes 786440 | tf_op jit(solution)/shard_map/ppermute | solution.py:73
  170.2 16.4 %collective-permute-start.26 = (f32[4,64,64]{2,1,0:T(8,128)S(1)}, f32[4,64,64]{2,1,0:T(8,128)S(1)}, u32[]{:S(2)}, u32[]{:S(2)}) collective-permute-start(f32[4,64,64]{2,1,0:T(8,128)S(1)} %bitcast_add_fusion.23), channel_id=1, source_target_pairs={{0,4},{4,12},{12,20},{20,28},{28,24},{24,16},{16,8},{8,0},{1,5},{5... | collective-permute-start | bytes 196616 | tf_op jit(solution)/shard_map/ppermute | solution.py:73
  175.4 9.0 %collective-permute-start.15 = (f32[16,16,256]{2,0,1:T(8,128)S(1)}, f32[16,16,256]{2,0,1:T(8,128)S(1)}, u32[]{:S(2)}, u32[]{:S(2)}) collective-permute-start(f32[16,16,256]{2,0,1:T(8,128)S(1)} %bitcast_add_fusion.6), channel_id=1, source_target_pairs={{0,8},{4,0},{12,4},{20,12},{28,20},{24,28},{16,24},{8,16},{1,9},{5... | collective-permute-start | bytes 786440 | tf_op jit(solution)/shard_map/ppermute | solution.py:73
  177.2 8.7 %collective-permute-start.8 = (f32[16,16,256]{2,0,1:T(8,128)S(1)}, f32[16,16,256]{2,0,1:T(8,128)S(1)}, u32[]{:S(2)}, u32[]{:S(2)}) collective-permute-start(f32[16,16,256]{2,0,1:T(8,128)S(1)} %bitcast_add_fusion.13), channel_id=1, source_target_pairs={{0,4},{4,12},{12,20},{20,28},{28,24},{24,16},{16,8},{8,0},{1,5},{5... | collective-permute-start | bytes 786440 | tf_op jit(solution)/shard_map/ppermute | solution.py:73
  178.7 16.7 %collective-permute-start.34 = (f32[4,64,64]{2,1,0:T(8,128)S(1)}, f32[4,64,64]{2,1,0:T(8,128)S(1)}, u32[]{:S(2)}, u32[]{:S(2)}) collective-permute-start(f32[4,64,64]{2,1,0:T(8,128)S(1)} %bitcast_add_fusion.15), channel_id=1, source_target_pairs={{0,8},{4,0},{12,4},{20,12},{28,20},{24,28},{16,24},{8,16},{1,9},{5... | collective-permute-start | bytes 196616 | tf_op jit(solution)/shard_map/ppermute | solution.py:73
  184.4 8.8 %collective-permute-start.16 = (f32[16,16,256]{2,0,1:T(8,128)S(1)}, f32[16,16,256]{2,0,1:T(8,128)S(1)}, u32[]{:S(2)}, u32[]{:S(2)}) collective-permute-start(f32[16,16,256]{2,0,1:T(8,128)S(1)} %bitcast_add_fusion.5), channel_id=1, source_target_pairs={{0,8},{4,0},{12,4},{20,12},{28,20},{24,28},{16,24},{8,16},{1,9},{5... | collective-permute-start | bytes 786440 | tf_op jit(solution)/shard_map/ppermute | solution.py:73
  185.9 9.0 %collective-permute-start.9 = (f32[16,16,256]{2,0,1:T(8,128)S(1)}, f32[16,16,256]{2,0,1:T(8,128)S(1)}, u32[]{:S(2)}, u32[]{:S(2)}) collective-permute-start(f32[16,16,256]{2,0,1:T(8,128)S(1)} %bitcast_add_fusion.12), channel_id=1, source_target_pairs={{0,4},{4,12},{12,20},{20,28},{28,24},{24,16},{16,8},{8,0},{1,5},{5... | collective-permute-start | bytes 786440 | tf_op jit(solution)/shard_map/ppermute | solution.py:73
  186.6 16.9 %collective-permute-start.27 = (f32[4,64,64]{2,1,0:T(8,128)S(1)}, f32[4,64,64]{2,1,0:T(8,128)S(1)}, u32[]{:S(2)}, u32[]{:S(2)}) collective-permute-start(f32[4,64,64]{2,1,0:T(8,128)S(1)} %bitcast_add_fusion.22), channel_id=1, source_target_pairs={{0,4},{4,12},{12,20},{20,28},{28,24},{24,16},{16,8},{8,0},{1,5},{5... | collective-permute-start | bytes 196616 | tf_op jit(solution)/shard_map/ppermute | solution.py:73
  194.9 8.1 %collective-permute-start.10 = (f32[16,16,256]{2,0,1:T(8,128)S(1)}, f32[16,16,256]{2,0,1:T(8,128)S(1)}, u32[]{:S(2)}, u32[]{:S(2)}) collective-permute-start(f32[16,16,256]{2,0,1:T(8,128)S(1)} %bitcast_add_fusion.11), channel_id=1, source_target_pairs={{0,4},{4,12},{12,20},{20,28},{28,24},{24,16},{16,8},{8,0},{1,5},{5... | collective-permute-start | bytes 786440 | tf_op jit(solution)/shard_map/ppermute | solution.py:73
  210.3 8.2 %collective-permute-start.12 = (f32[16,16,256]{2,0,1:T(8,128)S(1)}, f32[16,16,256]{2,0,1:T(8,128)S(1)}, u32[]{:S(2)}, u32[]{:S(2)}) collective-permute-start(f32[16,16,256]{2,0,1:T(8,128)S(1)} %bitcast_add_fusion.9), channel_id=1, source_target_pairs={{0,4},{4,12},{12,20},{20,28},{28,24},{24,16},{16,8},{8,0},{1,5},{5... | collective-permute-start | bytes 786440 | tf_op jit(solution)/shard_map/ppermute | solution.py:73
  216.8 8.3 %collective-permute-start.20 = (f32[16,16,256]{2,0,1:T(8,128)S(1)}, f32[16,16,256]{2,0,1:T(8,128)S(1)}, u32[]{:S(2)}, u32[]{:S(2)}) collective-permute-start(f32[16,16,256]{2,0,1:T(8,128)S(1)} %bitcast_add_fusion.1), channel_id=1, source_target_pairs={{0,8},{4,0},{12,4},{20,12},{28,20},{24,28},{16,24},{8,16},{1,9},{5... | collective-permute-start | bytes 786440 | tf_op jit(solution)/shard_map/ppermute | solution.py:73
  (23 other events, 269.6 us)

commit v8 on v7

--- a/solution.py
+++ b/solution.py
@@ -57,23 +57,20 @@
     n = len(ring)
     order = jnp.asarray(np.array(ring, np.int32))
     place = jnp.asarray(np.argsort(np.array(ring)).astype(np.int32))
-    here = place[lax.axis_index("dp")]
-    half = parts.shape[1] // 2
-    halves = (parts[:, :half], parts[:, half:])
+    me = lax.axis_index("dp")
+    here = place[me]
     forward = [(ring[p], ring[(p + 1) % n]) for p in range(n)]
     backward = [(ring[p], ring[(p - 1) % n]) for p in range(n)]
-    totals = []
-    for way, pairs, src in ((1, forward, halves[0]), (-1, backward, halves[1])):
+    total = lax.dynamic_index_in_dim(parts, me, axis=0, keepdims=False)
+    ahead = n // 2
+    for way, pairs, hops in ((1, forward, ahead), (-1, backward, n - 1 - ahead)):
         acc = None
-        for step in range(n):
-            owner = order[(here - way * (1 + step)) % n]
-            mine = lax.dynamic_index_in_dim(src, owner, axis=0, keepdims=False)
-            acc = mine if acc is None else acc + mine
-            if step < n - 1:
-                acc = lax.ppermute(acc, "dp", pairs)
-        totals.append(acc)
-    return jnp.concatenate(totals, axis=0)
-
+        for step in range(hops):
+            owner = order[(here + way * (hops - step)) % n]
+            mine = lax.dynamic_index_in_dim(parts, owner, axis=0, keepdims=False)
+            acc = lax.ppermute(mine if acc is None else acc + mine, "dp", pairs)
+        total = total + acc
+    return total
 
 def ring_all_gather(piece, ring):
     n = len(ring)

time: 229 us -> 224 us (0.978)
  waiting for transfers between devices: 68.4 us -> 105 us
  between operations: 41.5 us -> 21.5 us
  starting transfers between devices: 51.9 us -> 38.5 us
  other arithmetic: 12.7 us -> 7.09 us
    all_to_all x1, waiting for transfers between devices: 0.01 us -> 23.8 us  [body(): lax.all_to_all(back_cols, 'feat', split_axis=1, concat_axis=0, tiled=True)]
    all_to_all x1, waiting for transfers between devices: 1.3 us -> 17.9 us  [body(): lax.all_to_all(mixed_rows, 'feat', split_axis=1, concat_axis=0, tiled=True)]
    ppermute x28 -> x14, starting transfers between devices: 29.3 us -> 15.8 us  [ring_reduce_scatter(): acc = lax.ppermute(mine if acc is None else acc + mine, 'dp', pairs)]
    add x28 -> x6, other arithmetic: 11.8 us -> 5.05 us  [ring_reduce_scatter(): acc = lax.ppermute(mine if acc is None else acc + mine, 'dp', pairs)]
    ppermute x28 -> x14, waiting for transfers between devices: 45.3 us -> 41.3 us  [ring_reduce_scatter(): acc = lax.ppermute(mine if acc is None else acc + mine, 'dp', pairs)]
    slice x2 -> x0, local copies, waits for them, and re-layouts: 3.32 us -> none  [ring_reduce_scatter(): halves = (parts[:, :half], parts[:, half:])]
  transfers between devices with their start and end apart: 38 -> 24, of which waited for: 16 -> 13; matrix products, arithmetic and copies ran while one was open for 17% -> 16% of each run, Pallas kernels for 0% -> 0%
where the time goes in v8:
time: 224 us; the launch traced here: 223 us
  waiting for transfers between devices  105 us (47%)
  starting transfers between devices  38.5 us (17%)
  local copies, waits for them, and re-layouts  35.6 us (16%)
  between operations  21.5 us (10%)
  matrix products  15.8 us (7%)
  other arithmetic  7.09 us (3%)
    ppermute x14, waiting for transfers between devices, ring_reduce_scatter(): acc = lax.ppermute(mine if acc is None else acc + mine, 'dp', pairs)  41.3 us
    all_to_all x1, waiting for transfers between devices, body(): lax.all_to_all(back_cols, 'feat', split_axis=1, concat_axis=0, tiled=True)  23.8 us
    ppermute x7, waiting for transfers between devices, ring_all_gather(): cur = lax.ppermute(cur, 'dp', pairs)  21.8 us
    all_to_all x1, waiting for transfers between devices, body(): lax.all_to_all(mixed_rows, 'feat', split_axis=1, concat_axis=0, tiled=True)  17.9 us
    ppermute x14, starting transfers between devices, ring_reduce_scatter(): acc = lax.ppermute(mine if acc is None else acc + mine, 'dp', pairs)  15.8 us
    ppermute x7, starting transfers between devices, ring_all_gather(): cur = lax.ppermute(cur, 'dp', pairs)  8.93 us
    dot_general x1, matrix products, body(): jnp.einsum('obt,ibo->bit', back_rows, r_whole, preferred_element_type=jnp...  5.13 us
    dot_general x1, matrix products, body(): jnp.einsum('bst,bsc->cst', columns, l_blocks, preferred_element_type=jnp....  5.07 us
  transfers between devices with their start and end apart: 24, of which 13 were waited for; matrix products, arithmetic and copies ran while one was open for 16% of the time, Pallas kernels for 0%

profile of v8, /device:TPU:0, one launch (start us, length us, event | category | flops | bytes accessed | tf_op | source)
XLA Modules:
  0.0 223.2 jit_solution(5783341824366014954)
XLA Ops:
  3.1 3.0 %collective-permute-start = (bf16[640,256]{1,0:T(8,128)(2,1)S(1)}, bf16[640,256]{1,0:T(8,128)(2,1)}, u32[]{:S(2)}, u32[]{:S(2)}) collective-permute-start(bf16[640,256]{1,0:T(8,128)(2,1)S(1)} %pad_maximum_fusion), channel_id=1, source_target_pairs={{0,4},{4,12},{12,20},{20,28},{28,24},{24,16},{16,8},{8,0},{1,5},{5... | collective-permute-start | bytes 983048 | tf_op jit(solution)/shard_map/ppermute | solution.py:88
  6.2 7.7 %collective-permute-done = bf16[640,256]{1,0:T(8,128)(2,1)} collective-permute-done((bf16[640,256]{1,0:T(8,128)(2,1)S(1)}, bf16[640,256]{1,0:T(8,128)(2,1)}, u32[]{:S(2)}, u32[]{:S(2)}) %collective-permute-start) | collective-permute-done | bytes 327712 | tf_op jit(solution)/shard_map/ppermute | solution.py:88
  15.7 4.1 %copy.41 = bf16[16,256,256]{2,0,1:T(8,128)(2,1)} copy(bf16[16,256,256]{2,1,0:T(8,128)(2,1)} %bitcast.146) | data formatting | bytes 4194304 | tf_op jit(solution)/shard_map/reshape | solution.py:99
  19.8 4.6 %all-to-all-start = ((bf16[16,256,256]{2,0,1:T(8,128)(2,1)}), bf16[16,256,256]{2,0,1:T(8,128)(2,1)}, u32[]{:S(2)}, u32[]{:S(2)}) async-start(bf16[16,256,256]{2,0,1:T(8,128)(2,1)} %copy.41), calls=%async_computation | async-start | bytes 4194304 | tf_op jit(solution)/shard_map/all_to_all | solution.py:100
  47.5 6.8 %collective-permute-done.5 = bf16[640,256]{1,0:T(8,128)(2,1)S(1)} collective-permute-done((bf16[640,256]{1,0:T(8,128)(2,1)S(1)}, bf16[640,256]{1,0:T(8,128)(2,1)S(1)}, u32[]{:S(2)}, u32[]{:S(2)}) %collective-permute-start.5) | collective-permute-done | bytes 327712 | tf_op jit(solution)/shard_map/ppermute | solution.py:88
  56.4 7.2 %collective-permute-done.3 = bf16[640,256]{1,0:T(8,128)(2,1)S(1)} collective-permute-done((bf16[640,256]{1,0:T(8,128)(2,1)S(1)}, bf16[640,256]{1,0:T(8,128)(2,1)S(1)}, u32[]{:S(2)}, u32[]{:S(2)}) %collective-permute-start.3) | collective-permute-done | bytes 327712 | tf_op jit(solution)/shard_map/ppermute | solution.py:88
  67.0 2.6 %copy.44 = bf16[16,256,256]{2,0,1:T(8,128)(2,1)} copy(bf16[16,256,256]{2,1,0:T(8,128)(2,1)S(1)} %convolution_convert_fusion.1) | data formatting | bytes 4194304 | tf_op jit(solution)/shard_map/convert_element_type | solution.py:112
  69.5 4.7 %all-to-all-start.1 = ((bf16[16,256,256]{2,0,1:T(8,128)(2,1)}), bf16[16,256,256]{2,0,1:T(8,128)(2,1)}, u32[]{:S(2)}, u32[]{:S(2)}) async-start(bf16[16,256,256]{2,0,1:T(8,128)(2,1)} %copy.44), calls=%async_computation.1 | async-start | bytes 4194304 | tf_op jit(solution)/shard_map/all_to_all | solution.py:113
  77.7 4.2 %copy.42 = f32[16,4,64,256]{3,0,1,2:T(8,128)} copy(bf16[16,4,64,256]{3,0,2,1:T(8,128)(2,1)} %bitcast.68) | data formatting | bytes 6291456 | tf_op jit(solution)/shard_map/convert_element_type | solution.py:19
  81.9 17.9 %all-to-all-done.1 = bf16[16,256,256]{2,0,1:T(8,128)(2,1)} async-done(((bf16[16,256,256]{2,0,1:T(8,128)(2,1)}), bf16[16,256,256]{2,0,1:T(8,128)(2,1)}, u32[]{:S(2)}, u32[]{:S(2)}) %all-to-all-start.1) | async-done | bytes 2097184 | tf_op jit(solution)/shard_map/all_to_all | solution.py:113
  99.8 2.0 copy.45
  102.6 5.1 %fusion.6 = bf16[64,64,256]{2,0,1:T(8,128)(2,1)S(1)} fusion(f32[16,4,64,256]{3,0,1,2:T(8,128)S(1)} %copy-done.10, bf16[64,64,256]{2,0,1:T(8,128)(2,1)S(1)} %bitcast.144, bf16[64,64,64]{2,1,0:T(8,128)(2,1)S(1)} %reshape.90), kind=kOutput, calls=%fused_computation.8 | convolution fusion | flops 155189248 | bytes 8912896 | tf_op jit(solution)/shard_map/bst,bsc->cst/dot_general | solution.py:114
  109.1 2.5 %copy.48 = bf16[64,64,256]{2,0,1:T(8,128)(2,1)} copy(bf16[64,64,256]{2,1,0:T(8,128)(2,1)S(1)} %convolution_convert_fusion) | data formatting | bytes 4194304 | tf_op jit(solution)/shard_map/convert_element_type | solution.py:118
  111.6 4.4 %all-to-all-start.2 = ((bf16[64,64,256]{2,0,1:T(8,128)(2,1)}), bf16[64,64,256]{2,0,1:T(8,128)(2,1)}, u32[]{:S(2)}, u32[]{:S(2)}) async-start(bf16[64,64,256]{2,0,1:T(8,128)(2,1)} %copy.48), calls=%async_computation.2 | async-start | bytes 4194304 | tf_op jit(solution)/shard_map/all_to_all | solution.py:123
  118.0 23.8 %all-to-all-done.2 = bf16[64,64,256]{2,0,1:T(8,128)(2,1)} async-done(((bf16[64,64,256]{2,0,1:T(8,128)(2,1)}), bf16[64,64,256]{2,0,1:T(8,128)(2,1)}, u32[]{:S(2)}, u32[]{:S(2)}) %all-to-all-start.2) | async-done | bytes 2097184 | tf_op jit(solution)/shard_map/all_to_all | solution.py:123
  148.0 11.4 %collective-permute-done.7 = f32[32,16,256]{2,0,1:T(8,128)S(1)} collective-permute-done((f32[32,16,256]{2,0,1:T(8,128)S(1)}, f32[32,16,256]{2,0,1:T(8,128)S(1)}, u32[]{:S(2)}, u32[]{:S(2)}) %collective-permute-start.7) | collective-permute-done | bytes 524320 | tf_op jit(solution)/shard_map/ppermute | solution.py:71
  161.2 2.0 multiply_bitcast_fusion
  163.2 3.8 %copy.51 = f32[64,64,64]{2,1,0:T(8,128)} copy(f32[64,64,64]{0,2,1:T(8,128)} %multiply_bitcast_fusion) | data formatting | bytes 2097152 | tf_op jit(solution)/shard_map/mul | solution.py:120
  170.3 7.4 %collective-permute-done.14 = f32[8,64,64]{2,1,0:T(8,128)S(1)} collective-permute-done((f32[8,64,64]{2,1,0:T(8,128)S(1)}, f32[8,64,64]{2,1,0:T(8,128)S(1)}, u32[]{:S(2)}, u32[]{:S(2)}) %collective-permute-start.14) | collective-permute-done | bytes 131104 | tf_op jit(solution)/shard_map/ppermute | solution.py:71
  184.0 3.9 %collective-permute-done.15 = f32[8,64,64]{2,1,0:T(8,128)S(1)} collective-permute-done((f32[8,64,64]{2,1,0:T(8,128)S(1)}, f32[8,64,64]{2,1,0:T(8,128)S(1)}, u32[]{:S(2)}, u32[]{:S(2)}) %collective-permute-start.15) | collective-permute-done | bytes 131104 | tf_op jit(solution)/shard_map/ppermute | solution.py:71
  190.1 11.8 %collective-permute-done.16 = f32[8,64,64]{2,1,0:T(8,128)S(1)} collective-permute-done((f32[8,64,64]{2,1,0:T(8,128)S(1)}, f32[8,64,64]{2,1,0:T(8,128)S(1)}, u32[]{:S(2)}, u32[]{:S(2)}) %collective-permute-start.16) | collective-permute-done | bytes 131104 | tf_op jit(solution)/shard_map/ppermute | solution.py:71
  204.1 2.4 %bitcast_add_fusion.2 = (f32[32,16,256]{2,0,1:T(8,128)}, f32[32,16,256]{2,0,1:T(8,128)}) fusion(f32[32,16,256]{2,0,1:T(8,128)S(1)} %collective-permute-done.9, f32[8,32,16,256]{3,1,0,2:T(8,128)} %bitcast.142, s32[]{:T(128)S(6)} %select_n.239, f32[32,16,256]{2,0,1:T(8,128)S(1)} %collective-permute-done.12, s32[]{:T(128)S(6)} %select_n.227), kind=kLoop, calls=%fused_computation.25 | loop fusion | flops 262144 | bytes 3145736 | tf_op jit(solution)/shard_map/add | solution.py:71
  208.4 2.5 %collective-permute-done.17 = f32[8,64,64]{2,1,0:T(8,128)S(1)} collective-permute-done((f32[8,64,64]{2,1,0:T(8,128)S(1)}, f32[8,64,64]{2,1,0:T(8,128)S(1)}, u32[]{:S(2)}, u32[]{:S(2)}) %collective-permute-start.17) | collective-permute-done | bytes 131104 | tf_op jit(solution)/shard_map/ppermute | solution.py:71
  213.9 5.1 %add_convert_fusion = bf16[16,256,256]{2,1,0:T(8,128)(2,1)} fusion(bf16[16,256,256]{2,1,0:T(8,128)(2,1)} %bitcast.147, bf16[256,16,256]{2,0,1:T(8,128)(2,1)} %bitcast.138, bf16[256,16,256]{2,1,0:T(8,128)(2,1)} %bitcast.136), kind=kOutput, calls=%fused_computation.14 | convolution fusion | flops 540016640 | bytes 8388608 | tf_op jit(solution)/shard_map/obt,ibo->bit/dot_general | solution.py:124
  (94 shorter events, 50.8 us)
Async XLA Ops:
  3.1 10.9 %collective-permute-start = (bf16[640,256]{1,0:T(8,128)(2,1)S(1)}, bf16[640,256]{1,0:T(8,128)(2,1)}, u32[]{:S(2)}, u32[]{:S(2)}) collective-permute-start(bf16[640,256]{1,0:T(8,128)(2,1)S(1)} %pad_maximum_fusion), channel_id=1, source_target_pairs={{0,4},{4,12},{12,20},{20,28},{28,24},{24,16},{16,8},{8,0},{1,5},{5... | collective-permute-start | bytes 983048 | tf_op jit(solution)/shard_map/ppermute | solution.py:88
  6.1 38.1 %collective-permute-start.4 = (bf16[640,256]{1,0:T(8,128)(2,1)S(1)}, bf16[640,256]{1,0:T(8,128)(2,1)S(1)}, u32[]{:S(2)}, u32[]{:S(2)}) collective-permute-start(bf16[640,256]{1,0:T(8,128)(2,1)S(1)} %pad_maximum_fusion), channel_id=1, source_target_pairs={{0,8},{4,0},{12,4},{20,12},{28,20},{24,28},{16,24},{8,16},{1,9},{5... | collective-permute-start | bytes 983048 | tf_op jit(solution)/shard_map/ppermute | solution.py:88
  14.0 30.6 %collective-permute-start.1 = (bf16[640,256]{1,0:T(8,128)(2,1)}, bf16[640,256]{1,0:T(8,128)(2,1)S(1)}, u32[]{:S(2)}, u32[]{:S(2)}) collective-permute-start(bf16[640,256]{1,0:T(8,128)(2,1)} %collective-permute-done), channel_id=1, source_target_pairs={{0,4},{4,12},{12,20},{20,28},{28,24},{24,16},{16,8},{8,0},{1,5},{5... | collective-permute-start | bytes 983048 | tf_op jit(solution)/shard_map/ppermute | solution.py:88
  19.8 49.8 %all-to-all-start = ((bf16[16,256,256]{2,0,1:T(8,128)(2,1)}), bf16[16,256,256]{2,0,1:T(8,128)(2,1)}, u32[]{:S(2)}, u32[]{:S(2)}) async-start(bf16[16,256,256]{2,0,1:T(8,128)(2,1)} %copy.41), calls=%async_computation | async-start | bytes 4194304 | tf_op jit(solution)/shard_map/all_to_all | solution.py:100
  44.2 10.1 %collective-permute-start.5 = (bf16[640,256]{1,0:T(8,128)(2,1)S(1)}, bf16[640,256]{1,0:T(8,128)(2,1)S(1)}, u32[]{:S(2)}, u32[]{:S(2)}) collective-permute-start(bf16[640,256]{1,0:T(8,128)(2,1)S(1)} %collective-permute-done.4), channel_id=1, source_target_pairs={{0,8},{4,0},{12,4},{20,12},{28,20},{24,28},{16,24},{8,16},{1,9},{5... | collective-permute-start | bytes 983048 | tf_op jit(solution)/shard_map/ppermute | solution.py:88
  44.6 10.1 %collective-permute-start.2 = (bf16[640,256]{1,0:T(8,128)(2,1)S(1)}, bf16[640,256]{1,0:T(8,128)(2,1)S(1)}, u32[]{:S(2)}, u32[]{:S(2)}) collective-permute-start(bf16[640,256]{1,0:T(8,128)(2,1)S(1)} %collective-permute-done.1), channel_id=1, source_target_pairs={{0,4},{4,12},{12,20},{20,28},{28,24},{24,16},{16,8},{8,0},{1,5},{5... | collective-permute-start | bytes 983048 | tf_op jit(solution)/shard_map/ppermute | solution.py:88
  54.3 9.4 %collective-permute-start.6 = (bf16[640,256]{1,0:T(8,128)(2,1)S(1)}, bf16[640,256]{1,0:T(8,128)(2,1)S(1)}, u32[]{:S(2)}, u32[]{:S(2)}) collective-permute-start(bf16[640,256]{1,0:T(8,128)(2,1)S(1)} %collective-permute-done.5), channel_id=1, source_target_pairs={{0,8},{4,0},{12,4},{20,12},{28,20},{24,28},{16,24},{8,16},{1,9},{5... | collective-permute-start | bytes 983048 | tf_op jit(solution)/shard_map/ppermute | solution.py:88
  54.6 9.0 %collective-permute-start.3 = (bf16[640,256]{1,0:T(8,128)(2,1)S(1)}, bf16[640,256]{1,0:T(8,128)(2,1)S(1)}, u32[]{:S(2)}, u32[]{:S(2)}) collective-permute-start(bf16[640,256]{1,0:T(8,128)(2,1)S(1)} %collective-permute-done.2), channel_id=1, source_target_pairs={{0,4},{4,12},{12,20},{20,28},{28,24},{24,16},{16,8},{8,0},{1,5},{5... | collective-permute-start | bytes 983048 | tf_op jit(solution)/shard_map/ppermute | solution.py:88
  69.5 30.2 %all-to-all-start.1 = ((bf16[16,256,256]{2,0,1:T(8,128)(2,1)}), bf16[16,256,256]{2,0,1:T(8,128)(2,1)}, u32[]{:S(2)}, u32[]{:S(2)}) async-start(bf16[16,256,256]{2,0,1:T(8,128)(2,1)} %copy.44), calls=%async_computation.1 | async-start | bytes 4194304 | tf_op jit(solution)/shard_map/all_to_all | solution.py:113
  111.6 30.2 %all-to-all-start.2 = ((bf16[64,64,256]{2,0,1:T(8,128)(2,1)}), bf16[64,64,256]{2,0,1:T(8,128)(2,1)}, u32[]{:S(2)}, u32[]{:S(2)}) async-start(bf16[64,64,256]{2,0,1:T(8,128)(2,1)} %copy.48), calls=%async_computation.2 | async-start | bytes 4194304 | tf_op jit(solution)/shard_map/all_to_all | solution.py:123
  145.9 13.5 %collective-permute-start.7 = (f32[32,16,256]{2,0,1:T(8,128)S(1)}, f32[32,16,256]{2,0,1:T(8,128)S(1)}, u32[]{:S(2)}, u32[]{:S(2)}) collective-permute-start(f32[32,16,256]{2,0,1:T(8,128)S(1)} %get-tuple-element.7), channel_id=1, source_target_pairs={{0,4},{4,12},{12,20},{20,28},{28,24},{24,16},{16,8},{8,0},{1,5},{5... | collective-permute-start | bytes 1572872 | tf_op jit(solution)/shard_map/ppermute | solution.py:71
  147.6 32.8 %collective-permute-start.11 = (f32[32,16,256]{2,0,1:T(8,128)}, f32[32,16,256]{2,0,1:T(8,128)S(1)}, u32[]{:S(2)}, u32[]{:S(2)}) collective-permute-start(f32[32,16,256]{2,0,1:T(8,128)} %get-tuple-element.8), channel_id=1, source_target_pairs={{0,8},{4,0},{12,4},{20,12},{28,20},{24,28},{16,24},{8,16},{1,9},{5... | collective-permute-start | bytes 1572872 | tf_op jit(solution)/shard_map/ppermute | solution.py:71
  159.5 21.0 %collective-permute-start.8 = (f32[32,16,256]{2,0,1:T(8,128)S(1)}, f32[32,16,256]{2,0,1:T(8,128)}, u32[]{:S(2)}, u32[]{:S(2)}) collective-permute-start(f32[32,16,256]{2,0,1:T(8,128)S(1)} %bitcast_add_fusion.4), channel_id=1, source_target_pairs={{0,4},{4,12},{12,20},{20,28},{28,24},{24,16},{16,8},{8,0},{1,5},{5... | collective-permute-start | bytes 1572872 | tf_op jit(solution)/shard_map/ppermute | solution.py:71
  168.2 9.5 %collective-permute-start.14 = (f32[8,64,64]{2,1,0:T(8,128)S(1)}, f32[8,64,64]{2,1,0:T(8,128)S(1)}, u32[]{:S(2)}, u32[]{:S(2)}) collective-permute-start(f32[8,64,64]{2,1,0:T(8,128)S(1)} %get-tuple-element.13), channel_id=1, source_target_pairs={{0,4},{4,12},{12,20},{20,28},{28,24},{24,16},{16,8},{8,0},{1,5},{5... | collective-permute-start | bytes 393224 | tf_op jit(solution)/shard_map/ppermute | solution.py:71
  169.9 14.2 %collective-permute-start.18 = (f32[8,64,64]{2,1,0:T(8,128)S(1)}, f32[8,64,64]{2,1,0:T(8,128)S(1)}, u32[]{:S(2)}, u32[]{:S(2)}) collective-permute-start(f32[8,64,64]{2,1,0:T(8,128)S(1)} %get-tuple-element.14), channel_id=1, source_target_pairs={{0,8},{4,0},{12,4},{20,12},{28,20},{24,28},{16,24},{8,16},{1,9},{5... | collective-permute-start | bytes 393224 | tf_op jit(solution)/shard_map/ppermute | solution.py:71
  178.7 9.2 %collective-permute-start.15 = (f32[8,64,64]{2,1,0:T(8,128)S(1)}, f32[8,64,64]{2,1,0:T(8,128)S(1)}, u32[]{:S(2)}, u32[]{:S(2)}) collective-permute-start(f32[8,64,64]{2,1,0:T(8,128)S(1)} %bitcast_add_fusion.10), channel_id=1, source_target_pairs={{0,4},{4,12},{12,20},{20,28},{28,24},{24,16},{16,8},{8,0},{1,5},{5... | collective-permute-start | bytes 393224 | tf_op jit(solution)/shard_map/ppermute | solution.py:71
  182.0 22.1 %collective-permute-start.12 = (f32[32,16,256]{2,0,1:T(8,128)S(1)}, f32[32,16,256]{2,0,1:T(8,128)S(1)}, u32[]{:S(2)}, u32[]{:S(2)}) collective-permute-start(f32[32,16,256]{2,0,1:T(8,128)S(1)} %get-tuple-element.6), channel_id=1, source_target_pairs={{0,8},{4,0},{12,4},{20,12},{28,20},{24,28},{16,24},{8,16},{1,9},{5... | collective-permute-start | bytes 1572872 | tf_op jit(solution)/shard_map/ppermute | solution.py:71
  182.3 21.7 %collective-permute-start.9 = (f32[32,16,256]{2,0,1:T(8,128)S(1)}, f32[32,16,256]{2,0,1:T(8,128)S(1)}, u32[]{:S(2)}, u32[]{:S(2)}) collective-permute-start(f32[32,16,256]{2,0,1:T(8,128)S(1)} %get-tuple-element.5), channel_id=1, source_target_pairs={{0,4},{4,12},{12,20},{20,28},{28,24},{24,16},{16,8},{8,0},{1,5},{5... | collective-permute-start | bytes 1572872 | tf_op jit(solution)/shard_map/ppermute | solution.py:71
  188.0 13.9 %collective-permute-start.16 = (f32[8,64,64]{2,1,0:T(8,128)S(1)}, f32[8,64,64]{2,1,0:T(8,128)S(1)}, u32[]{:S(2)}, u32[]{:S(2)}) collective-permute-start(f32[8,64,64]{2,1,0:T(8,128)S(1)} %get-tuple-element.11), channel_id=1, source_target_pairs={{0,4},{4,12},{12,20},{20,28},{28,24},{24,16},{16,8},{8,0},{1,5},{5... | collective-permute-start | bytes 393224 | tf_op jit(solution)/shard_map/ppermute | solution.py:71
  189.7 12.2 %collective-permute-start.19 = (f32[8,64,64]{2,1,0:T(8,128)S(1)}, f32[8,64,64]{2,1,0:T(8,128)S(1)}, u32[]{:S(2)}, u32[]{:S(2)}) collective-permute-start(f32[8,64,64]{2,1,0:T(8,128)S(1)} %get-tuple-element.12), channel_id=1, source_target_pairs={{0,8},{4,0},{12,4},{20,12},{28,20},{24,28},{16,24},{8,16},{1,9},{5... | collective-permute-start | bytes 393224 | tf_op jit(solution)/shard_map/ppermute | solution.py:71
  202.0 8.9 %collective-permute-start.17 = (f32[8,64,64]{2,1,0:T(8,128)S(1)}, f32[8,64,64]{2,1,0:T(8,128)S(1)}, u32[]{:S(2)}, u32[]{:S(2)}) collective-permute-start(f32[8,64,64]{2,1,0:T(8,128)S(1)} %get-tuple-element.9), channel_id=1, source_target_pairs={{0,4},{4,12},{12,20},{20,28},{28,24},{24,16},{16,8},{8,0},{1,5},{5... | collective-permute-start | bytes 393224 | tf_op jit(solution)/shard_map/ppermute | solution.py:71
  203.7 9.2 %collective-permute-start.20 = (f32[8,64,64]{2,1,0:T(8,128)S(1)}, f32[8,64,64]{2,1,0:T(8,128)S(1)}, u32[]{:S(2)}, u32[]{:S(2)}) collective-permute-start(f32[8,64,64]{2,1,0:T(8,128)S(1)} %get-tuple-element.10), channel_id=1, source_target_pairs={{0,8},{4,0},{12,4},{20,12},{28,20},{24,28},{16,24},{8,16},{1,9},{5... | collective-permute-start | bytes 393224 | tf_op jit(solution)/shard_map/ppermute | solution.py:71
  206.4 13.2 %collective-permute-start.10 = (f32[32,16,256]{2,0,1:T(8,128)}, f32[32,16,256]{2,0,1:T(8,128)S(1)}, u32[]{:S(2)}, u32[]{:S(2)}) collective-permute-start(f32[32,16,256]{2,0,1:T(8,128)} %get-tuple-element.3), channel_id=1, source_target_pairs={{0,4},{4,12},{12,20},{20,28},{28,24},{24,16},{16,8},{8,0},{1,5},{5... | collective-permute-start | bytes 1572872 | tf_op jit(solution)/shard_map/ppermute | solution.py:71
  208.1 13.2 %collective-permute-start.13 = (f32[32,16,256]{2,0,1:T(8,128)}, f32[32,16,256]{2,0,1:T(8,128)S(1)}, u32[]{:S(2)}, u32[]{:S(2)}) collective-permute-start(f32[32,16,256]{2,0,1:T(8,128)} %get-tuple-element.4), channel_id=1, source_target_pairs={{0,8},{4,0},{12,4},{20,12},{28,20},{24,28},{16,24},{8,16},{1,9},{5... | collective-permute-start | bytes 1572872 | tf_op jit(solution)/shard_map/ppermute | solution.py:71
  (13 other events, 163.4 us)

commit v9 on v8

--- a/solution.py
+++ b/solution.py
@@ -61,16 +61,23 @@
     here = place[me]
     forward = [(ring[p], ring[(p + 1) % n]) for p in range(n)]
     backward = [(ring[p], ring[(p - 1) % n]) for p in range(n)]
-    total = lax.dynamic_index_in_dim(parts, me, axis=0, keepdims=False)
-    ahead = n // 2
-    for way, pairs, hops in ((1, forward, ahead), (-1, backward, n - 1 - ahead)):
-        acc = None
-        for step in range(hops):
-            owner = order[(here + way * (hops - step)) % n]
-            mine = lax.dynamic_index_in_dim(parts, owner, axis=0, keepdims=False)
-            acc = lax.ppermute(mine if acc is None else acc + mine, "dp", pairs)
-        total = total + acc
-    return total
+    half = parts.shape[1] // 2
+    sides = (parts[:, :half], parts[:, half:])
+    totals = [lax.dynamic_index_in_dim(side, me, axis=0, keepdims=False) for side in sides]
+    ahead, behind = n // 2, n - 1 - n // 2
+    for way, pairs, hops in ((1, forward, (ahead, behind)), (-1, backward, (behind, ahead))):
+        accs = [None, None]
+        for step in range(max(hops)):
+            live = [k for k in range(2) if step < hops[k]]
+            for k in live:
+                owner = order[(here + way * (hops[k] - step)) % n]
+                mine = lax.dynamic_index_in_dim(sides[k], owner, axis=0, keepdims=False)
+                accs[k] = mine if accs[k] is None else accs[k] + mine
+            sent = lax.ppermute(jnp.stack([accs[k] for k in live]), "dp", pairs)
+            for i, k in enumerate(live):
+                accs[k] = sent[i]
+        totals = [t + a for t, a in zip(totals, accs)]
+    return jnp.concatenate(totals, axis=0)
 
 def ring_all_gather(piece, ring):
     n = len(ring)

time: 224 us -> 244 us (1.089)
  waiting for transfers between devices: 105 us -> 116 us
  starting transfers between devices: 38.5 us -> 44.9 us
    ppermute x14 -> x16, waiting for transfers between devices: 41.3 us -> 63.1 us  [ring_reduce_scatter(): sent = lax.ppermute(jnp.stack([accs[k] for k in live]), 'dp', pairs)]
    all_to_all x1, waiting for transfers between devices: 23.8 us -> 13.1 us  [body(): lax.all_to_all(back_cols, 'feat', split_axis=1, concat_axis=0, tiled=True)]
    ppermute x14 -> x16, starting transfers between devices: 15.8 us -> 22.3 us  [ring_reduce_scatter(): sent = lax.ppermute(jnp.stack([accs[k] for k in live]), 'dp', pairs)]
    add x6 -> x13, other arithmetic: 5.05 us -> 3.76 us  [the longest x4 2.39 us: ring_reduce_scatter(): totals = [t + a for t, a in zip(totals, accs)]]
    unnamed x27 -> x33, local copies, waits for them, and re-layouts: 4.08 us -> 4.92 us
  transfers between devices with their start and end apart: 24 -> 26, of which waited for: 13 -> 14; matrix products, arithmetic and copies ran while one was open for 16% -> 15% of each run, Pallas kernels for 0% -> 0%
where the time goes in v9:
time: 244 us; the launch traced here: 243 us
  waiting for transfers between devices  116 us (48%)
  starting transfers between devices  44.9 us (18%)
  local copies, waits for them, and re-layouts  36.8 us (15%)
  between operations  21.4 us (9%)
  matrix products  18 us (7%)
  other arithmetic  5.8 us (2%)
    ppermute x16, waiting for transfers between devices, ring_reduce_scatter(): sent = lax.ppermute(jnp.stack([accs[k] for k in live]), 'dp', pairs)  63.1 us
    ppermute x16, starting transfers between devices, ring_reduce_scatter(): sent = lax.ppermute(jnp.stack([accs[k] for k in live]), 'dp', pairs)  22.3 us
    ppermute x7, waiting for transfers between devices, ring_all_gather(): cur = lax.ppermute(cur, 'dp', pairs)  21.8 us
    all_to_all x1, waiting for transfers between devices, body(): lax.all_to_all(mixed_rows, 'feat', split_axis=1, concat_axis=0, tiled=True)  17.9 us
    all_to_all x1, waiting for transfers between devices, body(): lax.all_to_all(back_cols, 'feat', split_axis=1, concat_axis=0, tiled=True)  13.1 us
    ppermute x7, starting transfers between devices, ring_all_gather(): cur = lax.ppermute(cur, 'dp', pairs)  8.93 us
    dot_general x1, matrix products, body(): jnp.einsum('obt,ibo->bit', back_rows, r_whole, preferred_element_type=jnp...  5.13 us
    dot_general x1, matrix products, body(): jnp.einsum('bst,bsc->cst', columns, l_blocks, preferred_element_type=jnp....  5.07 us
  transfers between devices with their start and end apart: 26, of which 14 were waited for; matrix products, arithmetic and copies ran while one was open for 15% of the time, Pallas kernels for 0%

profile of v9, /device:TPU:0, one launch (start us, length us, event | category | flops | bytes accessed | tf_op | source)
XLA Modules:
  0.0 242.8 jit_solution(5099071206750203981)
XLA Ops:
  3.1 3.0 %collective-permute-start = (bf16[640,256]{1,0:T(8,128)(2,1)S(1)}, bf16[640,256]{1,0:T(8,128)(2,1)}, u32[]{:S(2)}, u32[]{:S(2)}) collective-permute-start(bf16[640,256]{1,0:T(8,128)(2,1)S(1)} %pad_maximum_fusion.6), channel_id=1, source_target_pairs={{0,4},{4,12},{12,20},{20,28},{28,24},{24,16},{16,8},{8,0},{1,5},{5... | collective-permute-start | bytes 983048 | tf_op jit(solution)/shard_map/ppermute | solution.py:95
  6.2 7.7 %collective-permute-done = bf16[640,256]{1,0:T(8,128)(2,1)} collective-permute-done((bf16[640,256]{1,0:T(8,128)(2,1)S(1)}, bf16[640,256]{1,0:T(8,128)(2,1)}, u32[]{:S(2)}, u32[]{:S(2)}) %collective-permute-start) | collective-permute-done | bytes 327712 | tf_op jit(solution)/shard_map/ppermute | solution.py:95
  15.7 4.1 %copy.58 = bf16[16,256,256]{2,0,1:T(8,128)(2,1)} copy(bf16[16,256,256]{2,1,0:T(8,128)(2,1)} %bitcast.145) | data formatting | bytes 4194304 | tf_op jit(solution)/shard_map/reshape | solution.py:106
  19.8 4.6 %all-to-all-start = ((bf16[16,256,256]{2,0,1:T(8,128)(2,1)}), bf16[16,256,256]{2,0,1:T(8,128)(2,1)}, u32[]{:S(2)}, u32[]{:S(2)}) async-start(bf16[16,256,256]{2,0,1:T(8,128)(2,1)} %copy.58), calls=%async_computation | async-start | bytes 4194304 | tf_op jit(solution)/shard_map/all_to_all | solution.py:107
  47.3 6.8 %collective-permute-done.5 = bf16[640,256]{1,0:T(8,128)(2,1)S(1)} collective-permute-done((bf16[640,256]{1,0:T(8,128)(2,1)S(1)}, bf16[640,256]{1,0:T(8,128)(2,1)S(1)}, u32[]{:S(2)}, u32[]{:S(2)}) %collective-permute-start.5) | collective-permute-done | bytes 327712 | tf_op jit(solution)/shard_map/ppermute | solution.py:95
  56.2 7.2 %collective-permute-done.3 = bf16[640,256]{1,0:T(8,128)(2,1)S(1)} collective-permute-done((bf16[640,256]{1,0:T(8,128)(2,1)S(1)}, bf16[640,256]{1,0:T(8,128)(2,1)S(1)}, u32[]{:S(2)}, u32[]{:S(2)}) %collective-permute-start.3) | collective-permute-done | bytes 327712 | tf_op jit(solution)/shard_map/ppermute | solution.py:95
  66.6 2.6 %copy.61 = bf16[16,256,256]{2,0,1:T(8,128)(2,1)} copy(bf16[16,256,256]{2,1,0:T(8,128)(2,1)S(1)} %convolution_convert_fusion.1) | data formatting | bytes 4194304 | tf_op jit(solution)/shard_map/convert_element_type | solution.py:119
  69.2 4.6 %all-to-all-start.1 = ((bf16[16,256,256]{2,0,1:T(8,128)(2,1)}), bf16[16,256,256]{2,0,1:T(8,128)(2,1)}, u32[]{:S(2)}, u32[]{:S(2)}) async-start(bf16[16,256,256]{2,0,1:T(8,128)(2,1)} %copy.61), calls=%async_computation.1 | async-start | bytes 4194304 | tf_op jit(solution)/shard_map/all_to_all | solution.py:120
  77.3 4.2 %copy.59 = f32[16,4,64,256]{3,0,1,2:T(8,128)} copy(bf16[16,4,64,256]{3,0,2,1:T(8,128)(2,1)} %bitcast.56) | data formatting | bytes 6291456 | tf_op jit(solution)/shard_map/convert_element_type | solution.py:19
  81.5 17.9 %all-to-all-done.1 = bf16[16,256,256]{2,0,1:T(8,128)(2,1)} async-done(((bf16[16,256,256]{2,0,1:T(8,128)(2,1)}), bf16[16,256,256]{2,0,1:T(8,128)(2,1)}, u32[]{:S(2)}, u32[]{:S(2)}) %all-to-all-start.1) | async-done | bytes 2097184 | tf_op jit(solution)/shard_map/all_to_all | solution.py:120
  102.2 5.1 %fusion.6 = bf16[64,64,256]{2,0,1:T(8,128)(2,1)S(1)} fusion(f32[16,4,64,256]{3,0,1,2:T(8,128)S(1)} %copy-done.8, bf16[64,64,256]{2,0,1:T(8,128)(2,1)S(1)} %bitcast.142, bf16[64,64,64]{2,1,0:T(8,128)(2,1)S(1)} %reshape.102), kind=kOutput, calls=%fused_computation.8 | convolution fusion | flops 155189248 | bytes 8912896 | tf_op jit(solution)/shard_map/bst,bsc->cst/dot_general | solution.py:121
  111.2 4.5 %all-to-all-start.2 = ((bf16[64,64,256]{2,0,1:T(8,128)(2,1)}), bf16[64,64,256]{2,0,1:T(8,128)(2,1)}, u32[]{:S(2)}, u32[]{:S(2)}) async-start(bf16[64,64,256]{2,0,1:T(8,128)(2,1)} %copy.65), calls=%async_computation.2 | async-start | bytes 4194304 | tf_op jit(solution)/shard_map/all_to_all | solution.py:130
  117.6 4.2 %multiply_bitcast_fusion = f32[64,64,64]{0,2,1:T(8,128)} fusion(bf16[64,64,256]{2,0,1:T(8,128)(2,1)} %copy-done.5, bf16[64,64,256]{2,0,1:T(8,128)(2,1)} %bitcast.143), kind=kOutput, calls=%fused_computation.16 | convolution fusion | flops 134479872 | bytes 5242880 | tf_op jit(solution)/shard_map/bst,cst->bsc/dot_general | solution.py:126
  121.8 3.8 %copy.70 = f32[64,64,64]{2,1,0:T(8,128)} copy(f32[64,64,64]{0,2,1:T(8,128)} %multiply_bitcast_fusion) | data formatting | bytes 2097152 | tf_op jit(solution)/shard_map/mul | solution.py:127
  128.3 13.1 %all-to-all-done.2 = bf16[64,64,256]{2,0,1:T(8,128)(2,1)} async-done(((bf16[64,64,256]{2,0,1:T(8,128)(2,1)}), bf16[64,64,256]{2,0,1:T(8,128)(2,1)}, u32[]{:S(2)}, u32[]{:S(2)}) %all-to-all-start.2) | async-done | bytes 2097184 | tf_op jit(solution)/shard_map/all_to_all | solution.py:130
  148.8 15.8 %collective-permute-done.15 = f32[2,4,64,64]{3,2,1,0:T(8,128)S(1)} collective-permute-done((f32[2,4,64,64]{3,2,1,0:T(8,128)S(1)}, f32[2,4,64,64]{3,2,1,0:T(8,128)S(1)}, u32[]{:S(2)}, u32[]{:S(2)}) %collective-permute-start.15) | collective-permute-done | bytes 131104 | tf_op jit(solution)/shard_map/ppermute | solution.py:76
  168.7 14.2 %collective-permute-done.19 = f32[2,4,64,64]{3,2,1,0:T(8,128)S(1)} collective-permute-done((f32[2,4,64,64]{3,2,1,0:T(8,128)S(1)}, f32[2,4,64,64]{3,2,1,0:T(8,128)S(1)}, u32[]{:S(2)}, u32[]{:S(2)}) %collective-permute-start.19) | collective-permute-done | bytes 131104 | tf_op jit(solution)/shard_map/ppermute | solution.py:76
  186.5 5.7 %collective-permute-done.16 = f32[2,4,64,64]{3,2,1,0:T(8,128)S(1)} collective-permute-done((f32[2,4,64,64]{3,2,1,0:T(8,128)S(1)}, f32[2,4,64,64]{3,2,1,0:T(8,128)S(1)}, u32[]{:S(2)}, u32[]{:S(2)}) %collective-permute-start.16) | collective-permute-done | bytes 131104 | tf_op jit(solution)/shard_map/ppermute | solution.py:76
  194.1 4.6 %collective-permute-done.20 = f32[2,4,64,64]{3,2,1,0:T(8,128)S(1)} collective-permute-done((f32[2,4,64,64]{3,2,1,0:T(8,128)S(1)}, f32[2,4,64,64]{3,2,1,0:T(8,128)S(1)}, u32[]{:S(2)}, u32[]{:S(2)}) %collective-permute-start.20) | collective-permute-done | bytes 131104 | tf_op jit(solution)/shard_map/ppermute | solution.py:76
  203.4 7.5 %collective-permute-done.17 = f32[2,4,64,64]{3,2,1,0:T(8,128)S(1)} collective-permute-done((f32[2,4,64,64]{3,2,1,0:T(8,128)S(1)}, f32[2,4,64,64]{3,2,1,0:T(8,128)S(1)}, u32[]{:S(2)}, u32[]{:S(2)}) %collective-permute-start.17) | collective-permute-done | bytes 131104 | tf_op jit(solution)/shard_map/ppermute | solution.py:76
  213.1 2.9 %collective-permute-done.12 = f32[2,16,16,256]{3,1,2,0:T(8,128)S(1)} collective-permute-done((f32[2,16,16,256]{3,1,2,0:T(8,128)S(1)}, f32[2,16,16,256]{3,1,2,0:T(8,128)S(1)}, u32[]{:S(2)}, u32[]{:S(2)}) %collective-permute-start.12) | collective-permute-done | bytes 524320 | tf_op jit(solution)/shard_map/ppermute | solution.py:76
  218.6 3.0 %collective-permute-done.21 = f32[2,4,64,64]{3,2,1,0:T(8,128)S(1)} collective-permute-done((f32[2,4,64,64]{3,2,1,0:T(8,128)S(1)}, f32[2,4,64,64]{3,2,1,0:T(8,128)S(1)}, u32[]{:S(2)}, u32[]{:S(2)}) %collective-permute-start.21) | collective-permute-done | bytes 131104 | tf_op jit(solution)/shard_map/ppermute | solution.py:76
  223.7 8.0 %collective-permute-done.22 = f32[1,4,64,64]{3,2,1,0:T(8,128)S(1)} collective-permute-done((f32[1,4,64,64]{3,2,1,0:T(8,128)S(1)}, f32[1,4,64,64]{3,2,1,0:T(8,128)S(1)}, u32[]{:S(2)}, u32[]{:S(2)}) %collective-permute-start.22) | collective-permute-done | bytes 65568 | tf_op jit(solution)/shard_map/ppermute | solution.py:76
  235.8 5.1 %add_convert_fusion = bf16[16,256,256]{2,1,0:T(8,128)(2,1)} fusion(bf16[16,256,256]{2,1,0:T(8,128)(2,1)} %bitcast.146, bf16[256,16,256]{2,0,1:T(8,128)(2,1)} %bitcast.140, bf16[256,16,256]{2,1,0:T(8,128)(2,1)} %bitcast.138), kind=kOutput, calls=%fused_computation.14 | convolution fusion | flops 540016640 | bytes 8388608 | tf_op jit(solution)/shard_map/obt,ibo->bit/dot_general | solution.py:131
  (124 shorter events, 61.2 us)
Async XLA Ops:
  3.1 10.9 %collective-permute-start = (bf16[640,256]{1,0:T(8,128)(2,1)S(1)}, bf16[640,256]{1,0:T(8,128)(2,1)}, u32[]{:S(2)}, u32[]{:S(2)}) collective-permute-start(bf16[640,256]{1,0:T(8,128)(2,1)S(1)} %pad_maximum_fusion.6), channel_id=1, source_target_pairs={{0,4},{4,12},{12,20},{20,28},{28,24},{24,16},{16,8},{8,0},{1,5},{5... | collective-permute-start | bytes 983048 | tf_op jit(solution)/shard_map/ppermute | solution.py:95
  6.1 37.9 %collective-permute-start.4 = (bf16[640,256]{1,0:T(8,128)(2,1)S(1)}, bf16[640,256]{1,0:T(8,128)(2,1)S(1)}, u32[]{:S(2)}, u32[]{:S(2)}) collective-permute-start(bf16[640,256]{1,0:T(8,128)(2,1)S(1)} %pad_maximum_fusion.6), channel_id=1, source_target_pairs={{0,8},{4,0},{12,4},{20,12},{28,20},{24,28},{16,24},{8,16},{1,9},{5... | collective-permute-start | bytes 983048 | tf_op jit(solution)/shard_map/ppermute | solution.py:95
  14.0 30.4 %collective-permute-start.1 = (bf16[640,256]{1,0:T(8,128)(2,1)}, bf16[640,256]{1,0:T(8,128)(2,1)S(1)}, u32[]{:S(2)}, u32[]{:S(2)}) collective-permute-start(bf16[640,256]{1,0:T(8,128)(2,1)} %collective-permute-done), channel_id=1, source_target_pairs={{0,4},{4,12},{12,20},{20,28},{28,24},{24,16},{16,8},{8,0},{1,5},{5... | collective-permute-start | bytes 983048 | tf_op jit(solution)/shard_map/ppermute | solution.py:95
  19.8 49.4 %all-to-all-start = ((bf16[16,256,256]{2,0,1:T(8,128)(2,1)}), bf16[16,256,256]{2,0,1:T(8,128)(2,1)}, u32[]{:S(2)}, u32[]{:S(2)}) async-start(bf16[16,256,256]{2,0,1:T(8,128)(2,1)} %copy.58), calls=%async_computation | async-start | bytes 4194304 | tf_op jit(solution)/shard_map/all_to_all | solution.py:107
  44.0 10.1 %collective-permute-start.5 = (bf16[640,256]{1,0:T(8,128)(2,1)S(1)}, bf16[640,256]{1,0:T(8,128)(2,1)S(1)}, u32[]{:S(2)}, u32[]{:S(2)}) collective-permute-start(bf16[640,256]{1,0:T(8,128)(2,1)S(1)} %collective-permute-done.4), channel_id=1, source_target_pairs={{0,8},{4,0},{12,4},{20,12},{28,20},{24,28},{16,24},{8,16},{1,9},{5... | collective-permute-start | bytes 983048 | tf_op jit(solution)/shard_map/ppermute | solution.py:95
  44.4 10.1 %collective-permute-start.2 = (bf16[640,256]{1,0:T(8,128)(2,1)S(1)}, bf16[640,256]{1,0:T(8,128)(2,1)S(1)}, u32[]{:S(2)}, u32[]{:S(2)}) collective-permute-start(bf16[640,256]{1,0:T(8,128)(2,1)S(1)} %collective-permute-done.1), channel_id=1, source_target_pairs={{0,4},{4,12},{12,20},{20,28},{28,24},{24,16},{16,8},{8,0},{1,5},{5... | collective-permute-start | bytes 983048 | tf_op jit(solution)/shard_map/ppermute | solution.py:95
  54.1 9.4 %collective-permute-start.6 = (bf16[640,256]{1,0:T(8,128)(2,1)S(1)}, bf16[640,256]{1,0:T(8,128)(2,1)S(1)}, u32[]{:S(2)}, u32[]{:S(2)}) collective-permute-start(bf16[640,256]{1,0:T(8,128)(2,1)S(1)} %collective-permute-done.5), channel_id=1, source_target_pairs={{0,8},{4,0},{12,4},{20,12},{28,20},{24,28},{16,24},{8,16},{1,9},{5... | collective-permute-start | bytes 983048 | tf_op jit(solution)/shard_map/ppermute | solution.py:95
  54.5 9.0 %collective-permute-start.3 = (bf16[640,256]{1,0:T(8,128)(2,1)S(1)}, bf16[640,256]{1,0:T(8,128)(2,1)S(1)}, u32[]{:S(2)}, u32[]{:S(2)}) collective-permute-start(bf16[640,256]{1,0:T(8,128)(2,1)S(1)} %collective-permute-done.2), channel_id=1, source_target_pairs={{0,4},{4,12},{12,20},{20,28},{28,24},{24,16},{16,8},{8,0},{1,5},{5... | collective-permute-start | bytes 983048 | tf_op jit(solution)/shard_map/ppermute | solution.py:95
  69.2 30.2 %all-to-all-start.1 = ((bf16[16,256,256]{2,0,1:T(8,128)(2,1)}), bf16[16,256,256]{2,0,1:T(8,128)(2,1)}, u32[]{:S(2)}, u32[]{:S(2)}) async-start(bf16[16,256,256]{2,0,1:T(8,128)(2,1)} %copy.61), calls=%async_computation.1 | async-start | bytes 4194304 | tf_op jit(solution)/shard_map/all_to_all | solution.py:120
  111.2 30.2 %all-to-all-start.2 = ((bf16[64,64,256]{2,0,1:T(8,128)(2,1)}), bf16[64,64,256]{2,0,1:T(8,128)(2,1)}, u32[]{:S(2)}, u32[]{:S(2)}) async-start(bf16[64,64,256]{2,0,1:T(8,128)(2,1)} %copy.65), calls=%async_computation.2 | async-start | bytes 4194304 | tf_op jit(solution)/shard_map/all_to_all | solution.py:130
  145.4 21.0 %collective-permute-start.7 = (f32[2,16,16,256]{3,1,2,0:T(8,128)S(1)}, f32[2,16,16,256]{3,1,2,0:T(8,128)S(1)}, u32[]{:S(2)}, u32[]{:S(2)}) collective-permute-start(f32[2,16,16,256]{3,1,2,0:T(8,128)S(1)} %pad_maximum_fusion), channel_id=1, source_target_pairs={{0,4},{4,12},{12,20},{20,28},{28,24},{24,16},{16,8},{8,0},{1,5},{5... | collective-permute-start | bytes 1572872 | tf_op jit(solution)/shard_map/ppermute | solution.py:76
  147.2 17.4 %collective-permute-start.15 = (f32[2,4,64,64]{3,2,1,0:T(8,128)S(1)}, f32[2,4,64,64]{3,2,1,0:T(8,128)S(1)}, u32[]{:S(2)}, u32[]{:S(2)}) collective-permute-start(f32[2,4,64,64]{3,2,1,0:T(8,128)S(1)} %pad_maximum_fusion.7), channel_id=1, source_target_pairs={{0,4},{4,12},{12,20},{20,28},{28,24},{24,16},{16,8},{8,0},{1,5},{5... | collective-permute-start | bytes 393224 | tf_op jit(solution)/shard_map/ppermute | solution.py:76
  164.7 20.0 %collective-permute-start.11 = (f32[2,16,16,256]{3,1,2,0:T(8,128)S(1)}, f32[2,16,16,256]{3,1,2,0:T(8,128)S(1)}, u32[]{:S(2)}, u32[]{:S(2)}) collective-permute-start(f32[2,16,16,256]{3,1,2,0:T(8,128)S(1)} %pad_maximum_fusion.3), channel_id=1, source_target_pairs={{0,8},{4,0},{12,4},{20,12},{28,20},{24,28},{16,24},{8,16},{1,9},{5... | collective-permute-start | bytes 1572872 | tf_op jit(solution)/shard_map/ppermute | solution.py:76
  166.6 18.1 %collective-permute-start.8 = (f32[2,16,16,256]{3,1,2,0:T(8,128)S(1)}, f32[2,16,16,256]{3,1,2,0:T(8,128)S(1)}, u32[]{:S(2)}, u32[]{:S(2)}) collective-permute-start(f32[2,16,16,256]{3,1,2,0:T(8,128)S(1)} %pad_maximum_fusion.1), channel_id=1, source_target_pairs={{0,4},{4,12},{12,20},{20,28},{28,24},{24,16},{16,8},{8,0},{1,5},{5... | collective-permute-start | bytes 1572872 | tf_op jit(solution)/shard_map/ppermute | solution.py:76
  167.0 16.0 %collective-permute-start.19 = (f32[2,4,64,64]{3,2,1,0:T(8,128)S(1)}, f32[2,4,64,64]{3,2,1,0:T(8,128)S(1)}, u32[]{:S(2)}, u32[]{:S(2)}) collective-permute-start(f32[2,4,64,64]{3,2,1,0:T(8,128)S(1)} %pad_maximum_fusion.10), channel_id=1, source_target_pairs={{0,8},{4,0},{12,4},{20,12},{28,20},{24,28},{16,24},{8,16},{1,9},{5... | collective-permute-start | bytes 393224 | tf_op jit(solution)/shard_map/ppermute | solution.py:76
  183.0 9.3 %collective-permute-start.16 = (f32[2,4,64,64]{3,2,1,0:T(8,128)S(1)}, f32[2,4,64,64]{3,2,1,0:T(8,128)S(1)}, u32[]{:S(2)}, u32[]{:S(2)}) collective-permute-start(f32[2,4,64,64]{3,2,1,0:T(8,128)S(1)} %pad_maximum_fusion.8), channel_id=1, source_target_pairs={{0,4},{4,12},{12,20},{20,28},{28,24},{24,16},{16,8},{8,0},{1,5},{5... | collective-permute-start | bytes 393224 | tf_op jit(solution)/shard_map/ppermute | solution.py:76
  184.9 15.4 %collective-permute-start.9 = (f32[2,16,16,256]{3,1,2,0:T(8,128)S(1)}, f32[2,16,16,256]{3,1,2,0:T(8,128)S(1)}, u32[]{:S(2)}, u32[]{:S(2)}) collective-permute-start(f32[2,16,16,256]{3,1,2,0:T(8,128)S(1)} %pad_maximum_fusion.2), channel_id=1, source_target_pairs={{0,4},{4,12},{12,20},{20,28},{28,24},{24,16},{16,8},{8,0},{1,5},{5... | collective-permute-start | bytes 1572872 | tf_op jit(solution)/shard_map/ppermute | solution.py:76
  201.2 14.7 %collective-permute-start.12 = (f32[2,16,16,256]{3,1,2,0:T(8,128)S(1)}, f32[2,16,16,256]{3,1,2,0:T(8,128)S(1)}, u32[]{:S(2)}, u32[]{:S(2)}) collective-permute-start(f32[2,16,16,256]{3,1,2,0:T(8,128)S(1)} %pad_maximum_fusion.4), channel_id=1, source_target_pairs={{0,8},{4,0},{12,4},{20,12},{28,20},{24,28},{16,24},{8,16},{1,9},{5... | collective-permute-start | bytes 1572872 | tf_op jit(solution)/shard_map/ppermute | solution.py:76
  203.0 7.8 %collective-permute-start.17 = (f32[2,4,64,64]{3,2,1,0:T(8,128)S(1)}, f32[2,4,64,64]{3,2,1,0:T(8,128)S(1)}, u32[]{:S(2)}, u32[]{:S(2)}) collective-permute-start(f32[2,4,64,64]{3,2,1,0:T(8,128)S(1)} %pad_maximum_fusion.9), channel_id=1, source_target_pairs={{0,4},{4,12},{12,20},{20,28},{28,24},{24,16},{16,8},{8,0},{1,5},{5... | collective-permute-start | bytes 393224 | tf_op jit(solution)/shard_map/ppermute | solution.py:76
  210.9 7.7 %collective-permute-start.18 = (f32[1,4,64,64]{3,2,1,0:T(8,128)S(1)}, f32[1,4,64,64]{3,2,1,0:T(8,128)S(1)}, u32[]{:S(2)}, u32[]{:S(2)}) collective-permute-start(f32[1,4,64,64]{3,2,1,0:T(8,128)S(1)} %get-tuple-element.15), channel_id=1, source_target_pairs={{0,4},{4,12},{12,20},{20,28},{28,24},{24,16},{16,8},{8,0},{1,5},{5... | collective-permute-start | bytes 196616 | tf_op jit(solution)/shard_map/ppermute | solution.py:76
  211.3 10.3 %collective-permute-start.21 = (f32[2,4,64,64]{3,2,1,0:T(8,128)S(1)}, f32[2,4,64,64]{3,2,1,0:T(8,128)S(1)}, u32[]{:S(2)}, u32[]{:S(2)}) collective-permute-start(f32[2,4,64,64]{3,2,1,0:T(8,128)S(1)} %pad_maximum_fusion.12), channel_id=1, source_target_pairs={{0,8},{4,0},{12,4},{20,12},{28,20},{24,28},{16,24},{8,16},{1,9},{5... | collective-permute-start | bytes 393224 | tf_op jit(solution)/shard_map/ppermute | solution.py:76
  216.9 15.8 %collective-permute-start.13 = (f32[2,16,16,256]{3,1,2,0:T(8,128)}, f32[2,16,16,256]{3,1,2,0:T(8,128)}, u32[]{:S(2)}, u32[]{:S(2)}) collective-permute-start(f32[2,16,16,256]{3,1,2,0:T(8,128)} %pad_maximum_fusion.5), channel_id=1, source_target_pairs={{0,8},{4,0},{12,4},{20,12},{28,20},{24,28},{16,24},{8,16},{1,9},{5... | collective-permute-start | bytes 1572872 | tf_op jit(solution)/shard_map/ppermute | solution.py:76
  221.6 10.1 %collective-permute-start.22 = (f32[1,4,64,64]{3,2,1,0:T(8,128)S(1)}, f32[1,4,64,64]{3,2,1,0:T(8,128)S(1)}, u32[]{:S(2)}, u32[]{:S(2)}) collective-permute-start(f32[1,4,64,64]{3,2,1,0:T(8,128)S(1)} %get-tuple-element.35), channel_id=1, source_target_pairs={{0,8},{4,0},{12,4},{20,12},{28,20},{24,28},{16,24},{8,16},{1,9},{5... | collective-permute-start | bytes 196616 | tf_op jit(solution)/shard_map/ppermute | solution.py:76
  223.4 9.3 %collective-permute-start.10 = (f32[1,16,16,256]{3,1,2,0:T(8,128)}, f32[1,16,16,256]{3,1,2,0:T(8,128)S(1)}, u32[]{:S(2)}, u32[]{:S(2)}) collective-permute-start(f32[1,16,16,256]{3,1,2,0:T(8,128)} %get-tuple-element.7), channel_id=1, source_target_pairs={{0,4},{4,12},{12,20},{20,28},{28,24},{24,16},{16,8},{8,0},{1,5},{5... | collective-permute-start | bytes 786440 | tf_op jit(solution)/shard_map/ppermute | solution.py:76
  (17 other events, 286.9 us)

commit v10 on v8

--- a/solution.py
+++ b/solution.py
@@ -90,6 +90,19 @@
             held = lax.dynamic_update_index_in_dim(held, cur, owner, 0)
     return held
 
+def permute_all_to_all(blocks, axis):
+    n = lax.axis_size("feat")
+    me = lax.axis_index("feat")
+    pieces = jnp.stack(jnp.split(blocks, n, axis=axis))
+    by_shift = [lax.dynamic_index_in_dim(pieces, me, axis=0, keepdims=False)]
+    for shift in range(1, n):
+        mine = lax.dynamic_index_in_dim(pieces, (me + shift) % n, axis=0, keepdims=False)
+        by_shift.append(lax.ppermute(mine, "feat", [(f, (f + shift) % n) for f in range(n)]))
+    by_shift = jnp.stack(by_shift)
+    came = [lax.dynamic_index_in_dim(by_shift, (me - src) % n, axis=0, keepdims=False) for src in range(n)]
+    return jnp.concatenate(came, axis=0)
+
+
 def body(ring, activations, cotangent, r_mix, l_mix):
     tok_count = activations.shape[1]
     local_blocks = activations.shape[0] // WIDTH
@@ -97,7 +110,7 @@
     grad_scale = 1.0 / math.sqrt(tok_count * n_dp)
     x_blocks = activations.reshape(local_blocks, WIDTH, tok_count)
     g_blocks = cotangent.reshape(local_blocks, WIDTH, tok_count)
-    g_cols = lax.all_to_all(g_blocks, "feat", split_axis=1, concat_axis=0, tiled=True)
+    g_cols = permute_all_to_all(g_blocks, 1)
     local_cols = l_mix.shape[0]
     rows_r = r_mix.shape[1]
     r_lead = jnp.transpose(r_mix, (1, 0, 2)).reshape(-1, WIDTH)

time: 224 us -> 247 us (1.10)
  waiting for transfers between devices: 105 us -> 124 us
  other arithmetic: 7.09 us -> 12.2 us
  starting transfers between devices: 38.5 us -> 34.5 us
    ppermute x0 -> x3, waiting for transfers between devices: none -> 40.5 us  [permute_all_to_all(): lax.ppermute(mine, 'feat', [(f, (f + shift) % n) for f in range(n)])]
    all_to_all x1, waiting for transfers between devices: 17.9 us -> 0.01 us  [body(): lax.all_to_all(mixed_rows, 'feat', split_axis=1, concat_axis=0, tiled=True)]
    all_to_all x1 -> x0, starting transfers between devices: 4.58 us -> none  [body(): lax.all_to_all(g_blocks, 'feat', split_axis=1, concat_axis=0, tiled=True)]
    another operation x0 -> x2, other arithmetic: none -> 4.4 us  [the longest x1 2.78 us: permute_all_to_all(): pieces = jnp.stack(jnp.split(blocks, n, axis=axis))]
    convert_element_type x1 -> x0, local copies, waits for them, and re-layouts: 4.15 us -> none  [slope_of(): return pullback(upstream.astype(jnp.float32))[0].astype(jnp.bfloat16)]
    reshape x1 -> x0, local copies, waits for them, and re-layouts: 4.08 us -> none  [body(): g_blocks = cotangent.reshape(local_blocks, WIDTH, tok_count)]
    ppermute x7, waiting for transfers between devices: 21.8 us -> 18.3 us  [ring_all_gather(): cur = lax.ppermute(cur, 'dp', pairs)]
    squeeze x0 -> x2, local copies, waits for them, and re-layouts: none -> 3.11 us  [permute_all_to_all(): lax.dynamic_index_in_dim(by_shift, (me - src) % n, axis=0, keepdims=False)]
  transfers between devices with their start and end apart: 24 -> 26, of which waited for: 13 -> 14; matrix products, arithmetic and copies ran while one was open for 16% -> 16% of each run, Pallas kernels for 0% -> 0%
where the time goes in v10:
time: 247 us; the launch traced here: 246 us
  waiting for transfers between devices  124 us (50%)
  local copies, waits for them, and re-layouts  37.6 us (15%)
  starting transfers between devices  34.5 us (14%)
  between operations  21.4 us (9%)
  matrix products  16.4 us (7%)
  other arithmetic  12.2 us (5%)
    ppermute x14, waiting for transfers between devices, ring_reduce_scatter(): acc = lax.ppermute(mine if acc is None else acc + mine, 'dp', pairs)  41.6 us
    ppermute x3, waiting for transfers between devices, permute_all_to_all(): lax.ppermute(mine, 'feat', [(f, (f + shift) % n) for f in range(n)])  40.5 us
    all_to_all x1, waiting for transfers between devices, body(): lax.all_to_all(back_cols, 'feat', split_axis=1, concat_axis=0, tiled=True)  23.8 us
    ppermute x7, waiting for transfers between devices, ring_all_gather(): cur = lax.ppermute(cur, 'dp', pairs)  18.3 us
    ppermute x14, starting transfers between devices, ring_reduce_scatter(): acc = lax.ppermute(mine if acc is None else acc + mine, 'dp', pairs)  14.6 us
    ppermute x7, starting transfers between devices, ring_all_gather(): cur = lax.ppermute(cur, 'dp', pairs)  8.77 us
    dot_general x1, matrix products, body(): jnp.einsum('bst,bsc->cst', columns, l_blocks, preferred_element_type=jnp....  5.69 us
    dot_general x1, matrix products, body(): jnp.einsum('obt,ibo->bit', back_rows, r_whole, preferred_element_type=jnp...  5.13 us
  transfers between devices with their start and end apart: 26, of which 14 were waited for; matrix products, arithmetic and copies ran while one was open for 16% of the time, Pallas kernels for 0%

profile of v10, /device:TPU:0, one launch (start us, length us, event | category | flops | bytes accessed | tf_op | source)
XLA Modules:
  0.0 246.3 jit_solution(5985075600453437977)
XLA Ops:
  3.8 3.0 %collective-permute-start = (bf16[640,256]{1,0:T(8,128)(2,1)}, bf16[640,256]{1,0:T(8,128)(2,1)}, u32[]{:S(2)}, u32[]{:S(2)}) collective-permute-start(bf16[640,256]{1,0:T(8,128)(2,1)} %pad_maximum_fusion.2), channel_id=1, source_target_pairs={{0,4},{4,12},{12,20},{20,28},{28,24},{24,16},{16,8},{8,0},{1,5},{5... | collective-permute-start | bytes 983048 | tf_op jit(solution)/shard_map/ppermute | solution.py:88
  6.8 8.0 %collective-permute-done = bf16[640,256]{1,0:T(8,128)(2,1)} collective-permute-done((bf16[640,256]{1,0:T(8,128)(2,1)}, bf16[640,256]{1,0:T(8,128)(2,1)}, u32[]{:S(2)}, u32[]{:S(2)}) %collective-permute-start) | collective-permute-done | bytes 327712 | tf_op jit(solution)/shard_map/ppermute | solution.py:88
  37.0 2.7 %slice_bitcast_fusion.3 = (bf16[1,16,64,256]{3,2,1,0:T(8,128)(2,1)S(1)}, bf16[1,16,64,256]{3,2,1,0:T(8,128)(2,1)S(1)}, bf16[1,16,64,256]{3,2,1,0:T(8,128)(2,1)}, bf16[1,16,64,256]{3,2,1,0:T(8,128)(2,1)}) fusion(bf16[16,256,256]{2,1,0:T(8,128)(2,1)} %bitcast.154), kind=kLoop, calls=%fused_computation.28 | loop fusion | bytes 4194304 | tf_op jit(solution)/shard_map/stack | solution.py:96
  42.9 5.3 %collective-permute-done.5 = bf16[640,256]{1,0:T(8,128)(2,1)S(1)} collective-permute-done((bf16[640,256]{1,0:T(8,128)(2,1)}, bf16[640,256]{1,0:T(8,128)(2,1)S(1)}, u32[]{:S(2)}, u32[]{:S(2)}) %collective-permute-start.5) | collective-permute-done | bytes 327712 | tf_op jit(solution)/shard_map/ppermute | solution.py:88
  51.2 5.0 %collective-permute-done.3 = bf16[640,256]{1,0:T(8,128)(2,1)S(1)} collective-permute-done((bf16[640,256]{1,0:T(8,128)(2,1)S(1)}, bf16[640,256]{1,0:T(8,128)(2,1)S(1)}, u32[]{:S(2)}, u32[]{:S(2)}) %collective-permute-start.3) | collective-permute-done | bytes 327712 | tf_op jit(solution)/shard_map/ppermute | solution.py:88
  60.3 2.5 %copy.55 = bf16[16,256,256]{2,0,1:T(8,128)(2,1)} copy(bf16[16,256,256]{2,1,0:T(8,128)(2,1)S(1)} %convolution_convert_fusion.1) | data formatting | bytes 4194304 | tf_op jit(solution)/shard_map/convert_element_type | solution.py:125
  62.8 4.4 %all-to-all-start = ((bf16[16,256,256]{2,0,1:T(8,128)(2,1)}), bf16[16,256,256]{2,0,1:T(8,128)(2,1)}, u32[]{:S(2)}, u32[]{:S(2)}) async-start(bf16[16,256,256]{2,0,1:T(8,128)(2,1)} %copy.55), calls=%async_computation | async-start | bytes 4194304 | tf_op jit(solution)/shard_map/all_to_all | solution.py:126
  67.3 2.8 %pad_maximum_fusion = bf16[4,16,64,256]{3,2,1,0:T(8,128)(2,1)} fusion(bf16[1,16,64,256]{3,2,1,0:T(8,128)(2,1)S(1)} %get-tuple-element.24, bf16[1,16,64,256]{3,2,1,0:T(8,128)(2,1)} %get-tuple-element.25, bf16[1,16,64,256]{3,2,1,0:T(8,128)(2,1)} %get-tuple-element.26, bf16[1,16,64,256]{3,2,1,0:T(8,128)(2,1)S(1)} %get-tuple-element.23), kind=kLoop, calls=%fused_computation.16 | loop fusion | flops 3145728 | bytes 4194304 | tf_op jit(solution)/shard_map/stack | solution.py:96
  70.1 2.7 %constant_dynamic-slice_fusion.4 = (bf16[1,16,64,256]{3,2,1,0:T(8,128)(2,1)S(1)}, bf16[16,64,256]{2,1,0:T(8,128)(2,1)}, bf16[16,64,256]{2,1,0:T(8,128)(2,1)}, bf16[16,64,256]{2,1,0:T(8,128)(2,1)S(1)}) fusion(bf16[4,16,64,256]{3,2,1,0:T(8,128)(2,1)} %pad_maximum_fusion, s32[]{:T(128)S(6)} %select_n.299, s32[]{:T(128)S(6)} %select_n.305, s32[]{:T(128)S(6)} %select_n.303, ...), kind=kLoop, calls=%fused_computation.70 | loop fusion | bytes 4194320 | tf_op jit(solution)/shard_map/jit(dynamic_index_in_dim)/dynamic_slice | solution.py:97
  75.0 27.4 %collective-permute-done.9 = bf16[16,64,256]{2,1,0:T(8,128)(2,1)} collective-permute-done((bf16[16,64,256]{2,1,0:T(8,128)(2,1)}, bf16[16,64,256]{2,1,0:T(8,128)(2,1)}, u32[]{:S(2)}, u32[]{:S(2)}) %collective-permute-start.9) | collective-permute-done | bytes 524320 | tf_op jit(solution)/shard_map/ppermute | solution.py:100
  102.4 13.1 %collective-permute-done.8 = bf16[16,64,256]{2,1,0:T(8,128)(2,1)} collective-permute-done((bf16[16,64,256]{2,1,0:T(8,128)(2,1)}, bf16[16,64,256]{2,1,0:T(8,128)(2,1)}, u32[]{:S(2)}, u32[]{:S(2)}) %collective-permute-start.8) | collective-permute-done | bytes 524320 | tf_op jit(solution)/shard_map/ppermute | solution.py:100
  124.1 2.0 copy.56
  126.2 5.7 %fusion.2 = bf16[64,64,256]{2,0,1:T(8,128)(2,1)S(1)} fusion(bf16[64,64,256]{2,0,1:T(8,128)(2,1)S(1)} %bitcast.152, bf16[16,64,256]{2,0,1:T(8,128)(2,1)S(1)} %copy-done.12, bf16[16,64,256]{2,0,1:T(8,128)(2,1)S(1)} %copy-done.13, bf16[16,64,256]{2,0,1:T(8,128)(2,1)S(1)} %copy-done.10, bf16[16,64,256]{2,0,1:T(8,128)(2,1)S(1)} %copy-done.11, ...), kind=kOutput, calls=%fused_computation.6 | convolution fusion | flops 163577856 | bytes 6815744 | tf_op jit(solution)/shard_map/bst,bsc->cst/dot_general | solution.py:127
  133.3 2.5 %copy.59 = bf16[64,64,256]{2,0,1:T(8,128)(2,1)} copy(bf16[64,64,256]{2,1,0:T(8,128)(2,1)S(1)} %convolution_convert_fusion) | data formatting | bytes 4194304 | tf_op jit(solution)/shard_map/convert_element_type | solution.py:131
  135.8 4.5 %all-to-all-start.1 = ((bf16[64,64,256]{2,0,1:T(8,128)(2,1)}), bf16[64,64,256]{2,0,1:T(8,128)(2,1)}, u32[]{:S(2)}, u32[]{:S(2)}) async-start(bf16[64,64,256]{2,0,1:T(8,128)(2,1)} %copy.59), calls=%async_computation.1 | async-start | bytes 4194304 | tf_op jit(solution)/shard_map/all_to_all | solution.py:136
  142.2 23.8 %all-to-all-done.1 = bf16[64,64,256]{2,0,1:T(8,128)(2,1)} async-done(((bf16[64,64,256]{2,0,1:T(8,128)(2,1)}), bf16[64,64,256]{2,0,1:T(8,128)(2,1)}, u32[]{:S(2)}, u32[]{:S(2)}) %all-to-all-start.1) | async-done | bytes 2097184 | tf_op jit(solution)/shard_map/all_to_all | solution.py:136
  172.1 11.4 %collective-permute-done.10 = f32[32,16,256]{2,0,1:T(8,128)S(1)} collective-permute-done((f32[32,16,256]{2,0,1:T(8,128)S(1)}, f32[32,16,256]{2,0,1:T(8,128)S(1)}, u32[]{:S(2)}, u32[]{:S(2)}) %collective-permute-start.10) | collective-permute-done | bytes 524320 | tf_op jit(solution)/shard_map/ppermute | solution.py:71
  186.7 3.9 %copy.62 = f32[64,64,64]{2,1,0:T(8,128)} copy(f32[64,64,64]{0,2,1:T(8,128)} %multiply_bitcast_fusion) | data formatting | bytes 2097152 | tf_op jit(solution)/shard_map/mul | solution.py:133
  193.8 8.1 %collective-permute-done.17 = f32[8,64,64]{2,1,0:T(8,128)S(1)} collective-permute-done((f32[8,64,64]{2,1,0:T(8,128)S(1)}, f32[8,64,64]{2,1,0:T(8,128)S(1)}, u32[]{:S(2)}, u32[]{:S(2)}) %collective-permute-start.17) | collective-permute-done | bytes 131104 | tf_op jit(solution)/shard_map/ppermute | solution.py:71
  207.5 4.6 %collective-permute-done.18 = f32[8,64,64]{2,1,0:T(8,128)S(1)} collective-permute-done((f32[8,64,64]{2,1,0:T(8,128)S(1)}, f32[8,64,64]{2,1,0:T(8,128)S(1)}, u32[]{:S(2)}, u32[]{:S(2)}) %collective-permute-start.18) | collective-permute-done | bytes 131104 | tf_op jit(solution)/shard_map/ppermute | solution.py:71
  214.3 11.8 %collective-permute-done.19 = f32[8,64,64]{2,1,0:T(8,128)S(1)} collective-permute-done((f32[8,64,64]{2,1,0:T(8,128)S(1)}, f32[8,64,64]{2,1,0:T(8,128)S(1)}, u32[]{:S(2)}, u32[]{:S(2)}) %collective-permute-start.19) | collective-permute-done | bytes 131104 | tf_op jit(solution)/shard_map/ppermute | solution.py:71
  228.3 2.3 bitcast_add_fusion.2
  232.6 2.7 %collective-permute-done.20 = f32[8,64,64]{2,1,0:T(8,128)S(1)} collective-permute-done((f32[8,64,64]{2,1,0:T(8,128)S(1)}, f32[8,64,64]{2,1,0:T(8,128)S(1)}, u32[]{:S(2)}, u32[]{:S(2)}) %collective-permute-start.20) | collective-permute-done | bytes 131104 | tf_op jit(solution)/shard_map/ppermute | solution.py:71
  237.3 5.1 %add_convert_fusion = bf16[16,256,256]{2,1,0:T(8,128)(2,1)} fusion(bf16[16,256,256]{2,1,0:T(8,128)(2,1)} %bitcast.155, bf16[256,16,256]{2,0,1:T(8,128)(2,1)} %bitcast.146, bf16[256,16,256]{2,1,0:T(8,128)(2,1)} %bitcast.144), kind=kOutput, calls=%fused_computation.14 | convolution fusion | flops 540016640 | bytes 8388608 | tf_op jit(solution)/shard_map/obt,ibo->bit/dot_general | solution.py:137
  (107 shorter events, 59.6 us)
Async XLA Ops:
  3.8 11.0 %collective-permute-start = (bf16[640,256]{1,0:T(8,128)(2,1)}, bf16[640,256]{1,0:T(8,128)(2,1)}, u32[]{:S(2)}, u32[]{:S(2)}) collective-permute-start(bf16[640,256]{1,0:T(8,128)(2,1)} %pad_maximum_fusion.2), channel_id=1, source_target_pairs={{0,4},{4,12},{12,20},{20,28},{28,24},{24,16},{16,8},{8,0},{1,5},{5... | collective-permute-start | bytes 983048 | tf_op jit(solution)/shard_map/ppermute | solution.py:88
  6.8 32.9 %collective-permute-start.4 = (bf16[640,256]{1,0:T(8,128)(2,1)}, bf16[640,256]{1,0:T(8,128)(2,1)}, u32[]{:S(2)}, u32[]{:S(2)}) collective-permute-start(bf16[640,256]{1,0:T(8,128)(2,1)} %pad_maximum_fusion.2), channel_id=1, source_target_pairs={{0,8},{4,0},{12,4},{20,12},{28,20},{24,28},{16,24},{8,16},{1,9},{5... | collective-permute-start | bytes 983048 | tf_op jit(solution)/shard_map/ppermute | solution.py:88
  14.9 25.1 %collective-permute-start.1 = (bf16[640,256]{1,0:T(8,128)(2,1)}, bf16[640,256]{1,0:T(8,128)(2,1)}, u32[]{:S(2)}, u32[]{:S(2)}) collective-permute-start(bf16[640,256]{1,0:T(8,128)(2,1)} %collective-permute-done), channel_id=1, source_target_pairs={{0,4},{4,12},{12,20},{20,28},{28,24},{24,16},{16,8},{8,0},{1,5},{5... | collective-permute-start | bytes 983048 | tf_op jit(solution)/shard_map/ppermute | solution.py:88
  40.0 8.8 %collective-permute-start.2 = (bf16[640,256]{1,0:T(8,128)(2,1)}, bf16[640,256]{1,0:T(8,128)(2,1)S(1)}, u32[]{:S(2)}, u32[]{:S(2)}) collective-permute-start(bf16[640,256]{1,0:T(8,128)(2,1)} %collective-permute-done.1), channel_id=1, source_target_pairs={{0,4},{4,12},{12,20},{20,28},{28,24},{24,16},{16,8},{8,0},{1,5},{5... | collective-permute-start | bytes 983048 | tf_op jit(solution)/shard_map/ppermute | solution.py:88
  48.1 9.2 %collective-permute-start.6 = (bf16[640,256]{1,0:T(8,128)(2,1)S(1)}, bf16[640,256]{1,0:T(8,128)(2,1)S(1)}, u32[]{:S(2)}, u32[]{:S(2)}) collective-permute-start(bf16[640,256]{1,0:T(8,128)(2,1)S(1)} %collective-permute-done.5), channel_id=1, source_target_pairs={{0,8},{4,0},{12,4},{20,12},{28,20},{24,28},{16,24},{8,16},{1,9},{5... | collective-permute-start | bytes 983048 | tf_op jit(solution)/shard_map/ppermute | solution.py:88
  62.8 61.2 %all-to-all-start = ((bf16[16,256,256]{2,0,1:T(8,128)(2,1)}), bf16[16,256,256]{2,0,1:T(8,128)(2,1)}, u32[]{:S(2)}, u32[]{:S(2)}) async-start(bf16[16,256,256]{2,0,1:T(8,128)(2,1)} %copy.55), calls=%async_computation | async-start | bytes 4194304 | tf_op jit(solution)/shard_map/all_to_all | solution.py:126
  72.7 29.6 %collective-permute-start.9 = (bf16[16,64,256]{2,1,0:T(8,128)(2,1)}, bf16[16,64,256]{2,1,0:T(8,128)(2,1)}, u32[]{:S(2)}, u32[]{:S(2)}) collective-permute-start(bf16[16,64,256]{2,1,0:T(8,128)(2,1)} %get-tuple-element.20), channel_id=1, source_target_pairs={{0,3},{1,0},{2,1},{3,2},{4,7},{5,4},{6,5},{7,6},{8,11},{9,8},{10,9... | collective-permute-start | bytes 1572872 | tf_op jit(solution)/shard_map/ppermute | solution.py:100
  74.5 41.1 %collective-permute-start.8 = (bf16[16,64,256]{2,1,0:T(8,128)(2,1)}, bf16[16,64,256]{2,1,0:T(8,128)(2,1)}, u32[]{:S(2)}, u32[]{:S(2)}) collective-permute-start(bf16[16,64,256]{2,1,0:T(8,128)(2,1)} %get-tuple-element.21), channel_id=1, source_target_pairs={{0,2},{1,3},{2,0},{3,1},{4,6},{5,7},{6,4},{7,5},{8,10},{9,11},{10,... | collective-permute-start | bytes 1572872 | tf_op jit(solution)/shard_map/ppermute | solution.py:100
  74.8 40.7 %collective-permute-start.7 = (bf16[16,64,256]{2,1,0:T(8,128)(2,1)S(1)}, bf16[16,64,256]{2,1,0:T(8,128)(2,1)}, u32[]{:S(2)}, u32[]{:S(2)}) collective-permute-start(bf16[16,64,256]{2,1,0:T(8,128)(2,1)S(1)} %get-tuple-element.22), channel_id=1, source_target_pairs={{0,1},{1,2},{2,3},{3,0},{4,5},{5,6},{6,7},{7,4},{8,9},{9,10},{10,1... | collective-permute-start | bytes 1572872 | tf_op jit(solution)/shard_map/ppermute | solution.py:100
  135.8 30.2 %all-to-all-start.1 = ((bf16[64,64,256]{2,0,1:T(8,128)(2,1)}), bf16[64,64,256]{2,0,1:T(8,128)(2,1)}, u32[]{:S(2)}, u32[]{:S(2)}) async-start(bf16[64,64,256]{2,0,1:T(8,128)(2,1)} %copy.59), calls=%async_computation.1 | async-start | bytes 4194304 | tf_op jit(solution)/shard_map/all_to_all | solution.py:136
  170.1 13.5 %collective-permute-start.10 = (f32[32,16,256]{2,0,1:T(8,128)S(1)}, f32[32,16,256]{2,0,1:T(8,128)S(1)}, u32[]{:S(2)}, u32[]{:S(2)}) collective-permute-start(f32[32,16,256]{2,0,1:T(8,128)S(1)} %get-tuple-element.7), channel_id=1, source_target_pairs={{0,4},{4,12},{12,20},{20,28},{28,24},{24,16},{16,8},{8,0},{1,5},{5... | collective-permute-start | bytes 1572872 | tf_op jit(solution)/shard_map/ppermute | solution.py:71
  171.1 32.8 %collective-permute-start.14 = (f32[32,16,256]{2,0,1:T(8,128)}, f32[32,16,256]{2,0,1:T(8,128)S(1)}, u32[]{:S(2)}, u32[]{:S(2)}) collective-permute-start(f32[32,16,256]{2,0,1:T(8,128)} %get-tuple-element.8), channel_id=1, source_target_pairs={{0,8},{4,0},{12,4},{20,12},{28,20},{24,28},{16,24},{8,16},{1,9},{5... | collective-permute-start | bytes 1572872 | tf_op jit(solution)/shard_map/ppermute | solution.py:71
  183.6 20.3 %collective-permute-start.11 = (f32[32,16,256]{2,0,1:T(8,128)S(1)}, f32[32,16,256]{2,0,1:T(8,128)}, u32[]{:S(2)}, u32[]{:S(2)}) collective-permute-start(f32[32,16,256]{2,0,1:T(8,128)S(1)} %bitcast_add_fusion.4), channel_id=1, source_target_pairs={{0,4},{4,12},{12,20},{20,28},{28,24},{24,16},{16,8},{8,0},{1,5},{5... | collective-permute-start | bytes 1572872 | tf_op jit(solution)/shard_map/ppermute | solution.py:71
  191.7 10.2 %collective-permute-start.17 = (f32[8,64,64]{2,1,0:T(8,128)S(1)}, f32[8,64,64]{2,1,0:T(8,128)S(1)}, u32[]{:S(2)}, u32[]{:S(2)}) collective-permute-start(f32[8,64,64]{2,1,0:T(8,128)S(1)} %get-tuple-element.13), channel_id=1, source_target_pairs={{0,4},{4,12},{12,20},{20,28},{28,24},{24,16},{16,8},{8,0},{1,5},{5... | collective-permute-start | bytes 393224 | tf_op jit(solution)/shard_map/ppermute | solution.py:71
  193.3 14.2 %collective-permute-start.21 = (f32[8,64,64]{2,1,0:T(8,128)S(1)}, f32[8,64,64]{2,1,0:T(8,128)S(1)}, u32[]{:S(2)}, u32[]{:S(2)}) collective-permute-start(f32[8,64,64]{2,1,0:T(8,128)S(1)} %get-tuple-element.14), channel_id=1, source_target_pairs={{0,8},{4,0},{12,4},{20,12},{28,20},{24,28},{16,24},{8,16},{1,9},{5... | collective-permute-start | bytes 393224 | tf_op jit(solution)/shard_map/ppermute | solution.py:71
  202.8 9.3 %collective-permute-start.18 = (f32[8,64,64]{2,1,0:T(8,128)S(1)}, f32[8,64,64]{2,1,0:T(8,128)S(1)}, u32[]{:S(2)}, u32[]{:S(2)}) collective-permute-start(f32[8,64,64]{2,1,0:T(8,128)S(1)} %bitcast_add_fusion.10), channel_id=1, source_target_pairs={{0,4},{4,12},{12,20},{20,28},{28,24},{24,16},{16,8},{8,0},{1,5},{5... | collective-permute-start | bytes 393224 | tf_op jit(solution)/shard_map/ppermute | solution.py:71
  205.5 22.8 %collective-permute-start.12 = (f32[32,16,256]{2,0,1:T(8,128)S(1)}, f32[32,16,256]{2,0,1:T(8,128)S(1)}, u32[]{:S(2)}, u32[]{:S(2)}) collective-permute-start(f32[32,16,256]{2,0,1:T(8,128)S(1)} %get-tuple-element.5), channel_id=1, source_target_pairs={{0,4},{4,12},{12,20},{20,28},{28,24},{24,16},{16,8},{8,0},{1,5},{5... | collective-permute-start | bytes 1572872 | tf_op jit(solution)/shard_map/ppermute | solution.py:71
  207.1 21.2 %collective-permute-start.15 = (f32[32,16,256]{2,0,1:T(8,128)S(1)}, f32[32,16,256]{2,0,1:T(8,128)S(1)}, u32[]{:S(2)}, u32[]{:S(2)}) collective-permute-start(f32[32,16,256]{2,0,1:T(8,128)S(1)} %get-tuple-element.6), channel_id=1, source_target_pairs={{0,8},{4,0},{12,4},{20,12},{28,20},{24,28},{16,24},{8,16},{1,9},{5... | collective-permute-start | bytes 1572872 | tf_op jit(solution)/shard_map/ppermute | solution.py:71
  212.2 13.9 %collective-permute-start.19 = (f32[8,64,64]{2,1,0:T(8,128)S(1)}, f32[8,64,64]{2,1,0:T(8,128)S(1)}, u32[]{:S(2)}, u32[]{:S(2)}) collective-permute-start(f32[8,64,64]{2,1,0:T(8,128)S(1)} %get-tuple-element.11), channel_id=1, source_target_pairs={{0,4},{4,12},{12,20},{20,28},{28,24},{24,16},{16,8},{8,0},{1,5},{5... | collective-permute-start | bytes 393224 | tf_op jit(solution)/shard_map/ppermute | solution.py:71
  213.2 12.8 %collective-permute-start.22 = (f32[8,64,64]{2,1,0:T(8,128)S(1)}, f32[8,64,64]{2,1,0:T(8,128)S(1)}, u32[]{:S(2)}, u32[]{:S(2)}) collective-permute-start(f32[8,64,64]{2,1,0:T(8,128)S(1)} %get-tuple-element.12), channel_id=1, source_target_pairs={{0,8},{4,0},{12,4},{20,12},{28,20},{24,28},{16,24},{8,16},{1,9},{5... | collective-permute-start | bytes 393224 | tf_op jit(solution)/shard_map/ppermute | solution.py:71
  226.2 9.2 %collective-permute-start.20 = (f32[8,64,64]{2,1,0:T(8,128)S(1)}, f32[8,64,64]{2,1,0:T(8,128)S(1)}, u32[]{:S(2)}, u32[]{:S(2)}) collective-permute-start(f32[8,64,64]{2,1,0:T(8,128)S(1)} %get-tuple-element.9), channel_id=1, source_target_pairs={{0,4},{4,12},{12,20},{20,28},{28,24},{24,16},{16,8},{8,0},{1,5},{5... | collective-permute-start | bytes 393224 | tf_op jit(solution)/shard_map/ppermute | solution.py:71
  227.2 9.1 %collective-permute-start.23 = (f32[8,64,64]{2,1,0:T(8,128)S(1)}, f32[8,64,64]{2,1,0:T(8,128)S(1)}, u32[]{:S(2)}, u32[]{:S(2)}) collective-permute-start(f32[8,64,64]{2,1,0:T(8,128)S(1)} %get-tuple-element.10), channel_id=1, source_target_pairs={{0,8},{4,0},{12,4},{20,12},{28,20},{24,28},{16,24},{8,16},{1,9},{5... | collective-permute-start | bytes 393224 | tf_op jit(solution)/shard_map/ppermute | solution.py:71
  230.6 12.9 %collective-permute-start.13 = (f32[32,16,256]{2,0,1:T(8,128)}, f32[32,16,256]{2,0,1:T(8,128)S(1)}, u32[]{:S(2)}, u32[]{:S(2)}) collective-permute-start(f32[32,16,256]{2,0,1:T(8,128)} %get-tuple-element.3), channel_id=1, source_target_pairs={{0,4},{4,12},{12,20},{20,28},{28,24},{24,16},{16,8},{8,0},{1,5},{5... | collective-permute-start | bytes 1572872 | tf_op jit(solution)/shard_map/ppermute | solution.py:71
  231.6 12.8 %collective-permute-start.16 = (f32[32,16,256]{2,0,1:T(8,128)}, f32[32,16,256]{2,0,1:T(8,128)S(1)}, u32[]{:S(2)}, u32[]{:S(2)}) collective-permute-start(f32[32,16,256]{2,0,1:T(8,128)} %get-tuple-element.4), channel_id=1, source_target_pairs={{0,8},{4,0},{12,4},{20,12},{28,20},{24,28},{16,24},{8,16},{1,9},{5... | collective-permute-start | bytes 1572872 | tf_op jit(solution)/shard_map/ppermute | solution.py:71
  (17 other events, 183.6 us)

commit v11 on v8

--- a/solution.py
+++ b/solution.py
@@ -117,9 +117,7 @@
         "cst,bsc->sbt", slope_cols, l_blocks, preferred_element_type=jnp.float32
     ).astype(jnp.bfloat16)
     l_term = jnp.einsum("bst,cst->bsc", columns, slope_cols, preferred_element_type=jnp.float32)
-    l_term = (l_term * grad_scale).reshape(n_dp, -1, local_cols, BLOCKS)
-    grad_l = ring_reduce_scatter(l_term, ring)
-    grad_l = jnp.transpose(grad_l, (1, 0, 2)).reshape(local_cols, -1)
+    l_term = (l_term * grad_scale).reshape(n_dp, -1, WIDTH)
     back_rows = lax.all_to_all(back_cols, "feat", split_axis=1, concat_axis=0, tiled=True)
     through_r = jnp.einsum("obt,ibo->bit", back_rows, r_whole, preferred_element_type=jnp.float32)
     grad_x = (
@@ -130,9 +128,12 @@
     r_term = (
         jnp.einsum("bit,obt->ibo", x_blocks, back_rows, preferred_element_type=jnp.float32)
         * grad_scale
-    ).reshape(n_dp, rows_r, local_blocks, WIDTH)
-    grad_r = ring_reduce_scatter(r_term, ring)
-    grad_r = jnp.transpose(grad_r, (1, 0, 2))
+    ).reshape(n_dp, rows_r * local_blocks, WIDTH)
+    summed = ring_reduce_scatter(jnp.concatenate([r_term, l_term], axis=1), ring)
+    r_rows = r_term.shape[1]
+    grad_r = jnp.transpose(summed[:r_rows].reshape(rows_r, local_blocks, WIDTH), (1, 0, 2))
+    grad_l = summed[r_rows:].reshape(-1, local_cols, BLOCKS)
+    grad_l = jnp.transpose(grad_l, (1, 0, 2)).reshape(local_cols, -1)
     return (grad_x, grad_r, grad_l)
 
 

time: 224 us -> 225 us (level)
  waiting for transfers between devices: 105 us -> 116 us
  other arithmetic: 7.09 us -> 0.69 us
  starting transfers between devices: 38.5 us -> 32.3 us
  local copies, waits for them, and re-layouts: 35.6 us -> 38.4 us
    ppermute x14 -> x7, waiting for transfers between devices: 41.3 us -> 62.1 us  [ring_reduce_scatter(): acc = lax.ppermute(mine if acc is None else acc + mine, 'dp', pairs)]
    all_to_all x1, waiting for transfers between devices: 23.8 us -> 13.8 us  [body(): lax.all_to_all(back_cols, 'feat', split_axis=1, concat_axis=0, tiled=True)]
    ppermute x14 -> x7, starting transfers between devices: 15.8 us -> 9.62 us  [ring_reduce_scatter(): acc = lax.ppermute(mine if acc is None else acc + mine, 'dp', pairs)]
    add x6 -> x4, other arithmetic: 5.05 us -> 0.42 us  [ring_reduce_scatter(): acc = lax.ppermute(mine if acc is None else acc + mine, 'dp', pairs)]
    dot_general x1, matrix products: 5.13 us -> 2.28 us  [body(): jnp.einsum('obt,ibo->bit', back_rows, r_whole, preferred_element_type=jnp...]
    mul x1 -> x2, local copies, waits for them, and re-layouts: 3.78 us -> 6.23 us  [the longest x1 3.79 us: body(): l_term = (l_term * grad_scale).reshape(n_dp, -1, WIDTH)]
    dot_general x1, matrix products: 2.01 us -> 4.28 us  [body(): jnp.einsum('bst,cst->bsc', columns, slope_cols, preferred_element_type=jn...]
    unnamed x27 -> x22, local copies, waits for them, and re-layouts: 4.08 us -> 4.51 us
  transfers between devices with their start and end apart: 24 -> 17, of which waited for: 13 -> 10; matrix products, arithmetic and copies ran while one was open for 16% -> 14% of each run, Pallas kernels for 0% -> 0%
where the time goes in v11:
time: 225 us; the launch traced here: 224 us
  waiting for transfers between devices  116 us (52%)
  local copies, waits for them, and re-layouts  38.4 us (17%)
  starting transfers between devices  32.3 us (14%)
  between operations  21.4 us (10%)
  matrix products  15.2 us (7%)
    ppermute x7, waiting for transfers between devices, ring_reduce_scatter(): acc = lax.ppermute(mine if acc is None else acc + mine, 'dp', pairs)  62.1 us
    ppermute x7, waiting for transfers between devices, ring_all_gather(): cur = lax.ppermute(cur, 'dp', pairs)  21.8 us
    all_to_all x1, waiting for transfers between devices, body(): lax.all_to_all(mixed_rows, 'feat', split_axis=1, concat_axis=0, tiled=True)  17.9 us
    all_to_all x1, waiting for transfers between devices, body(): lax.all_to_all(back_cols, 'feat', split_axis=1, concat_axis=0, tiled=True)  13.8 us
    ppermute x7, starting transfers between devices, ring_reduce_scatter(): acc = lax.ppermute(mine if acc is None else acc + mine, 'dp', pairs)  9.62 us
    ppermute x7, starting transfers between devices, ring_all_gather(): cur = lax.ppermute(cur, 'dp', pairs)  8.93 us
    dot_general x1, matrix products, body(): jnp.einsum('bst,bsc->cst', columns, l_blocks, preferred_element_type=jnp....  5.07 us
    all_to_all x1, starting transfers between devices, body(): lax.all_to_all(mixed_rows, 'feat', split_axis=1, concat_axis=0, tiled=True)  4.7 us
  transfers between devices with their start and end apart: 17, of which 10 were waited for; matrix products, arithmetic and copies ran while one was open for 14% of the time, Pallas kernels for 0%

profile of v11, /device:TPU:0, one launch (start us, length us, event | category | flops | bytes accessed | tf_op | source)
XLA Modules:
  0.0 223.6 jit_solution(15475061984126503611)
XLA Ops:
  3.1 3.0 %collective-permute-start = (bf16[640,256]{1,0:T(8,128)(2,1)S(1)}, bf16[640,256]{1,0:T(8,128)(2,1)}, u32[]{:S(2)}, u32[]{:S(2)}) collective-permute-start(bf16[640,256]{1,0:T(8,128)(2,1)S(1)} %pad_maximum_fusion), channel_id=1, source_target_pairs={{0,4},{4,12},{12,20},{20,28},{28,24},{24,16},{16,8},{8,0},{1,5},{5... | collective-permute-start | bytes 983048 | tf_op jit(solution)/shard_map/ppermute | solution.py:88
  6.2 7.7 %collective-permute-done = bf16[640,256]{1,0:T(8,128)(2,1)} collective-permute-done((bf16[640,256]{1,0:T(8,128)(2,1)S(1)}, bf16[640,256]{1,0:T(8,128)(2,1)}, u32[]{:S(2)}, u32[]{:S(2)}) %collective-permute-start) | collective-permute-done | bytes 327712 | tf_op jit(solution)/shard_map/ppermute | solution.py:88
  15.7 4.1 %copy.43 = bf16[16,256,256]{2,0,1:T(8,128)(2,1)} copy(bf16[16,256,256]{2,1,0:T(8,128)(2,1)} %bitcast.136) | data formatting | bytes 4194304 | tf_op jit(solution)/shard_map/reshape | solution.py:99
  19.8 4.6 %all-to-all-start = ((bf16[16,256,256]{2,0,1:T(8,128)(2,1)}), bf16[16,256,256]{2,0,1:T(8,128)(2,1)}, u32[]{:S(2)}, u32[]{:S(2)}) async-start(bf16[16,256,256]{2,0,1:T(8,128)(2,1)} %copy.43), calls=%async_computation | async-start | bytes 4194304 | tf_op jit(solution)/shard_map/all_to_all | solution.py:100
  47.5 6.8 %collective-permute-done.5 = bf16[640,256]{1,0:T(8,128)(2,1)S(1)} collective-permute-done((bf16[640,256]{1,0:T(8,128)(2,1)S(1)}, bf16[640,256]{1,0:T(8,128)(2,1)S(1)}, u32[]{:S(2)}, u32[]{:S(2)}) %collective-permute-start.5) | collective-permute-done | bytes 327712 | tf_op jit(solution)/shard_map/ppermute | solution.py:88
  56.4 7.2 %collective-permute-done.3 = bf16[640,256]{1,0:T(8,128)(2,1)S(1)} collective-permute-done((bf16[640,256]{1,0:T(8,128)(2,1)S(1)}, bf16[640,256]{1,0:T(8,128)(2,1)S(1)}, u32[]{:S(2)}, u32[]{:S(2)}) %collective-permute-start.3) | collective-permute-done | bytes 327712 | tf_op jit(solution)/shard_map/ppermute | solution.py:88
  67.0 2.5 %copy.46 = bf16[16,256,256]{2,0,1:T(8,128)(2,1)} copy(bf16[16,256,256]{2,1,0:T(8,128)(2,1)S(1)} %convolution_convert_fusion.1) | data formatting | bytes 4194304 | tf_op jit(solution)/shard_map/convert_element_type | solution.py:112
  69.5 4.7 %all-to-all-start.1 = ((bf16[16,256,256]{2,0,1:T(8,128)(2,1)}), bf16[16,256,256]{2,0,1:T(8,128)(2,1)}, u32[]{:S(2)}, u32[]{:S(2)}) async-start(bf16[16,256,256]{2,0,1:T(8,128)(2,1)} %copy.46), calls=%async_computation.1 | async-start | bytes 4194304 | tf_op jit(solution)/shard_map/all_to_all | solution.py:113
  77.7 4.2 %copy.44 = f32[16,4,64,256]{3,0,1,2:T(8,128)} copy(bf16[16,4,64,256]{3,0,2,1:T(8,128)(2,1)} %bitcast.59) | data formatting | bytes 6291456 | tf_op jit(solution)/shard_map/convert_element_type | solution.py:19
  81.9 17.9 %all-to-all-done.1 = bf16[16,256,256]{2,0,1:T(8,128)(2,1)} async-done(((bf16[16,256,256]{2,0,1:T(8,128)(2,1)}), bf16[16,256,256]{2,0,1:T(8,128)(2,1)}, u32[]{:S(2)}, u32[]{:S(2)}) %all-to-all-start.1) | async-done | bytes 2097184 | tf_op jit(solution)/shard_map/all_to_all | solution.py:113
  99.8 2.0 copy.47
  102.6 5.1 %fusion.6 = bf16[64,64,256]{2,0,1:T(8,128)(2,1)S(1)} fusion(f32[16,4,64,256]{3,0,1,2:T(8,128)S(1)} %copy-done.7, bf16[64,64,256]{2,0,1:T(8,128)(2,1)S(1)} %bitcast.134, bf16[64,64,64]{2,1,0:T(8,128)(2,1)S(1)} %reshape.82), kind=kOutput, calls=%fused_computation.24 | convolution fusion | flops 155189248 | bytes 8912896 | tf_op jit(solution)/shard_map/bst,bsc->cst/dot_general | solution.py:114
  109.0 2.5 %copy.50 = bf16[64,64,256]{2,0,1:T(8,128)(2,1)} copy(bf16[64,64,256]{2,1,0:T(8,128)(2,1)S(1)} %convolution_convert_fusion) | data formatting | bytes 4194304 | tf_op jit(solution)/shard_map/convert_element_type | solution.py:118
  111.6 4.5 %all-to-all-start.2 = ((bf16[64,64,256]{2,0,1:T(8,128)(2,1)}), bf16[64,64,256]{2,0,1:T(8,128)(2,1)}, u32[]{:S(2)}, u32[]{:S(2)}) async-start(bf16[64,64,256]{2,0,1:T(8,128)(2,1)} %copy.50), calls=%async_computation.2 | async-start | bytes 4194304 | tf_op jit(solution)/shard_map/all_to_all | solution.py:121
  118.0 4.3 %multiply_bitcast_fusion.1 = f32[64,64,64]{0,2,1:T(8,128)} fusion(bf16[64,64,256]{2,0,1:T(8,128)(2,1)} %copy-done.5, bf16[64,64,256]{2,0,1:T(8,128)(2,1)} %bitcast.135), kind=kOutput, calls=%fused_computation.32 | convolution fusion | flops 134479872 | bytes 5242880 | tf_op jit(solution)/shard_map/bst,cst->bsc/dot_general | solution.py:119
  122.2 3.8 %copy.54 = f32[64,64,64]{2,1,0:T(8,128)} copy(f32[64,64,64]{0,2,1:T(8,128)} %multiply_bitcast_fusion.1) | data formatting | bytes 2097152 | tf_op jit(solution)/shard_map/mul | solution.py:120
  128.0 13.8 %all-to-all-done.2 = bf16[64,64,256]{2,0,1:T(8,128)(2,1)} async-done(((bf16[64,64,256]{2,0,1:T(8,128)(2,1)}), bf16[64,64,256]{2,0,1:T(8,128)(2,1)}, u32[]{:S(2)}, u32[]{:S(2)}) %all-to-all-start.2) | async-done | bytes 2097184 | tf_op jit(solution)/shard_map/all_to_all | solution.py:121
  144.3 2.4 %copy.53 = f32[256,16,256]{2,1,0:T(8,128)S(1)} copy(f32[256,16,256]{2,0,1:T(8,128)S(1)} %multiply_bitcast_fusion) | data formatting | bytes 8388608 | tf_op jit(solution)/shard_map/mul | solution.py:129
  148.5 14.6 %collective-permute-done.7 = f32[640,256]{1,0:T(8,128)S(1)} collective-permute-done((f32[640,256]{1,0:T(8,128)S(1)}, f32[640,256]{1,0:T(8,128)S(1)}, u32[]{:S(2)}, u32[]{:S(2)}) %collective-permute-start.7) | collective-permute-done | bytes 655392 | tf_op jit(solution)/shard_map/ppermute | solution.py:71
  165.3 13.3 %collective-permute-done.8 = f32[640,256]{1,0:T(8,128)S(1)} collective-permute-done((f32[640,256]{1,0:T(8,128)S(1)}, f32[640,256]{1,0:T(8,128)S(1)}, u32[]{:S(2)}, u32[]{:S(2)}) %collective-permute-start.8) | collective-permute-done | bytes 655392 | tf_op jit(solution)/shard_map/ppermute | solution.py:71
  180.7 12.8 %collective-permute-done.9 = f32[640,256]{1,0:T(8,128)S(1)} collective-permute-done((f32[640,256]{1,0:T(8,128)S(1)}, f32[640,256]{1,0:T(8,128)S(1)}, u32[]{:S(2)}, u32[]{:S(2)}) %collective-permute-start.9) | collective-permute-done | bytes 655392 | tf_op jit(solution)/shard_map/ppermute | solution.py:71
  195.7 12.7 %collective-permute-done.12 = f32[640,256]{1,0:T(8,128)S(1)} collective-permute-done((f32[640,256]{1,0:T(8,128)S(1)}, f32[640,256]{1,0:T(8,128)S(1)}, u32[]{:S(2)}, u32[]{:S(2)}) %collective-permute-start.12) | collective-permute-done | bytes 655392 | tf_op jit(solution)/shard_map/ppermute | solution.py:71
  210.3 2.3 %add_convert_fusion = bf16[16,256,256]{2,1,0:T(8,128)(2,1)} fusion(bf16[16,256,256]{2,1,0:T(8,128)(2,1)S(1)} %bitcast.137, bf16[256,16,256]{2,0,1:T(8,128)(2,1)S(1)} %bitcast.133, bf16[256,16,256]{2,1,0:T(8,128)(2,1)S(1)} %bitcast.131), kind=kOutput, calls=%fused_computation.31 | convolution fusion | flops 540016640 | bytes 8388608 | tf_op jit(solution)/shard_map/obt,ibo->bit/dot_general | solution.py:122
  212.6 8.7 %collective-permute-done.13 = f32[640,256]{1,0:T(8,128)S(1)} collective-permute-done((f32[640,256]{1,0:T(8,128)S(1)}, f32[640,256]{1,0:T(8,128)S(1)}, u32[]{:S(2)}, u32[]{:S(2)}) %collective-permute-start.13) | collective-permute-done | bytes 655392 | tf_op jit(solution)/shard_map/ppermute | solution.py:71
  (76 shorter events, 36.6 us)
Async XLA Ops:
  0.6 64.8 %copy-start = (bf16[4096,256]{1,0:T(8,128)(2,1)S(1)}, bf16[4096,256]{1,0:T(8,128)(2,1)}, u32[]{:S(2)}) copy-start(bf16[4096,256]{1,0:T(8,128)(2,1)} %param.8) | copy-start | bytes 6291460
  3.1 10.9 %collective-permute-start = (bf16[640,256]{1,0:T(8,128)(2,1)S(1)}, bf16[640,256]{1,0:T(8,128)(2,1)}, u32[]{:S(2)}, u32[]{:S(2)}) collective-permute-start(bf16[640,256]{1,0:T(8,128)(2,1)S(1)} %pad_maximum_fusion), channel_id=1, source_target_pairs={{0,4},{4,12},{12,20},{20,28},{28,24},{24,16},{16,8},{8,0},{1,5},{5... | collective-permute-start | bytes 983048 | tf_op jit(solution)/shard_map/ppermute | solution.py:88
  6.1 38.1 %collective-permute-start.4 = (bf16[640,256]{1,0:T(8,128)(2,1)S(1)}, bf16[640,256]{1,0:T(8,128)(2,1)S(1)}, u32[]{:S(2)}, u32[]{:S(2)}) collective-permute-start(bf16[640,256]{1,0:T(8,128)(2,1)S(1)} %pad_maximum_fusion), channel_id=1, source_target_pairs={{0,8},{4,0},{12,4},{20,12},{28,20},{24,28},{16,24},{8,16},{1,9},{5... | collective-permute-start | bytes 983048 | tf_op jit(solution)/shard_map/ppermute | solution.py:88
  14.0 30.6 %collective-permute-start.1 = (bf16[640,256]{1,0:T(8,128)(2,1)}, bf16[640,256]{1,0:T(8,128)(2,1)S(1)}, u32[]{:S(2)}, u32[]{:S(2)}) collective-permute-start(bf16[640,256]{1,0:T(8,128)(2,1)} %collective-permute-done), channel_id=1, source_target_pairs={{0,4},{4,12},{12,20},{20,28},{28,24},{24,16},{16,8},{8,0},{1,5},{5... | collective-permute-start | bytes 983048 | tf_op jit(solution)/shard_map/ppermute | solution.py:88
  19.7 4.6 %copy-start.9 = (s32[8]{0:T(128)S(1)}, s32[8]{0:T(128)}, u32[]{:S(2)}) copy-start(s32[8]{0:T(128)} %constant.166.clone) | copy-start | bytes 100
  19.7 10.5 %copy-start.8 = (s32[8]{0:T(128)S(1)}, s32[8]{0:T(128)}, u32[]{:S(2)}) copy-start(s32[8]{0:T(128)} %constant.165.clone) | copy-start | bytes 100
  19.8 49.8 %all-to-all-start = ((bf16[16,256,256]{2,0,1:T(8,128)(2,1)}), bf16[16,256,256]{2,0,1:T(8,128)(2,1)}, u32[]{:S(2)}, u32[]{:S(2)}) async-start(bf16[16,256,256]{2,0,1:T(8,128)(2,1)} %copy.43), calls=%async_computation | async-start | bytes 4194304 | tf_op jit(solution)/shard_map/all_to_all | solution.py:100
  44.2 10.1 %collective-permute-start.5 = (bf16[640,256]{1,0:T(8,128)(2,1)S(1)}, bf16[640,256]{1,0:T(8,128)(2,1)S(1)}, u32[]{:S(2)}, u32[]{:S(2)}) collective-permute-start(bf16[640,256]{1,0:T(8,128)(2,1)S(1)} %collective-permute-done.4), channel_id=1, source_target_pairs={{0,8},{4,0},{12,4},{20,12},{28,20},{24,28},{16,24},{8,16},{1,9},{5... | collective-permute-start | bytes 983048 | tf_op jit(solution)/shard_map/ppermute | solution.py:88
  44.6 10.1 %collective-permute-start.2 = (bf16[640,256]{1,0:T(8,128)(2,1)S(1)}, bf16[640,256]{1,0:T(8,128)(2,1)S(1)}, u32[]{:S(2)}, u32[]{:S(2)}) collective-permute-start(bf16[640,256]{1,0:T(8,128)(2,1)S(1)} %collective-permute-done.1), channel_id=1, source_target_pairs={{0,4},{4,12},{12,20},{20,28},{28,24},{24,16},{16,8},{8,0},{1,5},{5... | collective-permute-start | bytes 983048 | tf_op jit(solution)/shard_map/ppermute | solution.py:88
  54.3 9.4 %collective-permute-start.6 = (bf16[640,256]{1,0:T(8,128)(2,1)S(1)}, bf16[640,256]{1,0:T(8,128)(2,1)S(1)}, u32[]{:S(2)}, u32[]{:S(2)}) collective-permute-start(bf16[640,256]{1,0:T(8,128)(2,1)S(1)} %collective-permute-done.5), channel_id=1, source_target_pairs={{0,8},{4,0},{12,4},{20,12},{28,20},{24,28},{16,24},{8,16},{1,9},{5... | collective-permute-start | bytes 983048 | tf_op jit(solution)/shard_map/ppermute | solution.py:88
  54.6 9.0 %collective-permute-start.3 = (bf16[640,256]{1,0:T(8,128)(2,1)S(1)}, bf16[640,256]{1,0:T(8,128)(2,1)S(1)}, u32[]{:S(2)}, u32[]{:S(2)}) collective-permute-start(bf16[640,256]{1,0:T(8,128)(2,1)S(1)} %collective-permute-done.2), channel_id=1, source_target_pairs={{0,4},{4,12},{12,20},{20,28},{28,24},{24,16},{16,8},{8,0},{1,5},{5... | collective-permute-start | bytes 983048 | tf_op jit(solution)/shard_map/ppermute | solution.py:88
  69.5 30.3 %all-to-all-start.1 = ((bf16[16,256,256]{2,0,1:T(8,128)(2,1)}), bf16[16,256,256]{2,0,1:T(8,128)(2,1)}, u32[]{:S(2)}, u32[]{:S(2)}) async-start(bf16[16,256,256]{2,0,1:T(8,128)(2,1)} %copy.46), calls=%async_computation.1 | async-start | bytes 4194304 | tf_op jit(solution)/shard_map/all_to_all | solution.py:113
  99.8 2.8 %copy-start.7 = (f32[16,4,64,256]{3,0,1,2:T(8,128)S(1)}, f32[16,4,64,256]{3,0,1,2:T(8,128)}, u32[]{:S(2)}) copy-start(f32[16,4,64,256]{3,0,1,2:T(8,128)} %copy.44) | copy-start | bytes 12582916
  101.8 5.9 %copy-start.4 = (bf16[16,4,64,256]{3,0,1,2:T(8,128)(2,1)}, bf16[16,4,64,256]{3,0,1,2:T(8,128)(2,1)S(1)}, u32[]{:S(2)}) copy-start(bf16[16,4,64,256]{3,0,1,2:T(8,128)(2,1)S(1)} %copy.47) | copy-start | bytes 6291460
  111.6 30.2 %all-to-all-start.2 = ((bf16[64,64,256]{2,0,1:T(8,128)(2,1)}), bf16[64,64,256]{2,0,1:T(8,128)(2,1)}, u32[]{:S(2)}, u32[]{:S(2)}) async-start(bf16[64,64,256]{2,0,1:T(8,128)(2,1)} %copy.50), calls=%async_computation.2 | async-start | bytes 4194304 | tf_op jit(solution)/shard_map/all_to_all | solution.py:121
  146.8 16.3 %collective-permute-start.7 = (f32[640,256]{1,0:T(8,128)S(1)}, f32[640,256]{1,0:T(8,128)S(1)}, u32[]{:S(2)}, u32[]{:S(2)}) collective-permute-start(f32[640,256]{1,0:T(8,128)S(1)} %get-tuple-element.14), channel_id=1, source_target_pairs={{0,4},{4,12},{12,20},{20,28},{28,24},{24,16},{16,8},{8,0},{1,5},{5... | collective-permute-start | bytes 1966088 | tf_op jit(solution)/shard_map/ppermute | solution.py:71
  163.2 15.4 %collective-permute-start.8 = (f32[640,256]{1,0:T(8,128)S(1)}, f32[640,256]{1,0:T(8,128)S(1)}, u32[]{:S(2)}, u32[]{:S(2)}) collective-permute-start(f32[640,256]{1,0:T(8,128)S(1)} %fusion.25), channel_id=1, source_target_pairs={{0,4},{4,12},{12,20},{20,28},{28,24},{24,16},{16,8},{8,0},{1,5},{5... | collective-permute-start | bytes 1966088 | tf_op jit(solution)/shard_map/ppermute | solution.py:71
  165.0 15.7 %collective-permute-start.11 = (f32[640,256]{1,0:T(8,128)S(1)}, f32[640,256]{1,0:T(8,128)S(1)}, u32[]{:S(2)}, u32[]{:S(2)}) collective-permute-start(f32[640,256]{1,0:T(8,128)S(1)} %get-tuple-element.15), channel_id=1, source_target_pairs={{0,8},{4,0},{12,4},{20,12},{28,20},{24,28},{16,24},{8,16},{1,9},{5... | collective-permute-start | bytes 1966088 | tf_op jit(solution)/shard_map/ppermute | solution.py:71
  178.7 14.7 %collective-permute-start.9 = (f32[640,256]{1,0:T(8,128)S(1)}, f32[640,256]{1,0:T(8,128)S(1)}, u32[]{:S(2)}, u32[]{:S(2)}) collective-permute-start(f32[640,256]{1,0:T(8,128)S(1)} %fusion.28), channel_id=1, source_target_pairs={{0,4},{4,12},{12,20},{20,28},{28,24},{24,16},{16,8},{8,0},{1,5},{5... | collective-permute-start | bytes 1966088 | tf_op jit(solution)/shard_map/ppermute | solution.py:71
  193.6 14.8 %collective-permute-start.12 = (f32[640,256]{1,0:T(8,128)S(1)}, f32[640,256]{1,0:T(8,128)S(1)}, u32[]{:S(2)}, u32[]{:S(2)}) collective-permute-start(f32[640,256]{1,0:T(8,128)S(1)} %get-tuple-element.13), channel_id=1, source_target_pairs={{0,8},{4,0},{12,4},{20,12},{28,20},{24,28},{16,24},{8,16},{1,9},{5... | collective-permute-start | bytes 1966088 | tf_op jit(solution)/shard_map/ppermute | solution.py:71
  195.4 14.9 %copy-start.2 = (bf16[8,512,256]{2,1,0:T(8,128)(2,1)S(1)}, bf16[8,512,256]{2,1,0:T(8,128)(2,1)}, u32[]{:S(2)}) copy-start(bf16[8,512,256]{2,1,0:T(8,128)(2,1)} %copy-done.1) | copy-start | bytes 6291460
  195.4 14.9 %copy-start.6 = (bf16[4096,256]{1,0:T(8,128)(2,1)S(1)}, bf16[4096,256]{1,0:T(8,128)(2,1)}, u32[]{:S(2)}) copy-start(bf16[4096,256]{1,0:T(8,128)(2,1)} %param.9) | copy-start | bytes 6291460
  195.4 17.2 %collective-permute-start.10 = (f32[640,256]{1,0:T(8,128)S(1)}, f32[640,256]{1,0:T(8,128)S(1)}, u32[]{:S(2)}, u32[]{:S(2)}) collective-permute-start(f32[640,256]{1,0:T(8,128)S(1)} %get-tuple-element.12), channel_id=1, source_target_pairs={{0,4},{4,12},{12,20},{20,28},{28,24},{24,16},{16,8},{8,0},{1,5},{5... | collective-permute-start | bytes 1966088 | tf_op jit(solution)/shard_map/ppermute | solution.py:71
  208.5 12.7 %collective-permute-start.13 = (f32[640,256]{1,0:T(8,128)S(1)}, f32[640,256]{1,0:T(8,128)S(1)}, u32[]{:S(2)}, u32[]{:S(2)}) collective-permute-start(f32[640,256]{1,0:T(8,128)S(1)} %fusion.16), channel_id=1, source_target_pairs={{0,8},{4,0},{12,4},{20,12},{28,20},{24,28},{16,24},{8,16},{1,9},{5... | collective-permute-start | bytes 1966088 | tf_op jit(solution)/shard_map/ppermute | solution.py:71
  (3 other events, 4.4 us)

commit v12 on v8

--- a/solution.py
+++ b/solution.py
@@ -107,30 +107,32 @@
     packed = ring_all_gather(packed, ring)
     r_whole = packed[:, :r_size].reshape(n_dp * rows_r, local_blocks, WIDTH)
     l_blocks = packed[:, r_size:].reshape(-1, local_cols, BLOCKS)
-    mixed_rows = jnp.einsum(
-        "bit,ibo->bot", x_blocks, r_whole, preferred_element_type=jnp.float32
-    ).astype(jnp.bfloat16)
-    columns = lax.all_to_all(mixed_rows, "feat", split_axis=1, concat_axis=0, tiled=True)
-    pre_act = jnp.einsum("bst,bsc->cst", columns, l_blocks, preferred_element_type=jnp.float32)
-    slope_cols = slope_of(pre_act, g_cols)
-    back_cols = jnp.einsum(
-        "cst,bsc->sbt", slope_cols, l_blocks, preferred_element_type=jnp.float32
-    ).astype(jnp.bfloat16)
-    l_term = jnp.einsum("bst,cst->bsc", columns, slope_cols, preferred_element_type=jnp.float32)
+    cut = tok_count // 2
+    l_term = r_term = None
+    xs = []
+    for lo, hi in ((0, cut), (cut, tok_count)):
+        x_half = x_blocks[:, :, lo:hi]
+        mixed_rows = jnp.einsum(
+            "bit,ibo->bot", x_half, r_whole, preferred_element_type=jnp.float32
+        ).astype(jnp.bfloat16)
+        columns = lax.all_to_all(mixed_rows, "feat", split_axis=1, concat_axis=0, tiled=True)
+        pre_act = jnp.einsum("bst,bsc->cst", columns, l_blocks, preferred_element_type=jnp.float32)
+        slope_cols = slope_of(pre_act, g_cols[:, :, lo:hi])
+        back_cols = jnp.einsum(
+            "cst,bsc->sbt", slope_cols, l_blocks, preferred_element_type=jnp.float32
+        ).astype(jnp.bfloat16)
+        l_part = jnp.einsum("bst,cst->bsc", columns, slope_cols, preferred_element_type=jnp.float32)
+        l_term = l_part if l_term is None else l_term + l_part
+        back_rows = lax.all_to_all(back_cols, "feat", split_axis=1, concat_axis=0, tiled=True)
+        through_r = jnp.einsum("obt,ibo->bit", back_rows, r_whole, preferred_element_type=jnp.float32)
+        xs.append((g_blocks[:, :, lo:hi].astype(jnp.float32) + through_r).astype(jnp.bfloat16))
+        r_part = jnp.einsum("bit,obt->ibo", x_half, back_rows, preferred_element_type=jnp.float32)
+        r_term = r_part if r_term is None else r_term + r_part
+    grad_x = jnp.concatenate(xs, axis=2).reshape(local_blocks * WIDTH, tok_count)
     l_term = (l_term * grad_scale).reshape(n_dp, -1, local_cols, BLOCKS)
     grad_l = ring_reduce_scatter(l_term, ring)
     grad_l = jnp.transpose(grad_l, (1, 0, 2)).reshape(local_cols, -1)
-    back_rows = lax.all_to_all(back_cols, "feat", split_axis=1, concat_axis=0, tiled=True)
-    through_r = jnp.einsum("obt,ibo->bit", back_rows, r_whole, preferred_element_type=jnp.float32)
-    grad_x = (
-        (g_blocks.astype(jnp.float32) + through_r)
-        .astype(jnp.bfloat16)
-        .reshape(local_blocks * WIDTH, tok_count)
-    )
-    r_term = (
-        jnp.einsum("bit,obt->ibo", x_blocks, back_rows, preferred_element_type=jnp.float32)
-        * grad_scale
-    ).reshape(n_dp, rows_r, local_blocks, WIDTH)
+    r_term = (r_term * grad_scale).reshape(n_dp, rows_r, local_blocks, WIDTH)
     grad_r = ring_reduce_scatter(r_term, ring)
     grad_r = jnp.transpose(grad_r, (1, 0, 2))
     return (grad_x, grad_r, grad_l)

time: 224 us -> 233 us (1.040)
  waiting for transfers between devices: 105 us -> 80.4 us
  local copies, waits for them, and re-layouts: 35.6 us -> 53.2 us
  other arithmetic: 7.09 us -> 13.2 us
  starting transfers between devices: 38.5 us -> 44.1 us
  matrix products: 15.8 us -> 18.5 us
    all_to_all x1 -> x2, waiting for transfers between devices: 23.8 us -> 11.9 us  [body(): lax.all_to_all(back_cols, 'feat', split_axis=1, concat_axis=0, tiled=True)]
    ppermute x14, waiting for transfers between devices: 41.3 us -> 32.6 us  [ring_reduce_scatter(): acc = lax.ppermute(mine if acc is None else acc + mine, 'dp', pairs)]
    add x6, other arithmetic: 5.05 us -> 10.1 us  [ring_reduce_scatter(): acc = lax.ppermute(mine if acc is None else acc + mine, 'dp', pairs)]
    unnamed x27 -> x39, local copies, waits for them, and re-layouts: 4.08 us -> 8.97 us
    all_to_all x1 -> x2, waiting for transfers between devices: 17.9 us -> 13.1 us  [body(): lax.all_to_all(mixed_rows, 'feat', split_axis=1, concat_axis=0, tiled=True)]
    convert_element_type x2, local copies, waits for them, and re-layouts: 6.73 us -> 3.39 us  [body(): mixed_rows = jnp.einsum('bit,ibo->bot', x_half, r_whole, preferred_elemen...]
    all_to_all x1 -> x2, starting transfers between devices: 4.45 us -> 7.76 us  [body(): lax.all_to_all(back_cols, 'feat', split_axis=1, concat_axis=0, tiled=True)]
    all_to_all x0 -> x1, local copies, waits for them, and re-layouts: none -> 3.25 us  [body(): lax.all_to_all(g_blocks, 'feat', split_axis=1, concat_axis=0, tiled=True)]
  transfers between devices with their start and end apart: 24 -> 26, of which waited for: 13 -> 13; matrix products, arithmetic and copies ran while one was open for 16% -> 29% of each run, Pallas kernels for 0% -> 0%
where the time goes in v12:
time: 233 us; the launch traced here: 231 us
  waiting for transfers between devices  80.4 us (35%)
  local copies, waits for them, and re-layouts  53.2 us (23%)
  starting transfers between devices  44.1 us (19%)
  between operations  21.6 us (9%)
  matrix products  18.5 us (8%)
  other arithmetic  13.2 us (6%)
    ppermute x14, waiting for transfers between devices, ring_reduce_scatter(): acc = lax.ppermute(mine if acc is None else acc + mine, 'dp', pairs)  32.6 us
    ppermute x7, waiting for transfers between devices, ring_all_gather(): cur = lax.ppermute(cur, 'dp', pairs)  22.7 us
    ppermute x14, starting transfers between devices, ring_reduce_scatter(): acc = lax.ppermute(mine if acc is None else acc + mine, 'dp', pairs)  15.6 us
    all_to_all x2, waiting for transfers between devices, body(): lax.all_to_all(mixed_rows, 'feat', split_axis=1, concat_axis=0, tiled=True)  13.1 us
    all_to_all x2, waiting for transfers between devices, body(): lax.all_to_all(back_cols, 'feat', split_axis=1, concat_axis=0, tiled=True)  11.9 us
    add x6, other arithmetic, ring_reduce_scatter(): acc = lax.ppermute(mine if acc is None else acc + mine, 'dp', pairs)  10.1 us
    unnamed x39, local copies, waits for them, and re-layouts  8.97 us
    ppermute x7, starting transfers between devices, ring_all_gather(): cur = lax.ppermute(cur, 'dp', pairs)  8.93 us
  transfers between devices with their start and end apart: 26, of which 13 were waited for; matrix products, arithmetic and copies ran while one was open for 29% of the time, Pallas kernels for 0%

profile of v12, /device:TPU:0, one launch (start us, length us, event | category | flops | bytes accessed | tf_op | source)
XLA Modules:
  0.0 231.0 jit_solution(684837246581175973)
XLA Ops:
  2.9 3.0 %collective-permute-start = (bf16[640,256]{1,0:T(8,128)(2,1)S(1)}, bf16[640,256]{1,0:T(8,128)(2,1)S(1)}, u32[]{:S(2)}, u32[]{:S(2)}) collective-permute-start(bf16[640,256]{1,0:T(8,128)(2,1)S(1)} %pad_maximum_fusion.1), channel_id=1, source_target_pairs={{0,4},{4,12},{12,20},{20,28},{28,24},{24,16},{16,8},{8,0},{1,5},{5... | collective-permute-start | bytes 983048 | tf_op jit(solution)/shard_map/ppermute | solution.py:88
  6.1 7.6 %collective-permute-done = bf16[640,256]{1,0:T(8,128)(2,1)S(1)} collective-permute-done((bf16[640,256]{1,0:T(8,128)(2,1)S(1)}, bf16[640,256]{1,0:T(8,128)(2,1)S(1)}, u32[]{:S(2)}, u32[]{:S(2)}) %collective-permute-start) | collective-permute-done | bytes 327712 | tf_op jit(solution)/shard_map/ppermute | solution.py:88
  15.4 4.1 %copy.102 = bf16[16,256,256]{2,0,1:T(8,128)(2,1)} copy(bf16[16,256,256]{2,1,0:T(8,128)(2,1)} %bitcast.145) | data formatting | bytes 4194304 | tf_op jit(solution)/shard_map/reshape | solution.py:99
  19.5 4.6 %all-to-all-start = ((bf16[16,256,256]{2,0,1:T(8,128)(2,1)}), bf16[16,256,256]{2,0,1:T(8,128)(2,1)}, u32[]{:S(2)}, u32[]{:S(2)}) async-start(bf16[16,256,256]{2,0,1:T(8,128)(2,1)} %copy.102), calls=%async_computation | async-start | bytes 4194304 | tf_op jit(solution)/shard_map/all_to_all | solution.py:100
  46.4 7.8 %collective-permute-done.5 = bf16[640,256]{1,0:T(8,128)(2,1)S(1)} collective-permute-done((bf16[640,256]{1,0:T(8,128)(2,1)S(1)}, bf16[640,256]{1,0:T(8,128)(2,1)S(1)}, u32[]{:S(2)}, u32[]{:S(2)}) %collective-permute-start.5) | collective-permute-done | bytes 327712 | tf_op jit(solution)/shard_map/ppermute | solution.py:88
  56.3 7.2 %collective-permute-done.3 = bf16[640,256]{1,0:T(8,128)(2,1)S(1)} collective-permute-done((bf16[640,256]{1,0:T(8,128)(2,1)S(1)}, bf16[640,256]{1,0:T(8,128)(2,1)S(1)}, u32[]{:S(2)}, u32[]{:S(2)}) %collective-permute-start.3) | collective-permute-done | bytes 327712 | tf_op jit(solution)/shard_map/ppermute | solution.py:88
  65.8 3.0 %copy.105 = bf16[256,16,256]{0,2,1:T(8,128)(2,1)S(1)} copy(bf16[256,16,256]{2,1,0:T(8,128)(2,1)} %bitcast.147) | data formatting | bytes 4194304 | tf_op jit(solution)/shard_map/reshape | solution.py:108
  72.5 3.5 %all-to-all-start.3 = ((bf16[16,256,128]{2,0,1:T(8,128)(2,1)}), bf16[16,256,128]{2,0,1:T(8,128)(2,1)S(1)}, u32[]{:S(2)}, u32[]{:S(2)}) async-start(bf16[16,256,128]{2,0,1:T(8,128)(2,1)} %copy.117), calls=%async_computation.3 | async-start | bytes 2097152 | tf_op jit(solution)/shard_map/all_to_all | solution.py:118
  79.6 10.8 %all-to-all-done.3 = bf16[16,256,128]{2,0,1:T(8,128)(2,1)S(1)} async-done(((bf16[16,256,128]{2,0,1:T(8,128)(2,1)}), bf16[16,256,128]{2,0,1:T(8,128)(2,1)S(1)}, u32[]{:S(2)}, u32[]{:S(2)}) %all-to-all-start.3) | async-done | bytes 1048608 | tf_op jit(solution)/shard_map/all_to_all | solution.py:118
  90.5 3.7 %all-to-all-start.1 = ((bf16[16,256,128]{2,0,1:T(8,128)(2,1)}), bf16[16,256,128]{2,0,1:T(8,128)(2,1)S(1)}, u32[]{:S(2)}, u32[]{:S(2)}) async-start(bf16[16,256,128]{2,0,1:T(8,128)(2,1)} %copy.106), calls=%async_computation.1 | async-start | bytes 2097152 | tf_op jit(solution)/shard_map/all_to_all | solution.py:118
  101.6 3.2 %copy.104 = bf16[4,16,64,256]{3,1,0,2:T(8,128)(2,1)} copy(bf16[4,16,64,256]{3,1,2,0:T(8,128)(2,1)} %bitcast.29) | data formatting | bytes 4194304 | tf_op jit(solution)/shard_map/all_to_all | solution.py:100
  109.7 3.0 %fusion.7 = bf16[64,64,128]{2,0,1:T(8,128)(2,1)S(1)} fusion(bf16[64,64,64]{0,2,1:T(8,128)(2,1)S(1)} %copy-done.15, bf16[64,64,128]{2,0,1:T(8,128)(2,1)S(1)} %bitcast.166, bf16[64,64,256]{2,0,1:T(8,128)(2,1)} %bitcast.172), kind=kOutput, calls=%fused_computation.16 | convolution fusion | flops 78118912 | bytes 3670016 | tf_op jit(solution)/shard_map/bst,bsc->cst/dot_general | solution.py:119
  116.3 3.5 %all-to-all-start.4 = ((bf16[64,64,128]{2,0,1:T(8,128)(2,1)}), bf16[64,64,128]{2,0,1:T(8,128)(2,1)S(1)}, u32[]{:S(2)}, u32[]{:S(2)}) async-start(bf16[64,64,128]{2,0,1:T(8,128)(2,1)} %copy.121), calls=%async_computation.4 | async-start | bytes 2097152 | tf_op jit(solution)/shard_map/all_to_all | solution.py:126
  119.9 3.6 %fusion.2 = bf16[64,64,128]{2,0,1:T(8,128)(2,1)S(1)} fusion(bf16[64,64,64]{0,2,1:T(8,128)(2,1)} %copy.108, bf16[64,64,128]{2,0,1:T(8,128)(2,1)} %bitcast.168, bf16[64,64,256]{2,0,1:T(8,128)(2,1)} %bitcast.173), kind=kOutput, calls=%fused_computation.11 | convolution fusion | flops 78118912 | bytes 3670016 | tf_op jit(solution)/shard_map/bst,bsc->cst/dot_general | solution.py:119
  126.0 8.3 %all-to-all-done.4 = bf16[64,64,128]{2,0,1:T(8,128)(2,1)S(1)} async-done(((bf16[64,64,128]{2,0,1:T(8,128)(2,1)}), bf16[64,64,128]{2,0,1:T(8,128)(2,1)S(1)}, u32[]{:S(2)}, u32[]{:S(2)}) %all-to-all-start.4) | async-done | bytes 1048608 | tf_op jit(solution)/shard_map/all_to_all | solution.py:126
  134.3 4.2 %all-to-all-start.2 = ((bf16[64,64,128]{2,0,1:T(8,128)(2,1)}), bf16[64,64,128]{2,0,1:T(8,128)(2,1)}, u32[]{:S(2)}, u32[]{:S(2)}) async-start(bf16[64,64,128]{2,0,1:T(8,128)(2,1)} %copy.110), calls=%async_computation.2 | async-start | bytes 2097152 | tf_op jit(solution)/shard_map/all_to_all | solution.py:126
  140.8 2.8 %copy.129 = f32[64,64,64]{2,1,0:T(8,128)} copy(f32[64,64,64]{0,2,1:T(8,128)S(1)} %multiply_bitcast_fusion) | data formatting | bytes 2097152 | tf_op jit(solution)/shard_map/mul | solution.py:132
  149.4 3.7 %all-to-all-done.2 = bf16[64,64,128]{2,0,1:T(8,128)(2,1)} async-done(((bf16[64,64,128]{2,0,1:T(8,128)(2,1)}), bf16[64,64,128]{2,0,1:T(8,128)(2,1)}, u32[]{:S(2)}, u32[]{:S(2)}) %all-to-all-start.2) | async-done | bytes 1048608 | tf_op jit(solution)/shard_map/all_to_all | solution.py:126
  162.7 14.1 %collective-permute-done.15 = f32[8,64,64]{2,1,0:T(8,128)S(1)} collective-permute-done((f32[8,64,64]{2,1,0:T(8,128)S(1)}, f32[8,64,64]{2,1,0:T(8,128)S(1)}, u32[]{:S(2)}, u32[]{:S(2)}) %collective-permute-start.15) | collective-permute-done | bytes 131104 | tf_op jit(solution)/shard_map/ppermute | solution.py:71
  193.2 7.9 %collective-permute-done.11 = f32[32,16,256]{2,0,1:T(8,128)} collective-permute-done((f32[32,16,256]{2,0,1:T(8,128)}, f32[32,16,256]{2,0,1:T(8,128)}, u32[]{:S(2)}, u32[]{:S(2)}) %collective-permute-start.11) | collective-permute-done | bytes 524320 | tf_op jit(solution)/shard_map/ppermute | solution.py:71
  201.1 2.7 %bitcast_add_fusion.3 = (f32[32,16,256]{2,0,1:T(8,128)}, f32[32,16,256]{2,0,1:T(8,128)}) fusion(f32[32,16,256]{2,0,1:T(8,128)} %collective-permute-done.8, f32[8,32,16,256]{3,1,0,2:T(8,128)} %bitcast.142, s32[]{:T(128)S(6)} %select_n.242, f32[32,16,256]{2,0,1:T(8,128)} %collective-permute-done.11, s32[]{:T(128)S(6)} %select_n.230), kind=kLoop, calls=%fused_computation.55 | loop fusion | flops 262144 | bytes 3145736 | tf_op jit(solution)/shard_map/add | solution.py:71
  210.1 3.9 %collective-permute-done.9 = f32[32,16,256]{2,0,1:T(8,128)} collective-permute-done((f32[32,16,256]{2,0,1:T(8,128)}, f32[32,16,256]{2,0,1:T(8,128)}, u32[]{:S(2)}, u32[]{:S(2)}) %collective-permute-start.9) | collective-permute-done | bytes 524320 | tf_op jit(solution)/shard_map/ppermute | solution.py:71
  215.4 2.7 %bitcast_add_fusion.2 = (f32[32,16,256]{2,0,1:T(8,128)}, f32[32,16,256]{2,0,1:T(8,128)}) fusion(f32[32,16,256]{2,0,1:T(8,128)} %collective-permute-done.9, f32[8,32,16,256]{3,1,0,2:T(8,128)} %bitcast.143, s32[]{:T(128)S(6)} %select_n.239, f32[32,16,256]{2,0,1:T(8,128)} %collective-permute-done.12, s32[]{:T(128)S(6)} %select_n.227), kind=kLoop, calls=%fused_computation.54 | loop fusion | flops 262144 | bytes 3145736 | tf_op jit(solution)/shard_map/add | solution.py:71
  223.7 3.7 %collective-permute-done.10 = f32[32,16,256]{2,0,1:T(8,128)S(1)} collective-permute-done((f32[32,16,256]{2,0,1:T(8,128)}, f32[32,16,256]{2,0,1:T(8,128)S(1)}, u32[]{:S(2)}, u32[]{:S(2)}) %collective-permute-start.10) | collective-permute-done | bytes 524320 | tf_op jit(solution)/shard_map/ppermute | solution.py:71
  (125 shorter events, 86.7 us)
Async XLA Ops:
  2.9 10.8 %collective-permute-start = (bf16[640,256]{1,0:T(8,128)(2,1)S(1)}, bf16[640,256]{1,0:T(8,128)(2,1)S(1)}, u32[]{:S(2)}, u32[]{:S(2)}) collective-permute-start(bf16[640,256]{1,0:T(8,128)(2,1)S(1)} %pad_maximum_fusion.1), channel_id=1, source_target_pairs={{0,4},{4,12},{12,20},{20,28},{28,24},{24,16},{16,8},{8,0},{1,5},{5... | collective-permute-start | bytes 983048 | tf_op jit(solution)/shard_map/ppermute | solution.py:88
  5.9 38.1 %collective-permute-start.4 = (bf16[640,256]{1,0:T(8,128)(2,1)S(1)}, bf16[640,256]{1,0:T(8,128)(2,1)S(1)}, u32[]{:S(2)}, u32[]{:S(2)}) collective-permute-start(bf16[640,256]{1,0:T(8,128)(2,1)S(1)} %pad_maximum_fusion.1), channel_id=1, source_target_pairs={{0,8},{4,0},{12,4},{20,12},{28,20},{24,28},{16,24},{8,16},{1,9},{5... | collective-permute-start | bytes 983048 | tf_op jit(solution)/shard_map/ppermute | solution.py:88
  13.7 30.8 %collective-permute-start.1 = (bf16[640,256]{1,0:T(8,128)(2,1)S(1)}, bf16[640,256]{1,0:T(8,128)(2,1)S(1)}, u32[]{:S(2)}, u32[]{:S(2)}) collective-permute-start(bf16[640,256]{1,0:T(8,128)(2,1)S(1)} %collective-permute-done), channel_id=1, source_target_pairs={{0,4},{4,12},{12,20},{20,28},{28,24},{24,16},{16,8},{8,0},{1,5},{5... | collective-permute-start | bytes 983048 | tf_op jit(solution)/shard_map/ppermute | solution.py:88
  19.5 53.0 %all-to-all-start = ((bf16[16,256,256]{2,0,1:T(8,128)(2,1)}), bf16[16,256,256]{2,0,1:T(8,128)(2,1)}, u32[]{:S(2)}, u32[]{:S(2)}) async-start(bf16[16,256,256]{2,0,1:T(8,128)(2,1)} %copy.102), calls=%async_computation | async-start | bytes 4194304 | tf_op jit(solution)/shard_map/all_to_all | solution.py:100
  44.1 10.1 %collective-permute-start.5 = (bf16[640,256]{1,0:T(8,128)(2,1)S(1)}, bf16[640,256]{1,0:T(8,128)(2,1)S(1)}, u32[]{:S(2)}, u32[]{:S(2)}) collective-permute-start(bf16[640,256]{1,0:T(8,128)(2,1)S(1)} %collective-permute-done.4), channel_id=1, source_target_pairs={{0,8},{4,0},{12,4},{20,12},{28,20},{24,28},{16,24},{8,16},{1,9},{5... | collective-permute-start | bytes 983048 | tf_op jit(solution)/shard_map/ppermute | solution.py:88
  44.5 10.1 %collective-permute-start.2 = (bf16[640,256]{1,0:T(8,128)(2,1)S(1)}, bf16[640,256]{1,0:T(8,128)(2,1)S(1)}, u32[]{:S(2)}, u32[]{:S(2)}) collective-permute-start(bf16[640,256]{1,0:T(8,128)(2,1)S(1)} %collective-permute-done.1), channel_id=1, source_target_pairs={{0,4},{4,12},{12,20},{20,28},{28,24},{24,16},{16,8},{8,0},{1,5},{5... | collective-permute-start | bytes 983048 | tf_op jit(solution)/shard_map/ppermute | solution.py:88
  54.2 9.4 %collective-permute-start.6 = (bf16[640,256]{1,0:T(8,128)(2,1)S(1)}, bf16[640,256]{1,0:T(8,128)(2,1)S(1)}, u32[]{:S(2)}, u32[]{:S(2)}) collective-permute-start(bf16[640,256]{1,0:T(8,128)(2,1)S(1)} %collective-permute-done.5), channel_id=1, source_target_pairs={{0,8},{4,0},{12,4},{20,12},{28,20},{24,28},{16,24},{8,16},{1,9},{5... | collective-permute-start | bytes 983048 | tf_op jit(solution)/shard_map/ppermute | solution.py:88
  72.5 18.0 %all-to-all-start.3 = ((bf16[16,256,128]{2,0,1:T(8,128)(2,1)}), bf16[16,256,128]{2,0,1:T(8,128)(2,1)S(1)}, u32[]{:S(2)}, u32[]{:S(2)}) async-start(bf16[16,256,128]{2,0,1:T(8,128)(2,1)} %copy.117), calls=%async_computation.3 | async-start | bytes 2097152 | tf_op jit(solution)/shard_map/all_to_all | solution.py:118
  90.5 18.0 %all-to-all-start.1 = ((bf16[16,256,128]{2,0,1:T(8,128)(2,1)}), bf16[16,256,128]{2,0,1:T(8,128)(2,1)S(1)}, u32[]{:S(2)}, u32[]{:S(2)}) async-start(bf16[16,256,128]{2,0,1:T(8,128)(2,1)} %copy.106), calls=%async_computation.1 | async-start | bytes 2097152 | tf_op jit(solution)/shard_map/all_to_all | solution.py:118
  116.3 18.0 %all-to-all-start.4 = ((bf16[64,64,128]{2,0,1:T(8,128)(2,1)}), bf16[64,64,128]{2,0,1:T(8,128)(2,1)S(1)}, u32[]{:S(2)}, u32[]{:S(2)}) async-start(bf16[64,64,128]{2,0,1:T(8,128)(2,1)} %copy.121), calls=%async_computation.4 | async-start | bytes 2097152 | tf_op jit(solution)/shard_map/all_to_all | solution.py:126
  134.3 18.8 %all-to-all-start.2 = ((bf16[64,64,128]{2,0,1:T(8,128)(2,1)}), bf16[64,64,128]{2,0,1:T(8,128)(2,1)}, u32[]{:S(2)}, u32[]{:S(2)}) async-start(bf16[64,64,128]{2,0,1:T(8,128)(2,1)} %copy.110), calls=%async_computation.2 | async-start | bytes 2097152 | tf_op jit(solution)/shard_map/all_to_all | solution.py:126
  145.3 14.0 %collective-permute-start.14 = (f32[8,64,64]{2,1,0:T(8,128)}, f32[8,64,64]{2,1,0:T(8,128)}, u32[]{:S(2)}, u32[]{:S(2)}) collective-permute-start(f32[8,64,64]{2,1,0:T(8,128)} %get-tuple-element.13), channel_id=1, source_target_pairs={{0,4},{4,12},{12,20},{20,28},{28,24},{24,16},{16,8},{8,0},{1,5},{5... | collective-permute-start | bytes 393224 | tf_op jit(solution)/shard_map/ppermute | solution.py:71
  147.0 15.6 %collective-permute-start.18 = (f32[8,64,64]{2,1,0:T(8,128)S(1)}, f32[8,64,64]{2,1,0:T(8,128)}, u32[]{:S(2)}, u32[]{:S(2)}) collective-permute-start(f32[8,64,64]{2,1,0:T(8,128)S(1)} %get-tuple-element.14), channel_id=1, source_target_pairs={{0,8},{4,0},{12,4},{20,12},{28,20},{24,28},{16,24},{8,16},{1,9},{5... | collective-permute-start | bytes 393224 | tf_op jit(solution)/shard_map/ppermute | solution.py:71
  157.7 24.7 %collective-permute-start.7 = (f32[32,16,256]{2,0,1:T(8,128)S(1)}, f32[32,16,256]{2,0,1:T(8,128)S(1)}, u32[]{:S(2)}, u32[]{:S(2)}) collective-permute-start(f32[32,16,256]{2,0,1:T(8,128)S(1)} %get-tuple-element.7), channel_id=1, source_target_pairs={{0,4},{4,12},{12,20},{20,28},{28,24},{24,16},{16,8},{8,0},{1,5},{5... | collective-permute-start | bytes 1572872 | tf_op jit(solution)/shard_map/ppermute | solution.py:71
  160.9 15.8 %collective-permute-start.15 = (f32[8,64,64]{2,1,0:T(8,128)S(1)}, f32[8,64,64]{2,1,0:T(8,128)S(1)}, u32[]{:S(2)}, u32[]{:S(2)}) collective-permute-start(f32[8,64,64]{2,1,0:T(8,128)S(1)} %bitcast_add_fusion.10), channel_id=1, source_target_pairs={{0,4},{4,12},{12,20},{20,28},{28,24},{24,16},{16,8},{8,0},{1,5},{5... | collective-permute-start | bytes 393224 | tf_op jit(solution)/shard_map/ppermute | solution.py:71
  178.6 11.5 %collective-permute-start.16 = (f32[8,64,64]{2,1,0:T(8,128)}, f32[8,64,64]{2,1,0:T(8,128)S(1)}, u32[]{:S(2)}, u32[]{:S(2)}) collective-permute-start(f32[8,64,64]{2,1,0:T(8,128)} %get-tuple-element.11), channel_id=1, source_target_pairs={{0,4},{4,12},{12,20},{20,28},{28,24},{24,16},{16,8},{8,0},{1,5},{5... | collective-permute-start | bytes 393224 | tf_op jit(solution)/shard_map/ppermute | solution.py:71
  180.3 9.8 %collective-permute-start.19 = (f32[8,64,64]{2,1,0:T(8,128)}, f32[8,64,64]{2,1,0:T(8,128)}, u32[]{:S(2)}, u32[]{:S(2)}) collective-permute-start(f32[8,64,64]{2,1,0:T(8,128)} %get-tuple-element.12), channel_id=1, source_target_pairs={{0,8},{4,0},{12,4},{20,12},{28,20},{24,28},{16,24},{8,16},{1,9},{5... | collective-permute-start | bytes 393224 | tf_op jit(solution)/shard_map/ppermute | solution.py:71
  180.6 20.5 %collective-permute-start.11 = (f32[32,16,256]{2,0,1:T(8,128)}, f32[32,16,256]{2,0,1:T(8,128)}, u32[]{:S(2)}, u32[]{:S(2)}) collective-permute-start(f32[32,16,256]{2,0,1:T(8,128)} %get-tuple-element.8), channel_id=1, source_target_pairs={{0,8},{4,0},{12,4},{20,12},{28,20},{24,28},{16,24},{8,16},{1,9},{5... | collective-permute-start | bytes 1572872 | tf_op jit(solution)/shard_map/ppermute | solution.py:71
  183.3 17.8 %collective-permute-start.8 = (f32[32,16,256]{2,0,1:T(8,128)}, f32[32,16,256]{2,0,1:T(8,128)}, u32[]{:S(2)}, u32[]{:S(2)}) collective-permute-start(f32[32,16,256]{2,0,1:T(8,128)} %bitcast_add_fusion.4), channel_id=1, source_target_pairs={{0,4},{4,12},{12,20},{20,28},{28,24},{24,16},{16,8},{8,0},{1,5},{5... | collective-permute-start | bytes 1572872 | tf_op jit(solution)/shard_map/ppermute | solution.py:71
  191.1 14.7 %collective-permute-start.17 = (f32[8,64,64]{2,1,0:T(8,128)S(1)}, f32[8,64,64]{2,1,0:T(8,128)S(1)}, u32[]{:S(2)}, u32[]{:S(2)}) collective-permute-start(f32[8,64,64]{2,1,0:T(8,128)S(1)} %get-tuple-element.9), channel_id=1, source_target_pairs={{0,4},{4,12},{12,20},{20,28},{28,24},{24,16},{16,8},{8,0},{1,5},{5... | collective-permute-start | bytes 393224 | tf_op jit(solution)/shard_map/ppermute | solution.py:71
  192.8 13.0 %collective-permute-start.20 = (f32[8,64,64]{2,1,0:T(8,128)S(1)}, f32[8,64,64]{2,1,0:T(8,128)S(1)}, u32[]{:S(2)}, u32[]{:S(2)}) collective-permute-start(f32[8,64,64]{2,1,0:T(8,128)S(1)} %get-tuple-element.10), channel_id=1, source_target_pairs={{0,8},{4,0},{12,4},{20,12},{28,20},{24,28},{16,24},{8,16},{1,9},{5... | collective-permute-start | bytes 393224 | tf_op jit(solution)/shard_map/ppermute | solution.py:71
  203.8 10.2 %collective-permute-start.9 = (f32[32,16,256]{2,0,1:T(8,128)}, f32[32,16,256]{2,0,1:T(8,128)}, u32[]{:S(2)}, u32[]{:S(2)}) collective-permute-start(f32[32,16,256]{2,0,1:T(8,128)} %get-tuple-element.5), channel_id=1, source_target_pairs={{0,4},{4,12},{12,20},{20,28},{28,24},{24,16},{16,8},{8,0},{1,5},{5... | collective-permute-start | bytes 1572872 | tf_op jit(solution)/shard_map/ppermute | solution.py:71
  205.4 10.0 %collective-permute-start.12 = (f32[32,16,256]{2,0,1:T(8,128)}, f32[32,16,256]{2,0,1:T(8,128)}, u32[]{:S(2)}, u32[]{:S(2)}) collective-permute-start(f32[32,16,256]{2,0,1:T(8,128)} %get-tuple-element.6), channel_id=1, source_target_pairs={{0,8},{4,0},{12,4},{20,12},{28,20},{24,28},{16,24},{8,16},{1,9},{5... | collective-permute-start | bytes 1572872 | tf_op jit(solution)/shard_map/ppermute | solution.py:71
  218.1 9.4 %collective-permute-start.10 = (f32[32,16,256]{2,0,1:T(8,128)}, f32[32,16,256]{2,0,1:T(8,128)S(1)}, u32[]{:S(2)}, u32[]{:S(2)}) collective-permute-start(f32[32,16,256]{2,0,1:T(8,128)} %get-tuple-element.3), channel_id=1, source_target_pairs={{0,4},{4,12},{12,20},{20,28},{28,24},{24,16},{16,8},{8,0},{1,5},{5... | collective-permute-start | bytes 1572872 | tf_op jit(solution)/shard_map/ppermute | solution.py:71
  (20 other events, 161.7 us)

commit v13 on v8

--- a/solution.py
+++ b/solution.py
@@ -53,7 +53,7 @@
     return list(path) if grow() else list(range(size))
 
 
-def ring_reduce_scatter(parts, ring):
+def ring_reduce_scatter(parts, ring, lead=1):
     n = len(ring)
     order = jnp.asarray(np.array(ring, np.int32))
     place = jnp.asarray(np.argsort(np.array(ring)).astype(np.int32))
@@ -62,7 +62,7 @@
     forward = [(ring[p], ring[(p + 1) % n]) for p in range(n)]
     backward = [(ring[p], ring[(p - 1) % n]) for p in range(n)]
     total = lax.dynamic_index_in_dim(parts, me, axis=0, keepdims=False)
-    ahead = n // 2
+    ahead = n // 2 if lead > 0 else n - 1 - n // 2
     for way, pairs, hops in ((1, forward, ahead), (-1, backward, n - 1 - ahead)):
         acc = None
         for step in range(hops):
@@ -118,7 +118,7 @@
     ).astype(jnp.bfloat16)
     l_term = jnp.einsum("bst,cst->bsc", columns, slope_cols, preferred_element_type=jnp.float32)
     l_term = (l_term * grad_scale).reshape(n_dp, -1, local_cols, BLOCKS)
-    grad_l = ring_reduce_scatter(l_term, ring)
+    grad_l = ring_reduce_scatter(l_term, ring, lead=-1)
     grad_l = jnp.transpose(grad_l, (1, 0, 2)).reshape(local_cols, -1)
     back_rows = lax.all_to_all(back_cols, "feat", split_axis=1, concat_axis=0, tiled=True)
     through_r = jnp.einsum("obt,ibo->bit", back_rows, r_whole, preferred_element_type=jnp.float32)

time: 224 us -> 221 us (0.987)
  waiting for transfers between devices: 105 us -> 102 us
    ppermute x14, waiting for transfers between devices: 41.3 us -> 38.8 us  [ring_reduce_scatter(): acc = lax.ppermute(mine if acc is None else acc + mine, 'dp', pairs)]
  transfers between devices with their start and end apart: 24 -> 24, of which waited for: 13 -> 14; matrix products, arithmetic and copies ran while one was open for 16% -> 17% of each run, Pallas kernels for 0% -> 0%
where the time goes in v13:
time: 221 us; the launch traced here: 219 us
  waiting for transfers between devices  102 us (46%)
  starting transfers between devices  37.1 us (17%)
  local copies, waits for them, and re-layouts  35.6 us (16%)
  between operations  21.5 us (10%)
  matrix products  15.8 us (7%)
  other arithmetic  7.09 us (3%)
    ppermute x14, waiting for transfers between devices, ring_reduce_scatter(): acc = lax.ppermute(mine if acc is None else acc + mine, 'dp', pairs)  38.8 us
    all_to_all x1, waiting for transfers between devices, body(): lax.all_to_all(back_cols, 'feat', split_axis=1, concat_axis=0, tiled=True)  23.8 us
    ppermute x7, waiting for transfers between devices, ring_all_gather(): cur = lax.ppermute(cur, 'dp', pairs)  21.8 us
    all_to_all x1, waiting for transfers between devices, body(): lax.all_to_all(mixed_rows, 'feat', split_axis=1, concat_axis=0, tiled=True)  17.9 us
    ppermute x14, starting transfers between devices, ring_reduce_scatter(): acc = lax.ppermute(mine if acc is None else acc + mine, 'dp', pairs)  14.5 us
    ppermute x7, starting transfers between devices, ring_all_gather(): cur = lax.ppermute(cur, 'dp', pairs)  8.93 us
    dot_general x1, matrix products, body(): jnp.einsum('obt,ibo->bit', back_rows, r_whole, preferred_element_type=jnp...  5.13 us
    dot_general x1, matrix products, body(): jnp.einsum('bst,bsc->cst', columns, l_blocks, preferred_element_type=jnp....  5.07 us
  transfers between devices with their start and end apart: 24, of which 14 were waited for; matrix products, arithmetic and copies ran while one was open for 17% of the time, Pallas kernels for 0%

profile of v13, /device:TPU:0, one launch (start us, length us, event | category | flops | bytes accessed | tf_op | source)
XLA Modules:
  0.0 219.5 jit_solution(6735083410819900897)
XLA Ops:
  3.1 3.0 %collective-permute-start = (bf16[640,256]{1,0:T(8,128)(2,1)S(1)}, bf16[640,256]{1,0:T(8,128)(2,1)}, u32[]{:S(2)}, u32[]{:S(2)}) collective-permute-start(bf16[640,256]{1,0:T(8,128)(2,1)S(1)} %pad_maximum_fusion), channel_id=1, source_target_pairs={{0,4},{4,12},{12,20},{20,28},{28,24},{24,16},{16,8},{8,0},{1,5},{5... | collective-permute-start | bytes 983048 | tf_op jit(solution)/shard_map/ppermute | solution.py:88
  6.2 7.7 %collective-permute-done = bf16[640,256]{1,0:T(8,128)(2,1)} collective-permute-done((bf16[640,256]{1,0:T(8,128)(2,1)S(1)}, bf16[640,256]{1,0:T(8,128)(2,1)}, u32[]{:S(2)}, u32[]{:S(2)}) %collective-permute-start) | collective-permute-done | bytes 327712 | tf_op jit(solution)/shard_map/ppermute | solution.py:88
  15.7 4.1 %copy.41 = bf16[16,256,256]{2,0,1:T(8,128)(2,1)} copy(bf16[16,256,256]{2,1,0:T(8,128)(2,1)} %bitcast.146) | data formatting | bytes 4194304 | tf_op jit(solution)/shard_map/reshape | solution.py:99
  19.8 4.6 %all-to-all-start = ((bf16[16,256,256]{2,0,1:T(8,128)(2,1)}), bf16[16,256,256]{2,0,1:T(8,128)(2,1)}, u32[]{:S(2)}, u32[]{:S(2)}) async-start(bf16[16,256,256]{2,0,1:T(8,128)(2,1)} %copy.41), calls=%async_computation | async-start | bytes 4194304 | tf_op jit(solution)/shard_map/all_to_all | solution.py:100
  47.5 6.8 %collective-permute-done.5 = bf16[640,256]{1,0:T(8,128)(2,1)S(1)} collective-permute-done((bf16[640,256]{1,0:T(8,128)(2,1)S(1)}, bf16[640,256]{1,0:T(8,128)(2,1)S(1)}, u32[]{:S(2)}, u32[]{:S(2)}) %collective-permute-start.5) | collective-permute-done | bytes 327712 | tf_op jit(solution)/shard_map/ppermute | solution.py:88
  56.4 7.2 %collective-permute-done.3 = bf16[640,256]{1,0:T(8,128)(2,1)S(1)} collective-permute-done((bf16[640,256]{1,0:T(8,128)(2,1)S(1)}, bf16[640,256]{1,0:T(8,128)(2,1)S(1)}, u32[]{:S(2)}, u32[]{:S(2)}) %collective-permute-start.3) | collective-permute-done | bytes 327712 | tf_op jit(solution)/shard_map/ppermute | solution.py:88
  67.0 2.6 %copy.44 = bf16[16,256,256]{2,0,1:T(8,128)(2,1)} copy(bf16[16,256,256]{2,1,0:T(8,128)(2,1)S(1)} %convolution_convert_fusion.1) | data formatting | bytes 4194304 | tf_op jit(solution)/shard_map/convert_element_type | solution.py:112
  69.5 4.7 %all-to-all-start.1 = ((bf16[16,256,256]{2,0,1:T(8,128)(2,1)}), bf16[16,256,256]{2,0,1:T(8,128)(2,1)}, u32[]{:S(2)}, u32[]{:S(2)}) async-start(bf16[16,256,256]{2,0,1:T(8,128)(2,1)} %copy.44), calls=%async_computation.1 | async-start | bytes 4194304 | tf_op jit(solution)/shard_map/all_to_all | solution.py:113
  77.7 4.2 %copy.42 = f32[16,4,64,256]{3,0,1,2:T(8,128)} copy(bf16[16,4,64,256]{3,0,2,1:T(8,128)(2,1)} %bitcast.68) | data formatting | bytes 6291456 | tf_op jit(solution)/shard_map/convert_element_type | solution.py:19
  81.9 17.9 %all-to-all-done.1 = bf16[16,256,256]{2,0,1:T(8,128)(2,1)} async-done(((bf16[16,256,256]{2,0,1:T(8,128)(2,1)}), bf16[16,256,256]{2,0,1:T(8,128)(2,1)}, u32[]{:S(2)}, u32[]{:S(2)}) %all-to-all-start.1) | async-done | bytes 2097184 | tf_op jit(solution)/shard_map/all_to_all | solution.py:113
  99.8 2.0 copy.45
  102.6 5.1 %fusion.6 = bf16[64,64,256]{2,0,1:T(8,128)(2,1)S(1)} fusion(f32[16,4,64,256]{3,0,1,2:T(8,128)S(1)} %copy-done.10, bf16[64,64,256]{2,0,1:T(8,128)(2,1)S(1)} %bitcast.144, bf16[64,64,64]{2,1,0:T(8,128)(2,1)S(1)} %reshape.90), kind=kOutput, calls=%fused_computation.8 | convolution fusion | flops 155189248 | bytes 8912896 | tf_op jit(solution)/shard_map/bst,bsc->cst/dot_general | solution.py:114
  109.1 2.5 %copy.48 = bf16[64,64,256]{2,0,1:T(8,128)(2,1)} copy(bf16[64,64,256]{2,1,0:T(8,128)(2,1)S(1)} %convolution_convert_fusion) | data formatting | bytes 4194304 | tf_op jit(solution)/shard_map/convert_element_type | solution.py:118
  111.6 4.4 %all-to-all-start.2 = ((bf16[64,64,256]{2,0,1:T(8,128)(2,1)}), bf16[64,64,256]{2,0,1:T(8,128)(2,1)}, u32[]{:S(2)}, u32[]{:S(2)}) async-start(bf16[64,64,256]{2,0,1:T(8,128)(2,1)} %copy.48), calls=%async_computation.2 | async-start | bytes 4194304 | tf_op jit(solution)/shard_map/all_to_all | solution.py:123
  118.0 23.8 %all-to-all-done.2 = bf16[64,64,256]{2,0,1:T(8,128)(2,1)} async-done(((bf16[64,64,256]{2,0,1:T(8,128)(2,1)}), bf16[64,64,256]{2,0,1:T(8,128)(2,1)}, u32[]{:S(2)}, u32[]{:S(2)}) %all-to-all-start.2) | async-done | bytes 2097184 | tf_op jit(solution)/shard_map/all_to_all | solution.py:123
  148.0 11.4 %collective-permute-done.7 = f32[32,16,256]{2,0,1:T(8,128)S(1)} collective-permute-done((f32[32,16,256]{2,0,1:T(8,128)S(1)}, f32[32,16,256]{2,0,1:T(8,128)S(1)}, u32[]{:S(2)}, u32[]{:S(2)}) %collective-permute-start.7) | collective-permute-done | bytes 524320 | tf_op jit(solution)/shard_map/ppermute | solution.py:71
  163.2 3.8 %copy.51 = f32[64,64,64]{2,1,0:T(8,128)} copy(f32[64,64,64]{0,2,1:T(8,128)} %multiply_bitcast_fusion) | data formatting | bytes 2097152 | tf_op jit(solution)/shard_map/mul | solution.py:120
  170.3 4.6 %collective-permute-done.17 = f32[8,64,64]{2,1,0:T(8,128)S(1)} collective-permute-done((f32[8,64,64]{2,1,0:T(8,128)S(1)}, f32[8,64,64]{2,1,0:T(8,128)S(1)}, u32[]{:S(2)}, u32[]{:S(2)}) %collective-permute-start.17) | collective-permute-done | bytes 131104 | tf_op jit(solution)/shard_map/ppermute | solution.py:71
  180.0 5.3 %collective-permute-done.18 = f32[8,64,64]{2,1,0:T(8,128)S(1)} collective-permute-done((f32[8,64,64]{2,1,0:T(8,128)S(1)}, f32[8,64,64]{2,1,0:T(8,128)S(1)}, u32[]{:S(2)}, u32[]{:S(2)}) %collective-permute-start.18) | collective-permute-done | bytes 131104 | tf_op jit(solution)/shard_map/ppermute | solution.py:71
  187.4 8.8 %collective-permute-done.15 = f32[8,64,64]{2,1,0:T(8,128)S(1)} collective-permute-done((f32[8,64,64]{2,1,0:T(8,128)S(1)}, f32[8,64,64]{2,1,0:T(8,128)S(1)}, u32[]{:S(2)}, u32[]{:S(2)}) %collective-permute-start.15) | collective-permute-done | bytes 131104 | tf_op jit(solution)/shard_map/ppermute | solution.py:71
  196.2 2.5 %collective-permute-done.19 = f32[8,64,64]{2,1,0:T(8,128)S(1)} collective-permute-done((f32[8,64,64]{2,1,0:T(8,128)S(1)}, f32[8,64,64]{2,1,0:T(8,128)S(1)}, u32[]{:S(2)}, u32[]{:S(2)}) %collective-permute-start.19) | collective-permute-done | bytes 131104 | tf_op jit(solution)/shard_map/ppermute | solution.py:71
  200.9 2.4 %bitcast_add_fusion.2 = (f32[32,16,256]{2,0,1:T(8,128)}, f32[32,16,256]{2,0,1:T(8,128)}) fusion(f32[32,16,256]{2,0,1:T(8,128)S(1)} %collective-permute-done.9, f32[8,32,16,256]{3,1,0,2:T(8,128)} %bitcast.142, s32[]{:T(128)S(6)} %select_n.239, f32[32,16,256]{2,0,1:T(8,128)S(1)} %collective-permute-done.12, s32[]{:T(128)S(6)} %select_n.227), kind=kLoop, calls=%fused_computation.25 | loop fusion | flops 262144 | bytes 3145736 | tf_op jit(solution)/shard_map/add | solution.py:71
  205.3 2.8 %collective-permute-done.16 = f32[8,64,64]{2,1,0:T(8,128)S(1)} collective-permute-done((f32[8,64,64]{2,1,0:T(8,128)S(1)}, f32[8,64,64]{2,1,0:T(8,128)S(1)}, u32[]{:S(2)}, u32[]{:S(2)}) %collective-permute-start.16) | collective-permute-done | bytes 131104 | tf_op jit(solution)/shard_map/ppermute | solution.py:71
  210.5 5.1 %add_convert_fusion = bf16[16,256,256]{2,1,0:T(8,128)(2,1)} fusion(bf16[16,256,256]{2,1,0:T(8,128)(2,1)} %bitcast.147, bf16[256,16,256]{2,0,1:T(8,128)(2,1)} %bitcast.138, bf16[256,16,256]{2,1,0:T(8,128)(2,1)} %bitcast.136), kind=kOutput, calls=%fused_computation.14 | convolution fusion | flops 540016640 | bytes 8388608 | tf_op jit(solution)/shard_map/obt,ibo->bit/dot_general | solution.py:124
  (94 shorter events, 50.6 us)
Async XLA Ops:
  3.1 10.9 %collective-permute-start = (bf16[640,256]{1,0:T(8,128)(2,1)S(1)}, bf16[640,256]{1,0:T(8,128)(2,1)}, u32[]{:S(2)}, u32[]{:S(2)}) collective-permute-start(bf16[640,256]{1,0:T(8,128)(2,1)S(1)} %pad_maximum_fusion), channel_id=1, source_target_pairs={{0,4},{4,12},{12,20},{20,28},{28,24},{24,16},{16,8},{8,0},{1,5},{5... | collective-permute-start | bytes 983048 | tf_op jit(solution)/shard_map/ppermute | solution.py:88
  6.1 38.1 %collective-permute-start.4 = (bf16[640,256]{1,0:T(8,128)(2,1)S(1)}, bf16[640,256]{1,0:T(8,128)(2,1)S(1)}, u32[]{:S(2)}, u32[]{:S(2)}) collective-permute-start(bf16[640,256]{1,0:T(8,128)(2,1)S(1)} %pad_maximum_fusion), channel_id=1, source_target_pairs={{0,8},{4,0},{12,4},{20,12},{28,20},{24,28},{16,24},{8,16},{1,9},{5... | collective-permute-start | bytes 983048 | tf_op jit(solution)/shard_map/ppermute | solution.py:88
  14.0 30.6 %collective-permute-start.1 = (bf16[640,256]{1,0:T(8,128)(2,1)}, bf16[640,256]{1,0:T(8,128)(2,1)S(1)}, u32[]{:S(2)}, u32[]{:S(2)}) collective-permute-start(bf16[640,256]{1,0:T(8,128)(2,1)} %collective-permute-done), channel_id=1, source_target_pairs={{0,4},{4,12},{12,20},{20,28},{28,24},{24,16},{16,8},{8,0},{1,5},{5... | collective-permute-start | bytes 983048 | tf_op jit(solution)/shard_map/ppermute | solution.py:88
  19.8 49.8 %all-to-all-start = ((bf16[16,256,256]{2,0,1:T(8,128)(2,1)}), bf16[16,256,256]{2,0,1:T(8,128)(2,1)}, u32[]{:S(2)}, u32[]{:S(2)}) async-start(bf16[16,256,256]{2,0,1:T(8,128)(2,1)} %copy.41), calls=%async_computation | async-start | bytes 4194304 | tf_op jit(solution)/shard_map/all_to_all | solution.py:100
  44.2 10.1 %collective-permute-start.5 = (bf16[640,256]{1,0:T(8,128)(2,1)S(1)}, bf16[640,256]{1,0:T(8,128)(2,1)S(1)}, u32[]{:S(2)}, u32[]{:S(2)}) collective-permute-start(bf16[640,256]{1,0:T(8,128)(2,1)S(1)} %collective-permute-done.4), channel_id=1, source_target_pairs={{0,8},{4,0},{12,4},{20,12},{28,20},{24,28},{16,24},{8,16},{1,9},{5... | collective-permute-start | bytes 983048 | tf_op jit(solution)/shard_map/ppermute | solution.py:88
  44.6 10.1 %collective-permute-start.2 = (bf16[640,256]{1,0:T(8,128)(2,1)S(1)}, bf16[640,256]{1,0:T(8,128)(2,1)S(1)}, u32[]{:S(2)}, u32[]{:S(2)}) collective-permute-start(bf16[640,256]{1,0:T(8,128)(2,1)S(1)} %collective-permute-done.1), channel_id=1, source_target_pairs={{0,4},{4,12},{12,20},{20,28},{28,24},{24,16},{16,8},{8,0},{1,5},{5... | collective-permute-start | bytes 983048 | tf_op jit(solution)/shard_map/ppermute | solution.py:88
  54.3 9.4 %collective-permute-start.6 = (bf16[640,256]{1,0:T(8,128)(2,1)S(1)}, bf16[640,256]{1,0:T(8,128)(2,1)S(1)}, u32[]{:S(2)}, u32[]{:S(2)}) collective-permute-start(bf16[640,256]{1,0:T(8,128)(2,1)S(1)} %collective-permute-done.5), channel_id=1, source_target_pairs={{0,8},{4,0},{12,4},{20,12},{28,20},{24,28},{16,24},{8,16},{1,9},{5... | collective-permute-start | bytes 983048 | tf_op jit(solution)/shard_map/ppermute | solution.py:88
  54.6 9.0 %collective-permute-start.3 = (bf16[640,256]{1,0:T(8,128)(2,1)S(1)}, bf16[640,256]{1,0:T(8,128)(2,1)S(1)}, u32[]{:S(2)}, u32[]{:S(2)}) collective-permute-start(bf16[640,256]{1,0:T(8,128)(2,1)S(1)} %collective-permute-done.2), channel_id=1, source_target_pairs={{0,4},{4,12},{12,20},{20,28},{28,24},{24,16},{16,8},{8,0},{1,5},{5... | collective-permute-start | bytes 983048 | tf_op jit(solution)/shard_map/ppermute | solution.py:88
  69.5 30.2 %all-to-all-start.1 = ((bf16[16,256,256]{2,0,1:T(8,128)(2,1)}), bf16[16,256,256]{2,0,1:T(8,128)(2,1)}, u32[]{:S(2)}, u32[]{:S(2)}) async-start(bf16[16,256,256]{2,0,1:T(8,128)(2,1)} %copy.44), calls=%async_computation.1 | async-start | bytes 4194304 | tf_op jit(solution)/shard_map/all_to_all | solution.py:113
  111.6 30.2 %all-to-all-start.2 = ((bf16[64,64,256]{2,0,1:T(8,128)(2,1)}), bf16[64,64,256]{2,0,1:T(8,128)(2,1)}, u32[]{:S(2)}, u32[]{:S(2)}) async-start(bf16[64,64,256]{2,0,1:T(8,128)(2,1)} %copy.48), calls=%async_computation.2 | async-start | bytes 4194304 | tf_op jit(solution)/shard_map/all_to_all | solution.py:123
  145.9 13.5 %collective-permute-start.7 = (f32[32,16,256]{2,0,1:T(8,128)S(1)}, f32[32,16,256]{2,0,1:T(8,128)S(1)}, u32[]{:S(2)}, u32[]{:S(2)}) collective-permute-start(f32[32,16,256]{2,0,1:T(8,128)S(1)} %get-tuple-element.7), channel_id=1, source_target_pairs={{0,4},{4,12},{12,20},{20,28},{28,24},{24,16},{16,8},{8,0},{1,5},{5... | collective-permute-start | bytes 1572872 | tf_op jit(solution)/shard_map/ppermute | solution.py:71
  147.6 28.7 %collective-permute-start.11 = (f32[32,16,256]{2,0,1:T(8,128)}, f32[32,16,256]{2,0,1:T(8,128)S(1)}, u32[]{:S(2)}, u32[]{:S(2)}) collective-permute-start(f32[32,16,256]{2,0,1:T(8,128)} %get-tuple-element.8), channel_id=1, source_target_pairs={{0,8},{4,0},{12,4},{20,12},{28,20},{24,28},{16,24},{8,16},{1,9},{5... | collective-permute-start | bytes 1572872 | tf_op jit(solution)/shard_map/ppermute | solution.py:71
  159.5 16.9 %collective-permute-start.8 = (f32[32,16,256]{2,0,1:T(8,128)S(1)}, f32[32,16,256]{2,0,1:T(8,128)}, u32[]{:S(2)}, u32[]{:S(2)}) collective-permute-start(f32[32,16,256]{2,0,1:T(8,128)S(1)} %bitcast_add_fusion.4), channel_id=1, source_target_pairs={{0,4},{4,12},{12,20},{20,28},{28,24},{24,16},{16,8},{8,0},{1,5},{5... | collective-permute-start | bytes 1572872 | tf_op jit(solution)/shard_map/ppermute | solution.py:71
  168.2 6.7 %collective-permute-start.17 = (f32[8,64,64]{2,1,0:T(8,128)S(1)}, f32[8,64,64]{2,1,0:T(8,128)S(1)}, u32[]{:S(2)}, u32[]{:S(2)}) collective-permute-start(f32[8,64,64]{2,1,0:T(8,128)S(1)} %get-tuple-element.14), channel_id=1, source_target_pairs={{0,8},{4,0},{12,4},{20,12},{28,20},{24,28},{16,24},{8,16},{1,9},{5... | collective-permute-start | bytes 393224 | tf_op jit(solution)/shard_map/ppermute | solution.py:71
  168.6 11.3 %collective-permute-start.14 = (f32[8,64,64]{2,1,0:T(8,128)S(1)}, f32[8,64,64]{2,1,0:T(8,128)S(1)}, u32[]{:S(2)}, u32[]{:S(2)}) collective-permute-start(f32[8,64,64]{2,1,0:T(8,128)S(1)} %get-tuple-element.13), channel_id=1, source_target_pairs={{0,4},{4,12},{12,20},{20,28},{28,24},{24,16},{16,8},{8,0},{1,5},{5... | collective-permute-start | bytes 393224 | tf_op jit(solution)/shard_map/ppermute | solution.py:71
  175.9 9.3 %collective-permute-start.18 = (f32[8,64,64]{2,1,0:T(8,128)S(1)}, f32[8,64,64]{2,1,0:T(8,128)S(1)}, u32[]{:S(2)}, u32[]{:S(2)}) collective-permute-start(f32[8,64,64]{2,1,0:T(8,128)S(1)} %bitcast_add_fusion.8), channel_id=1, source_target_pairs={{0,8},{4,0},{12,4},{20,12},{28,20},{24,28},{16,24},{8,16},{1,9},{5... | collective-permute-start | bytes 393224 | tf_op jit(solution)/shard_map/ppermute | solution.py:71
  177.9 23.0 %collective-permute-start.12 = (f32[32,16,256]{2,0,1:T(8,128)S(1)}, f32[32,16,256]{2,0,1:T(8,128)S(1)}, u32[]{:S(2)}, u32[]{:S(2)}) collective-permute-start(f32[32,16,256]{2,0,1:T(8,128)S(1)} %get-tuple-element.6), channel_id=1, source_target_pairs={{0,8},{4,0},{12,4},{20,12},{28,20},{24,28},{16,24},{8,16},{1,9},{5... | collective-permute-start | bytes 1572872 | tf_op jit(solution)/shard_map/ppermute | solution.py:71
  179.6 21.2 %collective-permute-start.9 = (f32[32,16,256]{2,0,1:T(8,128)S(1)}, f32[32,16,256]{2,0,1:T(8,128)S(1)}, u32[]{:S(2)}, u32[]{:S(2)}) collective-permute-start(f32[32,16,256]{2,0,1:T(8,128)S(1)} %get-tuple-element.5), channel_id=1, source_target_pairs={{0,4},{4,12},{12,20},{20,28},{28,24},{24,16},{16,8},{8,0},{1,5},{5... | collective-permute-start | bytes 1572872 | tf_op jit(solution)/shard_map/ppermute | solution.py:71
  185.3 10.9 %collective-permute-start.15 = (f32[8,64,64]{2,1,0:T(8,128)S(1)}, f32[8,64,64]{2,1,0:T(8,128)S(1)}, u32[]{:S(2)}, u32[]{:S(2)}) collective-permute-start(f32[8,64,64]{2,1,0:T(8,128)S(1)} %get-tuple-element.11), channel_id=1, source_target_pairs={{0,4},{4,12},{12,20},{20,28},{28,24},{24,16},{16,8},{8,0},{1,5},{5... | collective-permute-start | bytes 393224 | tf_op jit(solution)/shard_map/ppermute | solution.py:71
  186.9 11.8 %collective-permute-start.19 = (f32[8,64,64]{2,1,0:T(8,128)S(1)}, f32[8,64,64]{2,1,0:T(8,128)S(1)}, u32[]{:S(2)}, u32[]{:S(2)}) collective-permute-start(f32[8,64,64]{2,1,0:T(8,128)S(1)} %get-tuple-element.12), channel_id=1, source_target_pairs={{0,8},{4,0},{12,4},{20,12},{28,20},{24,28},{16,24},{8,16},{1,9},{5... | collective-permute-start | bytes 393224 | tf_op jit(solution)/shard_map/ppermute | solution.py:71
  198.8 9.2 %collective-permute-start.16 = (f32[8,64,64]{2,1,0:T(8,128)S(1)}, f32[8,64,64]{2,1,0:T(8,128)S(1)}, u32[]{:S(2)}, u32[]{:S(2)}) collective-permute-start(f32[8,64,64]{2,1,0:T(8,128)S(1)} %get-tuple-element.9), channel_id=1, source_target_pairs={{0,4},{4,12},{12,20},{20,28},{28,24},{24,16},{16,8},{8,0},{1,5},{5... | collective-permute-start | bytes 393224 | tf_op jit(solution)/shard_map/ppermute | solution.py:71
  200.4 9.1 %collective-permute-start.20 = (f32[8,64,64]{2,1,0:T(8,128)S(1)}, f32[8,64,64]{2,1,0:T(8,128)S(1)}, u32[]{:S(2)}, u32[]{:S(2)}) collective-permute-start(f32[8,64,64]{2,1,0:T(8,128)S(1)} %get-tuple-element.10), channel_id=1, source_target_pairs={{0,8},{4,0},{12,4},{20,12},{28,20},{24,28},{16,24},{8,16},{1,9},{5... | collective-permute-start | bytes 393224 | tf_op jit(solution)/shard_map/ppermute | solution.py:71
  203.2 13.0 %collective-permute-start.10 = (f32[32,16,256]{2,0,1:T(8,128)}, f32[32,16,256]{2,0,1:T(8,128)S(1)}, u32[]{:S(2)}, u32[]{:S(2)}) collective-permute-start(f32[32,16,256]{2,0,1:T(8,128)} %get-tuple-element.3), channel_id=1, source_target_pairs={{0,4},{4,12},{12,20},{20,28},{28,24},{24,16},{16,8},{8,0},{1,5},{5... | collective-permute-start | bytes 1572872 | tf_op jit(solution)/shard_map/ppermute | solution.py:71
  204.8 12.7 %collective-permute-start.13 = (f32[32,16,256]{2,0,1:T(8,128)}, f32[32,16,256]{2,0,1:T(8,128)S(1)}, u32[]{:S(2)}, u32[]{:S(2)}) collective-permute-start(f32[32,16,256]{2,0,1:T(8,128)} %get-tuple-element.4), channel_id=1, source_target_pairs={{0,8},{4,0},{12,4},{20,12},{28,20},{24,28},{16,24},{8,16},{1,9},{5... | collective-permute-start | bytes 1572872 | tf_op jit(solution)/shard_map/ppermute | solution.py:71
  (13 other events, 160.7 us)

commit v14 on v13

--- a/solution.py
+++ b/solution.py
@@ -131,7 +131,11 @@
         jnp.einsum("bit,obt->ibo", x_blocks, back_rows, preferred_element_type=jnp.float32)
         * grad_scale
     ).reshape(n_dp, rows_r, local_blocks, WIDTH)
-    grad_r = ring_reduce_scatter(r_term, ring)
+    cut = rows_r // 2
+    grad_r = jnp.concatenate(
+        [ring_reduce_scatter(r_term[:, :cut], ring), ring_reduce_scatter(r_term[:, cut:], ring, lead=-1)],
+        axis=0,
+    )
     grad_r = jnp.transpose(grad_r, (1, 0, 2))
     return (grad_x, grad_r, grad_l)
 

time: 221 us -> 203 us (0.919)
  waiting for transfers between devices: 102 us -> 69.6 us
  starting transfers between devices: 37.1 us -> 49 us
    all_to_all x1, waiting for transfers between devices: 23.8 us -> 5.06 us  [body(): lax.all_to_all(back_cols, 'feat', split_axis=1, concat_axis=0, tiled=True)]
    ppermute x14 -> x21, waiting for transfers between devices: 38.8 us -> 24.9 us  [ring_reduce_scatter(): acc = lax.ppermute(mine if acc is None else acc + mine, 'dp', pairs)]
    ppermute x14 -> x21, starting transfers between devices: 14.5 us -> 26.4 us  [ring_reduce_scatter(): acc = lax.ppermute(mine if acc is None else acc + mine, 'dp', pairs)]
    dot_general x1, matrix products: 2.01 us -> 4.33 us  [body(): jnp.einsum('bst,cst->bsc', columns, slope_cols, preferred_element_type=jn...]
    add x6 -> x9, other arithmetic: 5.05 us -> 5.14 us  [ring_reduce_scatter(): acc = lax.ppermute(mine if acc is None else acc + mine, 'dp', pairs)]
  transfers between devices with their start and end apart: 24 -> 31, of which waited for: 14 -> 19; matrix products, arithmetic and copies ran while one was open for 17% -> 21% of each run, Pallas kernels for 0% -> 0%
where the time goes in v14:
time: 203 us; the launch traced here: 202 us
  waiting for transfers between devices  69.6 us (34%)
  starting transfers between devices  49 us (24%)
  local copies, waits for them, and re-layouts  36 us (18%)
  between operations  21.5 us (11%)
  matrix products  17.5 us (9%)
  other arithmetic  8.09 us (4%)
    ppermute x21, starting transfers between devices, ring_reduce_scatter(): acc = lax.ppermute(mine if acc is None else acc + mine, 'dp', pairs)  26.4 us
    ppermute x21, waiting for transfers between devices, ring_reduce_scatter(): acc = lax.ppermute(mine if acc is None else acc + mine, 'dp', pairs)  24.9 us
    ppermute x7, waiting for transfers between devices, ring_all_gather(): cur = lax.ppermute(cur, 'dp', pairs)  21.8 us
    all_to_all x1, waiting for transfers between devices, body(): lax.all_to_all(mixed_rows, 'feat', split_axis=1, concat_axis=0, tiled=True)  17.9 us
    ppermute x7, starting transfers between devices, ring_all_gather(): cur = lax.ppermute(cur, 'dp', pairs)  8.93 us
    add x9, other arithmetic, ring_reduce_scatter(): acc = lax.ppermute(mine if acc is None else acc + mine, 'dp', pairs)  5.14 us
    dot_general x1, matrix products, body(): jnp.einsum('bst,bsc->cst', columns, l_blocks, preferred_element_type=jnp....  5.07 us
    all_to_all x1, waiting for transfers between devices, body(): lax.all_to_all(back_cols, 'feat', split_axis=1, concat_axis=0, tiled=True)  5.06 us
  transfers between devices with their start and end apart: 31, of which 19 were waited for; matrix products, arithmetic and copies ran while one was open for 21% of the time, Pallas kernels for 0%

profile of v14, /device:TPU:0, one launch (start us, length us, event | category | flops | bytes accessed | tf_op | source)
XLA Modules:
  0.0 201.7 jit_solution(18405172470930502855)
XLA Ops:
  3.1 3.0 %collective-permute-start = (bf16[640,256]{1,0:T(8,128)(2,1)S(1)}, bf16[640,256]{1,0:T(8,128)(2,1)}, u32[]{:S(2)}, u32[]{:S(2)}) collective-permute-start(bf16[640,256]{1,0:T(8,128)(2,1)S(1)} %pad_maximum_fusion), channel_id=1, source_target_pairs={{0,4},{4,12},{12,20},{20,28},{28,24},{24,16},{16,8},{8,0},{1,5},{5... | collective-permute-start | bytes 983048 | tf_op jit(solution)/shard_map/ppermute | solution.py:88
  6.2 7.7 %collective-permute-done = bf16[640,256]{1,0:T(8,128)(2,1)} collective-permute-done((bf16[640,256]{1,0:T(8,128)(2,1)S(1)}, bf16[640,256]{1,0:T(8,128)(2,1)}, u32[]{:S(2)}, u32[]{:S(2)}) %collective-permute-start) | collective-permute-done | bytes 327712 | tf_op jit(solution)/shard_map/ppermute | solution.py:88
  15.7 4.1 %copy.43 = bf16[16,256,256]{2,0,1:T(8,128)(2,1)} copy(bf16[16,256,256]{2,1,0:T(8,128)(2,1)} %bitcast.158) | data formatting | bytes 4194304 | tf_op jit(solution)/shard_map/reshape | solution.py:99
  19.8 4.6 %all-to-all-start = ((bf16[16,256,256]{2,0,1:T(8,128)(2,1)}), bf16[16,256,256]{2,0,1:T(8,128)(2,1)}, u32[]{:S(2)}, u32[]{:S(2)}) async-start(bf16[16,256,256]{2,0,1:T(8,128)(2,1)} %copy.43), calls=%async_computation | async-start | bytes 4194304 | tf_op jit(solution)/shard_map/all_to_all | solution.py:100
  47.5 6.8 %collective-permute-done.5 = bf16[640,256]{1,0:T(8,128)(2,1)S(1)} collective-permute-done((bf16[640,256]{1,0:T(8,128)(2,1)S(1)}, bf16[640,256]{1,0:T(8,128)(2,1)S(1)}, u32[]{:S(2)}, u32[]{:S(2)}) %collective-permute-start.5) | collective-permute-done | bytes 327712 | tf_op jit(solution)/shard_map/ppermute | solution.py:88
  56.4 7.2 %collective-permute-done.3 = bf16[640,256]{1,0:T(8,128)(2,1)S(1)} collective-permute-done((bf16[640,256]{1,0:T(8,128)(2,1)S(1)}, bf16[640,256]{1,0:T(8,128)(2,1)S(1)}, u32[]{:S(2)}, u32[]{:S(2)}) %collective-permute-start.3) | collective-permute-done | bytes 327712 | tf_op jit(solution)/shard_map/ppermute | solution.py:88
  66.8 2.6 %copy.46 = bf16[16,256,256]{2,0,1:T(8,128)(2,1)} copy(bf16[16,256,256]{2,1,0:T(8,128)(2,1)S(1)} %convolution_convert_fusion.1) | data formatting | bytes 4194304 | tf_op jit(solution)/shard_map/convert_element_type | solution.py:112
  69.4 4.6 %all-to-all-start.1 = ((bf16[16,256,256]{2,0,1:T(8,128)(2,1)}), bf16[16,256,256]{2,0,1:T(8,128)(2,1)}, u32[]{:S(2)}, u32[]{:S(2)}) async-start(bf16[16,256,256]{2,0,1:T(8,128)(2,1)} %copy.46), calls=%async_computation.1 | async-start | bytes 4194304 | tf_op jit(solution)/shard_map/all_to_all | solution.py:113
  77.5 4.2 %copy.44 = f32[16,4,64,256]{3,0,1,2:T(8,128)} copy(bf16[16,4,64,256]{3,0,2,1:T(8,128)(2,1)} %bitcast.76) | data formatting | bytes 6291456 | tf_op jit(solution)/shard_map/convert_element_type | solution.py:19
  81.7 17.9 %all-to-all-done.1 = bf16[16,256,256]{2,0,1:T(8,128)(2,1)} async-done(((bf16[16,256,256]{2,0,1:T(8,128)(2,1)}), bf16[16,256,256]{2,0,1:T(8,128)(2,1)}, u32[]{:S(2)}, u32[]{:S(2)}) %all-to-all-start.1) | async-done | bytes 2097184 | tf_op jit(solution)/shard_map/all_to_all | solution.py:113
  99.6 2.0 %copy.47 = bf16[16,4,64,256]{3,0,1,2:T(8,128)(2,1)S(1)} copy(bf16[16,4,64,256]{3,0,2,1:T(8,128)(2,1)} %bitcast.31) | data formatting | bytes 4194304 | tf_op jit(solution)/shard_map/all_to_all | solution.py:113
  102.4 5.1 %fusion.6 = bf16[64,64,256]{2,0,1:T(8,128)(2,1)S(1)} fusion(f32[16,4,64,256]{3,0,1,2:T(8,128)S(1)} %copy-done.10, bf16[64,64,256]{2,0,1:T(8,128)(2,1)S(1)} %bitcast.156, bf16[64,64,64]{2,1,0:T(8,128)(2,1)S(1)} %reshape.104), kind=kOutput, calls=%fused_computation.8 | convolution fusion | flops 155189248 | bytes 8912896 | tf_op jit(solution)/shard_map/bst,bsc->cst/dot_general | solution.py:114
  108.9 2.5 %copy.50 = bf16[64,64,256]{2,0,1:T(8,128)(2,1)} copy(bf16[64,64,256]{2,1,0:T(8,128)(2,1)S(1)} %convolution_convert_fusion) | data formatting | bytes 4194304 | tf_op jit(solution)/shard_map/convert_element_type | solution.py:118
  111.4 4.5 %all-to-all-start.2 = ((bf16[64,64,256]{2,0,1:T(8,128)(2,1)}), bf16[64,64,256]{2,0,1:T(8,128)(2,1)}, u32[]{:S(2)}, u32[]{:S(2)}) async-start(bf16[64,64,256]{2,0,1:T(8,128)(2,1)} %copy.50), calls=%async_computation.2 | async-start | bytes 4194304 | tf_op jit(solution)/shard_map/all_to_all | solution.py:123
  115.9 4.3 %multiply_bitcast_fusion = f32[64,64,64]{0,2,1:T(8,128)} fusion(bf16[64,64,256]{2,0,1:T(8,128)(2,1)} %copy-done.6, bf16[64,64,256]{2,0,1:T(8,128)(2,1)} %bitcast.157), kind=kOutput, calls=%fused_computation.16 | convolution fusion | flops 134479872 | bytes 5242880 | tf_op jit(solution)/shard_map/bst,cst->bsc/dot_general | solution.py:119
  120.2 3.8 %copy.53 = f32[64,64,64]{2,1,0:T(8,128)} copy(f32[64,64,64]{0,2,1:T(8,128)} %multiply_bitcast_fusion) | data formatting | bytes 2097152 | tf_op jit(solution)/shard_map/mul | solution.py:120
  129.1 4.6 %collective-permute-done.24 = f32[8,64,64]{2,1,0:T(8,128)S(1)} collective-permute-done((f32[8,64,64]{2,1,0:T(8,128)S(1)}, f32[8,64,64]{2,1,0:T(8,128)S(1)}, u32[]{:S(2)}, u32[]{:S(2)}) %collective-permute-start.24) | collective-permute-done | bytes 131104 | tf_op jit(solution)/shard_map/ppermute | solution.py:71
  136.6 5.1 %all-to-all-done.2 = bf16[64,64,256]{2,0,1:T(8,128)(2,1)} async-done(((bf16[64,64,256]{2,0,1:T(8,128)(2,1)}), bf16[64,64,256]{2,0,1:T(8,128)(2,1)}, u32[]{:S(2)}, u32[]{:S(2)}) %all-to-all-start.2) | async-done | bytes 2097184 | tf_op jit(solution)/shard_map/all_to_all | solution.py:123
  152.5 2.3 %collective-permute-done.7 = f32[16,16,256]{2,0,1:T(8,128)S(1)} collective-permute-done((f32[16,16,256]{2,0,1:T(8,128)S(1)}, f32[16,16,256]{2,0,1:T(8,128)S(1)}, u32[]{:S(2)}, u32[]{:S(2)}) %collective-permute-start.7) | collective-permute-done | bytes 262176 | tf_op jit(solution)/shard_map/ppermute | solution.py:71
  158.2 2.2 %collective-permute-done.22 = f32[8,64,64]{2,1,0:T(8,128)S(1)} collective-permute-done((f32[8,64,64]{2,1,0:T(8,128)S(1)}, f32[8,64,64]{2,1,0:T(8,128)S(1)}, u32[]{:S(2)}, u32[]{:S(2)}) %collective-permute-start.22) | collective-permute-done | bytes 131104 | tf_op jit(solution)/shard_map/ppermute | solution.py:71
  163.9 3.9 %collective-permute-done.11 = f32[16,16,256]{2,0,1:T(8,128)S(1)} collective-permute-done((f32[16,16,256]{2,0,1:T(8,128)S(1)}, f32[16,16,256]{2,0,1:T(8,128)S(1)}, u32[]{:S(2)}, u32[]{:S(2)}) %collective-permute-start.11) | collective-permute-done | bytes 262176 | tf_op jit(solution)/shard_map/ppermute | solution.py:71
  168.2 3.5 %collective-permute-done.8 = f32[16,16,256]{2,0,1:T(8,128)S(1)} collective-permute-done((f32[16,16,256]{2,0,1:T(8,128)S(1)}, f32[16,16,256]{2,0,1:T(8,128)S(1)}, u32[]{:S(2)}, u32[]{:S(2)}) %collective-permute-start.8) | collective-permute-done | bytes 262176 | tf_op jit(solution)/shard_map/ppermute | solution.py:71
  180.1 2.8 %collective-permute-done.9 = f32[16,16,256]{2,0,1:T(8,128)S(1)} collective-permute-done((f32[16,16,256]{2,0,1:T(8,128)}, f32[16,16,256]{2,0,1:T(8,128)S(1)}, u32[]{:S(2)}, u32[]{:S(2)}) %collective-permute-start.9) | collective-permute-done | bytes 262176 | tf_op jit(solution)/shard_map/ppermute | solution.py:71
  193.7 4.5 %add_convert_fusion = bf16[16,256,256]{2,1,0:T(8,128)(2,1)} fusion(bf16[16,256,256]{2,1,0:T(8,128)(2,1)} %bitcast.159, bf16[256,16,256]{2,0,1:T(8,128)(2,1)} %bitcast.154, bf16[256,16,256]{2,1,0:T(8,128)(2,1)S(1)} %bitcast.152), kind=kOutput, calls=%fused_computation.14 | convolution fusion | flops 540016640 | bytes 8388608 | tf_op jit(solution)/shard_map/obt,ibo->bit/dot_general | solution.py:124
  (115 shorter events, 66.2 us)
Async XLA Ops:
  3.1 10.9 %collective-permute-start = (bf16[640,256]{1,0:T(8,128)(2,1)S(1)}, bf16[640,256]{1,0:T(8,128)(2,1)}, u32[]{:S(2)}, u32[]{:S(2)}) collective-permute-start(bf16[640,256]{1,0:T(8,128)(2,1)S(1)} %pad_maximum_fusion), channel_id=1, source_target_pairs={{0,4},{4,12},{12,20},{20,28},{28,24},{24,16},{16,8},{8,0},{1,5},{5... | collective-permute-start | bytes 983048 | tf_op jit(solution)/shard_map/ppermute | solution.py:88
  6.1 38.1 %collective-permute-start.4 = (bf16[640,256]{1,0:T(8,128)(2,1)S(1)}, bf16[640,256]{1,0:T(8,128)(2,1)S(1)}, u32[]{:S(2)}, u32[]{:S(2)}) collective-permute-start(bf16[640,256]{1,0:T(8,128)(2,1)S(1)} %pad_maximum_fusion), channel_id=1, source_target_pairs={{0,8},{4,0},{12,4},{20,12},{28,20},{24,28},{16,24},{8,16},{1,9},{5... | collective-permute-start | bytes 983048 | tf_op jit(solution)/shard_map/ppermute | solution.py:88
  14.0 30.6 %collective-permute-start.1 = (bf16[640,256]{1,0:T(8,128)(2,1)}, bf16[640,256]{1,0:T(8,128)(2,1)S(1)}, u32[]{:S(2)}, u32[]{:S(2)}) collective-permute-start(bf16[640,256]{1,0:T(8,128)(2,1)} %collective-permute-done), channel_id=1, source_target_pairs={{0,4},{4,12},{12,20},{20,28},{28,24},{24,16},{16,8},{8,0},{1,5},{5... | collective-permute-start | bytes 983048 | tf_op jit(solution)/shard_map/ppermute | solution.py:88
  19.8 49.6 %all-to-all-start = ((bf16[16,256,256]{2,0,1:T(8,128)(2,1)}), bf16[16,256,256]{2,0,1:T(8,128)(2,1)}, u32[]{:S(2)}, u32[]{:S(2)}) async-start(bf16[16,256,256]{2,0,1:T(8,128)(2,1)} %copy.43), calls=%async_computation | async-start | bytes 4194304 | tf_op jit(solution)/shard_map/all_to_all | solution.py:100
  44.2 10.1 %collective-permute-start.5 = (bf16[640,256]{1,0:T(8,128)(2,1)S(1)}, bf16[640,256]{1,0:T(8,128)(2,1)S(1)}, u32[]{:S(2)}, u32[]{:S(2)}) collective-permute-start(bf16[640,256]{1,0:T(8,128)(2,1)S(1)} %collective-permute-done.4), channel_id=1, source_target_pairs={{0,8},{4,0},{12,4},{20,12},{28,20},{24,28},{16,24},{8,16},{1,9},{5... | collective-permute-start | bytes 983048 | tf_op jit(solution)/shard_map/ppermute | solution.py:88
  44.6 10.1 %collective-permute-start.2 = (bf16[640,256]{1,0:T(8,128)(2,1)S(1)}, bf16[640,256]{1,0:T(8,128)(2,1)S(1)}, u32[]{:S(2)}, u32[]{:S(2)}) collective-permute-start(bf16[640,256]{1,0:T(8,128)(2,1)S(1)} %collective-permute-done.1), channel_id=1, source_target_pairs={{0,4},{4,12},{12,20},{20,28},{28,24},{24,16},{16,8},{8,0},{1,5},{5... | collective-permute-start | bytes 983048 | tf_op jit(solution)/shard_map/ppermute | solution.py:88
  69.4 30.2 %all-to-all-start.1 = ((bf16[16,256,256]{2,0,1:T(8,128)(2,1)}), bf16[16,256,256]{2,0,1:T(8,128)(2,1)}, u32[]{:S(2)}, u32[]{:S(2)}) async-start(bf16[16,256,256]{2,0,1:T(8,128)(2,1)} %copy.46), calls=%async_computation.1 | async-start | bytes 4194304 | tf_op jit(solution)/shard_map/all_to_all | solution.py:113
  111.4 30.2 %all-to-all-start.2 = ((bf16[64,64,256]{2,0,1:T(8,128)(2,1)}), bf16[64,64,256]{2,0,1:T(8,128)(2,1)}, u32[]{:S(2)}, u32[]{:S(2)}) async-start(bf16[64,64,256]{2,0,1:T(8,128)(2,1)} %copy.50), calls=%async_computation.2 | async-start | bytes 4194304 | tf_op jit(solution)/shard_map/all_to_all | solution.py:123
  128.8 18.9 %collective-permute-start.21 = (f32[8,64,64]{2,1,0:T(8,128)S(1)}, f32[8,64,64]{2,1,0:T(8,128)S(1)}, u32[]{:S(2)}, u32[]{:S(2)}) collective-permute-start(f32[8,64,64]{2,1,0:T(8,128)S(1)} %get-tuple-element.9), channel_id=1, source_target_pairs={{0,4},{4,12},{12,20},{20,28},{28,24},{24,16},{16,8},{8,0},{1,5},{5... | collective-permute-start | bytes 393224 | tf_op jit(solution)/shard_map/ppermute | solution.py:71
  134.8 12.9 %collective-permute-start.25 = (f32[8,64,64]{2,1,0:T(8,128)S(1)}, f32[8,64,64]{2,1,0:T(8,128)S(1)}, u32[]{:S(2)}, u32[]{:S(2)}) collective-permute-start(f32[8,64,64]{2,1,0:T(8,128)S(1)} %bitcast_add_fusion.2), channel_id=1, source_target_pairs={{0,8},{4,0},{12,4},{20,12},{28,20},{24,28},{16,24},{8,16},{1,9},{5... | collective-permute-start | bytes 393224 | tf_op jit(solution)/shard_map/ppermute | solution.py:71
  148.7 11.8 %collective-permute-start.22 = (f32[8,64,64]{2,1,0:T(8,128)S(1)}, f32[8,64,64]{2,1,0:T(8,128)S(1)}, u32[]{:S(2)}, u32[]{:S(2)}) collective-permute-start(f32[8,64,64]{2,1,0:T(8,128)S(1)} %get-tuple-element.7), channel_id=1, source_target_pairs={{0,4},{4,12},{12,20},{20,28},{28,24},{24,16},{16,8},{8,0},{1,5},{5... | collective-permute-start | bytes 393224 | tf_op jit(solution)/shard_map/ppermute | solution.py:71
  150.4 11.8 %collective-permute-start.26 = (f32[8,64,64]{2,1,0:T(8,128)S(1)}, f32[8,64,64]{2,1,0:T(8,128)S(1)}, u32[]{:S(2)}, u32[]{:S(2)}) collective-permute-start(f32[8,64,64]{2,1,0:T(8,128)S(1)} %get-tuple-element.8), channel_id=1, source_target_pairs={{0,8},{4,0},{12,4},{20,12},{28,20},{24,28},{16,24},{8,16},{1,9},{5... | collective-permute-start | bytes 393224 | tf_op jit(solution)/shard_map/ppermute | solution.py:71
  150.7 17.1 %collective-permute-start.11 = (f32[16,16,256]{2,0,1:T(8,128)S(1)}, f32[16,16,256]{2,0,1:T(8,128)S(1)}, u32[]{:S(2)}, u32[]{:S(2)}) collective-permute-start(f32[16,16,256]{2,0,1:T(8,128)S(1)} %get-tuple-element.16), channel_id=1, source_target_pairs={{0,8},{4,0},{12,4},{20,12},{28,20},{24,28},{16,24},{8,16},{1,9},{5... | collective-permute-start | bytes 786440 | tf_op jit(solution)/shard_map/ppermute | solution.py:71
  154.8 19.3 %collective-permute-start.14 = (f32[16,16,256]{2,0,1:T(8,128)S(1)}, f32[16,16,256]{2,0,1:T(8,128)S(1)}, u32[]{:S(2)}, u32[]{:S(2)}) collective-permute-start(f32[16,16,256]{2,0,1:T(8,128)S(1)} %get-tuple-element.21), channel_id=1, source_target_pairs={{0,4},{4,12},{12,20},{20,28},{28,24},{24,16},{16,8},{8,0},{1,5},{5... | collective-permute-start | bytes 786440 | tf_op jit(solution)/shard_map/ppermute | solution.py:71
  156.6 15.0 %collective-permute-start.8 = (f32[16,16,256]{2,0,1:T(8,128)S(1)}, f32[16,16,256]{2,0,1:T(8,128)S(1)}, u32[]{:S(2)}, u32[]{:S(2)}) collective-permute-start(f32[16,16,256]{2,0,1:T(8,128)S(1)} %bitcast_add_fusion.16), channel_id=1, source_target_pairs={{0,4},{4,12},{12,20},{20,28},{28,24},{24,16},{16,8},{8,0},{1,5},{5... | collective-permute-start | bytes 786440 | tf_op jit(solution)/shard_map/ppermute | solution.py:71
  160.4 14.1 %collective-permute-start.18 = (f32[16,16,256]{2,0,1:T(8,128)S(1)}, f32[16,16,256]{2,0,1:T(8,128)S(1)}, u32[]{:S(2)}, u32[]{:S(2)}) collective-permute-start(f32[16,16,256]{2,0,1:T(8,128)S(1)} %bitcast_add_fusion.8), channel_id=1, source_target_pairs={{0,8},{4,0},{12,4},{20,12},{28,20},{24,28},{16,24},{8,16},{1,9},{5... | collective-permute-start | bytes 786440 | tf_op jit(solution)/shard_map/ppermute | solution.py:71
  162.3 15.0 %collective-permute-start.23 = (f32[8,64,64]{2,1,0:T(8,128)S(1)}, f32[8,64,64]{2,1,0:T(8,128)S(1)}, u32[]{:S(2)}, u32[]{:S(2)}) collective-permute-start(f32[8,64,64]{2,1,0:T(8,128)S(1)} %get-tuple-element.5), channel_id=1, source_target_pairs={{0,4},{4,12},{12,20},{20,28},{28,24},{24,16},{16,8},{8,0},{1,5},{5... | collective-permute-start | bytes 393224 | tf_op jit(solution)/shard_map/ppermute | solution.py:71
  167.8 11.2 %collective-permute-start.27 = (f32[8,64,64]{2,1,0:T(8,128)S(1)}, f32[8,64,64]{2,1,0:T(8,128)S(1)}, u32[]{:S(2)}, u32[]{:S(2)}) collective-permute-start(f32[8,64,64]{2,1,0:T(8,128)S(1)} %get-tuple-element.6), channel_id=1, source_target_pairs={{0,8},{4,0},{12,4},{20,12},{28,20},{24,28},{16,24},{8,16},{1,9},{5... | collective-permute-start | bytes 393224 | tf_op jit(solution)/shard_map/ppermute | solution.py:71
  172.4 10.5 %collective-permute-start.9 = (f32[16,16,256]{2,0,1:T(8,128)}, f32[16,16,256]{2,0,1:T(8,128)S(1)}, u32[]{:S(2)}, u32[]{:S(2)}) collective-permute-start(f32[16,16,256]{2,0,1:T(8,128)} %get-tuple-element.13), channel_id=1, source_target_pairs={{0,4},{4,12},{12,20},{20,28},{28,24},{24,16},{16,8},{8,0},{1,5},{5... | collective-permute-start | bytes 786440 | tf_op jit(solution)/shard_map/ppermute | solution.py:71
  174.1 10.7 %collective-permute-start.12 = (f32[16,16,256]{2,0,1:T(8,128)S(1)}, f32[16,16,256]{2,0,1:T(8,128)}, u32[]{:S(2)}, u32[]{:S(2)}) collective-permute-start(f32[16,16,256]{2,0,1:T(8,128)S(1)} %get-tuple-element.14), channel_id=1, source_target_pairs={{0,8},{4,0},{12,4},{20,12},{28,20},{24,28},{16,24},{8,16},{1,9},{5... | collective-permute-start | bytes 786440 | tf_op jit(solution)/shard_map/ppermute | solution.py:71
  175.3 13.3 %collective-permute-start.15 = (f32[16,16,256]{2,0,1:T(8,128)}, f32[16,16,256]{2,0,1:T(8,128)S(1)}, u32[]{:S(2)}, u32[]{:S(2)}) collective-permute-start(f32[16,16,256]{2,0,1:T(8,128)} %get-tuple-element.19), channel_id=1, source_target_pairs={{0,4},{4,12},{12,20},{20,28},{28,24},{24,16},{16,8},{8,0},{1,5},{5... | collective-permute-start | bytes 786440 | tf_op jit(solution)/shard_map/ppermute | solution.py:71
  177.3 13.1 %collective-permute-start.19 = (f32[16,16,256]{2,0,1:T(8,128)S(1)}, f32[16,16,256]{2,0,1:T(8,128)}, u32[]{:S(2)}, u32[]{:S(2)}) collective-permute-start(f32[16,16,256]{2,0,1:T(8,128)S(1)} %get-tuple-element.20), channel_id=1, source_target_pairs={{0,8},{4,0},{12,4},{20,12},{28,20},{24,28},{16,24},{8,16},{1,9},{5... | collective-permute-start | bytes 786440 | tf_op jit(solution)/shard_map/ppermute | solution.py:71
  186.0 12.2 %collective-permute-start.10 = (f32[16,16,256]{2,0,1:T(8,128)S(1)}, f32[16,16,256]{2,0,1:T(8,128)S(1)}, u32[]{:S(2)}, u32[]{:S(2)}) collective-permute-start(f32[16,16,256]{2,0,1:T(8,128)S(1)} %get-tuple-element.11), channel_id=1, source_target_pairs={{0,4},{4,12},{12,20},{20,28},{28,24},{24,16},{16,8},{8,0},{1,5},{5... | collective-permute-start | bytes 786440 | tf_op jit(solution)/shard_map/ppermute | solution.py:71
  187.6 10.6 %collective-permute-start.13 = (f32[16,16,256]{2,0,1:T(8,128)S(1)}, f32[16,16,256]{2,0,1:T(8,128)S(1)}, u32[]{:S(2)}, u32[]{:S(2)}) collective-permute-start(f32[16,16,256]{2,0,1:T(8,128)S(1)} %get-tuple-element.12), channel_id=1, source_target_pairs={{0,8},{4,0},{12,4},{20,12},{28,20},{24,28},{16,24},{8,16},{1,9},{5... | collective-permute-start | bytes 786440 | tf_op jit(solution)/shard_map/ppermute | solution.py:71
  (20 other events, 226.1 us)

commit v15 on v14

--- a/solution.py
+++ b/solution.py
@@ -72,7 +72,7 @@
         total = total + acc
     return total
 
-def ring_all_gather(piece, ring):
+def ring_all_gather(piece, ring, lead=1):
     n = len(ring)
     order = jnp.asarray(np.array(ring, np.int32))
     place = jnp.asarray(np.argsort(np.array(ring)).astype(np.int32))
@@ -81,7 +81,7 @@
     forward = [(ring[p], ring[(p + 1) % n]) for p in range(n)]
     backward = [(ring[p], ring[(p - 1) % n]) for p in range(n)]
     held = lax.dynamic_update_index_in_dim(jnp.zeros((n,) + piece.shape, piece.dtype), piece, me, 0)
-    ahead = n // 2
+    ahead = n // 2 if lead > 0 else n - 1 - n // 2
     for way, pairs, hops in ((1, forward, ahead), (-1, backward, n - 1 - ahead)):
         cur = piece
         for step in range(hops):
@@ -104,7 +104,10 @@
     l_lead = jnp.transpose(l_mix.reshape(local_cols, -1, BLOCKS), (1, 0, 2)).reshape(-1, WIDTH)
     r_size = r_lead.shape[0]
     packed = jnp.concatenate([r_lead, l_lead], axis=0)
-    packed = ring_all_gather(packed, ring)
+    split = packed.shape[0] // 2
+    packed = jnp.concatenate(
+        [ring_all_gather(packed[:split], ring), ring_all_gather(packed[split:], ring, lead=-1)], axis=1
+    )
     r_whole = packed[:, :r_size].reshape(n_dp * rows_r, local_blocks, WIDTH)
     l_blocks = packed[:, r_size:].reshape(-1, local_cols, BLOCKS)
     mixed_rows = jnp.einsum(

time: 203 us -> 203 us (level)
  waiting for transfers between devices: 69.6 us -> 59.8 us
  starting transfers between devices: 49 us -> 56 us
    ppermute x7 -> x14, waiting for transfers between devices: 21.8 us -> 9.43 us  [ring_all_gather(): cur = lax.ppermute(cur, 'dp', pairs)]
    ppermute x7 -> x14, starting transfers between devices: 8.93 us -> 15.3 us  [ring_all_gather(): cur = lax.ppermute(cur, 'dp', pairs)]
    dynamic_update_slice x7 -> x14, local copies, waits for them, and re-layouts: 1.17 us -> 3.9 us  [ring_all_gather(): held = lax.dynamic_update_index_in_dim(held, cur, owner, 0)]
  transfers between devices with their start and end apart: 31 -> 38, of which waited for: 19 -> 21; matrix products, arithmetic and copies ran while one was open for 21% -> 24% of each run, Pallas kernels for 0% -> 0%
where the time goes in v15:
time: 203 us; the launch traced here: 202 us
  waiting for transfers between devices  59.8 us (29%)
  starting transfers between devices  56 us (28%)
  local copies, waits for them, and re-layouts  37.8 us (19%)
  between operations  21.2 us (10%)
  matrix products  17.5 us (9%)
  other arithmetic  9.76 us (5%)
    ppermute x21, starting transfers between devices, ring_reduce_scatter(): acc = lax.ppermute(mine if acc is None else acc + mine, 'dp', pairs)  27 us
    ppermute x21, waiting for transfers between devices, ring_reduce_scatter(): acc = lax.ppermute(mine if acc is None else acc + mine, 'dp', pairs)  26.5 us
    all_to_all x1, waiting for transfers between devices, body(): lax.all_to_all(mixed_rows, 'feat', split_axis=1, concat_axis=0, tiled=True)  18.9 us
    ppermute x14, starting transfers between devices, ring_all_gather(): cur = lax.ppermute(cur, 'dp', pairs)  15.3 us
    ppermute x14, waiting for transfers between devices, ring_all_gather(): cur = lax.ppermute(cur, 'dp', pairs)  9.43 us
    add x9, other arithmetic, ring_reduce_scatter(): acc = lax.ppermute(mine if acc is None else acc + mine, 'dp', pairs)  5.14 us
    dot_general x1, matrix products, body(): jnp.einsum('bst,bsc->cst', columns, l_blocks, preferred_element_type=jnp....  5.07 us
    all_to_all x1, waiting for transfers between devices, body(): lax.all_to_all(back_cols, 'feat', split_axis=1, concat_axis=0, tiled=True)  4.96 us
  transfers between devices with their start and end apart: 38, of which 21 were waited for; matrix products, arithmetic and copies ran while one was open for 24% of the time, Pallas kernels for 0%

profile of v15, /device:TPU:0, one launch (start us, length us, event | category | flops | bytes accessed | tf_op | source)
XLA Modules:
  0.0 202.0 jit_solution(4270638859396135132)
XLA Ops:
  2.6 3.0 %collective-permute-start.4 = (bf16[320,256]{1,0:T(8,128)(2,1)}, bf16[320,256]{1,0:T(8,128)(2,1)}, u32[]{:S(2)}, u32[]{:S(2)}) collective-permute-start(bf16[320,256]{1,0:T(8,128)(2,1)} %bitcast.3), channel_id=1, source_target_pairs={{0,8},{4,0},{12,4},{20,12},{28,20},{24,28},{16,24},{8,16},{1,9},{5... | collective-permute-start | bytes 491528 | tf_op jit(solution)/shard_map/ppermute | solution.py:88
  10.5 4.1 %copy.45 = bf16[16,256,256]{2,0,1:T(8,128)(2,1)} copy(bf16[16,256,256]{2,1,0:T(8,128)(2,1)} %bitcast.178) | data formatting | bytes 4194304 | tf_op jit(solution)/shard_map/reshape | solution.py:99
  14.6 4.6 %all-to-all-start = ((bf16[16,256,256]{2,0,1:T(8,128)(2,1)}), bf16[16,256,256]{2,0,1:T(8,128)(2,1)}, u32[]{:S(2)}, u32[]{:S(2)}) async-start(bf16[16,256,256]{2,0,1:T(8,128)(2,1)} %copy.45), calls=%async_computation | async-start | bytes 4194304 | tf_op jit(solution)/shard_map/all_to_all | solution.py:100
  41.6 2.1 %collective-permute-start.5 = (bf16[320,256]{1,0:T(8,128)(2,1)}, bf16[320,256]{1,0:T(8,128)(2,1)S(1)}, u32[]{:S(2)}, u32[]{:S(2)}) collective-permute-start(bf16[320,256]{1,0:T(8,128)(2,1)} %collective-permute-done.4), channel_id=1, source_target_pairs={{0,8},{4,0},{12,4},{20,12},{28,20},{24,28},{16,24},{8,16},{1,9},{5... | collective-permute-start | bytes 491528 | tf_op jit(solution)/shard_map/ppermute | solution.py:88
  51.0 3.5 %collective-permute-done.8 = bf16[320,256]{1,0:T(8,128)(2,1)S(1)} collective-permute-done((bf16[320,256]{1,0:T(8,128)(2,1)}, bf16[320,256]{1,0:T(8,128)(2,1)S(1)}, u32[]{:S(2)}, u32[]{:S(2)}) %collective-permute-start.8) | collective-permute-done | bytes 163872 | tf_op jit(solution)/shard_map/ppermute | solution.py:88
  67.0 2.6 %copy.48 = bf16[16,256,256]{2,0,1:T(8,128)(2,1)} copy(bf16[16,256,256]{2,1,0:T(8,128)(2,1)S(1)} %convolution_convert_fusion.1) | data formatting | bytes 4194304 | tf_op jit(solution)/shard_map/convert_element_type | solution.py:115
  69.6 4.6 %all-to-all-start.1 = ((bf16[16,256,256]{2,0,1:T(8,128)(2,1)}), bf16[16,256,256]{2,0,1:T(8,128)(2,1)}, u32[]{:S(2)}, u32[]{:S(2)}) async-start(bf16[16,256,256]{2,0,1:T(8,128)(2,1)} %copy.48), calls=%async_computation.1 | async-start | bytes 4194304 | tf_op jit(solution)/shard_map/all_to_all | solution.py:116
  76.7 4.2 %copy.46 = f32[16,4,64,256]{3,0,1,2:T(8,128)} copy(bf16[16,4,64,256]{3,0,2,1:T(8,128)(2,1)} %bitcast.85) | data formatting | bytes 6291456 | tf_op jit(solution)/shard_map/convert_element_type | solution.py:19
  80.9 18.9 %all-to-all-done.1 = bf16[16,256,256]{2,0,1:T(8,128)(2,1)} async-done(((bf16[16,256,256]{2,0,1:T(8,128)(2,1)}), bf16[16,256,256]{2,0,1:T(8,128)(2,1)}, u32[]{:S(2)}, u32[]{:S(2)}) %all-to-all-start.1) | async-done | bytes 2097184 | tf_op jit(solution)/shard_map/all_to_all | solution.py:116
  102.6 5.1 %fusion.6 = bf16[64,64,256]{2,0,1:T(8,128)(2,1)S(1)} fusion(f32[16,4,64,256]{3,0,1,2:T(8,128)S(1)} %copy-done.9, bf16[64,64,256]{2,0,1:T(8,128)(2,1)S(1)} %bitcast.176, bf16[64,64,64]{2,1,0:T(8,128)(2,1)S(1)} %reshape.120), kind=kOutput, calls=%fused_computation.8 | convolution fusion | flops 155189248 | bytes 8912896 | tf_op jit(solution)/shard_map/bst,bsc->cst/dot_general | solution.py:117
  109.1 2.5 %copy.52 = bf16[64,64,256]{2,0,1:T(8,128)(2,1)} copy(bf16[64,64,256]{2,1,0:T(8,128)(2,1)S(1)} %convolution_convert_fusion) | data formatting | bytes 4194304 | tf_op jit(solution)/shard_map/convert_element_type | solution.py:121
  111.6 4.5 %all-to-all-start.2 = ((bf16[64,64,256]{2,0,1:T(8,128)(2,1)}), bf16[64,64,256]{2,0,1:T(8,128)(2,1)}, u32[]{:S(2)}, u32[]{:S(2)}) async-start(bf16[64,64,256]{2,0,1:T(8,128)(2,1)} %copy.52), calls=%async_computation.2 | async-start | bytes 4194304 | tf_op jit(solution)/shard_map/all_to_all | solution.py:126
  116.0 4.3 %multiply_bitcast_fusion = f32[64,64,64]{0,2,1:T(8,128)} fusion(bf16[64,64,256]{2,0,1:T(8,128)(2,1)} %copy-done.5, bf16[64,64,256]{2,0,1:T(8,128)(2,1)} %bitcast.177), kind=kOutput, calls=%fused_computation.17 | convolution fusion | flops 134479872 | bytes 5242880 | tf_op jit(solution)/shard_map/bst,cst->bsc/dot_general | solution.py:122
  120.4 3.8 %copy.55 = f32[64,64,64]{2,1,0:T(8,128)} copy(f32[64,64,64]{0,2,1:T(8,128)} %multiply_bitcast_fusion) | data formatting | bytes 2097152 | tf_op jit(solution)/shard_map/mul | solution.py:123
  127.3 6.7 %collective-permute-done.31 = f32[8,64,64]{2,1,0:T(8,128)S(1)} collective-permute-done((f32[8,64,64]{2,1,0:T(8,128)S(1)}, f32[8,64,64]{2,1,0:T(8,128)S(1)}, u32[]{:S(2)}, u32[]{:S(2)}) %collective-permute-start.31) | collective-permute-done | bytes 131104 | tf_op jit(solution)/shard_map/ppermute | solution.py:71
  136.8 5.0 %all-to-all-done.2 = bf16[64,64,256]{2,0,1:T(8,128)(2,1)} async-done(((bf16[64,64,256]{2,0,1:T(8,128)(2,1)}), bf16[64,64,256]{2,0,1:T(8,128)(2,1)}, u32[]{:S(2)}, u32[]{:S(2)}) %all-to-all-start.2) | async-done | bytes 2097184 | tf_op jit(solution)/shard_map/all_to_all | solution.py:126
  152.8 2.2 %collective-permute-done.14 = f32[16,16,256]{2,0,1:T(8,128)S(1)} collective-permute-done((f32[16,16,256]{2,0,1:T(8,128)S(1)}, f32[16,16,256]{2,0,1:T(8,128)S(1)}, u32[]{:S(2)}, u32[]{:S(2)}) %collective-permute-start.14) | collective-permute-done | bytes 262176 | tf_op jit(solution)/shard_map/ppermute | solution.py:71
  158.5 2.1 %collective-permute-done.29 = f32[8,64,64]{2,1,0:T(8,128)S(1)} collective-permute-done((f32[8,64,64]{2,1,0:T(8,128)S(1)}, f32[8,64,64]{2,1,0:T(8,128)S(1)}, u32[]{:S(2)}, u32[]{:S(2)}) %collective-permute-start.29) | collective-permute-done | bytes 131104 | tf_op jit(solution)/shard_map/ppermute | solution.py:71
  164.2 3.9 %collective-permute-done.18 = f32[16,16,256]{2,0,1:T(8,128)S(1)} collective-permute-done((f32[16,16,256]{2,0,1:T(8,128)S(1)}, f32[16,16,256]{2,0,1:T(8,128)S(1)}, u32[]{:S(2)}, u32[]{:S(2)}) %collective-permute-start.18) | collective-permute-done | bytes 262176 | tf_op jit(solution)/shard_map/ppermute | solution.py:71
  168.4 3.5 %collective-permute-done.15 = f32[16,16,256]{2,0,1:T(8,128)S(1)} collective-permute-done((f32[16,16,256]{2,0,1:T(8,128)S(1)}, f32[16,16,256]{2,0,1:T(8,128)S(1)}, u32[]{:S(2)}, u32[]{:S(2)}) %collective-permute-start.15) | collective-permute-done | bytes 262176 | tf_op jit(solution)/shard_map/ppermute | solution.py:71
  180.4 2.7 %collective-permute-done.16 = f32[16,16,256]{2,0,1:T(8,128)S(1)} collective-permute-done((f32[16,16,256]{2,0,1:T(8,128)}, f32[16,16,256]{2,0,1:T(8,128)S(1)}, u32[]{:S(2)}, u32[]{:S(2)}) %collective-permute-start.16) | collective-permute-done | bytes 262176 | tf_op jit(solution)/shard_map/ppermute | solution.py:71
  183.1 2.1 %collective-permute-done.19 = f32[16,16,256]{2,0,1:T(8,128)} collective-permute-done((f32[16,16,256]{2,0,1:T(8,128)S(1)}, f32[16,16,256]{2,0,1:T(8,128)}, u32[]{:S(2)}, u32[]{:S(2)}) %collective-permute-start.19) | collective-permute-done | bytes 262176 | tf_op jit(solution)/shard_map/ppermute | solution.py:71
  188.7 2.1 %collective-permute-done.26 = f32[16,16,256]{2,0,1:T(8,128)} collective-permute-done((f32[16,16,256]{2,0,1:T(8,128)S(1)}, f32[16,16,256]{2,0,1:T(8,128)}, u32[]{:S(2)}, u32[]{:S(2)}) %collective-permute-start.26) | collective-permute-done | bytes 262176 | tf_op jit(solution)/shard_map/ppermute | solution.py:71
  194.0 4.5 %add_convert_fusion = bf16[16,256,256]{2,1,0:T(8,128)(2,1)} fusion(bf16[16,256,256]{2,1,0:T(8,128)(2,1)} %bitcast.179, bf16[256,16,256]{2,0,1:T(8,128)(2,1)} %bitcast.174, bf16[256,16,256]{2,1,0:T(8,128)(2,1)S(1)} %bitcast.172), kind=kOutput, calls=%fused_computation.14 | convolution fusion | flops 540016640 | bytes 8388608 | tf_op jit(solution)/shard_map/obt,ibo->bit/dot_general | solution.py:127
  (138 shorter events, 78.5 us)
Async XLA Ops:
  2.6 39.0 %collective-permute-start.4 = (bf16[320,256]{1,0:T(8,128)(2,1)}, bf16[320,256]{1,0:T(8,128)(2,1)}, u32[]{:S(2)}, u32[]{:S(2)}) collective-permute-start(bf16[320,256]{1,0:T(8,128)(2,1)} %bitcast.3), channel_id=1, source_target_pairs={{0,8},{4,0},{12,4},{20,12},{28,20},{24,28},{16,24},{8,16},{1,9},{5... | collective-permute-start | bytes 491528 | tf_op jit(solution)/shard_map/ppermute | solution.py:88
  5.6 38.1 %collective-permute-start = (bf16[320,256]{1,0:T(8,128)(2,1)}, bf16[320,256]{1,0:T(8,128)(2,1)}, u32[]{:S(2)}, u32[]{:S(2)}) collective-permute-start(bf16[320,256]{1,0:T(8,128)(2,1)} %bitcast.3), channel_id=1, source_target_pairs={{0,4},{4,12},{12,20},{20,28},{28,24},{24,16},{16,8},{8,0},{1,5},{5... | collective-permute-start | bytes 491528 | tf_op jit(solution)/shard_map/ppermute | solution.py:88
  8.5 35.3 %collective-permute-start.7 = (bf16[320,256]{1,0:T(8,128)(2,1)}, bf16[320,256]{1,0:T(8,128)(2,1)}, u32[]{:S(2)}, u32[]{:S(2)}) collective-permute-start(bf16[320,256]{1,0:T(8,128)(2,1)} %get-tuple-element.4), channel_id=1, source_target_pairs={{0,4},{4,12},{12,20},{20,28},{28,24},{24,16},{16,8},{8,0},{1,5},{5... | collective-permute-start | bytes 491528 | tf_op jit(solution)/shard_map/ppermute | solution.py:88
  10.5 35.2 %collective-permute-start.10 = (bf16[320,256]{1,0:T(8,128)(2,1)}, bf16[320,256]{1,0:T(8,128)(2,1)}, u32[]{:S(2)}, u32[]{:S(2)}) collective-permute-start(bf16[320,256]{1,0:T(8,128)(2,1)} %get-tuple-element.4), channel_id=1, source_target_pairs={{0,8},{4,0},{12,4},{20,12},{28,20},{24,28},{16,24},{8,16},{1,9},{5... | collective-permute-start | bytes 491528 | tf_op jit(solution)/shard_map/ppermute | solution.py:88
  14.6 55.0 %all-to-all-start = ((bf16[16,256,256]{2,0,1:T(8,128)(2,1)}), bf16[16,256,256]{2,0,1:T(8,128)(2,1)}, u32[]{:S(2)}, u32[]{:S(2)}) async-start(bf16[16,256,256]{2,0,1:T(8,128)(2,1)} %copy.45), calls=%async_computation | async-start | bytes 4194304 | tf_op jit(solution)/shard_map/all_to_all | solution.py:100
  43.7 10.7 %collective-permute-start.8 = (bf16[320,256]{1,0:T(8,128)(2,1)}, bf16[320,256]{1,0:T(8,128)(2,1)S(1)}, u32[]{:S(2)}, u32[]{:S(2)}) collective-permute-start(bf16[320,256]{1,0:T(8,128)(2,1)} %collective-permute-done.7), channel_id=1, source_target_pairs={{0,4},{4,12},{12,20},{20,28},{28,24},{24,16},{16,8},{8,0},{1,5},{5... | collective-permute-start | bytes 491528 | tf_op jit(solution)/shard_map/ppermute | solution.py:88
  49.0 16.3 %collective-permute-start.6 = (bf16[320,256]{1,0:T(8,128)(2,1)S(1)}, bf16[320,256]{1,0:T(8,128)(2,1)S(1)}, u32[]{:S(2)}, u32[]{:S(2)}) collective-permute-start(bf16[320,256]{1,0:T(8,128)(2,1)S(1)} %collective-permute-done.5), channel_id=1, source_target_pairs={{0,8},{4,0},{12,4},{20,12},{28,20},{24,28},{16,24},{8,16},{1,9},{5... | collective-permute-start | bytes 491528 | tf_op jit(solution)/shard_map/ppermute | solution.py:88
  69.6 30.2 %all-to-all-start.1 = ((bf16[16,256,256]{2,0,1:T(8,128)(2,1)}), bf16[16,256,256]{2,0,1:T(8,128)(2,1)}, u32[]{:S(2)}, u32[]{:S(2)}) async-start(bf16[16,256,256]{2,0,1:T(8,128)(2,1)} %copy.48), calls=%async_computation.1 | async-start | bytes 4194304 | tf_op jit(solution)/shard_map/all_to_all | solution.py:116
  111.6 30.2 %all-to-all-start.2 = ((bf16[64,64,256]{2,0,1:T(8,128)(2,1)}), bf16[64,64,256]{2,0,1:T(8,128)(2,1)}, u32[]{:S(2)}, u32[]{:S(2)}) async-start(bf16[64,64,256]{2,0,1:T(8,128)(2,1)} %copy.52), calls=%async_computation.2 | async-start | bytes 4194304 | tf_op jit(solution)/shard_map/all_to_all | solution.py:126
  127.1 20.7 %collective-permute-start.28 = (f32[8,64,64]{2,1,0:T(8,128)S(1)}, f32[8,64,64]{2,1,0:T(8,128)S(1)}, u32[]{:S(2)}, u32[]{:S(2)}) collective-permute-start(f32[8,64,64]{2,1,0:T(8,128)S(1)} %get-tuple-element.11), channel_id=1, source_target_pairs={{0,4},{4,12},{12,20},{20,28},{28,24},{24,16},{16,8},{8,0},{1,5},{5... | collective-permute-start | bytes 393224 | tf_op jit(solution)/shard_map/ppermute | solution.py:71
  135.0 12.9 %collective-permute-start.32 = (f32[8,64,64]{2,1,0:T(8,128)S(1)}, f32[8,64,64]{2,1,0:T(8,128)S(1)}, u32[]{:S(2)}, u32[]{:S(2)}) collective-permute-start(f32[8,64,64]{2,1,0:T(8,128)S(1)} %bitcast_add_fusion.2), channel_id=1, source_target_pairs={{0,8},{4,0},{12,4},{20,12},{28,20},{24,28},{16,24},{8,16},{1,9},{5... | collective-permute-start | bytes 393224 | tf_op jit(solution)/shard_map/ppermute | solution.py:71
  148.8 11.7 %collective-permute-start.29 = (f32[8,64,64]{2,1,0:T(8,128)S(1)}, f32[8,64,64]{2,1,0:T(8,128)S(1)}, u32[]{:S(2)}, u32[]{:S(2)}) collective-permute-start(f32[8,64,64]{2,1,0:T(8,128)S(1)} %get-tuple-element.9), channel_id=1, source_target_pairs={{0,4},{4,12},{12,20},{20,28},{28,24},{24,16},{16,8},{8,0},{1,5},{5... | collective-permute-start | bytes 393224 | tf_op jit(solution)/shard_map/ppermute | solution.py:71
  150.7 11.8 %collective-permute-start.33 = (f32[8,64,64]{2,1,0:T(8,128)S(1)}, f32[8,64,64]{2,1,0:T(8,128)S(1)}, u32[]{:S(2)}, u32[]{:S(2)}) collective-permute-start(f32[8,64,64]{2,1,0:T(8,128)S(1)} %get-tuple-element.10), channel_id=1, source_target_pairs={{0,8},{4,0},{12,4},{20,12},{28,20},{24,28},{16,24},{8,16},{1,9},{5... | collective-permute-start | bytes 393224 | tf_op jit(solution)/shard_map/ppermute | solution.py:71
  150.9 17.2 %collective-permute-start.18 = (f32[16,16,256]{2,0,1:T(8,128)S(1)}, f32[16,16,256]{2,0,1:T(8,128)S(1)}, u32[]{:S(2)}, u32[]{:S(2)}) collective-permute-start(f32[16,16,256]{2,0,1:T(8,128)S(1)} %get-tuple-element.18), channel_id=1, source_target_pairs={{0,8},{4,0},{12,4},{20,12},{28,20},{24,28},{16,24},{8,16},{1,9},{5... | collective-permute-start | bytes 786440 | tf_op jit(solution)/shard_map/ppermute | solution.py:71
  155.0 19.5 %collective-permute-start.21 = (f32[16,16,256]{2,0,1:T(8,128)S(1)}, f32[16,16,256]{2,0,1:T(8,128)S(1)}, u32[]{:S(2)}, u32[]{:S(2)}) collective-permute-start(f32[16,16,256]{2,0,1:T(8,128)S(1)} %get-tuple-element.23), channel_id=1, source_target_pairs={{0,4},{4,12},{12,20},{20,28},{28,24},{24,16},{16,8},{8,0},{1,5},{5... | collective-permute-start | bytes 786440 | tf_op jit(solution)/shard_map/ppermute | solution.py:71
  156.9 14.9 %collective-permute-start.15 = (f32[16,16,256]{2,0,1:T(8,128)S(1)}, f32[16,16,256]{2,0,1:T(8,128)S(1)}, u32[]{:S(2)}, u32[]{:S(2)}) collective-permute-start(f32[16,16,256]{2,0,1:T(8,128)S(1)} %bitcast_add_fusion.16), channel_id=1, source_target_pairs={{0,4},{4,12},{12,20},{20,28},{28,24},{24,16},{16,8},{8,0},{1,5},{5... | collective-permute-start | bytes 786440 | tf_op jit(solution)/shard_map/ppermute | solution.py:71
  160.6 14.1 %collective-permute-start.25 = (f32[16,16,256]{2,0,1:T(8,128)S(1)}, f32[16,16,256]{2,0,1:T(8,128)S(1)}, u32[]{:S(2)}, u32[]{:S(2)}) collective-permute-start(f32[16,16,256]{2,0,1:T(8,128)S(1)} %bitcast_add_fusion.8), channel_id=1, source_target_pairs={{0,8},{4,0},{12,4},{20,12},{28,20},{24,28},{16,24},{8,16},{1,9},{5... | collective-permute-start | bytes 786440 | tf_op jit(solution)/shard_map/ppermute | solution.py:71
  162.6 14.8 %collective-permute-start.30 = (f32[8,64,64]{2,1,0:T(8,128)S(1)}, f32[8,64,64]{2,1,0:T(8,128)S(1)}, u32[]{:S(2)}, u32[]{:S(2)}) collective-permute-start(f32[8,64,64]{2,1,0:T(8,128)S(1)} %get-tuple-element.7), channel_id=1, source_target_pairs={{0,4},{4,12},{12,20},{20,28},{28,24},{24,16},{16,8},{8,0},{1,5},{5... | collective-permute-start | bytes 393224 | tf_op jit(solution)/shard_map/ppermute | solution.py:71
  168.2 11.2 %collective-permute-start.34 = (f32[8,64,64]{2,1,0:T(8,128)S(1)}, f32[8,64,64]{2,1,0:T(8,128)S(1)}, u32[]{:S(2)}, u32[]{:S(2)}) collective-permute-start(f32[8,64,64]{2,1,0:T(8,128)S(1)} %get-tuple-element.8), channel_id=1, source_target_pairs={{0,8},{4,0},{12,4},{20,12},{28,20},{24,28},{16,24},{8,16},{1,9},{5... | collective-permute-start | bytes 393224 | tf_op jit(solution)/shard_map/ppermute | solution.py:71
  174.4 10.7 %collective-permute-start.19 = (f32[16,16,256]{2,0,1:T(8,128)S(1)}, f32[16,16,256]{2,0,1:T(8,128)}, u32[]{:S(2)}, u32[]{:S(2)}) collective-permute-start(f32[16,16,256]{2,0,1:T(8,128)S(1)} %get-tuple-element.16), channel_id=1, source_target_pairs={{0,8},{4,0},{12,4},{20,12},{28,20},{24,28},{16,24},{8,16},{1,9},{5... | collective-permute-start | bytes 786440 | tf_op jit(solution)/shard_map/ppermute | solution.py:71
  175.4 13.3 %collective-permute-start.22 = (f32[16,16,256]{2,0,1:T(8,128)}, f32[16,16,256]{2,0,1:T(8,128)S(1)}, u32[]{:S(2)}, u32[]{:S(2)}) collective-permute-start(f32[16,16,256]{2,0,1:T(8,128)} %get-tuple-element.21), channel_id=1, source_target_pairs={{0,4},{4,12},{12,20},{20,28},{28,24},{24,16},{16,8},{8,0},{1,5},{5... | collective-permute-start | bytes 786440 | tf_op jit(solution)/shard_map/ppermute | solution.py:71
  177.4 13.3 %collective-permute-start.26 = (f32[16,16,256]{2,0,1:T(8,128)S(1)}, f32[16,16,256]{2,0,1:T(8,128)}, u32[]{:S(2)}, u32[]{:S(2)}) collective-permute-start(f32[16,16,256]{2,0,1:T(8,128)S(1)} %get-tuple-element.22), channel_id=1, source_target_pairs={{0,8},{4,0},{12,4},{20,12},{28,20},{24,28},{16,24},{8,16},{1,9},{5... | collective-permute-start | bytes 786440 | tf_op jit(solution)/shard_map/ppermute | solution.py:71
  186.3 12.2 %collective-permute-start.17 = (f32[16,16,256]{2,0,1:T(8,128)S(1)}, f32[16,16,256]{2,0,1:T(8,128)S(1)}, u32[]{:S(2)}, u32[]{:S(2)}) collective-permute-start(f32[16,16,256]{2,0,1:T(8,128)S(1)} %get-tuple-element.13), channel_id=1, source_target_pairs={{0,4},{4,12},{12,20},{20,28},{28,24},{24,16},{16,8},{8,0},{1,5},{5... | collective-permute-start | bytes 786440 | tf_op jit(solution)/shard_map/ppermute | solution.py:71
  187.9 10.6 %collective-permute-start.20 = (f32[16,16,256]{2,0,1:T(8,128)S(1)}, f32[16,16,256]{2,0,1:T(8,128)S(1)}, u32[]{:S(2)}, u32[]{:S(2)}) collective-permute-start(f32[16,16,256]{2,0,1:T(8,128)S(1)} %get-tuple-element.14), channel_id=1, source_target_pairs={{0,8},{4,0},{12,4},{20,12},{28,20},{24,28},{16,24},{8,16},{1,9},{5... | collective-permute-start | bytes 786440 | tf_op jit(solution)/shard_map/ppermute | solution.py:71
  (27 other events, 276.5 us)

commit v16 on v14

--- a/solution.py
+++ b/solution.py
@@ -131,9 +131,12 @@
         jnp.einsum("bit,obt->ibo", x_blocks, back_rows, preferred_element_type=jnp.float32)
         * grad_scale
     ).reshape(n_dp, rows_r, local_blocks, WIDTH)
-    cut = rows_r // 2
+    step = rows_r // 4
     grad_r = jnp.concatenate(
-        [ring_reduce_scatter(r_term[:, :cut], ring), ring_reduce_scatter(r_term[:, cut:], ring, lead=-1)],
+        [
+            ring_reduce_scatter(r_term[:, k * step:(k + 1) * step], ring, lead=1 - 2 * (k % 2))
+            for k in range(4)
+        ],
         axis=0,
     )
     grad_r = jnp.transpose(grad_r, (1, 0, 2))

time: 203 us -> 220 us (1.084)
  waiting for transfers between devices: 69.6 us -> 84.1 us
  starting transfers between devices: 49 us -> 59.4 us
  matrix products: 17.5 us -> 12.9 us
  other arithmetic: 8.09 us -> 5.62 us
    ppermute x21 -> x35, waiting for transfers between devices: 24.9 us -> 44.4 us  [ring_reduce_scatter(): acc = lax.ppermute(mine if acc is None else acc + mine, 'dp', pairs)]
    ppermute x21 -> x35, starting transfers between devices: 26.4 us -> 36.8 us  [ring_reduce_scatter(): acc = lax.ppermute(mine if acc is None else acc + mine, 'dp', pairs)]
    all_to_all x1, waiting for transfers between devices: 5.06 us -> 0.01 us  [body(): lax.all_to_all(back_cols, 'feat', split_axis=1, concat_axis=0, tiled=True)]
    dot_general x1, matrix products: 4.33 us -> 2.04 us  [body(): jnp.einsum('bst,cst->bsc', columns, slope_cols, preferred_element_type=jn...]
    dot_general x1, matrix products: 4.5 us -> 2.27 us  [body(): jnp.einsum('obt,ibo->bit', back_rows, r_whole, preferred_element_type=jnp...]
    add x9 -> x15, other arithmetic: 5.14 us -> 3.62 us  [ring_reduce_scatter(): acc = lax.ppermute(mine if acc is None else acc + mine, 'dp', pairs)]
    unnamed x27 -> x17, local copies, waits for them, and re-layouts: 4.69 us -> 4.34 us
  transfers between devices with their start and end apart: 31 -> 45, of which waited for: 19 -> 25; matrix products, arithmetic and copies ran while one was open for 21% -> 12% of each run, Pallas kernels for 0% -> 0%
where the time goes in v16:
time: 220 us; the launch traced here: 219 us
  waiting for transfers between devices  84.1 us (38%)
  starting transfers between devices  59.4 us (27%)
  local copies, waits for them, and re-layouts  35.7 us (16%)
  between operations  21.2 us (10%)
  matrix products  12.9 us (6%)
  other arithmetic  5.62 us (3%)
    ppermute x35, waiting for transfers between devices, ring_reduce_scatter(): acc = lax.ppermute(mine if acc is None else acc + mine, 'dp', pairs)  44.4 us
    ppermute x35, starting transfers between devices, ring_reduce_scatter(): acc = lax.ppermute(mine if acc is None else acc + mine, 'dp', pairs)  36.8 us
    ppermute x7, waiting for transfers between devices, ring_all_gather(): cur = lax.ppermute(cur, 'dp', pairs)  21.8 us
    all_to_all x1, waiting for transfers between devices, body(): lax.all_to_all(mixed_rows, 'feat', split_axis=1, concat_axis=0, tiled=True)  17.9 us
    ppermute x7, starting transfers between devices, ring_all_gather(): cur = lax.ppermute(cur, 'dp', pairs)  8.93 us
    dot_general x1, matrix products, body(): jnp.einsum('bst,bsc->cst', columns, l_blocks, preferred_element_type=jnp....  5.07 us
    all_to_all x1, starting transfers between devices, body(): lax.all_to_all(mixed_rows, 'feat', split_axis=1, concat_axis=0, tiled=True)  4.63 us
    all_to_all x1, starting transfers between devices, body(): lax.all_to_all(g_blocks, 'feat', split_axis=1, concat_axis=0, tiled=True)  4.61 us
  transfers between devices with their start and end apart: 45, of which 25 were waited for; matrix products, arithmetic and copies ran while one was open for 12% of the time, Pallas kernels for 0%

profile of v16, /device:TPU:0, one launch (start us, length us, event | category | flops | bytes accessed | tf_op | source)
XLA Modules:
  0.0 218.9 jit_solution(7141277616852897129)
XLA Ops:
  3.1 3.0 %collective-permute-start = (bf16[640,256]{1,0:T(8,128)(2,1)S(1)}, bf16[640,256]{1,0:T(8,128)(2,1)}, u32[]{:S(2)}, u32[]{:S(2)}) collective-permute-start(bf16[640,256]{1,0:T(8,128)(2,1)S(1)} %pad_maximum_fusion), channel_id=1, source_target_pairs={{0,4},{4,12},{12,20},{20,28},{28,24},{24,16},{16,8},{8,0},{1,5},{5... | collective-permute-start | bytes 983048 | tf_op jit(solution)/shard_map/ppermute | solution.py:88
  6.2 7.7 %collective-permute-done = bf16[640,256]{1,0:T(8,128)(2,1)} collective-permute-done((bf16[640,256]{1,0:T(8,128)(2,1)S(1)}, bf16[640,256]{1,0:T(8,128)(2,1)}, u32[]{:S(2)}, u32[]{:S(2)}) %collective-permute-start) | collective-permute-done | bytes 327712 | tf_op jit(solution)/shard_map/ppermute | solution.py:88
  15.7 4.1 %copy.47 = bf16[16,256,256]{2,0,1:T(8,128)(2,1)} copy(bf16[16,256,256]{2,1,0:T(8,128)(2,1)} %bitcast.194) | data formatting | bytes 4194304 | tf_op jit(solution)/shard_map/reshape | solution.py:99
  19.8 4.6 %all-to-all-start = ((bf16[16,256,256]{2,0,1:T(8,128)(2,1)}), bf16[16,256,256]{2,0,1:T(8,128)(2,1)}, u32[]{:S(2)}, u32[]{:S(2)}) async-start(bf16[16,256,256]{2,0,1:T(8,128)(2,1)} %copy.47), calls=%async_computation | async-start | bytes 4194304 | tf_op jit(solution)/shard_map/all_to_all | solution.py:100
  47.2 6.8 %collective-permute-done.5 = bf16[640,256]{1,0:T(8,128)(2,1)S(1)} collective-permute-done((bf16[640,256]{1,0:T(8,128)(2,1)S(1)}, bf16[640,256]{1,0:T(8,128)(2,1)S(1)}, u32[]{:S(2)}, u32[]{:S(2)}) %collective-permute-start.5) | collective-permute-done | bytes 327712 | tf_op jit(solution)/shard_map/ppermute | solution.py:88
  56.1 7.2 %collective-permute-done.3 = bf16[640,256]{1,0:T(8,128)(2,1)S(1)} collective-permute-done((bf16[640,256]{1,0:T(8,128)(2,1)S(1)}, bf16[640,256]{1,0:T(8,128)(2,1)S(1)}, u32[]{:S(2)}, u32[]{:S(2)}) %collective-permute-start.3) | collective-permute-done | bytes 327712 | tf_op jit(solution)/shard_map/ppermute | solution.py:88
  66.6 2.6 %copy.50 = bf16[16,256,256]{2,0,1:T(8,128)(2,1)} copy(bf16[16,256,256]{2,1,0:T(8,128)(2,1)S(1)} %convolution_convert_fusion.1) | data formatting | bytes 4194304 | tf_op jit(solution)/shard_map/convert_element_type | solution.py:112
  69.2 4.6 %all-to-all-start.1 = ((bf16[16,256,256]{2,0,1:T(8,128)(2,1)}), bf16[16,256,256]{2,0,1:T(8,128)(2,1)}, u32[]{:S(2)}, u32[]{:S(2)}) async-start(bf16[16,256,256]{2,0,1:T(8,128)(2,1)} %copy.50), calls=%async_computation.1 | async-start | bytes 4194304 | tf_op jit(solution)/shard_map/all_to_all | solution.py:113
  77.4 4.2 %copy.48 = f32[16,4,64,256]{3,0,1,2:T(8,128)} copy(bf16[16,4,64,256]{3,0,2,1:T(8,128)(2,1)} %bitcast.92) | data formatting | bytes 6291456 | tf_op jit(solution)/shard_map/convert_element_type | solution.py:19
  81.6 17.9 %all-to-all-done.1 = bf16[16,256,256]{2,0,1:T(8,128)(2,1)} async-done(((bf16[16,256,256]{2,0,1:T(8,128)(2,1)}), bf16[16,256,256]{2,0,1:T(8,128)(2,1)}, u32[]{:S(2)}, u32[]{:S(2)}) %all-to-all-start.1) | async-done | bytes 2097184 | tf_op jit(solution)/shard_map/all_to_all | solution.py:113
  99.5 2.0 copy.51
  102.3 5.1 %fusion.6 = bf16[64,64,256]{2,0,1:T(8,128)(2,1)S(1)} fusion(f32[16,4,64,256]{3,0,1,2:T(8,128)S(1)} %copy-done.5, bf16[64,64,256]{2,0,1:T(8,128)(2,1)S(1)} %bitcast.192, bf16[64,64,64]{2,1,0:T(8,128)(2,1)S(1)} %reshape.132), kind=kOutput, calls=%fused_computation.8 | convolution fusion | flops 155189248 | bytes 8912896 | tf_op jit(solution)/shard_map/bst,bsc->cst/dot_general | solution.py:114
  107.3 2.0 multiply_bitcast_fusion
  110.7 2.5 %copy.54 = bf16[64,64,256]{2,0,1:T(8,128)(2,1)} copy(bf16[64,64,256]{2,1,0:T(8,128)(2,1)S(1)} %convolution_convert_fusion) | data formatting | bytes 4194304 | tf_op jit(solution)/shard_map/convert_element_type | solution.py:118
  113.2 3.8 %copy.57 = f32[64,64,64]{2,1,0:T(8,128)} copy(f32[64,64,64]{0,2,1:T(8,128)} %multiply_bitcast_fusion) | data formatting | bytes 2097152 | tf_op jit(solution)/shard_map/mul | solution.py:120
  117.0 4.5 %all-to-all-start.2 = ((bf16[64,64,256]{2,0,1:T(8,128)(2,1)}), bf16[64,64,256]{2,0,1:T(8,128)(2,1)}, u32[]{:S(2)}, u32[]{:S(2)}) async-start(bf16[64,64,256]{2,0,1:T(8,128)(2,1)} %copy.54), calls=%async_computation.2 | async-start | bytes 4194304 | tf_op jit(solution)/shard_map/all_to_all | solution.py:123
  124.6 6.6 %collective-permute-done.38 = f32[8,64,64]{2,1,0:T(8,128)S(1)} collective-permute-done((f32[8,64,64]{2,1,0:T(8,128)S(1)}, f32[8,64,64]{2,1,0:T(8,128)S(1)}, u32[]{:S(2)}, u32[]{:S(2)}) %collective-permute-start.38) | collective-permute-done | bytes 131104 | tf_op jit(solution)/shard_map/ppermute | solution.py:71
  134.0 6.2 %collective-permute-done.39 = f32[8,64,64]{2,1,0:T(8,128)S(1)} collective-permute-done((f32[8,64,64]{2,1,0:T(8,128)S(1)}, f32[8,64,64]{2,1,0:T(8,128)S(1)}, u32[]{:S(2)}, u32[]{:S(2)}) %collective-permute-start.39) | collective-permute-done | bytes 131104 | tf_op jit(solution)/shard_map/ppermute | solution.py:71
  143.5 5.2 %collective-permute-done.36 = f32[8,64,64]{2,1,0:T(8,128)S(1)} collective-permute-done((f32[8,64,64]{2,1,0:T(8,128)S(1)}, f32[8,64,64]{2,1,0:T(8,128)S(1)}, u32[]{:S(2)}, u32[]{:S(2)}) %collective-permute-start.36) | collective-permute-done | bytes 131104 | tf_op jit(solution)/shard_map/ppermute | solution.py:71
  155.2 2.4 %collective-permute-done.37 = f32[8,64,64]{2,1,0:T(8,128)S(1)} collective-permute-done((f32[8,64,64]{2,1,0:T(8,128)S(1)}, f32[8,64,64]{2,1,0:T(8,128)S(1)}, u32[]{:S(2)}, u32[]{:S(2)}) %collective-permute-start.37) | collective-permute-done | bytes 131104 | tf_op jit(solution)/shard_map/ppermute | solution.py:71
  163.9 2.3 %add_convert_fusion = bf16[16,256,256]{2,1,0:T(8,128)(2,1)} fusion(bf16[16,256,256]{2,1,0:T(8,128)(2,1)S(1)} %bitcast.195, bf16[256,16,256]{2,0,1:T(8,128)(2,1)S(1)} %bitcast.189, bf16[256,16,256]{2,1,0:T(8,128)(2,1)S(1)} %bitcast.188), kind=kOutput, calls=%fused_computation.14 | convolution fusion | flops 540016640 | bytes 8388608 | tf_op jit(solution)/shard_map/obt,ibo->bit/dot_general | solution.py:124
  177.2 1.9 collective-permute-done.31
  179.6 4.5 %collective-permute-done.17 = f32[8,16,256]{2,0,1:T(8,128)S(1)} collective-permute-done((f32[8,16,256]{2,0,1:T(8,128)S(1)}, f32[8,16,256]{2,0,1:T(8,128)S(1)}, u32[]{:S(2)}, u32[]{:S(2)}) %collective-permute-start.17) | collective-permute-done | bytes 131104 | tf_op jit(solution)/shard_map/ppermute | solution.py:71
  186.5 3.5 %collective-permute-done.8 = f32[8,16,256]{2,0,1:T(8,128)S(1)} collective-permute-done((f32[8,16,256]{2,0,1:T(8,128)S(1)}, f32[8,16,256]{2,0,1:T(8,128)S(1)}, u32[]{:S(2)}, u32[]{:S(2)}) %collective-permute-start.8) | collective-permute-done | bytes 131104 | tf_op jit(solution)/shard_map/ppermute | solution.py:71
  (143 shorter events, 82.3 us)
Async XLA Ops:
  3.1 10.9 %collective-permute-start = (bf16[640,256]{1,0:T(8,128)(2,1)S(1)}, bf16[640,256]{1,0:T(8,128)(2,1)}, u32[]{:S(2)}, u32[]{:S(2)}) collective-permute-start(bf16[640,256]{1,0:T(8,128)(2,1)S(1)} %pad_maximum_fusion), channel_id=1, source_target_pairs={{0,4},{4,12},{12,20},{20,28},{28,24},{24,16},{16,8},{8,0},{1,5},{5... | collective-permute-start | bytes 983048 | tf_op jit(solution)/shard_map/ppermute | solution.py:88
  6.1 37.7 %collective-permute-start.4 = (bf16[640,256]{1,0:T(8,128)(2,1)S(1)}, bf16[640,256]{1,0:T(8,128)(2,1)S(1)}, u32[]{:S(2)}, u32[]{:S(2)}) collective-permute-start(bf16[640,256]{1,0:T(8,128)(2,1)S(1)} %pad_maximum_fusion), channel_id=1, source_target_pairs={{0,8},{4,0},{12,4},{20,12},{28,20},{24,28},{16,24},{8,16},{1,9},{5... | collective-permute-start | bytes 983048 | tf_op jit(solution)/shard_map/ppermute | solution.py:88
  14.0 30.3 %collective-permute-start.1 = (bf16[640,256]{1,0:T(8,128)(2,1)}, bf16[640,256]{1,0:T(8,128)(2,1)S(1)}, u32[]{:S(2)}, u32[]{:S(2)}) collective-permute-start(bf16[640,256]{1,0:T(8,128)(2,1)} %collective-permute-done), channel_id=1, source_target_pairs={{0,4},{4,12},{12,20},{20,28},{28,24},{24,16},{16,8},{8,0},{1,5},{5... | collective-permute-start | bytes 983048 | tf_op jit(solution)/shard_map/ppermute | solution.py:88
  19.8 49.5 %all-to-all-start = ((bf16[16,256,256]{2,0,1:T(8,128)(2,1)}), bf16[16,256,256]{2,0,1:T(8,128)(2,1)}, u32[]{:S(2)}, u32[]{:S(2)}) async-start(bf16[16,256,256]{2,0,1:T(8,128)(2,1)} %copy.47), calls=%async_computation | async-start | bytes 4194304 | tf_op jit(solution)/shard_map/all_to_all | solution.py:100
  43.9 10.1 %collective-permute-start.5 = (bf16[640,256]{1,0:T(8,128)(2,1)S(1)}, bf16[640,256]{1,0:T(8,128)(2,1)S(1)}, u32[]{:S(2)}, u32[]{:S(2)}) collective-permute-start(bf16[640,256]{1,0:T(8,128)(2,1)S(1)} %collective-permute-done.4), channel_id=1, source_target_pairs={{0,8},{4,0},{12,4},{20,12},{28,20},{24,28},{16,24},{8,16},{1,9},{5... | collective-permute-start | bytes 983048 | tf_op jit(solution)/shard_map/ppermute | solution.py:88
  44.3 10.1 %collective-permute-start.2 = (bf16[640,256]{1,0:T(8,128)(2,1)S(1)}, bf16[640,256]{1,0:T(8,128)(2,1)S(1)}, u32[]{:S(2)}, u32[]{:S(2)}) collective-permute-start(bf16[640,256]{1,0:T(8,128)(2,1)S(1)} %collective-permute-done.1), channel_id=1, source_target_pairs={{0,4},{4,12},{12,20},{20,28},{28,24},{24,16},{16,8},{8,0},{1,5},{5... | collective-permute-start | bytes 983048 | tf_op jit(solution)/shard_map/ppermute | solution.py:88
  54.0 9.4 %collective-permute-start.6 = (bf16[640,256]{1,0:T(8,128)(2,1)S(1)}, bf16[640,256]{1,0:T(8,128)(2,1)S(1)}, u32[]{:S(2)}, u32[]{:S(2)}) collective-permute-start(bf16[640,256]{1,0:T(8,128)(2,1)S(1)} %collective-permute-done.5), channel_id=1, source_target_pairs={{0,8},{4,0},{12,4},{20,12},{28,20},{24,28},{16,24},{8,16},{1,9},{5... | collective-permute-start | bytes 983048 | tf_op jit(solution)/shard_map/ppermute | solution.py:88
  54.3 9.0 %collective-permute-start.3 = (bf16[640,256]{1,0:T(8,128)(2,1)S(1)}, bf16[640,256]{1,0:T(8,128)(2,1)S(1)}, u32[]{:S(2)}, u32[]{:S(2)}) collective-permute-start(bf16[640,256]{1,0:T(8,128)(2,1)S(1)} %collective-permute-done.2), channel_id=1, source_target_pairs={{0,4},{4,12},{12,20},{20,28},{28,24},{24,16},{16,8},{8,0},{1,5},{5... | collective-permute-start | bytes 983048 | tf_op jit(solution)/shard_map/ppermute | solution.py:88
  69.2 30.2 %all-to-all-start.1 = ((bf16[16,256,256]{2,0,1:T(8,128)(2,1)}), bf16[16,256,256]{2,0,1:T(8,128)(2,1)}, u32[]{:S(2)}, u32[]{:S(2)}) async-start(bf16[16,256,256]{2,0,1:T(8,128)(2,1)} %copy.50), calls=%async_computation.1 | async-start | bytes 4194304 | tf_op jit(solution)/shard_map/all_to_all | solution.py:113
  117.0 44.1 %all-to-all-start.2 = ((bf16[64,64,256]{2,0,1:T(8,128)(2,1)}), bf16[64,64,256]{2,0,1:T(8,128)(2,1)}, u32[]{:S(2)}, u32[]{:S(2)}) async-start(bf16[64,64,256]{2,0,1:T(8,128)(2,1)} %copy.54), calls=%async_computation.2 | async-start | bytes 4194304 | tf_op jit(solution)/shard_map/all_to_all | solution.py:123
  122.5 8.7 %collective-permute-start.38 = (f32[8,64,64]{2,1,0:T(8,128)S(1)}, f32[8,64,64]{2,1,0:T(8,128)S(1)}, u32[]{:S(2)}, u32[]{:S(2)}) collective-permute-start(f32[8,64,64]{2,1,0:T(8,128)S(1)} %get-tuple-element.12), channel_id=1, source_target_pairs={{0,8},{4,0},{12,4},{20,12},{28,20},{24,28},{16,24},{8,16},{1,9},{5... | collective-permute-start | bytes 393224 | tf_op jit(solution)/shard_map/ppermute | solution.py:71
  124.3 9.7 %collective-permute-start.35 = (f32[8,64,64]{2,1,0:T(8,128)S(1)}, f32[8,64,64]{2,1,0:T(8,128)S(1)}, u32[]{:S(2)}, u32[]{:S(2)}) collective-permute-start(f32[8,64,64]{2,1,0:T(8,128)S(1)} %get-tuple-element.11), channel_id=1, source_target_pairs={{0,4},{4,12},{12,20},{20,28},{28,24},{24,16},{16,8},{8,0},{1,5},{5... | collective-permute-start | bytes 393224 | tf_op jit(solution)/shard_map/ppermute | solution.py:71
  132.2 8.0 %collective-permute-start.39 = (f32[8,64,64]{2,1,0:T(8,128)S(1)}, f32[8,64,64]{2,1,0:T(8,128)S(1)}, u32[]{:S(2)}, u32[]{:S(2)}) collective-permute-start(f32[8,64,64]{2,1,0:T(8,128)S(1)} %bitcast_add_fusion.2), channel_id=1, source_target_pairs={{0,8},{4,0},{12,4},{20,12},{28,20},{24,28},{16,24},{8,16},{1,9},{5... | collective-permute-start | bytes 393224 | tf_op jit(solution)/shard_map/ppermute | solution.py:71
  141.4 7.3 %collective-permute-start.36 = (f32[8,64,64]{2,1,0:T(8,128)S(1)}, f32[8,64,64]{2,1,0:T(8,128)S(1)}, u32[]{:S(2)}, u32[]{:S(2)}) collective-permute-start(f32[8,64,64]{2,1,0:T(8,128)S(1)} %get-tuple-element.9), channel_id=1, source_target_pairs={{0,4},{4,12},{12,20},{20,28},{28,24},{24,16},{16,8},{8,0},{1,5},{5... | collective-permute-start | bytes 393224 | tf_op jit(solution)/shard_map/ppermute | solution.py:71
  169.2 16.4 %collective-permute-start.11 = (f32[8,16,256]{2,0,1:T(8,128)S(1)}, f32[8,16,256]{2,0,1:T(8,128)S(1)}, u32[]{:S(2)}, u32[]{:S(2)}) collective-permute-start(f32[8,16,256]{2,0,1:T(8,128)S(1)} %get-tuple-element.18), channel_id=1, source_target_pairs={{0,8},{4,0},{12,4},{20,12},{28,20},{24,28},{16,24},{8,16},{1,9},{5... | collective-permute-start | bytes 393224 | tf_op jit(solution)/shard_map/ppermute | solution.py:71
  171.3 19.1 %collective-permute-start.25 = (f32[8,16,256]{2,0,1:T(8,128)S(1)}, f32[8,16,256]{2,0,1:T(8,128)S(1)}, u32[]{:S(2)}, u32[]{:S(2)}) collective-permute-start(f32[8,16,256]{2,0,1:T(8,128)S(1)} %get-tuple-element.30), channel_id=1, source_target_pairs={{0,8},{4,0},{12,4},{20,12},{28,20},{24,28},{16,24},{8,16},{1,9},{5... | collective-permute-start | bytes 393224 | tf_op jit(solution)/shard_map/ppermute | solution.py:71
  171.8 22.6 %collective-permute-start.28 = (f32[8,16,256]{2,0,1:T(8,128)S(1)}, f32[8,16,256]{2,0,1:T(8,128)S(1)}, u32[]{:S(2)}, u32[]{:S(2)}) collective-permute-start(f32[8,16,256]{2,0,1:T(8,128)S(1)} %get-tuple-element.35), channel_id=1, source_target_pairs={{0,4},{4,12},{12,20},{20,28},{28,24},{24,16},{16,8},{8,0},{1,5},{5... | collective-permute-start | bytes 393224 | tf_op jit(solution)/shard_map/ppermute | solution.py:71
  175.6 21.9 %collective-permute-start.14 = (f32[8,16,256]{2,0,1:T(8,128)S(1)}, f32[8,16,256]{2,0,1:T(8,128)S(1)}, u32[]{:S(2)}, u32[]{:S(2)}) collective-permute-start(f32[8,16,256]{2,0,1:T(8,128)S(1)} %get-tuple-element.23), channel_id=1, source_target_pairs={{0,4},{4,12},{12,20},{20,28},{28,24},{24,16},{16,8},{8,0},{1,5},{5... | collective-permute-start | bytes 393224 | tf_op jit(solution)/shard_map/ppermute | solution.py:71
  185.7 7.1 %collective-permute-start.22 = (f32[8,16,256]{2,0,1:T(8,128)S(1)}, f32[8,16,256]{2,0,1:T(8,128)S(1)}, u32[]{:S(2)}, u32[]{:S(2)}) collective-permute-start(f32[8,16,256]{2,0,1:T(8,128)S(1)} %bitcast_add_fusion.16), channel_id=1, source_target_pairs={{0,4},{4,12},{12,20},{20,28},{28,24},{24,16},{16,8},{8,0},{1,5},{5... | collective-permute-start | bytes 393224 | tf_op jit(solution)/shard_map/ppermute | solution.py:71
  190.5 8.2 %collective-permute-start.18 = (f32[8,16,256]{2,0,1:T(8,128)S(1)}, f32[8,16,256]{2,0,1:T(8,128)S(1)}, u32[]{:S(2)}, u32[]{:S(2)}) collective-permute-start(f32[8,16,256]{2,0,1:T(8,128)S(1)} %bitcast_add_fusion.20), channel_id=1, source_target_pairs={{0,8},{4,0},{12,4},{20,12},{28,20},{24,28},{16,24},{8,16},{1,9},{5... | collective-permute-start | bytes 393224 | tf_op jit(solution)/shard_map/ppermute | solution.py:71
  192.8 7.5 %collective-permute-start.9 = (f32[8,16,256]{2,0,1:T(8,128)S(1)}, f32[8,16,256]{2,0,1:T(8,128)S(1)}, u32[]{:S(2)}, u32[]{:S(2)}) collective-permute-start(f32[8,16,256]{2,0,1:T(8,128)S(1)} %get-tuple-element.15), channel_id=1, source_target_pairs={{0,4},{4,12},{12,20},{20,28},{28,24},{24,16},{16,8},{8,0},{1,5},{5... | collective-permute-start | bytes 393224 | tf_op jit(solution)/shard_map/ppermute | solution.py:71
  195.9 7.2 %collective-permute-start.23 = (f32[8,16,256]{2,0,1:T(8,128)S(1)}, f32[8,16,256]{2,0,1:T(8,128)S(1)}, u32[]{:S(2)}, u32[]{:S(2)}) collective-permute-start(f32[8,16,256]{2,0,1:T(8,128)S(1)} %get-tuple-element.27), channel_id=1, source_target_pairs={{0,4},{4,12},{12,20},{20,28},{28,24},{24,16},{16,8},{8,0},{1,5},{5... | collective-permute-start | bytes 393224 | tf_op jit(solution)/shard_map/ppermute | solution.py:71
  198.7 7.2 %collective-permute-start.29 = (f32[8,16,256]{2,0,1:T(8,128)S(1)}, f32[8,16,256]{2,0,1:T(8,128)S(1)}, u32[]{:S(2)}, u32[]{:S(2)}) collective-permute-start(f32[8,16,256]{2,0,1:T(8,128)S(1)} %get-tuple-element.33), channel_id=1, source_target_pairs={{0,4},{4,12},{12,20},{20,28},{28,24},{24,16},{16,8},{8,0},{1,5},{5... | collective-permute-start | bytes 393224 | tf_op jit(solution)/shard_map/ppermute | solution.py:71
  201.5 7.2 %collective-permute-start.15 = (f32[8,16,256]{2,0,1:T(8,128)S(1)}, f32[8,16,256]{2,0,1:T(8,128)S(1)}, u32[]{:S(2)}, u32[]{:S(2)}) collective-permute-start(f32[8,16,256]{2,0,1:T(8,128)S(1)} %get-tuple-element.21), channel_id=1, source_target_pairs={{0,4},{4,12},{12,20},{20,28},{28,24},{24,16},{16,8},{8,0},{1,5},{5... | collective-permute-start | bytes 393224 | tf_op jit(solution)/shard_map/ppermute | solution.py:71
  (29 other events, 214.1 us)

commit v17 on v14

--- a/solution.py
+++ b/solution.py
@@ -118,7 +118,11 @@
     ).astype(jnp.bfloat16)
     l_term = jnp.einsum("bst,cst->bsc", columns, slope_cols, preferred_element_type=jnp.float32)
     l_term = (l_term * grad_scale).reshape(n_dp, -1, local_cols, BLOCKS)
-    grad_l = ring_reduce_scatter(l_term, ring, lead=-1)
+    half_l = l_term.shape[1] // 2
+    grad_l = jnp.concatenate(
+        [ring_reduce_scatter(l_term[:, :half_l], ring), ring_reduce_scatter(l_term[:, half_l:], ring, lead=-1)],
+        axis=0,
+    )
     grad_l = jnp.transpose(grad_l, (1, 0, 2)).reshape(local_cols, -1)
     back_rows = lax.all_to_all(back_cols, "feat", split_axis=1, concat_axis=0, tiled=True)
     through_r = jnp.einsum("obt,ibo->bit", back_rows, r_whole, preferred_element_type=jnp.float32)

time: 203 us -> 204 us (level)
  waiting for transfers between devices: 69.6 us -> 61.4 us
  other arithmetic: 8.09 us -> 12.4 us
  starting transfers between devices: 49 us -> 52.6 us
  matrix products: 17.5 us -> 15.2 us
    all_to_all x1, waiting for transfers between devices: 5.06 us -> 0.01 us  [body(): lax.all_to_all(back_cols, 'feat', split_axis=1, concat_axis=0, tiled=True)]
    ppermute x21 -> x28, starting transfers between devices: 26.4 us -> 30 us  [ring_reduce_scatter(): acc = lax.ppermute(mine if acc is None else acc + mine, 'dp', pairs)]
    add x9 -> x12, other arithmetic: 5.14 us -> 8.47 us  [ring_reduce_scatter(): acc = lax.ppermute(mine if acc is None else acc + mine, 'dp', pairs)]
    slice x0 -> x1, local copies, waits for them, and re-layouts: none -> 2.7 us  [body(): l_term[:, :half_l]]
    dot_general x1, matrix products: 4.33 us -> 2.07 us  [body(): jnp.einsum('bst,cst->bsc', columns, slope_cols, preferred_element_type=jn...]
    ppermute x21 -> x28, waiting for transfers between devices: 24.9 us -> 23.6 us  [ring_reduce_scatter(): acc = lax.ppermute(mine if acc is None else acc + mine, 'dp', pairs)]
    unnamed x27 -> x21, local copies, waits for them, and re-layouts: 4.69 us -> 3.78 us
  transfers between devices with their start and end apart: 31 -> 38, of which waited for: 19 -> 18; matrix products, arithmetic and copies ran while one was open for 21% -> 19% of each run, Pallas kernels for 0% -> 0%
where the time goes in v17:
time: 204 us; the launch traced here: 201 us
  waiting for transfers between devices  61.4 us (30%)
  starting transfers between devices  52.6 us (26%)
  local copies, waits for them, and re-layouts  37.7 us (18%)
  between operations  21.4 us (10%)
  matrix products  15.2 us (7%)
  other arithmetic  12.4 us (6%)
    ppermute x28, starting transfers between devices, ring_reduce_scatter(): acc = lax.ppermute(mine if acc is None else acc + mine, 'dp', pairs)  30 us
    ppermute x28, waiting for transfers between devices, ring_reduce_scatter(): acc = lax.ppermute(mine if acc is None else acc + mine, 'dp', pairs)  23.6 us
    ppermute x7, waiting for transfers between devices, ring_all_gather(): cur = lax.ppermute(cur, 'dp', pairs)  21.8 us
    all_to_all x1, waiting for transfers between devices, body(): lax.all_to_all(mixed_rows, 'feat', split_axis=1, concat_axis=0, tiled=True)  16 us
    ppermute x7, starting transfers between devices, ring_all_gather(): cur = lax.ppermute(cur, 'dp', pairs)  8.93 us
    add x12, other arithmetic, ring_reduce_scatter(): acc = lax.ppermute(mine if acc is None else acc + mine, 'dp', pairs)  8.47 us
    dot_general x1, matrix products, body(): jnp.einsum('bst,bsc->cst', columns, l_blocks, preferred_element_type=jnp....  5.07 us
    all_to_all x1, starting transfers between devices, body(): lax.all_to_all(mixed_rows, 'feat', split_axis=1, concat_axis=0, tiled=True)  4.63 us
  transfers between devices with their start and end apart: 38, of which 18 were waited for; matrix products, arithmetic and copies ran while one was open for 19% of the time, Pallas kernels for 0%

profile of v17, /device:TPU:0, one launch (start us, length us, event | category | flops | bytes accessed | tf_op | source)
XLA Modules:
  0.0 200.7 jit_solution(4374427816443076151)
XLA Ops:
  3.1 3.0 %collective-permute-start = (bf16[640,256]{1,0:T(8,128)(2,1)S(1)}, bf16[640,256]{1,0:T(8,128)(2,1)}, u32[]{:S(2)}, u32[]{:S(2)}) collective-permute-start(bf16[640,256]{1,0:T(8,128)(2,1)S(1)} %pad_maximum_fusion), channel_id=1, source_target_pairs={{0,4},{4,12},{12,20},{20,28},{28,24},{24,16},{16,8},{8,0},{1,5},{5... | collective-permute-start | bytes 983048 | tf_op jit(solution)/shard_map/ppermute | solution.py:88
  6.2 7.7 %collective-permute-done = bf16[640,256]{1,0:T(8,128)(2,1)} collective-permute-done((bf16[640,256]{1,0:T(8,128)(2,1)S(1)}, bf16[640,256]{1,0:T(8,128)(2,1)}, u32[]{:S(2)}, u32[]{:S(2)}) %collective-permute-start) | collective-permute-done | bytes 327712 | tf_op jit(solution)/shard_map/ppermute | solution.py:88
  15.7 4.1 %copy.45 = bf16[16,256,256]{2,0,1:T(8,128)(2,1)} copy(bf16[16,256,256]{2,1,0:T(8,128)(2,1)} %bitcast.175) | data formatting | bytes 4194304 | tf_op jit(solution)/shard_map/reshape | solution.py:99
  19.8 4.6 %all-to-all-start = ((bf16[16,256,256]{2,0,1:T(8,128)(2,1)}), bf16[16,256,256]{2,0,1:T(8,128)(2,1)}, u32[]{:S(2)}, u32[]{:S(2)}) async-start(bf16[16,256,256]{2,0,1:T(8,128)(2,1)} %copy.45), calls=%async_computation | async-start | bytes 4194304 | tf_op jit(solution)/shard_map/all_to_all | solution.py:100
  47.4 6.8 %collective-permute-done.5 = bf16[640,256]{1,0:T(8,128)(2,1)S(1)} collective-permute-done((bf16[640,256]{1,0:T(8,128)(2,1)S(1)}, bf16[640,256]{1,0:T(8,128)(2,1)S(1)}, u32[]{:S(2)}, u32[]{:S(2)}) %collective-permute-start.5) | collective-permute-done | bytes 327712 | tf_op jit(solution)/shard_map/ppermute | solution.py:88
  56.3 7.2 %collective-permute-done.3 = bf16[640,256]{1,0:T(8,128)(2,1)S(1)} collective-permute-done((bf16[640,256]{1,0:T(8,128)(2,1)S(1)}, bf16[640,256]{1,0:T(8,128)(2,1)S(1)}, u32[]{:S(2)}, u32[]{:S(2)}) %collective-permute-start.3) | collective-permute-done | bytes 327712 | tf_op jit(solution)/shard_map/ppermute | solution.py:88
  66.7 2.6 %copy.48 = bf16[16,256,256]{2,0,1:T(8,128)(2,1)} copy(bf16[16,256,256]{2,1,0:T(8,128)(2,1)S(1)} %convolution_convert_fusion.1) | data formatting | bytes 4194304 | tf_op jit(solution)/shard_map/convert_element_type | solution.py:112
  69.2 4.6 %all-to-all-start.1 = ((bf16[16,256,256]{2,0,1:T(8,128)(2,1)}), bf16[16,256,256]{2,0,1:T(8,128)(2,1)}, u32[]{:S(2)}, u32[]{:S(2)}) async-start(bf16[16,256,256]{2,0,1:T(8,128)(2,1)} %copy.48), calls=%async_computation.1 | async-start | bytes 4194304 | tf_op jit(solution)/shard_map/all_to_all | solution.py:113
  79.3 4.2 %copy.46 = f32[16,4,64,256]{3,0,1,2:T(8,128)} copy(bf16[16,4,64,256]{3,0,2,1:T(8,128)(2,1)} %bitcast.84) | data formatting | bytes 6291456 | tf_op jit(solution)/shard_map/convert_element_type | solution.py:19
  83.5 16.0 %all-to-all-done.1 = bf16[16,256,256]{2,0,1:T(8,128)(2,1)} async-done(((bf16[16,256,256]{2,0,1:T(8,128)(2,1)}), bf16[16,256,256]{2,0,1:T(8,128)(2,1)}, u32[]{:S(2)}, u32[]{:S(2)}) %all-to-all-start.1) | async-done | bytes 2097184 | tf_op jit(solution)/shard_map/all_to_all | solution.py:113
  102.3 5.1 %fusion.6 = bf16[64,64,256]{2,0,1:T(8,128)(2,1)S(1)} fusion(f32[16,4,64,256]{3,0,1,2:T(8,128)S(1)} %copy-done.7, bf16[64,64,256]{2,0,1:T(8,128)(2,1)S(1)} %bitcast.172, bf16[64,64,64]{2,1,0:T(8,128)(2,1)S(1)} %reshape.118), kind=kOutput, calls=%fused_computation.8 | convolution fusion | flops 155189248 | bytes 8912896 | tf_op jit(solution)/shard_map/bst,bsc->cst/dot_general | solution.py:114
  110.7 2.5 %copy.52 = bf16[64,64,256]{2,0,1:T(8,128)(2,1)} copy(bf16[64,64,256]{2,1,0:T(8,128)(2,1)S(1)} %convolution_convert_fusion) | data formatting | bytes 4194304 | tf_op jit(solution)/shard_map/convert_element_type | solution.py:118
  113.3 3.8 %copy.55 = f32[64,64,64]{2,1,0:T(8,128)} copy(f32[64,64,64]{0,2,1:T(8,128)} %multiply_bitcast_fusion) | data formatting | bytes 2097152 | tf_op jit(solution)/shard_map/mul | solution.py:120
  117.1 2.7 %fusion.19 = (f32[8,4,64,64]{3,2,1,0:T(8,128)}, f32[8,4,64,64]{3,2,1,0:T(8,128)S(1)}) fusion(f32[8,8,64,64]{3,2,1,0:T(8,128)} %bitcast.174), kind=kLoop, calls=%fused_computation.72 | loop fusion | bytes 2097152 | tf_op jit(solution)/shard_map/slice | solution.py:123
  119.8 4.5 %all-to-all-start.2 = ((bf16[64,64,256]{2,0,1:T(8,128)(2,1)}), bf16[64,64,256]{2,0,1:T(8,128)(2,1)}, u32[]{:S(2)}, u32[]{:S(2)}) async-start(bf16[64,64,256]{2,0,1:T(8,128)(2,1)} %copy.52), calls=%async_computation.2 | async-start | bytes 4194304 | tf_op jit(solution)/shard_map/all_to_all | solution.py:127
  129.4 2.2 %collective-permute-done.21 = f32[4,64,64]{2,1,0:T(8,128)S(1)} collective-permute-done((f32[4,64,64]{2,1,0:T(8,128)S(1)}, f32[4,64,64]{2,1,0:T(8,128)S(1)}, u32[]{:S(2)}, u32[]{:S(2)}) %collective-permute-start.21) | collective-permute-done | bytes 65568 | tf_op jit(solution)/shard_map/ppermute | solution.py:71
  159.6 2.8 %collective-permute-done.7 = f32[16,16,256]{2,0,1:T(8,128)S(1)} collective-permute-done((f32[16,16,256]{2,0,1:T(8,128)S(1)}, f32[16,16,256]{2,0,1:T(8,128)S(1)}, u32[]{:S(2)}, u32[]{:S(2)}) %collective-permute-start.7) | collective-permute-done | bytes 262176 | tf_op jit(solution)/shard_map/ppermute | solution.py:71
  162.4 2.4 %collective-permute-start.14 = (f32[16,16,256]{2,0,1:T(8,128)S(1)}, f32[16,16,256]{2,0,1:T(8,128)S(1)}, u32[]{:S(2)}, u32[]{:S(2)}) collective-permute-start(f32[16,16,256]{2,0,1:T(8,128)S(1)} %get-tuple-element.17), channel_id=1, source_target_pairs={{0,4},{4,12},{12,20},{20,28},{28,24},{24,16},{16,8},{8,0},{1,5},{5... | collective-permute-start | bytes 786440 | tf_op jit(solution)/shard_map/ppermute | solution.py:71
  164.8 2.1 %collective-permute-done.17 = f32[16,16,256]{2,0,1:T(8,128)S(1)} collective-permute-done((f32[16,16,256]{2,0,1:T(8,128)S(1)}, f32[16,16,256]{2,0,1:T(8,128)S(1)}, u32[]{:S(2)}, u32[]{:S(2)}) %collective-permute-start.17) | collective-permute-done | bytes 262176 | tf_op jit(solution)/shard_map/ppermute | solution.py:71
  169.1 2.6 %collective-permute-done.11 = f32[16,16,256]{2,0,1:T(8,128)S(1)} collective-permute-done((f32[16,16,256]{2,0,1:T(8,128)S(1)}, f32[16,16,256]{2,0,1:T(8,128)S(1)}, u32[]{:S(2)}, u32[]{:S(2)}) %collective-permute-start.11) | collective-permute-done | bytes 262176 | tf_op jit(solution)/shard_map/ppermute | solution.py:71
  174.4 2.2 %collective-permute-start.9 = (f32[16,16,256]{2,0,1:T(8,128)}, f32[16,16,256]{2,0,1:T(8,128)S(1)}, u32[]{:S(2)}, u32[]{:S(2)}) collective-permute-start(f32[16,16,256]{2,0,1:T(8,128)} %get-tuple-element.9), channel_id=1, source_target_pairs={{0,4},{4,12},{12,20},{20,28},{28,24},{24,16},{16,8},{8,0},{1,5},{5... | collective-permute-start | bytes 786440 | tf_op jit(solution)/shard_map/ppermute | solution.py:71
  180.4 3.3 %collective-permute-done.9 = f32[16,16,256]{2,0,1:T(8,128)S(1)} collective-permute-done((f32[16,16,256]{2,0,1:T(8,128)}, f32[16,16,256]{2,0,1:T(8,128)S(1)}, u32[]{:S(2)}, u32[]{:S(2)}) %collective-permute-start.9) | collective-permute-done | bytes 262176 | tf_op jit(solution)/shard_map/ppermute | solution.py:71
  187.3 2.1 %collective-permute-done.15 = f32[16,16,256]{2,0,1:T(8,128)S(1)} collective-permute-done((f32[16,16,256]{2,0,1:T(8,128)}, f32[16,16,256]{2,0,1:T(8,128)S(1)}, u32[]{:S(2)}, u32[]{:S(2)}) %collective-permute-start.15) | collective-permute-done | bytes 262176 | tf_op jit(solution)/shard_map/ppermute | solution.py:71
  192.9 4.5 %add_convert_fusion = bf16[16,256,256]{2,1,0:T(8,128)(2,1)} fusion(bf16[16,256,256]{2,1,0:T(8,128)(2,1)} %bitcast.176, bf16[256,16,256]{2,0,1:T(8,128)(2,1)} %bitcast.170, bf16[256,16,256]{2,1,0:T(8,128)(2,1)S(1)} %bitcast.168), kind=kOutput, calls=%fused_computation.14 | convolution fusion | flops 540016640 | bytes 8388608 | tf_op jit(solution)/shard_map/obt,ibo->bit/dot_general | solution.py:128
  (130 shorter events, 75.6 us)
Async XLA Ops:
  3.1 10.9 %collective-permute-start = (bf16[640,256]{1,0:T(8,128)(2,1)S(1)}, bf16[640,256]{1,0:T(8,128)(2,1)}, u32[]{:S(2)}, u32[]{:S(2)}) collective-permute-start(bf16[640,256]{1,0:T(8,128)(2,1)S(1)} %pad_maximum_fusion), channel_id=1, source_target_pairs={{0,4},{4,12},{12,20},{20,28},{28,24},{24,16},{16,8},{8,0},{1,5},{5... | collective-permute-start | bytes 983048 | tf_op jit(solution)/shard_map/ppermute | solution.py:88
  6.1 38.0 %collective-permute-start.4 = (bf16[640,256]{1,0:T(8,128)(2,1)S(1)}, bf16[640,256]{1,0:T(8,128)(2,1)S(1)}, u32[]{:S(2)}, u32[]{:S(2)}) collective-permute-start(bf16[640,256]{1,0:T(8,128)(2,1)S(1)} %pad_maximum_fusion), channel_id=1, source_target_pairs={{0,8},{4,0},{12,4},{20,12},{28,20},{24,28},{16,24},{8,16},{1,9},{5... | collective-permute-start | bytes 983048 | tf_op jit(solution)/shard_map/ppermute | solution.py:88
  14.0 30.5 %collective-permute-start.1 = (bf16[640,256]{1,0:T(8,128)(2,1)}, bf16[640,256]{1,0:T(8,128)(2,1)S(1)}, u32[]{:S(2)}, u32[]{:S(2)}) collective-permute-start(bf16[640,256]{1,0:T(8,128)(2,1)} %collective-permute-done), channel_id=1, source_target_pairs={{0,4},{4,12},{12,20},{20,28},{28,24},{24,16},{16,8},{8,0},{1,5},{5... | collective-permute-start | bytes 983048 | tf_op jit(solution)/shard_map/ppermute | solution.py:88
  19.8 49.5 %all-to-all-start = ((bf16[16,256,256]{2,0,1:T(8,128)(2,1)}), bf16[16,256,256]{2,0,1:T(8,128)(2,1)}, u32[]{:S(2)}, u32[]{:S(2)}) async-start(bf16[16,256,256]{2,0,1:T(8,128)(2,1)} %copy.45), calls=%async_computation | async-start | bytes 4194304 | tf_op jit(solution)/shard_map/all_to_all | solution.py:100
  44.1 10.1 %collective-permute-start.5 = (bf16[640,256]{1,0:T(8,128)(2,1)S(1)}, bf16[640,256]{1,0:T(8,128)(2,1)S(1)}, u32[]{:S(2)}, u32[]{:S(2)}) collective-permute-start(bf16[640,256]{1,0:T(8,128)(2,1)S(1)} %collective-permute-done.4), channel_id=1, source_target_pairs={{0,8},{4,0},{12,4},{20,12},{28,20},{24,28},{16,24},{8,16},{1,9},{5... | collective-permute-start | bytes 983048 | tf_op jit(solution)/shard_map/ppermute | solution.py:88
  44.5 10.1 %collective-permute-start.2 = (bf16[640,256]{1,0:T(8,128)(2,1)S(1)}, bf16[640,256]{1,0:T(8,128)(2,1)S(1)}, u32[]{:S(2)}, u32[]{:S(2)}) collective-permute-start(bf16[640,256]{1,0:T(8,128)(2,1)S(1)} %collective-permute-done.1), channel_id=1, source_target_pairs={{0,4},{4,12},{12,20},{20,28},{28,24},{24,16},{16,8},{8,0},{1,5},{5... | collective-permute-start | bytes 983048 | tf_op jit(solution)/shard_map/ppermute | solution.py:88
  54.2 9.4 %collective-permute-start.6 = (bf16[640,256]{1,0:T(8,128)(2,1)S(1)}, bf16[640,256]{1,0:T(8,128)(2,1)S(1)}, u32[]{:S(2)}, u32[]{:S(2)}) collective-permute-start(bf16[640,256]{1,0:T(8,128)(2,1)S(1)} %collective-permute-done.5), channel_id=1, source_target_pairs={{0,8},{4,0},{12,4},{20,12},{28,20},{24,28},{16,24},{8,16},{1,9},{5... | collective-permute-start | bytes 983048 | tf_op jit(solution)/shard_map/ppermute | solution.py:88
  54.5 9.0 %collective-permute-start.3 = (bf16[640,256]{1,0:T(8,128)(2,1)S(1)}, bf16[640,256]{1,0:T(8,128)(2,1)S(1)}, u32[]{:S(2)}, u32[]{:S(2)}) collective-permute-start(bf16[640,256]{1,0:T(8,128)(2,1)S(1)} %collective-permute-done.2), channel_id=1, source_target_pairs={{0,4},{4,12},{12,20},{20,28},{28,24},{24,16},{16,8},{8,0},{1,5},{5... | collective-permute-start | bytes 983048 | tf_op jit(solution)/shard_map/ppermute | solution.py:88
  69.2 30.2 %all-to-all-start.1 = ((bf16[16,256,256]{2,0,1:T(8,128)(2,1)}), bf16[16,256,256]{2,0,1:T(8,128)(2,1)}, u32[]{:S(2)}, u32[]{:S(2)}) async-start(bf16[16,256,256]{2,0,1:T(8,128)(2,1)} %copy.48), calls=%async_computation.1 | async-start | bytes 4194304 | tf_op jit(solution)/shard_map/all_to_all | solution.py:113
  119.8 32.3 %all-to-all-start.2 = ((bf16[64,64,256]{2,0,1:T(8,128)(2,1)}), bf16[64,64,256]{2,0,1:T(8,128)(2,1)}, u32[]{:S(2)}, u32[]{:S(2)}) async-start(bf16[64,64,256]{2,0,1:T(8,128)(2,1)} %copy.52), calls=%async_computation.2 | async-start | bytes 4194304 | tf_op jit(solution)/shard_map/all_to_all | solution.py:127
  127.0 8.9 %collective-permute-start.25 = (f32[4,64,64]{2,1,0:T(8,128)S(1)}, f32[4,64,64]{2,1,0:T(8,128)S(1)}, u32[]{:S(2)}, u32[]{:S(2)}) collective-permute-start(f32[4,64,64]{2,1,0:T(8,128)S(1)} %get-tuple-element.24), channel_id=1, source_target_pairs={{0,8},{4,0},{12,4},{20,12},{28,20},{24,28},{16,24},{8,16},{1,9},{5... | collective-permute-start | bytes 196616 | tf_op jit(solution)/shard_map/ppermute | solution.py:71
  127.3 13.3 %collective-permute-start.28 = (f32[4,64,64]{2,1,0:T(8,128)S(1)}, f32[4,64,64]{2,1,0:T(8,128)S(1)}, u32[]{:S(2)}, u32[]{:S(2)}) collective-permute-start(f32[4,64,64]{2,1,0:T(8,128)S(1)} %get-tuple-element.29), channel_id=1, source_target_pairs={{0,4},{4,12},{12,20},{20,28},{28,24},{24,16},{16,8},{8,0},{1,5},{5... | collective-permute-start | bytes 196616 | tf_op jit(solution)/shard_map/ppermute | solution.py:71
  147.3 10.4 %collective-permute-start.24 = (f32[4,64,64]{2,1,0:T(8,128)}, f32[4,64,64]{2,1,0:T(8,128)S(1)}, u32[]{:S(2)}, u32[]{:S(2)}) collective-permute-start(f32[4,64,64]{2,1,0:T(8,128)} %get-tuple-element.19), channel_id=1, source_target_pairs={{0,4},{4,12},{12,20},{20,28},{28,24},{24,16},{16,8},{8,0},{1,5},{5... | collective-permute-start | bytes 196616 | tf_op jit(solution)/shard_map/ppermute | solution.py:71
  148.8 9.3 %collective-permute-start.27 = (f32[4,64,64]{2,1,0:T(8,128)}, f32[4,64,64]{2,1,0:T(8,128)}, u32[]{:S(2)}, u32[]{:S(2)}) collective-permute-start(f32[4,64,64]{2,1,0:T(8,128)} %get-tuple-element.20), channel_id=1, source_target_pairs={{0,8},{4,0},{12,4},{20,12},{28,20},{24,28},{16,24},{8,16},{1,9},{5... | collective-permute-start | bytes 196616 | tf_op jit(solution)/shard_map/ppermute | solution.py:71
  150.0 18.5 %collective-permute-start.30 = (f32[4,64,64]{2,1,0:T(8,128)}, f32[4,64,64]{2,1,0:T(8,128)S(1)}, u32[]{:S(2)}, u32[]{:S(2)}) collective-permute-start(f32[4,64,64]{2,1,0:T(8,128)} %get-tuple-element.25), channel_id=1, source_target_pairs={{0,4},{4,12},{12,20},{20,28},{28,24},{24,16},{16,8},{8,0},{1,5},{5... | collective-permute-start | bytes 196616 | tf_op jit(solution)/shard_map/ppermute | solution.py:71
  151.6 17.5 %collective-permute-start.34 = (f32[4,64,64]{2,1,0:T(8,128)}, f32[4,64,64]{2,1,0:T(8,128)S(1)}, u32[]{:S(2)}, u32[]{:S(2)}) collective-permute-start(f32[4,64,64]{2,1,0:T(8,128)} %get-tuple-element.26), channel_id=1, source_target_pairs={{0,8},{4,0},{12,4},{20,12},{28,20},{24,28},{16,24},{8,16},{1,9},{5... | collective-permute-start | bytes 196616 | tf_op jit(solution)/shard_map/ppermute | solution.py:71
  157.6 9.3 %collective-permute-start.17 = (f32[16,16,256]{2,0,1:T(8,128)S(1)}, f32[16,16,256]{2,0,1:T(8,128)S(1)}, u32[]{:S(2)}, u32[]{:S(2)}) collective-permute-start(f32[16,16,256]{2,0,1:T(8,128)S(1)} %get-tuple-element.18), channel_id=1, source_target_pairs={{0,8},{4,0},{12,4},{20,12},{28,20},{24,28},{16,24},{8,16},{1,9},{5... | collective-permute-start | bytes 786440 | tf_op jit(solution)/shard_map/ppermute | solution.py:71
  159.2 12.6 %collective-permute-start.11 = (f32[16,16,256]{2,0,1:T(8,128)S(1)}, f32[16,16,256]{2,0,1:T(8,128)S(1)}, u32[]{:S(2)}, u32[]{:S(2)}) collective-permute-start(f32[16,16,256]{2,0,1:T(8,128)S(1)} %get-tuple-element.12), channel_id=1, source_target_pairs={{0,8},{4,0},{12,4},{20,12},{28,20},{24,28},{16,24},{8,16},{1,9},{5... | collective-permute-start | bytes 786440 | tf_op jit(solution)/shard_map/ppermute | solution.py:71
  162.4 14.2 %collective-permute-start.14 = (f32[16,16,256]{2,0,1:T(8,128)S(1)}, f32[16,16,256]{2,0,1:T(8,128)S(1)}, u32[]{:S(2)}, u32[]{:S(2)}) collective-permute-start(f32[16,16,256]{2,0,1:T(8,128)S(1)} %get-tuple-element.17), channel_id=1, source_target_pairs={{0,4},{4,12},{12,20},{20,28},{28,24},{24,16},{16,8},{8,0},{1,5},{5... | collective-permute-start | bytes 786440 | tf_op jit(solution)/shard_map/ppermute | solution.py:71
  174.4 9.3 %collective-permute-start.9 = (f32[16,16,256]{2,0,1:T(8,128)}, f32[16,16,256]{2,0,1:T(8,128)S(1)}, u32[]{:S(2)}, u32[]{:S(2)}) collective-permute-start(f32[16,16,256]{2,0,1:T(8,128)} %get-tuple-element.9), channel_id=1, source_target_pairs={{0,4},{4,12},{12,20},{20,28},{28,24},{24,16},{16,8},{8,0},{1,5},{5... | collective-permute-start | bytes 786440 | tf_op jit(solution)/shard_map/ppermute | solution.py:71
  177.4 11.9 %collective-permute-start.15 = (f32[16,16,256]{2,0,1:T(8,128)}, f32[16,16,256]{2,0,1:T(8,128)S(1)}, u32[]{:S(2)}, u32[]{:S(2)}) collective-permute-start(f32[16,16,256]{2,0,1:T(8,128)} %get-tuple-element.15), channel_id=1, source_target_pairs={{0,4},{4,12},{12,20},{20,28},{28,24},{24,16},{16,8},{8,0},{1,5},{5... | collective-permute-start | bytes 786440 | tf_op jit(solution)/shard_map/ppermute | solution.py:71
  179.5 10.2 %collective-permute-start.19 = (f32[16,16,256]{2,0,1:T(8,128)S(1)}, f32[16,16,256]{2,0,1:T(8,128)}, u32[]{:S(2)}, u32[]{:S(2)}) collective-permute-start(f32[16,16,256]{2,0,1:T(8,128)S(1)} %get-tuple-element.16), channel_id=1, source_target_pairs={{0,8},{4,0},{12,4},{20,12},{28,20},{24,28},{16,24},{8,16},{1,9},{5... | collective-permute-start | bytes 786440 | tf_op jit(solution)/shard_map/ppermute | solution.py:71
  185.2 12.2 %collective-permute-start.10 = (f32[16,16,256]{2,0,1:T(8,128)S(1)}, f32[16,16,256]{2,0,1:T(8,128)S(1)}, u32[]{:S(2)}, u32[]{:S(2)}) collective-permute-start(f32[16,16,256]{2,0,1:T(8,128)S(1)} %get-tuple-element.7), channel_id=1, source_target_pairs={{0,4},{4,12},{12,20},{20,28},{28,24},{24,16},{16,8},{8,0},{1,5},{5... | collective-permute-start | bytes 786440 | tf_op jit(solution)/shard_map/ppermute | solution.py:71
  186.9 10.5 %collective-permute-start.13 = (f32[16,16,256]{2,0,1:T(8,128)S(1)}, f32[16,16,256]{2,0,1:T(8,128)S(1)}, u32[]{:S(2)}, u32[]{:S(2)}) collective-permute-start(f32[16,16,256]{2,0,1:T(8,128)S(1)} %get-tuple-element.8), channel_id=1, source_target_pairs={{0,8},{4,0},{12,4},{20,12},{28,20},{24,28},{16,24},{8,16},{1,9},{5... | collective-permute-start | bytes 786440 | tf_op jit(solution)/shard_map/ppermute | solution.py:71
  (24 other events, 229.5 us)

commit v18 on v14

--- a/solution.py
+++ b/solution.py
@@ -90,6 +90,19 @@
             held = lax.dynamic_update_index_in_dim(held, cur, owner, 0)
     return held
 
+def permute_all_to_all(blocks, axis):
+    n = lax.axis_size("feat")
+    me = lax.axis_index("feat")
+    pieces = jnp.stack(jnp.split(blocks, n, axis=axis))
+    by_shift = [lax.dynamic_index_in_dim(pieces, me, axis=0, keepdims=False)]
+    for shift in range(1, n):
+        mine = lax.dynamic_index_in_dim(pieces, (me + shift) % n, axis=0, keepdims=False)
+        by_shift.append(lax.ppermute(mine, "feat", [(f, (f + shift) % n) for f in range(n)]))
+    by_shift = jnp.stack(by_shift)
+    came = [lax.dynamic_index_in_dim(by_shift, (me - src) % n, axis=0, keepdims=False) for src in range(n)]
+    return jnp.concatenate(came, axis=0)
+
+
 def body(ring, activations, cotangent, r_mix, l_mix):
     tok_count = activations.shape[1]
     local_blocks = activations.shape[0] // WIDTH
@@ -110,7 +123,7 @@
     mixed_rows = jnp.einsum(
         "bit,ibo->bot", x_blocks, r_whole, preferred_element_type=jnp.float32
     ).astype(jnp.bfloat16)
-    columns = lax.all_to_all(mixed_rows, "feat", split_axis=1, concat_axis=0, tiled=True)
+    columns = permute_all_to_all(mixed_rows, 1)
     pre_act = jnp.einsum("bst,bsc->cst", columns, l_blocks, preferred_element_type=jnp.float32)
     slope_cols = slope_of(pre_act, g_cols)
     back_cols = jnp.einsum(

time: 203 us -> 197 us (0.970)
  local copies, waits for them, and re-layouts: 36 us -> 31.7 us
    all_to_all x1 -> x0, waiting for transfers between devices: 17.9 us -> none  [body(): lax.all_to_all(mixed_rows, 'feat', split_axis=1, concat_axis=0, tiled=True)]
    ppermute x0 -> x3, waiting for transfers between devices: none -> 16 us  [permute_all_to_all(): lax.ppermute(mine, 'feat', [(f, (f + shift) % n) for f in range(n)])]
    all_to_all x1 -> x0, starting transfers between devices: 4.63 us -> none  [body(): lax.all_to_all(mixed_rows, 'feat', split_axis=1, concat_axis=0, tiled=True)]
    ppermute x0 -> x3, starting transfers between devices: none -> 2.8 us  [permute_all_to_all(): lax.ppermute(mine, 'feat', [(f, (f + shift) % n) for f in range(n)])]
    convert_element_type x1 -> x0, local copies, waits for them, and re-layouts: 2.6 us -> none  [body(): mixed_rows = jnp.einsum('bit,ibo->bot', x_blocks, r_whole, preferred_elem...]
    all_to_all x1 -> x0, local copies, waits for them, and re-layouts: 2.03 us -> none  [body(): lax.all_to_all(mixed_rows, 'feat', split_axis=1, concat_axis=0, tiled=True)]
    unnamed x27 -> x30, local copies, waits for them, and re-layouts: 4.69 us -> 4.93 us
  transfers between devices with their start and end apart: 31 -> 33, of which waited for: 19 -> 21; matrix products, arithmetic and copies ran while one was open for 21% -> 20% of each run, Pallas kernels for 0% -> 0%
where the time goes in v18:
time: 197 us; the launch traced here: 196 us
  waiting for transfers between devices  68.1 us (35%)
  starting transfers between devices  47.2 us (24%)
  local copies, waits for them, and re-layouts  31.7 us (16%)
  between operations  21.5 us (11%)
  matrix products  17.5 us (9%)
  other arithmetic  9.97 us (5%)
    ppermute x21, starting transfers between devices, ring_reduce_scatter(): acc = lax.ppermute(mine if acc is None else acc + mine, 'dp', pairs)  26.4 us
    ppermute x21, waiting for transfers between devices, ring_reduce_scatter(): acc = lax.ppermute(mine if acc is None else acc + mine, 'dp', pairs)  25.5 us
    ppermute x7, waiting for transfers between devices, ring_all_gather(): cur = lax.ppermute(cur, 'dp', pairs)  21.8 us
    ppermute x3, waiting for transfers between devices, permute_all_to_all(): lax.ppermute(mine, 'feat', [(f, (f + shift) % n) for f in range(n)])  16 us
    ppermute x7, starting transfers between devices, ring_all_gather(): cur = lax.ppermute(cur, 'dp', pairs)  8.93 us
    add x9, other arithmetic, ring_reduce_scatter(): acc = lax.ppermute(mine if acc is None else acc + mine, 'dp', pairs)  5.14 us
    dot_general x1, matrix products, body(): jnp.einsum('bst,bsc->cst', columns, l_blocks, preferred_element_type=jnp....  5.09 us
    unnamed x30, local copies, waits for them, and re-layouts  4.93 us
  transfers between devices with their start and end apart: 33, of which 21 were waited for; matrix products, arithmetic and copies ran while one was open for 20% of the time, Pallas kernels for 0%

profile of v18, /device:TPU:0, one launch (start us, length us, event | category | flops | bytes accessed | tf_op | source)
XLA Modules:
  0.0 196.0 jit_solution(15523495781645039433)
XLA Ops:
  3.1 3.0 %collective-permute-start = (bf16[640,256]{1,0:T(8,128)(2,1)S(1)}, bf16[640,256]{1,0:T(8,128)(2,1)}, u32[]{:S(2)}, u32[]{:S(2)}) collective-permute-start(bf16[640,256]{1,0:T(8,128)(2,1)S(1)} %pad_maximum_fusion.2), channel_id=1, source_target_pairs={{0,4},{4,12},{12,20},{20,28},{28,24},{24,16},{16,8},{8,0},{1,5},{5... | collective-permute-start | bytes 983048 | tf_op jit(solution)/shard_map/ppermute | solution.py:88
  6.2 7.7 %collective-permute-done = bf16[640,256]{1,0:T(8,128)(2,1)} collective-permute-done((bf16[640,256]{1,0:T(8,128)(2,1)S(1)}, bf16[640,256]{1,0:T(8,128)(2,1)}, u32[]{:S(2)}, u32[]{:S(2)}) %collective-permute-start) | collective-permute-done | bytes 327712 | tf_op jit(solution)/shard_map/ppermute | solution.py:88
  15.7 4.1 %copy.48 = bf16[16,256,256]{2,0,1:T(8,128)(2,1)} copy(bf16[16,256,256]{2,1,0:T(8,128)(2,1)} %bitcast.177) | data formatting | bytes 4194304 | tf_op jit(solution)/shard_map/reshape | solution.py:112
  19.8 4.6 %all-to-all-start = ((bf16[16,256,256]{2,0,1:T(8,128)(2,1)}), bf16[16,256,256]{2,0,1:T(8,128)(2,1)}, u32[]{:S(2)}, u32[]{:S(2)}) async-start(bf16[16,256,256]{2,0,1:T(8,128)(2,1)} %copy.48), calls=%async_computation | async-start | bytes 4194304 | tf_op jit(solution)/shard_map/all_to_all | solution.py:113
  47.5 6.8 %collective-permute-done.5 = bf16[640,256]{1,0:T(8,128)(2,1)S(1)} collective-permute-done((bf16[640,256]{1,0:T(8,128)(2,1)S(1)}, bf16[640,256]{1,0:T(8,128)(2,1)S(1)}, u32[]{:S(2)}, u32[]{:S(2)}) %collective-permute-start.5) | collective-permute-done | bytes 327712 | tf_op jit(solution)/shard_map/ppermute | solution.py:88
  56.4 7.2 %collective-permute-done.3 = bf16[640,256]{1,0:T(8,128)(2,1)S(1)} collective-permute-done((bf16[640,256]{1,0:T(8,128)(2,1)S(1)}, bf16[640,256]{1,0:T(8,128)(2,1)S(1)}, u32[]{:S(2)}, u32[]{:S(2)}) %collective-permute-start.3) | collective-permute-done | bytes 327712 | tf_op jit(solution)/shard_map/ppermute | solution.py:88
  75.0 2.2 %copy.49 = f32[16,4,64,256]{3,0,1,2:T(8,128)S(1)} copy(bf16[16,4,64,256]{3,0,2,1:T(8,128)(2,1)} %bitcast.86) | data formatting | bytes 6291456 | tf_op jit(solution)/shard_map/convert_element_type | solution.py:19
  77.2 5.4 %collective-permute-done.7 = bf16[16,64,256]{2,1,0:T(8,128)(2,1)} collective-permute-done((bf16[16,64,256]{2,1,0:T(8,128)(2,1)}, bf16[16,64,256]{2,1,0:T(8,128)(2,1)}, u32[]{:S(2)}, u32[]{:S(2)}) %collective-permute-start.7) | collective-permute-done | bytes 524320 | tf_op jit(solution)/shard_map/ppermute | solution.py:100
  83.7 9.5 %collective-permute-done.9 = bf16[16,64,256]{2,1,0:T(8,128)(2,1)} collective-permute-done((bf16[16,64,256]{2,1,0:T(8,128)(2,1)}, bf16[16,64,256]{2,1,0:T(8,128)(2,1)}, u32[]{:S(2)}, u32[]{:S(2)}) %collective-permute-start.9) | collective-permute-done | bytes 524320 | tf_op jit(solution)/shard_map/ppermute | solution.py:100
  96.4 5.1 %fusion.6 = bf16[64,64,256]{2,0,1:T(8,128)(2,1)S(1)} fusion(f32[16,4,64,256]{3,0,1,2:T(8,128)S(1)} %copy.49, bf16[64,64,256]{2,0,1:T(8,128)(2,1)S(1)} %copy_dynamic-update-slice_fusion, bf16[64,64,64]{2,1,0:T(8,128)(2,1)S(1)} %reshape.104), kind=kOutput, calls=%fused_computation.8 | convolution fusion | flops 155189248 | bytes 8912896 | tf_op jit(solution)/shard_map/bst,bsc->cst/dot_general | solution.py:127
  102.8 2.5 %copy.57 = bf16[64,64,256]{2,0,1:T(8,128)(2,1)} copy(bf16[64,64,256]{2,1,0:T(8,128)(2,1)S(1)} %convolution_convert_fusion) | data formatting | bytes 4194304 | tf_op jit(solution)/shard_map/convert_element_type | solution.py:131
  105.3 4.4 %all-to-all-start.1 = ((bf16[64,64,256]{2,0,1:T(8,128)(2,1)}), bf16[64,64,256]{2,0,1:T(8,128)(2,1)}, u32[]{:S(2)}, u32[]{:S(2)}) async-start(bf16[64,64,256]{2,0,1:T(8,128)(2,1)} %copy.57), calls=%async_computation.1 | async-start | bytes 4194304 | tf_op jit(solution)/shard_map/all_to_all | solution.py:136
  109.8 4.3 %multiply_bitcast_fusion = f32[64,64,64]{0,2,1:T(8,128)} fusion(bf16[64,64,256]{2,0,1:T(8,128)(2,1)} %copy-done.5, bf16[64,64,256]{2,0,1:T(8,128)(2,1)} %copy-done.9), kind=kOutput, calls=%fused_computation.18 | convolution fusion | flops 134479872 | bytes 5242880 | tf_op jit(solution)/shard_map/bst,cst->bsc/dot_general | solution.py:132
  114.1 3.8 %copy.60 = f32[64,64,64]{2,1,0:T(8,128)} copy(f32[64,64,64]{0,2,1:T(8,128)} %multiply_bitcast_fusion) | data formatting | bytes 2097152 | tf_op jit(solution)/shard_map/mul | solution.py:133
  123.1 5.2 %collective-permute-done.27 = f32[8,64,64]{2,1,0:T(8,128)S(1)} collective-permute-done((f32[8,64,64]{2,1,0:T(8,128)S(1)}, f32[8,64,64]{2,1,0:T(8,128)S(1)}, u32[]{:S(2)}, u32[]{:S(2)}) %collective-permute-start.27) | collective-permute-done | bytes 131104 | tf_op jit(solution)/shard_map/ppermute | solution.py:71
  131.0 4.7 %all-to-all-done.1 = bf16[64,64,256]{2,0,1:T(8,128)(2,1)} async-done(((bf16[64,64,256]{2,0,1:T(8,128)(2,1)}), bf16[64,64,256]{2,0,1:T(8,128)(2,1)}, u32[]{:S(2)}, u32[]{:S(2)}) %all-to-all-start.1) | async-done | bytes 2097184 | tf_op jit(solution)/shard_map/all_to_all | solution.py:136
  146.6 2.3 %collective-permute-done.10 = f32[16,16,256]{2,0,1:T(8,128)S(1)} collective-permute-done((f32[16,16,256]{2,0,1:T(8,128)S(1)}, f32[16,16,256]{2,0,1:T(8,128)S(1)}, u32[]{:S(2)}, u32[]{:S(2)}) %collective-permute-start.10) | collective-permute-done | bytes 262176 | tf_op jit(solution)/shard_map/ppermute | solution.py:71
  152.3 2.2 %collective-permute-done.25 = f32[8,64,64]{2,1,0:T(8,128)S(1)} collective-permute-done((f32[8,64,64]{2,1,0:T(8,128)S(1)}, f32[8,64,64]{2,1,0:T(8,128)S(1)}, u32[]{:S(2)}, u32[]{:S(2)}) %collective-permute-start.25) | collective-permute-done | bytes 131104 | tf_op jit(solution)/shard_map/ppermute | solution.py:71
  158.0 3.9 %collective-permute-done.14 = f32[16,16,256]{2,0,1:T(8,128)S(1)} collective-permute-done((f32[16,16,256]{2,0,1:T(8,128)S(1)}, f32[16,16,256]{2,0,1:T(8,128)S(1)}, u32[]{:S(2)}, u32[]{:S(2)}) %collective-permute-start.14) | collective-permute-done | bytes 262176 | tf_op jit(solution)/shard_map/ppermute | solution.py:71
  162.3 3.5 %collective-permute-done.11 = f32[16,16,256]{2,0,1:T(8,128)S(1)} collective-permute-done((f32[16,16,256]{2,0,1:T(8,128)S(1)}, f32[16,16,256]{2,0,1:T(8,128)S(1)}, u32[]{:S(2)}, u32[]{:S(2)}) %collective-permute-start.11) | collective-permute-done | bytes 262176 | tf_op jit(solution)/shard_map/ppermute | solution.py:71
  174.1 2.8 %collective-permute-done.12 = f32[16,16,256]{2,0,1:T(8,128)S(1)} collective-permute-done((f32[16,16,256]{2,0,1:T(8,128)}, f32[16,16,256]{2,0,1:T(8,128)S(1)}, u32[]{:S(2)}, u32[]{:S(2)}) %collective-permute-start.12) | collective-permute-done | bytes 262176 | tf_op jit(solution)/shard_map/ppermute | solution.py:71
  177.0 1.9 collective-permute-done.15
  182.6 1.9 collective-permute-done.22
  187.8 4.5 %add_convert_fusion = bf16[16,256,256]{2,1,0:T(8,128)(2,1)} fusion(bf16[16,256,256]{2,1,0:T(8,128)(2,1)} %bitcast.178, bf16[256,16,256]{2,0,1:T(8,128)(2,1)} %bitcast.175, bf16[256,16,256]{2,1,0:T(8,128)(2,1)S(1)} %bitcast.173), kind=kOutput, calls=%fused_computation.14 | convolution fusion | flops 540016640 | bytes 8388608 | tf_op jit(solution)/shard_map/obt,ibo->bit/dot_general | solution.py:137
  (126 shorter events, 70.7 us)
Async XLA Ops:
  3.1 10.9 %collective-permute-start = (bf16[640,256]{1,0:T(8,128)(2,1)S(1)}, bf16[640,256]{1,0:T(8,128)(2,1)}, u32[]{:S(2)}, u32[]{:S(2)}) collective-permute-start(bf16[640,256]{1,0:T(8,128)(2,1)S(1)} %pad_maximum_fusion.2), channel_id=1, source_target_pairs={{0,4},{4,12},{12,20},{20,28},{28,24},{24,16},{16,8},{8,0},{1,5},{5... | collective-permute-start | bytes 983048 | tf_op jit(solution)/shard_map/ppermute | solution.py:88
  6.1 38.0 %collective-permute-start.4 = (bf16[640,256]{1,0:T(8,128)(2,1)S(1)}, bf16[640,256]{1,0:T(8,128)(2,1)S(1)}, u32[]{:S(2)}, u32[]{:S(2)}) collective-permute-start(bf16[640,256]{1,0:T(8,128)(2,1)S(1)} %pad_maximum_fusion.2), channel_id=1, source_target_pairs={{0,8},{4,0},{12,4},{20,12},{28,20},{24,28},{16,24},{8,16},{1,9},{5... | collective-permute-start | bytes 983048 | tf_op jit(solution)/shard_map/ppermute | solution.py:88
  14.0 30.6 %collective-permute-start.1 = (bf16[640,256]{1,0:T(8,128)(2,1)}, bf16[640,256]{1,0:T(8,128)(2,1)S(1)}, u32[]{:S(2)}, u32[]{:S(2)}) collective-permute-start(bf16[640,256]{1,0:T(8,128)(2,1)} %collective-permute-done), channel_id=1, source_target_pairs={{0,4},{4,12},{12,20},{20,28},{28,24},{24,16},{16,8},{8,0},{1,5},{5... | collective-permute-start | bytes 983048 | tf_op jit(solution)/shard_map/ppermute | solution.py:88
  19.8 55.2 %all-to-all-start = ((bf16[16,256,256]{2,0,1:T(8,128)(2,1)}), bf16[16,256,256]{2,0,1:T(8,128)(2,1)}, u32[]{:S(2)}, u32[]{:S(2)}) async-start(bf16[16,256,256]{2,0,1:T(8,128)(2,1)} %copy.48), calls=%async_computation | async-start | bytes 4194304 | tf_op jit(solution)/shard_map/all_to_all | solution.py:113
  68.6 14.0 %collective-permute-start.7 = (bf16[16,64,256]{2,1,0:T(8,128)(2,1)}, bf16[16,64,256]{2,1,0:T(8,128)(2,1)}, u32[]{:S(2)}, u32[]{:S(2)}) collective-permute-start(bf16[16,64,256]{2,1,0:T(8,128)(2,1)} %get-tuple-element.30), channel_id=1, source_target_pairs={{0,1},{1,2},{2,3},{3,0},{4,5},{5,6},{6,7},{7,4},{8,9},{9,10},{10,1... | collective-permute-start | bytes 1572872 | tf_op jit(solution)/shard_map/ppermute | solution.py:100
  68.6 15.1 %collective-permute-start.8 = (bf16[16,64,256]{2,1,0:T(8,128)(2,1)}, bf16[16,64,256]{2,1,0:T(8,128)(2,1)}, u32[]{:S(2)}, u32[]{:S(2)}) collective-permute-start(bf16[16,64,256]{2,1,0:T(8,128)(2,1)} %get-tuple-element.29), channel_id=1, source_target_pairs={{0,2},{1,3},{2,0},{3,1},{4,6},{5,7},{6,4},{7,5},{8,10},{9,11},{10,... | collective-permute-start | bytes 1572872 | tf_op jit(solution)/shard_map/ppermute | solution.py:100
  70.0 23.3 %collective-permute-start.9 = (bf16[16,64,256]{2,1,0:T(8,128)(2,1)}, bf16[16,64,256]{2,1,0:T(8,128)(2,1)}, u32[]{:S(2)}, u32[]{:S(2)}) collective-permute-start(bf16[16,64,256]{2,1,0:T(8,128)(2,1)} %get-tuple-element.28), channel_id=1, source_target_pairs={{0,3},{1,0},{2,1},{3,2},{4,7},{5,4},{6,5},{7,6},{8,11},{9,8},{10,9... | collective-permute-start | bytes 1572872 | tf_op jit(solution)/shard_map/ppermute | solution.py:100
  105.3 30.4 %all-to-all-start.1 = ((bf16[64,64,256]{2,0,1:T(8,128)(2,1)}), bf16[64,64,256]{2,0,1:T(8,128)(2,1)}, u32[]{:S(2)}, u32[]{:S(2)}) async-start(bf16[64,64,256]{2,0,1:T(8,128)(2,1)} %copy.57), calls=%async_computation.1 | async-start | bytes 4194304 | tf_op jit(solution)/shard_map/all_to_all | solution.py:136
  122.7 19.1 %collective-permute-start.24 = (f32[8,64,64]{2,1,0:T(8,128)S(1)}, f32[8,64,64]{2,1,0:T(8,128)S(1)}, u32[]{:S(2)}, u32[]{:S(2)}) collective-permute-start(f32[8,64,64]{2,1,0:T(8,128)S(1)} %get-tuple-element.9), channel_id=1, source_target_pairs={{0,4},{4,12},{12,20},{20,28},{28,24},{24,16},{16,8},{8,0},{1,5},{5... | collective-permute-start | bytes 393224 | tf_op jit(solution)/shard_map/ppermute | solution.py:71
  129.2 12.6 %collective-permute-start.28 = (f32[8,64,64]{2,1,0:T(8,128)S(1)}, f32[8,64,64]{2,1,0:T(8,128)S(1)}, u32[]{:S(2)}, u32[]{:S(2)}) collective-permute-start(f32[8,64,64]{2,1,0:T(8,128)S(1)} %bitcast_add_fusion.2), channel_id=1, source_target_pairs={{0,8},{4,0},{12,4},{20,12},{28,20},{24,28},{16,24},{8,16},{1,9},{5... | collective-permute-start | bytes 393224 | tf_op jit(solution)/shard_map/ppermute | solution.py:71
  142.8 11.7 %collective-permute-start.25 = (f32[8,64,64]{2,1,0:T(8,128)S(1)}, f32[8,64,64]{2,1,0:T(8,128)S(1)}, u32[]{:S(2)}, u32[]{:S(2)}) collective-permute-start(f32[8,64,64]{2,1,0:T(8,128)S(1)} %get-tuple-element.7), channel_id=1, source_target_pairs={{0,4},{4,12},{12,20},{20,28},{28,24},{24,16},{16,8},{8,0},{1,5},{5... | collective-permute-start | bytes 393224 | tf_op jit(solution)/shard_map/ppermute | solution.py:71
  144.5 11.8 %collective-permute-start.29 = (f32[8,64,64]{2,1,0:T(8,128)S(1)}, f32[8,64,64]{2,1,0:T(8,128)S(1)}, u32[]{:S(2)}, u32[]{:S(2)}) collective-permute-start(f32[8,64,64]{2,1,0:T(8,128)S(1)} %get-tuple-element.8), channel_id=1, source_target_pairs={{0,8},{4,0},{12,4},{20,12},{28,20},{24,28},{16,24},{8,16},{1,9},{5... | collective-permute-start | bytes 393224 | tf_op jit(solution)/shard_map/ppermute | solution.py:71
  144.8 17.1 %collective-permute-start.14 = (f32[16,16,256]{2,0,1:T(8,128)S(1)}, f32[16,16,256]{2,0,1:T(8,128)S(1)}, u32[]{:S(2)}, u32[]{:S(2)}) collective-permute-start(f32[16,16,256]{2,0,1:T(8,128)S(1)} %get-tuple-element.16), channel_id=1, source_target_pairs={{0,8},{4,0},{12,4},{20,12},{28,20},{24,28},{16,24},{8,16},{1,9},{5... | collective-permute-start | bytes 786440 | tf_op jit(solution)/shard_map/ppermute | solution.py:71
  148.9 19.3 %collective-permute-start.17 = (f32[16,16,256]{2,0,1:T(8,128)S(1)}, f32[16,16,256]{2,0,1:T(8,128)S(1)}, u32[]{:S(2)}, u32[]{:S(2)}) collective-permute-start(f32[16,16,256]{2,0,1:T(8,128)S(1)} %get-tuple-element.21), channel_id=1, source_target_pairs={{0,4},{4,12},{12,20},{20,28},{28,24},{24,16},{16,8},{8,0},{1,5},{5... | collective-permute-start | bytes 786440 | tf_op jit(solution)/shard_map/ppermute | solution.py:71
  150.7 15.0 %collective-permute-start.11 = (f32[16,16,256]{2,0,1:T(8,128)S(1)}, f32[16,16,256]{2,0,1:T(8,128)S(1)}, u32[]{:S(2)}, u32[]{:S(2)}) collective-permute-start(f32[16,16,256]{2,0,1:T(8,128)S(1)} %bitcast_add_fusion.16), channel_id=1, source_target_pairs={{0,4},{4,12},{12,20},{20,28},{28,24},{24,16},{16,8},{8,0},{1,5},{5... | collective-permute-start | bytes 786440 | tf_op jit(solution)/shard_map/ppermute | solution.py:71
  154.5 14.1 %collective-permute-start.21 = (f32[16,16,256]{2,0,1:T(8,128)S(1)}, f32[16,16,256]{2,0,1:T(8,128)S(1)}, u32[]{:S(2)}, u32[]{:S(2)}) collective-permute-start(f32[16,16,256]{2,0,1:T(8,128)S(1)} %bitcast_add_fusion.8), channel_id=1, source_target_pairs={{0,8},{4,0},{12,4},{20,12},{28,20},{24,28},{16,24},{8,16},{1,9},{5... | collective-permute-start | bytes 786440 | tf_op jit(solution)/shard_map/ppermute | solution.py:71
  156.4 15.0 %collective-permute-start.26 = (f32[8,64,64]{2,1,0:T(8,128)S(1)}, f32[8,64,64]{2,1,0:T(8,128)S(1)}, u32[]{:S(2)}, u32[]{:S(2)}) collective-permute-start(f32[8,64,64]{2,1,0:T(8,128)S(1)} %get-tuple-element.5), channel_id=1, source_target_pairs={{0,4},{4,12},{12,20},{20,28},{28,24},{24,16},{16,8},{8,0},{1,5},{5... | collective-permute-start | bytes 393224 | tf_op jit(solution)/shard_map/ppermute | solution.py:71
  161.9 11.2 %collective-permute-start.30 = (f32[8,64,64]{2,1,0:T(8,128)S(1)}, f32[8,64,64]{2,1,0:T(8,128)S(1)}, u32[]{:S(2)}, u32[]{:S(2)}) collective-permute-start(f32[8,64,64]{2,1,0:T(8,128)S(1)} %get-tuple-element.6), channel_id=1, source_target_pairs={{0,8},{4,0},{12,4},{20,12},{28,20},{24,28},{16,24},{8,16},{1,9},{5... | collective-permute-start | bytes 393224 | tf_op jit(solution)/shard_map/ppermute | solution.py:71
  166.5 10.5 %collective-permute-start.12 = (f32[16,16,256]{2,0,1:T(8,128)}, f32[16,16,256]{2,0,1:T(8,128)S(1)}, u32[]{:S(2)}, u32[]{:S(2)}) collective-permute-start(f32[16,16,256]{2,0,1:T(8,128)} %get-tuple-element.13), channel_id=1, source_target_pairs={{0,4},{4,12},{12,20},{20,28},{28,24},{24,16},{16,8},{8,0},{1,5},{5... | collective-permute-start | bytes 786440 | tf_op jit(solution)/shard_map/ppermute | solution.py:71
  168.2 10.7 %collective-permute-start.15 = (f32[16,16,256]{2,0,1:T(8,128)S(1)}, f32[16,16,256]{2,0,1:T(8,128)}, u32[]{:S(2)}, u32[]{:S(2)}) collective-permute-start(f32[16,16,256]{2,0,1:T(8,128)S(1)} %get-tuple-element.14), channel_id=1, source_target_pairs={{0,8},{4,0},{12,4},{20,12},{28,20},{24,28},{16,24},{8,16},{1,9},{5... | collective-permute-start | bytes 786440 | tf_op jit(solution)/shard_map/ppermute | solution.py:71
  169.3 13.3 %collective-permute-start.18 = (f32[16,16,256]{2,0,1:T(8,128)}, f32[16,16,256]{2,0,1:T(8,128)S(1)}, u32[]{:S(2)}, u32[]{:S(2)}) collective-permute-start(f32[16,16,256]{2,0,1:T(8,128)} %get-tuple-element.19), channel_id=1, source_target_pairs={{0,4},{4,12},{12,20},{20,28},{28,24},{24,16},{16,8},{8,0},{1,5},{5... | collective-permute-start | bytes 786440 | tf_op jit(solution)/shard_map/ppermute | solution.py:71
  171.3 13.2 %collective-permute-start.22 = (f32[16,16,256]{2,0,1:T(8,128)S(1)}, f32[16,16,256]{2,0,1:T(8,128)}, u32[]{:S(2)}, u32[]{:S(2)}) collective-permute-start(f32[16,16,256]{2,0,1:T(8,128)S(1)} %get-tuple-element.20), channel_id=1, source_target_pairs={{0,8},{4,0},{12,4},{20,12},{28,20},{24,28},{16,24},{8,16},{1,9},{5... | collective-permute-start | bytes 786440 | tf_op jit(solution)/shard_map/ppermute | solution.py:71
  180.1 12.2 %collective-permute-start.13 = (f32[16,16,256]{2,0,1:T(8,128)S(1)}, f32[16,16,256]{2,0,1:T(8,128)S(1)}, u32[]{:S(2)}, u32[]{:S(2)}) collective-permute-start(f32[16,16,256]{2,0,1:T(8,128)S(1)} %get-tuple-element.11), channel_id=1, source_target_pairs={{0,4},{4,12},{12,20},{20,28},{28,24},{24,16},{16,8},{8,0},{1,5},{5... | collective-permute-start | bytes 786440 | tf_op jit(solution)/shard_map/ppermute | solution.py:71
  181.7 10.6 %collective-permute-start.16 = (f32[16,16,256]{2,0,1:T(8,128)S(1)}, f32[16,16,256]{2,0,1:T(8,128)S(1)}, u32[]{:S(2)}, u32[]{:S(2)}) collective-permute-start(f32[16,16,256]{2,0,1:T(8,128)S(1)} %get-tuple-element.12), channel_id=1, source_target_pairs={{0,8},{4,0},{12,4},{20,12},{28,20},{24,28},{16,24},{8,16},{1,9},{5... | collective-permute-start | bytes 786440 | tf_op jit(solution)/shard_map/ppermute | solution.py:71
  (22 other events, 263.1 us)

commit v19 on v18

--- a/solution.py
+++ b/solution.py
@@ -133,7 +133,7 @@
     l_term = (l_term * grad_scale).reshape(n_dp, -1, local_cols, BLOCKS)
     grad_l = ring_reduce_scatter(l_term, ring, lead=-1)
     grad_l = jnp.transpose(grad_l, (1, 0, 2)).reshape(local_cols, -1)
-    back_rows = lax.all_to_all(back_cols, "feat", split_axis=1, concat_axis=0, tiled=True)
+    back_rows = permute_all_to_all(back_cols, 1)
     through_r = jnp.einsum("obt,ibo->bit", back_rows, r_whole, preferred_element_type=jnp.float32)
     grad_x = (
         (g_blocks.astype(jnp.float32) + through_r)

time: 197 us -> 193 us (0.980)
  waiting for transfers between devices: 68.1 us -> 73.9 us
  matrix products: 17.5 us -> 12.9 us
  starting transfers between devices: 47.2 us -> 45.1 us
  local copies, waits for them, and re-layouts: 31.7 us -> 29.6 us
    ppermute x21, waiting for transfers between devices: 25.5 us -> 33.8 us  [ring_reduce_scatter(): acc = lax.ppermute(mine if acc is None else acc + mine, 'dp', pairs)]
    all_to_all x1 -> x0, waiting for transfers between devices: 4.72 us -> none  [body(): lax.all_to_all(back_cols, 'feat', split_axis=1, concat_axis=0, tiled=True)]
    all_to_all x1 -> x0, starting transfers between devices: 4.45 us -> none  [body(): lax.all_to_all(back_cols, 'feat', split_axis=1, concat_axis=0, tiled=True)]
    add x9, other arithmetic: 5.14 us -> 2.39 us  [ring_reduce_scatter(): acc = lax.ppermute(mine if acc is None else acc + mine, 'dp', pairs)]
    convert_element_type x1 -> x0, local copies, waits for them, and re-layouts: 2.51 us -> none  [body(): back_cols = jnp.einsum('cst,bsc->sbt', slope_cols, l_blocks, preferred_el...]
    ppermute x3 -> x6, starting transfers between devices: 2.8 us -> 5.14 us  [permute_all_to_all(): lax.ppermute(mine, 'feat', [(f, (f + shift) % n) for f in range(n)])]
    dot_general x1, matrix products: 4.33 us -> 2.01 us  [body(): jnp.einsum('bst,cst->bsc', columns, slope_cols, preferred_element_type=jn...]
    ppermute x3 -> x6, waiting for transfers between devices: 16 us -> 18.3 us  [permute_all_to_all(): lax.ppermute(mine, 'feat', [(f, (f + shift) % n) for f in range(n)])]
  transfers between devices with their start and end apart: 33 -> 35, of which waited for: 21 -> 19; matrix products, arithmetic and copies ran while one was open for 20% -> 18% of each run, Pallas kernels for 0% -> 0%
where the time goes in v19:
time: 193 us; the launch traced here: 192 us
  waiting for transfers between devices  73.9 us (38%)
  starting transfers between devices  45.1 us (23%)
  local copies, waits for them, and re-layouts  29.6 us (15%)
  between operations  21.6 us (11%)
  matrix products  12.9 us (7%)
  other arithmetic  9.28 us (5%)
    ppermute x21, waiting for transfers between devices, ring_reduce_scatter(): acc = lax.ppermute(mine if acc is None else acc + mine, 'dp', pairs)  33.8 us
    ppermute x21, starting transfers between devices, ring_reduce_scatter(): acc = lax.ppermute(mine if acc is None else acc + mine, 'dp', pairs)  26.5 us
    ppermute x7, waiting for transfers between devices, ring_all_gather(): cur = lax.ppermute(cur, 'dp', pairs)  21.8 us
    ppermute x6, waiting for transfers between devices, permute_all_to_all(): lax.ppermute(mine, 'feat', [(f, (f + shift) % n) for f in range(n)])  18.3 us
    ppermute x7, starting transfers between devices, ring_all_gather(): cur = lax.ppermute(cur, 'dp', pairs)  8.93 us
    ppermute x6, starting transfers between devices, permute_all_to_all(): lax.ppermute(mine, 'feat', [(f, (f + shift) % n) for f in range(n)])  5.14 us
    dot_general x1, matrix products, body(): jnp.einsum('bst,bsc->cst', columns, l_blocks, preferred_element_type=jnp....  5.08 us
    unnamed x29, local copies, waits for them, and re-layouts  4.67 us
  transfers between devices with their start and end apart: 35, of which 19 were waited for; matrix products, arithmetic and copies ran while one was open for 18% of the time, Pallas kernels for 0%

profile of v19, /device:TPU:0, one launch (start us, length us, event | category | flops | bytes accessed | tf_op | source)
XLA Modules:
  0.0 192.4 jit_solution(656429067144878010)
XLA Ops:
  3.1 3.0 %collective-permute-start = (bf16[640,256]{1,0:T(8,128)(2,1)S(1)}, bf16[640,256]{1,0:T(8,128)(2,1)}, u32[]{:S(2)}, u32[]{:S(2)}) collective-permute-start(bf16[640,256]{1,0:T(8,128)(2,1)S(1)} %pad_maximum_fusion.4), channel_id=1, source_target_pairs={{0,4},{4,12},{12,20},{20,28},{28,24},{24,16},{16,8},{8,0},{1,5},{5... | collective-permute-start | bytes 983048 | tf_op jit(solution)/shard_map/ppermute | solution.py:88
  6.2 7.7 %collective-permute-done = bf16[640,256]{1,0:T(8,128)(2,1)} collective-permute-done((bf16[640,256]{1,0:T(8,128)(2,1)S(1)}, bf16[640,256]{1,0:T(8,128)(2,1)}, u32[]{:S(2)}, u32[]{:S(2)}) %collective-permute-start) | collective-permute-done | bytes 327712 | tf_op jit(solution)/shard_map/ppermute | solution.py:88
  15.7 4.1 %copy.53 = bf16[16,256,256]{2,0,1:T(8,128)(2,1)} copy(bf16[16,256,256]{2,1,0:T(8,128)(2,1)} %bitcast.196) | data formatting | bytes 4194304 | tf_op jit(solution)/shard_map/reshape | solution.py:112
  19.8 4.6 %all-to-all-start = ((bf16[16,256,256]{2,0,1:T(8,128)(2,1)}), bf16[16,256,256]{2,0,1:T(8,128)(2,1)}, u32[]{:S(2)}, u32[]{:S(2)}) async-start(bf16[16,256,256]{2,0,1:T(8,128)(2,1)} %copy.53), calls=%async_computation | async-start | bytes 4194304 | tf_op jit(solution)/shard_map/all_to_all | solution.py:113
  47.5 6.8 %collective-permute-done.5 = bf16[640,256]{1,0:T(8,128)(2,1)S(1)} collective-permute-done((bf16[640,256]{1,0:T(8,128)(2,1)S(1)}, bf16[640,256]{1,0:T(8,128)(2,1)S(1)}, u32[]{:S(2)}, u32[]{:S(2)}) %collective-permute-start.5) | collective-permute-done | bytes 327712 | tf_op jit(solution)/shard_map/ppermute | solution.py:88
  56.4 7.2 %collective-permute-done.3 = bf16[640,256]{1,0:T(8,128)(2,1)S(1)} collective-permute-done((bf16[640,256]{1,0:T(8,128)(2,1)S(1)}, bf16[640,256]{1,0:T(8,128)(2,1)S(1)}, u32[]{:S(2)}, u32[]{:S(2)}) %collective-permute-start.3) | collective-permute-done | bytes 327712 | tf_op jit(solution)/shard_map/ppermute | solution.py:88
  71.5 1.9 slice.17
  75.0 2.2 %copy.54 = f32[16,4,64,256]{3,0,1,2:T(8,128)S(1)} copy(bf16[16,4,64,256]{3,0,2,1:T(8,128)(2,1)} %bitcast.96) | data formatting | bytes 6291456 | tf_op jit(solution)/shard_map/convert_element_type | solution.py:19
  77.3 5.4 %collective-permute-done.7 = bf16[16,64,256]{2,1,0:T(8,128)(2,1)} collective-permute-done((bf16[16,64,256]{2,1,0:T(8,128)(2,1)}, bf16[16,64,256]{2,1,0:T(8,128)(2,1)}, u32[]{:S(2)}, u32[]{:S(2)}) %collective-permute-start.7) | collective-permute-done | bytes 524320 | tf_op jit(solution)/shard_map/ppermute | solution.py:100
  83.8 9.5 %collective-permute-done.9 = bf16[16,64,256]{2,1,0:T(8,128)(2,1)} collective-permute-done((bf16[16,64,256]{2,1,0:T(8,128)(2,1)}, bf16[16,64,256]{2,1,0:T(8,128)(2,1)}, u32[]{:S(2)}, u32[]{:S(2)}) %collective-permute-start.9) | collective-permute-done | bytes 524320 | tf_op jit(solution)/shard_map/ppermute | solution.py:100
  96.4 5.1 %fusion.6 = bf16[64,64,256]{2,0,1:T(8,128)(2,1)S(1)} fusion(f32[16,4,64,256]{3,0,1,2:T(8,128)S(1)} %copy.54, bf16[64,64,256]{2,0,1:T(8,128)(2,1)S(1)} %copy_dynamic-update-slice_fusion.4, bf16[64,64,64]{2,1,0:T(8,128)(2,1)S(1)} %reshape.104), kind=kOutput, calls=%fused_computation.8 | convolution fusion | flops 155189248 | bytes 8912896 | tf_op jit(solution)/shard_map/bst,bsc->cst/dot_general | solution.py:127
  106.8 2.0 %multiply_bitcast_fusion = f32[64,64,64]{0,2,1:T(8,128)} fusion(bf16[64,64,256]{2,0,1:T(8,128)(2,1)S(1)} %fusion.6, bf16[64,64,256]{2,0,1:T(8,128)(2,1)S(1)} %copy_dynamic-update-slice_fusion.4), kind=kOutput, calls=%fused_computation.20 | convolution fusion | flops 134479872 | bytes 5242880 | tf_op jit(solution)/shard_map/bst,cst->bsc/dot_general | solution.py:132
  108.8 3.8 %copy.67 = f32[64,64,64]{2,1,0:T(8,128)} copy(f32[64,64,64]{0,2,1:T(8,128)} %multiply_bitcast_fusion) | data formatting | bytes 2097152 | tf_op jit(solution)/shard_map/mul | solution.py:133
  118.4 5.0 %collective-permute-done.30 = f32[8,64,64]{2,1,0:T(8,128)} collective-permute-done((f32[8,64,64]{2,1,0:T(8,128)}, f32[8,64,64]{2,1,0:T(8,128)}, u32[]{:S(2)}, u32[]{:S(2)}) %collective-permute-start.30) | collective-permute-done | bytes 131104 | tf_op jit(solution)/shard_map/ppermute | solution.py:71
  124.5 1.8 collective-permute-start.31
  126.3 2.2 %collective-permute-done.12 = bf16[64,16,256]{2,1,0:T(8,128)(2,1)} collective-permute-done((bf16[64,16,256]{2,1,0:T(8,128)(2,1)S(1)}, bf16[64,16,256]{2,1,0:T(8,128)(2,1)}, u32[]{:S(2)}, u32[]{:S(2)}) %collective-permute-start.12) | collective-permute-done | bytes 524320 | tf_op jit(solution)/shard_map/ppermute | solution.py:100
  144.4 1.9 collective-permute-done.28
  150.1 3.9 %collective-permute-done.17 = f32[16,16,256]{2,0,1:T(8,128)S(1)} collective-permute-done((f32[16,16,256]{2,0,1:T(8,128)S(1)}, f32[16,16,256]{2,0,1:T(8,128)S(1)}, u32[]{:S(2)}, u32[]{:S(2)}) %collective-permute-start.17) | collective-permute-done | bytes 262176 | tf_op jit(solution)/shard_map/ppermute | solution.py:71
  154.0 3.5 %collective-permute-done.14 = f32[16,16,256]{2,0,1:T(8,128)S(1)} collective-permute-done((f32[16,16,256]{2,0,1:T(8,128)S(1)}, f32[16,16,256]{2,0,1:T(8,128)S(1)}, u32[]{:S(2)}, u32[]{:S(2)}) %collective-permute-start.14) | collective-permute-done | bytes 262176 | tf_op jit(solution)/shard_map/ppermute | solution.py:71
  161.9 2.3 %add_convert_fusion = bf16[16,256,256]{2,1,0:T(8,128)(2,1)} fusion(bf16[16,256,256]{2,1,0:T(8,128)(2,1)S(1)} %bitcast.197, bf16[256,16,256]{2,0,1:T(8,128)(2,1)S(1)} %copy_dynamic-update-slice_fusion, bf16[256,16,256]{2,1,0:T(8,128)(2,1)S(1)} %bitcast.194), kind=kOutput, calls=%fused_computation.14 | convolution fusion | flops 540016640 | bytes 8388608 | tf_op jit(solution)/shard_map/obt,ibo->bit/dot_general | solution.py:137
  164.2 4.6 %collective-permute-done.15 = f32[16,16,256]{2,0,1:T(8,128)S(1)} collective-permute-done((f32[16,16,256]{2,0,1:T(8,128)S(1)}, f32[16,16,256]{2,0,1:T(8,128)S(1)}, u32[]{:S(2)}, u32[]{:S(2)}) %collective-permute-start.15) | collective-permute-done | bytes 262176 | tf_op jit(solution)/shard_map/ppermute | solution.py:71
  171.0 3.4 %collective-permute-done.21 = f32[16,16,256]{2,0,1:T(8,128)S(1)} collective-permute-done((f32[16,16,256]{2,0,1:T(8,128)S(1)}, f32[16,16,256]{2,0,1:T(8,128)S(1)}, u32[]{:S(2)}, u32[]{:S(2)}) %collective-permute-start.21) | collective-permute-done | bytes 262176 | tf_op jit(solution)/shard_map/ppermute | solution.py:71
  180.1 4.6 %collective-permute-done.19 = f32[16,16,256]{2,0,1:T(8,128)S(1)} collective-permute-done((f32[16,16,256]{2,0,1:T(8,128)S(1)}, f32[16,16,256]{2,0,1:T(8,128)S(1)}, u32[]{:S(2)}, u32[]{:S(2)}) %collective-permute-start.19) | collective-permute-done | bytes 262176 | tf_op jit(solution)/shard_map/ppermute | solution.py:71
  186.2 4.3 %collective-permute-done.26 = f32[16,16,256]{2,0,1:T(8,128)} collective-permute-done((f32[16,16,256]{2,0,1:T(8,128)}, f32[16,16,256]{2,0,1:T(8,128)}, u32[]{:S(2)}, u32[]{:S(2)}) %collective-permute-start.26) | collective-permute-done | bytes 262176 | tf_op jit(solution)/shard_map/ppermute | solution.py:71
  (133 shorter events, 69.8 us)
Async XLA Ops:
  3.1 10.9 %collective-permute-start = (bf16[640,256]{1,0:T(8,128)(2,1)S(1)}, bf16[640,256]{1,0:T(8,128)(2,1)}, u32[]{:S(2)}, u32[]{:S(2)}) collective-permute-start(bf16[640,256]{1,0:T(8,128)(2,1)S(1)} %pad_maximum_fusion.4), channel_id=1, source_target_pairs={{0,4},{4,12},{12,20},{20,28},{28,24},{24,16},{16,8},{8,0},{1,5},{5... | collective-permute-start | bytes 983048 | tf_op jit(solution)/shard_map/ppermute | solution.py:88
  6.1 38.1 %collective-permute-start.4 = (bf16[640,256]{1,0:T(8,128)(2,1)S(1)}, bf16[640,256]{1,0:T(8,128)(2,1)S(1)}, u32[]{:S(2)}, u32[]{:S(2)}) collective-permute-start(bf16[640,256]{1,0:T(8,128)(2,1)S(1)} %pad_maximum_fusion.4), channel_id=1, source_target_pairs={{0,8},{4,0},{12,4},{20,12},{28,20},{24,28},{16,24},{8,16},{1,9},{5... | collective-permute-start | bytes 983048 | tf_op jit(solution)/shard_map/ppermute | solution.py:88
  14.0 30.7 %collective-permute-start.1 = (bf16[640,256]{1,0:T(8,128)(2,1)}, bf16[640,256]{1,0:T(8,128)(2,1)S(1)}, u32[]{:S(2)}, u32[]{:S(2)}) collective-permute-start(bf16[640,256]{1,0:T(8,128)(2,1)} %collective-permute-done), channel_id=1, source_target_pairs={{0,4},{4,12},{12,20},{20,28},{28,24},{24,16},{16,8},{8,0},{1,5},{5... | collective-permute-start | bytes 983048 | tf_op jit(solution)/shard_map/ppermute | solution.py:88
  19.8 55.2 %all-to-all-start = ((bf16[16,256,256]{2,0,1:T(8,128)(2,1)}), bf16[16,256,256]{2,0,1:T(8,128)(2,1)}, u32[]{:S(2)}, u32[]{:S(2)}) async-start(bf16[16,256,256]{2,0,1:T(8,128)(2,1)} %copy.53), calls=%async_computation | async-start | bytes 4194304 | tf_op jit(solution)/shard_map/all_to_all | solution.py:113
  68.7 14.0 %collective-permute-start.7 = (bf16[16,64,256]{2,1,0:T(8,128)(2,1)}, bf16[16,64,256]{2,1,0:T(8,128)(2,1)}, u32[]{:S(2)}, u32[]{:S(2)}) collective-permute-start(bf16[16,64,256]{2,1,0:T(8,128)(2,1)} %get-tuple-element.42), channel_id=1, source_target_pairs={{0,1},{1,2},{2,3},{3,0},{4,5},{5,6},{6,7},{7,4},{8,9},{9,10},{10,1... | collective-permute-start | bytes 1572872 | tf_op jit(solution)/shard_map/ppermute | solution.py:100
  68.7 15.1 %collective-permute-start.8 = (bf16[16,64,256]{2,1,0:T(8,128)(2,1)}, bf16[16,64,256]{2,1,0:T(8,128)(2,1)}, u32[]{:S(2)}, u32[]{:S(2)}) collective-permute-start(bf16[16,64,256]{2,1,0:T(8,128)(2,1)} %get-tuple-element.41), channel_id=1, source_target_pairs={{0,2},{1,3},{2,0},{3,1},{4,6},{5,7},{6,4},{7,5},{8,10},{9,11},{10,... | collective-permute-start | bytes 1572872 | tf_op jit(solution)/shard_map/ppermute | solution.py:100
  70.0 23.3 %collective-permute-start.9 = (bf16[16,64,256]{2,1,0:T(8,128)(2,1)}, bf16[16,64,256]{2,1,0:T(8,128)(2,1)}, u32[]{:S(2)}, u32[]{:S(2)}) collective-permute-start(bf16[16,64,256]{2,1,0:T(8,128)(2,1)} %get-tuple-element.40), channel_id=1, source_target_pairs={{0,3},{1,0},{2,1},{3,2},{4,7},{5,4},{6,5},{7,6},{8,11},{9,8},{10,9... | collective-permute-start | bytes 1572872 | tf_op jit(solution)/shard_map/ppermute | solution.py:100
  104.4 21.8 %collective-permute-start.10 = (bf16[64,16,256]{2,1,0:T(8,128)(2,1)}, bf16[64,16,256]{2,1,0:T(8,128)(2,1)}, u32[]{:S(2)}, u32[]{:S(2)}) collective-permute-start(bf16[64,16,256]{2,1,0:T(8,128)(2,1)} %get-tuple-element.30), channel_id=1, source_target_pairs={{0,1},{1,2},{2,3},{3,0},{4,5},{5,6},{6,7},{7,4},{8,9},{9,10},{10,1... | collective-permute-start | bytes 1572872 | tf_op jit(solution)/shard_map/ppermute | solution.py:100
  105.4 20.9 %collective-permute-start.11 = (bf16[64,16,256]{2,1,0:T(8,128)(2,1)}, bf16[64,16,256]{2,1,0:T(8,128)(2,1)}, u32[]{:S(2)}, u32[]{:S(2)}) collective-permute-start(bf16[64,16,256]{2,1,0:T(8,128)(2,1)} %get-tuple-element.29), channel_id=1, source_target_pairs={{0,2},{1,3},{2,0},{3,1},{4,6},{5,7},{6,4},{7,5},{8,10},{9,11},{10,... | collective-permute-start | bytes 1572872 | tf_op jit(solution)/shard_map/ppermute | solution.py:100
  106.7 21.7 %collective-permute-start.12 = (bf16[64,16,256]{2,1,0:T(8,128)(2,1)S(1)}, bf16[64,16,256]{2,1,0:T(8,128)(2,1)}, u32[]{:S(2)}, u32[]{:S(2)}) collective-permute-start(bf16[64,16,256]{2,1,0:T(8,128)(2,1)S(1)} %get-tuple-element.28), channel_id=1, source_target_pairs={{0,3},{1,0},{2,1},{3,2},{4,7},{5,4},{6,5},{7,6},{8,11},{9,8},{10,9... | collective-permute-start | bytes 1572872 | tf_op jit(solution)/shard_map/ppermute | solution.py:100
  118.1 16.5 %collective-permute-start.27 = (f32[8,64,64]{2,1,0:T(8,128)S(1)}, f32[8,64,64]{2,1,0:T(8,128)S(1)}, u32[]{:S(2)}, u32[]{:S(2)}) collective-permute-start(f32[8,64,64]{2,1,0:T(8,128)S(1)} %get-tuple-element.9), channel_id=1, source_target_pairs={{0,4},{4,12},{12,20},{20,28},{28,24},{24,16},{16,8},{8,0},{1,5},{5... | collective-permute-start | bytes 393224 | tf_op jit(solution)/shard_map/ppermute | solution.py:71
  135.5 10.8 %collective-permute-start.28 = (f32[8,64,64]{2,1,0:T(8,128)S(1)}, f32[8,64,64]{2,1,0:T(8,128)S(1)}, u32[]{:S(2)}, u32[]{:S(2)}) collective-permute-start(f32[8,64,64]{2,1,0:T(8,128)S(1)} %get-tuple-element.7), channel_id=1, source_target_pairs={{0,4},{4,12},{12,20},{20,28},{28,24},{24,16},{16,8},{8,0},{1,5},{5... | collective-permute-start | bytes 393224 | tf_op jit(solution)/shard_map/ppermute | solution.py:71
  137.3 11.2 %collective-permute-start.32 = (f32[8,64,64]{2,1,0:T(8,128)S(1)}, f32[8,64,64]{2,1,0:T(8,128)S(1)}, u32[]{:S(2)}, u32[]{:S(2)}) collective-permute-start(f32[8,64,64]{2,1,0:T(8,128)S(1)} %get-tuple-element.8), channel_id=1, source_target_pairs={{0,8},{4,0},{12,4},{20,12},{28,20},{24,28},{16,24},{8,16},{1,9},{5... | collective-permute-start | bytes 393224 | tf_op jit(solution)/shard_map/ppermute | solution.py:71
  137.6 16.4 %collective-permute-start.17 = (f32[16,16,256]{2,0,1:T(8,128)S(1)}, f32[16,16,256]{2,0,1:T(8,128)S(1)}, u32[]{:S(2)}, u32[]{:S(2)}) collective-permute-start(f32[16,16,256]{2,0,1:T(8,128)S(1)} %get-tuple-element.16), channel_id=1, source_target_pairs={{0,8},{4,0},{12,4},{20,12},{28,20},{24,28},{16,24},{8,16},{1,9},{5... | collective-permute-start | bytes 786440 | tf_op jit(solution)/shard_map/ppermute | solution.py:71
  140.7 19.0 %collective-permute-start.20 = (f32[16,16,256]{2,0,1:T(8,128)S(1)}, f32[16,16,256]{2,0,1:T(8,128)S(1)}, u32[]{:S(2)}, u32[]{:S(2)}) collective-permute-start(f32[16,16,256]{2,0,1:T(8,128)S(1)} %get-tuple-element.21), channel_id=1, source_target_pairs={{0,4},{4,12},{12,20},{20,28},{28,24},{24,16},{16,8},{8,0},{1,5},{5... | collective-permute-start | bytes 786440 | tf_op jit(solution)/shard_map/ppermute | solution.py:71
  142.8 14.8 %collective-permute-start.14 = (f32[16,16,256]{2,0,1:T(8,128)S(1)}, f32[16,16,256]{2,0,1:T(8,128)S(1)}, u32[]{:S(2)}, u32[]{:S(2)}) collective-permute-start(f32[16,16,256]{2,0,1:T(8,128)S(1)} %bitcast_add_fusion.16), channel_id=1, source_target_pairs={{0,4},{4,12},{12,20},{20,28},{28,24},{24,16},{16,8},{8,0},{1,5},{5... | collective-permute-start | bytes 786440 | tf_op jit(solution)/shard_map/ppermute | solution.py:71
  146.3 13.4 %collective-permute-start.24 = (f32[16,16,256]{2,0,1:T(8,128)S(1)}, f32[16,16,256]{2,0,1:T(8,128)S(1)}, u32[]{:S(2)}, u32[]{:S(2)}) collective-permute-start(f32[16,16,256]{2,0,1:T(8,128)S(1)} %bitcast_add_fusion.8), channel_id=1, source_target_pairs={{0,8},{4,0},{12,4},{20,12},{28,20},{24,28},{16,24},{8,16},{1,9},{5... | collective-permute-start | bytes 786440 | tf_op jit(solution)/shard_map/ppermute | solution.py:71
  148.5 28.8 %collective-permute-start.29 = (f32[8,64,64]{2,1,0:T(8,128)S(1)}, f32[8,64,64]{2,1,0:T(8,128)S(1)}, u32[]{:S(2)}, u32[]{:S(2)}) collective-permute-start(f32[8,64,64]{2,1,0:T(8,128)S(1)} %get-tuple-element.5), channel_id=1, source_target_pairs={{0,4},{4,12},{12,20},{20,28},{28,24},{24,16},{16,8},{8,0},{1,5},{5... | collective-permute-start | bytes 393224 | tf_op jit(solution)/shard_map/ppermute | solution.py:71
  157.6 11.1 %collective-permute-start.15 = (f32[16,16,256]{2,0,1:T(8,128)S(1)}, f32[16,16,256]{2,0,1:T(8,128)S(1)}, u32[]{:S(2)}, u32[]{:S(2)}) collective-permute-start(f32[16,16,256]{2,0,1:T(8,128)S(1)} %get-tuple-element.13), channel_id=1, source_target_pairs={{0,4},{4,12},{12,20},{20,28},{28,24},{24,16},{16,8},{8,0},{1,5},{5... | collective-permute-start | bytes 786440 | tf_op jit(solution)/shard_map/ppermute | solution.py:71
  159.4 11.2 %collective-permute-start.18 = (f32[16,16,256]{2,0,1:T(8,128)S(1)}, f32[16,16,256]{2,0,1:T(8,128)S(1)}, u32[]{:S(2)}, u32[]{:S(2)}) collective-permute-start(f32[16,16,256]{2,0,1:T(8,128)S(1)} %get-tuple-element.14), channel_id=1, source_target_pairs={{0,8},{4,0},{12,4},{20,12},{28,20},{24,28},{16,24},{8,16},{1,9},{5... | collective-permute-start | bytes 786440 | tf_op jit(solution)/shard_map/ppermute | solution.py:71
  159.8 14.6 %collective-permute-start.21 = (f32[16,16,256]{2,0,1:T(8,128)S(1)}, f32[16,16,256]{2,0,1:T(8,128)S(1)}, u32[]{:S(2)}, u32[]{:S(2)}) collective-permute-start(f32[16,16,256]{2,0,1:T(8,128)S(1)} %get-tuple-element.19), channel_id=1, source_target_pairs={{0,4},{4,12},{12,20},{20,28},{28,24},{24,16},{16,8},{8,0},{1,5},{5... | collective-permute-start | bytes 786440 | tf_op jit(solution)/shard_map/ppermute | solution.py:71
  161.6 14.6 %collective-permute-start.25 = (f32[16,16,256]{2,0,1:T(8,128)S(1)}, f32[16,16,256]{2,0,1:T(8,128)S(1)}, u32[]{:S(2)}, u32[]{:S(2)}) collective-permute-start(f32[16,16,256]{2,0,1:T(8,128)S(1)} %get-tuple-element.20), channel_id=1, source_target_pairs={{0,8},{4,0},{12,4},{20,12},{28,20},{24,28},{16,24},{8,16},{1,9},{5... | collective-permute-start | bytes 786440 | tf_op jit(solution)/shard_map/ppermute | solution.py:71
  168.8 10.3 %collective-permute-start.33 = (f32[8,64,64]{2,1,0:T(8,128)S(1)}, f32[8,64,64]{2,1,0:T(8,128)S(1)}, u32[]{:S(2)}, u32[]{:S(2)}) collective-permute-start(f32[8,64,64]{2,1,0:T(8,128)S(1)} %get-tuple-element.6), channel_id=1, source_target_pairs={{0,8},{4,0},{12,4},{20,12},{28,20},{24,28},{16,24},{8,16},{1,9},{5... | collective-permute-start | bytes 393224 | tf_op jit(solution)/shard_map/ppermute | solution.py:71
  177.3 13.1 %collective-permute-start.26 = (f32[16,16,256]{2,0,1:T(8,128)}, f32[16,16,256]{2,0,1:T(8,128)}, u32[]{:S(2)}, u32[]{:S(2)}) collective-permute-start(f32[16,16,256]{2,0,1:T(8,128)} %get-tuple-element.18), channel_id=1, source_target_pairs={{0,8},{4,0},{12,4},{20,12},{28,20},{24,28},{16,24},{8,16},{1,9},{5... | collective-permute-start | bytes 786440 | tf_op jit(solution)/shard_map/ppermute | solution.py:71
  (22 other events, 326.1 us)

commit v20 on v19

--- a/solution.py
+++ b/solution.py
@@ -110,7 +110,7 @@
     grad_scale = 1.0 / math.sqrt(tok_count * n_dp)
     x_blocks = activations.reshape(local_blocks, WIDTH, tok_count)
     g_blocks = cotangent.reshape(local_blocks, WIDTH, tok_count)
-    g_cols = lax.all_to_all(g_blocks, "feat", split_axis=1, concat_axis=0, tiled=True)
+    g_cols = permute_all_to_all(g_blocks, 1)
     local_cols = l_mix.shape[0]
     rows_r = r_mix.shape[1]
     r_lead = jnp.transpose(r_mix, (1, 0, 2)).reshape(-1, WIDTH)

time: 193 us -> 193 us (level)
  starting transfers between devices: 45.1 us -> 39 us
  other arithmetic: 9.28 us -> 13.3 us
    ppermute x6 -> x9, waiting for transfers between devices: 18.3 us -> 23.1 us  [permute_all_to_all(): lax.ppermute(mine, 'feat', [(f, (f + shift) % n) for f in range(n)])]
    all_to_all x1 -> x0, starting transfers between devices: 4.6 us -> none  [body(): lax.all_to_all(g_blocks, 'feat', split_axis=1, concat_axis=0, tiled=True)]
    reshape x1 -> x0, local copies, waits for them, and re-layouts: 4.08 us -> none  [body(): g_blocks = cotangent.reshape(local_blocks, WIDTH, tok_count)]
    squeeze x2 -> x4, local copies, waits for them, and re-layouts: 0.4 us -> 3.54 us  [permute_all_to_all(): lax.dynamic_index_in_dim(by_shift, (me - src) % n, axis=0, keepdims=False)]
    dynamic_slice x2 -> x3, local copies, waits for them, and re-layouts: 2.61 us -> 5.28 us  [permute_all_to_all(): by_shift = [lax.dynamic_index_in_dim(pieces, me, axis=0, keepdims=False)]]
    convert_element_type x1 -> x0, local copies, waits for them, and re-layouts: 2.24 us -> none  [slope_of(): return pullback(upstream.astype(jnp.float32))[0].astype(jnp.bfloat16)]
    ppermute x21, waiting for transfers between devices: 33.8 us -> 31.7 us  [ring_reduce_scatter(): acc = lax.ppermute(mine if acc is None else acc + mine, 'dp', pairs)]
    another operation x2 -> x3, other arithmetic: 3.24 us -> 5.02 us  [permute_all_to_all(): by_shift = jnp.stack(by_shift)]
  transfers between devices with their start and end apart: 35 -> 37, of which waited for: 19 -> 18; matrix products, arithmetic and copies ran while one was open for 18% -> 18% of each run, Pallas kernels for 0% -> 0%
where the time goes in v20:
time: 193 us; the launch traced here: 192 us
  waiting for transfers between devices  74.9 us (39%)
  starting transfers between devices  39 us (20%)
  local copies, waits for them, and re-layouts  29.8 us (15%)
  between operations  21.4 us (11%)
  matrix products  13.6 us (7%)
  other arithmetic  13.3 us (7%)
    ppermute x21, waiting for transfers between devices, ring_reduce_scatter(): acc = lax.ppermute(mine if acc is None else acc + mine, 'dp', pairs)  31.7 us
    ppermute x21, starting transfers between devices, ring_reduce_scatter(): acc = lax.ppermute(mine if acc is None else acc + mine, 'dp', pairs)  25.6 us
    ppermute x9, waiting for transfers between devices, permute_all_to_all(): lax.ppermute(mine, 'feat', [(f, (f + shift) % n) for f in range(n)])  23.1 us
    ppermute x7, waiting for transfers between devices, ring_all_gather(): cur = lax.ppermute(cur, 'dp', pairs)  20.1 us
    ppermute x7, starting transfers between devices, ring_all_gather(): cur = lax.ppermute(cur, 'dp', pairs)  8.75 us
    dot_general x1, matrix products, body(): jnp.einsum('bst,bsc->cst', columns, l_blocks, preferred_element_type=jnp....  5.68 us
    dynamic_slice x3, local copies, waits for them, and re-layouts, permute_all_to_all(): by_shift = [lax.dynamic_index_in_dim(pieces, me, axis=0, keepdims=False)]  5.28 us
    another operation x3, other arithmetic, permute_all_to_all(): by_shift = jnp.stack(by_shift)  5.02 us
  transfers between devices with their start and end apart: 37, of which 18 were waited for; matrix products, arithmetic and copies ran while one was open for 18% of the time, Pallas kernels for 0%

profile of v20, /device:TPU:0, one launch (start us, length us, event | category | flops | bytes accessed | tf_op | source)
XLA Modules:
  0.0 192.0 jit_solution(1629360227443448844)
XLA Ops:
  3.8 3.0 %collective-permute-start = (bf16[640,256]{1,0:T(8,128)(2,1)}, bf16[640,256]{1,0:T(8,128)(2,1)}, u32[]{:S(2)}, u32[]{:S(2)}) collective-permute-start(bf16[640,256]{1,0:T(8,128)(2,1)} %pad_maximum_fusion.6), channel_id=1, source_target_pairs={{0,4},{4,12},{12,20},{20,28},{28,24},{24,16},{16,8},{8,0},{1,5},{5... | collective-permute-start | bytes 983048 | tf_op jit(solution)/shard_map/ppermute | solution.py:88
  6.8 1.7 slice_bitcast_fusion.11
  10.1 2.7 %constant_dynamic-slice_fusion.6 = (bf16[1,16,64,256]{3,2,1,0:T(8,128)(2,1)S(1)}, bf16[16,64,256]{2,1,0:T(8,128)(2,1)}, bf16[16,64,256]{2,1,0:T(8,128)(2,1)}, bf16[16,64,256]{2,1,0:T(8,128)(2,1)S(1)}) fusion(bf16[4,16,64,256]{3,2,1,0:T(8,128)(2,1)} %pad_maximum_fusion, s32[]{:T(128)S(6)} %select_n.416, s32[]{:T(128)S(6)} %select_n.422, s32[]{:T(128)S(6)} %select_n.420, ...), kind=kLoop, calls=%fused_computation.115 | loop fusion | bytes 4194320 | tf_op jit(solution)/shard_map/jit(dynamic_index_in_dim)/dynamic_slice | solution.py:97
  37.9 7.3 %collective-permute-done.1 = bf16[640,256]{1,0:T(8,128)(2,1)S(1)} collective-permute-done((bf16[640,256]{1,0:T(8,128)(2,1)}, bf16[640,256]{1,0:T(8,128)(2,1)S(1)}, u32[]{:S(2)}, u32[]{:S(2)}) %collective-permute-start.1) | collective-permute-done | bytes 327712 | tf_op jit(solution)/shard_map/ppermute | solution.py:88
  49.1 5.7 %collective-permute-done.2 = bf16[640,256]{1,0:T(8,128)(2,1)S(1)} collective-permute-done((bf16[640,256]{1,0:T(8,128)(2,1)S(1)}, bf16[640,256]{1,0:T(8,128)(2,1)S(1)}, u32[]{:S(2)}, u32[]{:S(2)}) %collective-permute-start.2) | collective-permute-done | bytes 327712 | tf_op jit(solution)/shard_map/ppermute | solution.py:88
  56.4 7.1 %collective-permute-done.3 = bf16[640,256]{1,0:T(8,128)(2,1)S(1)} collective-permute-done((bf16[640,256]{1,0:T(8,128)(2,1)S(1)}, bf16[640,256]{1,0:T(8,128)(2,1)S(1)}, u32[]{:S(2)}, u32[]{:S(2)}) %collective-permute-start.3) | collective-permute-done | bytes 327712 | tf_op jit(solution)/shard_map/ppermute | solution.py:88
  75.5 4.2 %collective-permute-done.12 = bf16[16,64,256]{2,1,0:T(8,128)(2,1)} collective-permute-done((bf16[16,64,256]{2,1,0:T(8,128)(2,1)}, bf16[16,64,256]{2,1,0:T(8,128)(2,1)}, u32[]{:S(2)}, u32[]{:S(2)}) %collective-permute-start.12) | collective-permute-done | bytes 524320 | tf_op jit(solution)/shard_map/ppermute | solution.py:100
  79.7 14.2 %collective-permute-done.11 = bf16[16,64,256]{2,1,0:T(8,128)(2,1)} collective-permute-done((bf16[16,64,256]{2,1,0:T(8,128)(2,1)}, bf16[16,64,256]{2,1,0:T(8,128)(2,1)}, u32[]{:S(2)}, u32[]{:S(2)}) %collective-permute-start.11) | collective-permute-done | bytes 524320 | tf_op jit(solution)/shard_map/ppermute | solution.py:100
  93.9 1.8 pad_maximum_fusion.3
  97.5 5.7 %fusion.2 = bf16[64,64,256]{2,0,1:T(8,128)(2,1)S(1)} fusion(bf16[64,64,256]{2,0,1:T(8,128)(2,1)S(1)} %copy_dynamic-update-slice_fusion.4, bf16[16,64,256]{2,0,1:T(8,128)(2,1)S(1)} %copy-done.9, bf16[16,64,256]{2,0,1:T(8,128)(2,1)S(1)} %copy-done.10, bf16[16,64,256]{2,0,1:T(8,128)(2,1)S(1)} %copy-done.7, bf16[16,64,256]{2,0,1:T(8,128)(2,1)S(1)} %copy-done.8, ...), kind=kOutput, calls=%fused_computation.6 | convolution fusion | flops 163577856 | bytes 6815744 | tf_op jit(solution)/shard_map/bst,bsc->cst/dot_general | solution.py:127
  106.9 2.0 %multiply_bitcast_fusion = f32[64,64,64]{0,2,1:T(8,128)} fusion(bf16[64,64,256]{2,0,1:T(8,128)(2,1)S(1)} %fusion.2, bf16[64,64,256]{2,0,1:T(8,128)(2,1)S(1)} %copy_dynamic-update-slice_fusion.4), kind=kOutput, calls=%fused_computation.22 | convolution fusion | flops 134479872 | bytes 5242880 | tf_op jit(solution)/shard_map/bst,cst->bsc/dot_general | solution.py:132
  109.0 3.8 %copy.58 = f32[64,64,64]{2,1,0:T(8,128)} copy(f32[64,64,64]{0,2,1:T(8,128)} %multiply_bitcast_fusion) | data formatting | bytes 2097152 | tf_op jit(solution)/shard_map/mul | solution.py:133
  112.8 1.8 dynamic-slice_bitcast_fusion.18
  118.6 5.1 %collective-permute-done.33 = f32[8,64,64]{2,1,0:T(8,128)} collective-permute-done((f32[8,64,64]{2,1,0:T(8,128)}, f32[8,64,64]{2,1,0:T(8,128)}, u32[]{:S(2)}, u32[]{:S(2)}) %collective-permute-start.33) | collective-permute-done | bytes 131104 | tf_op jit(solution)/shard_map/ppermute | solution.py:71
  126.4 3.6 %collective-permute-done.14 = bf16[64,16,256]{2,1,0:T(8,128)(2,1)} collective-permute-done((bf16[64,16,256]{2,1,0:T(8,128)(2,1)}, bf16[64,16,256]{2,1,0:T(8,128)(2,1)}, u32[]{:S(2)}, u32[]{:S(2)}) %collective-permute-start.14) | collective-permute-done | bytes 524320 | tf_op jit(solution)/shard_map/ppermute | solution.py:100
  141.7 2.5 %collective-permute-done.16 = f32[16,16,256]{2,0,1:T(8,128)S(1)} collective-permute-done((f32[16,16,256]{2,0,1:T(8,128)S(1)}, f32[16,16,256]{2,0,1:T(8,128)S(1)}, u32[]{:S(2)}, u32[]{:S(2)}) %collective-permute-start.16) | collective-permute-done | bytes 262176 | tf_op jit(solution)/shard_map/ppermute | solution.py:71
  147.5 2.4 %collective-permute-done.31 = f32[8,64,64]{2,1,0:T(8,128)S(1)} collective-permute-done((f32[8,64,64]{2,1,0:T(8,128)S(1)}, f32[8,64,64]{2,1,0:T(8,128)S(1)}, u32[]{:S(2)}, u32[]{:S(2)}) %collective-permute-start.31) | collective-permute-done | bytes 131104 | tf_op jit(solution)/shard_map/ppermute | solution.py:71
  153.2 3.9 %collective-permute-done.20 = f32[16,16,256]{2,0,1:T(8,128)S(1)} collective-permute-done((f32[16,16,256]{2,0,1:T(8,128)S(1)}, f32[16,16,256]{2,0,1:T(8,128)S(1)}, u32[]{:S(2)}, u32[]{:S(2)}) %collective-permute-start.20) | collective-permute-done | bytes 262176 | tf_op jit(solution)/shard_map/ppermute | solution.py:71
  157.1 4.0 %collective-permute-done.17 = f32[16,16,256]{2,0,1:T(8,128)S(1)} collective-permute-done((f32[16,16,256]{2,0,1:T(8,128)S(1)}, f32[16,16,256]{2,0,1:T(8,128)S(1)}, u32[]{:S(2)}, u32[]{:S(2)}) %collective-permute-start.17) | collective-permute-done | bytes 262176 | tf_op jit(solution)/shard_map/ppermute | solution.py:71
  165.4 2.3 %add_convert_fusion = bf16[16,256,256]{2,1,0:T(8,128)(2,1)} fusion(bf16[16,256,256]{2,1,0:T(8,128)(2,1)S(1)} %bitcast.205, bf16[256,16,256]{2,0,1:T(8,128)(2,1)S(1)} %copy_dynamic-update-slice_fusion, bf16[256,16,256]{2,1,0:T(8,128)(2,1)S(1)} %bitcast.202), kind=kOutput, calls=%fused_computation.14 | convolution fusion | flops 540016640 | bytes 8388608 | tf_op jit(solution)/shard_map/obt,ibo->bit/dot_general | solution.py:137
  167.7 4.6 %collective-permute-done.18 = f32[16,16,256]{2,0,1:T(8,128)S(1)} collective-permute-done((f32[16,16,256]{2,0,1:T(8,128)S(1)}, f32[16,16,256]{2,0,1:T(8,128)S(1)}, u32[]{:S(2)}, u32[]{:S(2)}) %collective-permute-start.18) | collective-permute-done | bytes 262176 | tf_op jit(solution)/shard_map/ppermute | solution.py:71
  174.5 3.4 %collective-permute-done.24 = f32[16,16,256]{2,0,1:T(8,128)S(1)} collective-permute-done((f32[16,16,256]{2,0,1:T(8,128)S(1)}, f32[16,16,256]{2,0,1:T(8,128)S(1)}, u32[]{:S(2)}, u32[]{:S(2)}) %collective-permute-start.24) | collective-permute-done | bytes 262176 | tf_op jit(solution)/shard_map/ppermute | solution.py:71
  183.6 3.6 %collective-permute-done.22 = f32[16,16,256]{2,0,1:T(8,128)S(1)} collective-permute-done((f32[16,16,256]{2,0,1:T(8,128)S(1)}, f32[16,16,256]{2,0,1:T(8,128)S(1)}, u32[]{:S(2)}, u32[]{:S(2)}) %collective-permute-start.22) | collective-permute-done | bytes 262176 | tf_op jit(solution)/shard_map/ppermute | solution.py:71
  188.1 1.9 collective-permute-done.29
  (146 shorter events, 72.3 us)
Async XLA Ops:
  3.8 30.8 %collective-permute-start = (bf16[640,256]{1,0:T(8,128)(2,1)}, bf16[640,256]{1,0:T(8,128)(2,1)}, u32[]{:S(2)}, u32[]{:S(2)}) collective-permute-start(bf16[640,256]{1,0:T(8,128)(2,1)} %pad_maximum_fusion.6), channel_id=1, source_target_pairs={{0,4},{4,12},{12,20},{20,28},{28,24},{24,16},{16,8},{8,0},{1,5},{5... | collective-permute-start | bytes 983048 | tf_op jit(solution)/shard_map/ppermute | solution.py:88
  6.8 29.6 %collective-permute-start.4 = (bf16[640,256]{1,0:T(8,128)(2,1)}, bf16[640,256]{1,0:T(8,128)(2,1)}, u32[]{:S(2)}, u32[]{:S(2)}) collective-permute-start(bf16[640,256]{1,0:T(8,128)(2,1)} %pad_maximum_fusion.6), channel_id=1, source_target_pairs={{0,8},{4,0},{12,4},{20,12},{28,20},{24,28},{16,24},{8,16},{1,9},{5... | collective-permute-start | bytes 983048 | tf_op jit(solution)/shard_map/ppermute | solution.py:88
  12.8 34.0 %collective-permute-start.9 = (bf16[16,64,256]{2,1,0:T(8,128)(2,1)}, bf16[16,64,256]{2,1,0:T(8,128)(2,1)}, u32[]{:S(2)}, u32[]{:S(2)}) collective-permute-start(bf16[16,64,256]{2,1,0:T(8,128)(2,1)} %get-tuple-element.40), channel_id=1, source_target_pairs={{0,3},{1,0},{2,1},{3,2},{4,7},{5,4},{6,5},{7,6},{8,11},{9,8},{10,9... | collective-permute-start | bytes 1572872 | tf_op jit(solution)/shard_map/ppermute | solution.py:100
  13.6 33.2 %collective-permute-start.8 = (bf16[16,64,256]{2,1,0:T(8,128)(2,1)}, bf16[16,64,256]{2,1,0:T(8,128)(2,1)}, u32[]{:S(2)}, u32[]{:S(2)}) collective-permute-start(bf16[16,64,256]{2,1,0:T(8,128)(2,1)} %get-tuple-element.41), channel_id=1, source_target_pairs={{0,2},{1,3},{2,0},{3,1},{4,6},{5,7},{6,4},{7,5},{8,10},{9,11},{10,... | collective-permute-start | bytes 1572872 | tf_op jit(solution)/shard_map/ppermute | solution.py:100
  14.7 32.1 %collective-permute-start.7 = (bf16[16,64,256]{2,1,0:T(8,128)(2,1)S(1)}, bf16[16,64,256]{2,1,0:T(8,128)(2,1)}, u32[]{:S(2)}, u32[]{:S(2)}) collective-permute-start(bf16[16,64,256]{2,1,0:T(8,128)(2,1)S(1)} %get-tuple-element.42), channel_id=1, source_target_pairs={{0,1},{1,2},{2,3},{3,0},{4,5},{5,6},{6,7},{7,4},{8,9},{9,10},{10,1... | collective-permute-start | bytes 1572872 | tf_op jit(solution)/shard_map/ppermute | solution.py:100
  36.4 12.2 %collective-permute-start.5 = (bf16[640,256]{1,0:T(8,128)(2,1)}, bf16[640,256]{1,0:T(8,128)(2,1)S(1)}, u32[]{:S(2)}, u32[]{:S(2)}) collective-permute-start(bf16[640,256]{1,0:T(8,128)(2,1)} %collective-permute-done.4), channel_id=1, source_target_pairs={{0,8},{4,0},{12,4},{20,12},{28,20},{24,28},{16,24},{8,16},{1,9},{5... | collective-permute-start | bytes 983048 | tf_op jit(solution)/shard_map/ppermute | solution.py:88
  48.6 16.0 %collective-permute-start.6 = (bf16[640,256]{1,0:T(8,128)(2,1)S(1)}, bf16[640,256]{1,0:T(8,128)(2,1)S(1)}, u32[]{:S(2)}, u32[]{:S(2)}) collective-permute-start(bf16[640,256]{1,0:T(8,128)(2,1)S(1)} %collective-permute-done.5), channel_id=1, source_target_pairs={{0,8},{4,0},{12,4},{20,12},{28,20},{24,28},{16,24},{8,16},{1,9},{5... | collective-permute-start | bytes 983048 | tf_op jit(solution)/shard_map/ppermute | solution.py:88
  68.1 11.6 %collective-permute-start.12 = (bf16[16,64,256]{2,1,0:T(8,128)(2,1)}, bf16[16,64,256]{2,1,0:T(8,128)(2,1)}, u32[]{:S(2)}, u32[]{:S(2)}) collective-permute-start(bf16[16,64,256]{2,1,0:T(8,128)(2,1)} %get-tuple-element.52), channel_id=1, source_target_pairs={{0,3},{1,0},{2,1},{3,2},{4,7},{5,4},{6,5},{7,6},{8,11},{9,8},{10,9... | collective-permute-start | bytes 1572872 | tf_op jit(solution)/shard_map/ppermute | solution.py:100
  68.1 25.8 %collective-permute-start.11 = (bf16[16,64,256]{2,1,0:T(8,128)(2,1)}, bf16[16,64,256]{2,1,0:T(8,128)(2,1)}, u32[]{:S(2)}, u32[]{:S(2)}) collective-permute-start(bf16[16,64,256]{2,1,0:T(8,128)(2,1)} %get-tuple-element.53), channel_id=1, source_target_pairs={{0,2},{1,3},{2,0},{3,1},{4,6},{5,7},{6,4},{7,5},{8,10},{9,11},{10,... | collective-permute-start | bytes 1572872 | tf_op jit(solution)/shard_map/ppermute | solution.py:100
  69.6 24.3 %collective-permute-start.10 = (bf16[16,64,256]{2,1,0:T(8,128)(2,1)}, bf16[16,64,256]{2,1,0:T(8,128)(2,1)}, u32[]{:S(2)}, u32[]{:S(2)}) collective-permute-start(bf16[16,64,256]{2,1,0:T(8,128)(2,1)} %get-tuple-element.54), channel_id=1, source_target_pairs={{0,1},{1,2},{2,3},{3,0},{4,5},{5,6},{6,7},{7,4},{8,9},{9,10},{10,1... | collective-permute-start | bytes 1572872 | tf_op jit(solution)/shard_map/ppermute | solution.py:100
  106.2 20.2 %collective-permute-start.15 = (bf16[64,16,256]{2,1,0:T(8,128)(2,1)}, bf16[64,16,256]{2,1,0:T(8,128)(2,1)}, u32[]{:S(2)}, u32[]{:S(2)}) collective-permute-start(bf16[64,16,256]{2,1,0:T(8,128)(2,1)} %get-tuple-element.28), channel_id=1, source_target_pairs={{0,3},{1,0},{2,1},{3,2},{4,7},{5,4},{6,5},{7,6},{8,11},{9,8},{10,9... | collective-permute-start | bytes 1572872 | tf_op jit(solution)/shard_map/ppermute | solution.py:100
  106.2 23.8 %collective-permute-start.14 = (bf16[64,16,256]{2,1,0:T(8,128)(2,1)}, bf16[64,16,256]{2,1,0:T(8,128)(2,1)}, u32[]{:S(2)}, u32[]{:S(2)}) collective-permute-start(bf16[64,16,256]{2,1,0:T(8,128)(2,1)} %get-tuple-element.29), channel_id=1, source_target_pairs={{0,2},{1,3},{2,0},{3,1},{4,6},{5,7},{6,4},{7,5},{8,10},{9,11},{10,... | collective-permute-start | bytes 1572872 | tf_op jit(solution)/shard_map/ppermute | solution.py:100
  106.7 24.3 %collective-permute-start.13 = (bf16[64,16,256]{2,1,0:T(8,128)(2,1)S(1)}, bf16[64,16,256]{2,1,0:T(8,128)(2,1)}, u32[]{:S(2)}, u32[]{:S(2)}) collective-permute-start(bf16[64,16,256]{2,1,0:T(8,128)(2,1)S(1)} %get-tuple-element.30), channel_id=1, source_target_pairs={{0,1},{1,2},{2,3},{3,0},{4,5},{5,6},{6,7},{7,4},{8,9},{9,10},{10,1... | collective-permute-start | bytes 1572872 | tf_op jit(solution)/shard_map/ppermute | solution.py:100
  118.1 19.0 %collective-permute-start.30 = (f32[8,64,64]{2,1,0:T(8,128)S(1)}, f32[8,64,64]{2,1,0:T(8,128)S(1)}, u32[]{:S(2)}, u32[]{:S(2)}) collective-permute-start(f32[8,64,64]{2,1,0:T(8,128)S(1)} %get-tuple-element.9), channel_id=1, source_target_pairs={{0,4},{4,12},{12,20},{20,28},{28,24},{24,16},{16,8},{8,0},{1,5},{5... | collective-permute-start | bytes 393224 | tf_op jit(solution)/shard_map/ppermute | solution.py:71
  124.8 12.4 %collective-permute-start.34 = (f32[8,64,64]{2,1,0:T(8,128)S(1)}, f32[8,64,64]{2,1,0:T(8,128)S(1)}, u32[]{:S(2)}, u32[]{:S(2)}) collective-permute-start(f32[8,64,64]{2,1,0:T(8,128)S(1)} %bitcast_add_fusion.2), channel_id=1, source_target_pairs={{0,8},{4,0},{12,4},{20,12},{28,20},{24,28},{16,24},{8,16},{1,9},{5... | collective-permute-start | bytes 393224 | tf_op jit(solution)/shard_map/ppermute | solution.py:71
  138.1 11.8 %collective-permute-start.31 = (f32[8,64,64]{2,1,0:T(8,128)S(1)}, f32[8,64,64]{2,1,0:T(8,128)S(1)}, u32[]{:S(2)}, u32[]{:S(2)}) collective-permute-start(f32[8,64,64]{2,1,0:T(8,128)S(1)} %get-tuple-element.7), channel_id=1, source_target_pairs={{0,4},{4,12},{12,20},{20,28},{28,24},{24,16},{16,8},{8,0},{1,5},{5... | collective-permute-start | bytes 393224 | tf_op jit(solution)/shard_map/ppermute | solution.py:71
  139.6 11.8 %collective-permute-start.35 = (f32[8,64,64]{2,1,0:T(8,128)S(1)}, f32[8,64,64]{2,1,0:T(8,128)S(1)}, u32[]{:S(2)}, u32[]{:S(2)}) collective-permute-start(f32[8,64,64]{2,1,0:T(8,128)S(1)} %get-tuple-element.8), channel_id=1, source_target_pairs={{0,8},{4,0},{12,4},{20,12},{28,20},{24,28},{16,24},{8,16},{1,9},{5... | collective-permute-start | bytes 393224 | tf_op jit(solution)/shard_map/ppermute | solution.py:71
  140.1 16.9 %collective-permute-start.20 = (f32[16,16,256]{2,0,1:T(8,128)S(1)}, f32[16,16,256]{2,0,1:T(8,128)S(1)}, u32[]{:S(2)}, u32[]{:S(2)}) collective-permute-start(f32[16,16,256]{2,0,1:T(8,128)S(1)} %get-tuple-element.16), channel_id=1, source_target_pairs={{0,8},{4,0},{12,4},{20,12},{28,20},{24,28},{16,24},{8,16},{1,9},{5... | collective-permute-start | bytes 786440 | tf_op jit(solution)/shard_map/ppermute | solution.py:71
  144.2 19.0 %collective-permute-start.23 = (f32[16,16,256]{2,0,1:T(8,128)S(1)}, f32[16,16,256]{2,0,1:T(8,128)S(1)}, u32[]{:S(2)}, u32[]{:S(2)}) collective-permute-start(f32[16,16,256]{2,0,1:T(8,128)S(1)} %get-tuple-element.21), channel_id=1, source_target_pairs={{0,4},{4,12},{12,20},{20,28},{28,24},{24,16},{16,8},{8,0},{1,5},{5... | collective-permute-start | bytes 786440 | tf_op jit(solution)/shard_map/ppermute | solution.py:71
  145.8 15.2 %collective-permute-start.17 = (f32[16,16,256]{2,0,1:T(8,128)S(1)}, f32[16,16,256]{2,0,1:T(8,128)S(1)}, u32[]{:S(2)}, u32[]{:S(2)}) collective-permute-start(f32[16,16,256]{2,0,1:T(8,128)S(1)} %bitcast_add_fusion.16), channel_id=1, source_target_pairs={{0,4},{4,12},{12,20},{20,28},{28,24},{24,16},{16,8},{8,0},{1,5},{5... | collective-permute-start | bytes 786440 | tf_op jit(solution)/shard_map/ppermute | solution.py:71
  149.8 13.4 %collective-permute-start.27 = (f32[16,16,256]{2,0,1:T(8,128)S(1)}, f32[16,16,256]{2,0,1:T(8,128)S(1)}, u32[]{:S(2)}, u32[]{:S(2)}) collective-permute-start(f32[16,16,256]{2,0,1:T(8,128)S(1)} %bitcast_add_fusion.8), channel_id=1, source_target_pairs={{0,8},{4,0},{12,4},{20,12},{28,20},{24,28},{16,24},{8,16},{1,9},{5... | collective-permute-start | bytes 786440 | tf_op jit(solution)/shard_map/ppermute | solution.py:71
  151.5 29.3 %collective-permute-start.32 = (f32[8,64,64]{2,1,0:T(8,128)S(1)}, f32[8,64,64]{2,1,0:T(8,128)S(1)}, u32[]{:S(2)}, u32[]{:S(2)}) collective-permute-start(f32[8,64,64]{2,1,0:T(8,128)S(1)} %get-tuple-element.5), channel_id=1, source_target_pairs={{0,4},{4,12},{12,20},{20,28},{28,24},{24,16},{16,8},{8,0},{1,5},{5... | collective-permute-start | bytes 393224 | tf_op jit(solution)/shard_map/ppermute | solution.py:71
  163.4 14.6 %collective-permute-start.24 = (f32[16,16,256]{2,0,1:T(8,128)S(1)}, f32[16,16,256]{2,0,1:T(8,128)S(1)}, u32[]{:S(2)}, u32[]{:S(2)}) collective-permute-start(f32[16,16,256]{2,0,1:T(8,128)S(1)} %get-tuple-element.19), channel_id=1, source_target_pairs={{0,4},{4,12},{12,20},{20,28},{28,24},{24,16},{16,8},{8,0},{1,5},{5... | collective-permute-start | bytes 786440 | tf_op jit(solution)/shard_map/ppermute | solution.py:71
  164.9 14.6 %collective-permute-start.28 = (f32[16,16,256]{2,0,1:T(8,128)S(1)}, f32[16,16,256]{2,0,1:T(8,128)S(1)}, u32[]{:S(2)}, u32[]{:S(2)}) collective-permute-start(f32[16,16,256]{2,0,1:T(8,128)S(1)} %get-tuple-element.20), channel_id=1, source_target_pairs={{0,8},{4,0},{12,4},{20,12},{28,20},{24,28},{16,24},{8,16},{1,9},{5... | collective-permute-start | bytes 786440 | tf_op jit(solution)/shard_map/ppermute | solution.py:71
  (26 other events, 334.1 us)

commit v21 on v20

--- a/solution.py
+++ b/solution.py
@@ -72,7 +72,7 @@
         total = total + acc
     return total
 
-def ring_all_gather(piece, ring):
+def ring_all_gather(piece, ring, lead=1):
     n = len(ring)
     order = jnp.asarray(np.array(ring, np.int32))
     place = jnp.asarray(np.argsort(np.array(ring)).astype(np.int32))
@@ -81,7 +81,7 @@
     forward = [(ring[p], ring[(p + 1) % n]) for p in range(n)]
     backward = [(ring[p], ring[(p - 1) % n]) for p in range(n)]
     held = lax.dynamic_update_index_in_dim(jnp.zeros((n,) + piece.shape, piece.dtype), piece, me, 0)
-    ahead = n // 2
+    ahead = n // 2 if lead > 0 else n - 1 - n // 2
     for way, pairs, hops in ((1, forward, ahead), (-1, backward, n - 1 - ahead)):
         cur = piece
         for step in range(hops):
@@ -117,7 +117,10 @@
     l_lead = jnp.transpose(l_mix.reshape(local_cols, -1, BLOCKS), (1, 0, 2)).reshape(-1, WIDTH)
     r_size = r_lead.shape[0]
     packed = jnp.concatenate([r_lead, l_lead], axis=0)
-    packed = ring_all_gather(packed, ring)
+    split = packed.shape[0] // 2
+    packed = jnp.concatenate(
+        [ring_all_gather(packed[:split], ring), ring_all_gather(packed[split:], ring, lead=-1)], axis=1
+    )
     r_whole = packed[:, :r_size].reshape(n_dp * rows_r, local_blocks, WIDTH)
     l_blocks = packed[:, r_size:].reshape(-1, local_cols, BLOCKS)
     mixed_rows = jnp.einsum(

time: 193 us -> 209 us (1.083)
  waiting for transfers between devices: 74.9 us -> 80.9 us
  other arithmetic: 13.3 us -> 16.8 us
  local copies, waits for them, and re-layouts: 29.8 us -> 32.8 us
  matrix products: 13.6 us -> 15.8 us
    ppermute x7 -> x14, starting transfers between devices: 8.75 us -> 16 us  [ring_all_gather(): cur = lax.ppermute(cur, 'dp', pairs)]
    ppermute x21, starting transfers between devices: 25.6 us -> 19.1 us  [ring_reduce_scatter(): acc = lax.ppermute(mine if acc is None else acc + mine, 'dp', pairs)]
    ppermute x7 -> x14, waiting for transfers between devices: 20.1 us -> 23.3 us  [ring_all_gather(): cur = lax.ppermute(cur, 'dp', pairs)]
    add x9, other arithmetic: 2.38 us -> 5.13 us  [ring_reduce_scatter(): acc = lax.ppermute(mine if acc is None else acc + mine, 'dp', pairs)]
    ppermute x9, waiting for transfers between devices: 23.1 us -> 25.6 us  [permute_all_to_all(): lax.ppermute(mine, 'feat', [(f, (f + shift) % n) for f in range(n)])]
    dot_general x1, matrix products: 2.28 us -> 4.5 us  [body(): jnp.einsum('obt,ibo->bit', back_rows, r_whole, preferred_element_type=jnp...]
    unnamed x33 -> x39, local copies, waits for them, and re-layouts: 3.66 us -> 4.35 us
  transfers between devices with their start and end apart: 37 -> 44, of which waited for: 18 -> 26; matrix products, arithmetic and copies ran while one was open for 18% -> 21% of each run, Pallas kernels for 0% -> 0%
where the time goes in v21:
time: 209 us; the launch traced here: 208 us
  waiting for transfers between devices  80.9 us (39%)
  starting transfers between devices  39.7 us (19%)
  local copies, waits for them, and re-layouts  32.8 us (16%)
  between operations  21.6 us (10%)
  other arithmetic  16.8 us (8%)
  matrix products  15.8 us (8%)
    ppermute x21, waiting for transfers between devices, ring_reduce_scatter(): acc = lax.ppermute(mine if acc is None else acc + mine, 'dp', pairs)  32 us
    ppermute x9, waiting for transfers between devices, permute_all_to_all(): lax.ppermute(mine, 'feat', [(f, (f + shift) % n) for f in range(n)])  25.6 us
    ppermute x14, waiting for transfers between devices, ring_all_gather(): cur = lax.ppermute(cur, 'dp', pairs)  23.3 us
    ppermute x21, starting transfers between devices, ring_reduce_scatter(): acc = lax.ppermute(mine if acc is None else acc + mine, 'dp', pairs)  19.1 us
    ppermute x14, starting transfers between devices, ring_all_gather(): cur = lax.ppermute(cur, 'dp', pairs)  16 us
    dot_general x1, matrix products, body(): jnp.einsum('bst,bsc->cst', columns, l_blocks, preferred_element_type=jnp....  5.68 us
    add x9, other arithmetic, ring_reduce_scatter(): acc = lax.ppermute(mine if acc is None else acc + mine, 'dp', pairs)  5.13 us
    another operation x3, other arithmetic, permute_all_to_all(): by_shift = jnp.stack(by_shift)  4.7 us
  transfers between devices with their start and end apart: 44, of which 26 were waited for; matrix products, arithmetic and copies ran while one was open for 21% of the time, Pallas kernels for 0%

profile of v21, /device:TPU:0, one launch (start us, length us, event | category | flops | bytes accessed | tf_op | source)
XLA Modules:
  0.0 207.5 jit_solution(10509341740503699871)
XLA Ops:
  2.6 3.0 %collective-permute-start.4 = (bf16[320,256]{1,0:T(8,128)(2,1)}, bf16[320,256]{1,0:T(8,128)(2,1)}, u32[]{:S(2)}, u32[]{:S(2)}) collective-permute-start(bf16[320,256]{1,0:T(8,128)(2,1)} %bitcast.3), channel_id=1, source_target_pairs={{0,8},{4,0},{12,4},{20,12},{28,20},{24,28},{16,24},{8,16},{1,9},{5... | collective-permute-start | bytes 491528 | tf_op jit(solution)/shard_map/ppermute | solution.py:88
  8.5 2.0 collective-permute-start.7
  10.5 2.9 %slice_bitcast_fusion.11 = (bf16[1,16,64,256]{3,2,1,0:T(8,128)(2,1)}, bf16[1,16,64,256]{3,2,1,0:T(8,128)(2,1)}, bf16[1,16,64,256]{3,2,1,0:T(8,128)(2,1)}, bf16[1,16,64,256]{3,2,1,0:T(8,128)(2,1)}) fusion(bf16[16,256,256]{2,1,0:T(8,128)(2,1)} %bitcast.224), kind=kLoop, calls=%fused_computation.41 | loop fusion | bytes 4194304 | tf_op jit(solution)/shard_map/stack | solution.py:96
  44.8 4.1 %collective-permute-done.8 = bf16[320,256]{1,0:T(8,128)(2,1)S(1)} collective-permute-done((bf16[320,256]{1,0:T(8,128)(2,1)}, bf16[320,256]{1,0:T(8,128)(2,1)S(1)}, u32[]{:S(2)}, u32[]{:S(2)}) %collective-permute-start.8) | collective-permute-done | bytes 163872 | tf_op jit(solution)/shard_map/ppermute | solution.py:88
  50.4 4.2 %collective-permute-done.1 = bf16[320,256]{1,0:T(8,128)(2,1)S(1)} collective-permute-done((bf16[320,256]{1,0:T(8,128)(2,1)}, bf16[320,256]{1,0:T(8,128)(2,1)S(1)}, u32[]{:S(2)}, u32[]{:S(2)}) %collective-permute-start.1) | collective-permute-done | bytes 163872 | tf_op jit(solution)/shard_map/ppermute | solution.py:88
  56.8 3.1 %collective-permute-done.9 = bf16[320,256]{1,0:T(8,128)(2,1)S(1)} collective-permute-done((bf16[320,256]{1,0:T(8,128)(2,1)S(1)}, bf16[320,256]{1,0:T(8,128)(2,1)S(1)}, u32[]{:S(2)}, u32[]{:S(2)}) %collective-permute-start.9) | collective-permute-done | bytes 163872 | tf_op jit(solution)/shard_map/ppermute | solution.py:88
  62.5 4.2 %collective-permute-done.11 = bf16[320,256]{1,0:T(8,128)(2,1)S(1)} collective-permute-done((bf16[320,256]{1,0:T(8,128)(2,1)}, bf16[320,256]{1,0:T(8,128)(2,1)S(1)}, u32[]{:S(2)}, u32[]{:S(2)}) %collective-permute-start.11) | collective-permute-done | bytes 163872 | tf_op jit(solution)/shard_map/ppermute | solution.py:88
  68.8 3.5 %collective-permute-done.2 = bf16[320,256]{1,0:T(8,128)(2,1)S(1)} collective-permute-done((bf16[320,256]{1,0:T(8,128)(2,1)S(1)}, bf16[320,256]{1,0:T(8,128)(2,1)S(1)}, u32[]{:S(2)}, u32[]{:S(2)}) %collective-permute-start.2) | collective-permute-done | bytes 163872 | tf_op jit(solution)/shard_map/ppermute | solution.py:88
  92.0 4.4 %collective-permute-done.19 = bf16[16,64,256]{2,1,0:T(8,128)(2,1)} collective-permute-done((bf16[16,64,256]{2,1,0:T(8,128)(2,1)}, bf16[16,64,256]{2,1,0:T(8,128)(2,1)}, u32[]{:S(2)}, u32[]{:S(2)}) %collective-permute-start.19) | collective-permute-done | bytes 524320 | tf_op jit(solution)/shard_map/ppermute | solution.py:100
  96.3 14.0 %collective-permute-done.18 = bf16[16,64,256]{2,1,0:T(8,128)(2,1)} collective-permute-done((bf16[16,64,256]{2,1,0:T(8,128)(2,1)}, bf16[16,64,256]{2,1,0:T(8,128)(2,1)}, u32[]{:S(2)}, u32[]{:S(2)}) %collective-permute-start.18) | collective-permute-done | bytes 524320 | tf_op jit(solution)/shard_map/ppermute | solution.py:100
  114.0 5.7 %fusion.2 = bf16[64,64,256]{2,0,1:T(8,128)(2,1)S(1)} fusion(bf16[64,64,256]{2,0,1:T(8,128)(2,1)S(1)} %copy_dynamic-update-slice_fusion.4, bf16[16,64,256]{2,0,1:T(8,128)(2,1)S(1)} %copy-done.11, bf16[16,64,256]{2,0,1:T(8,128)(2,1)S(1)} %copy-done.12, bf16[16,64,256]{2,0,1:T(8,128)(2,1)S(1)} %copy-done.9, bf16[16,64,256]{2,0,1:T(8,128)(2,1)S(1)} %copy-done.10, ...), kind=kOutput, calls=%fused_computation.6 | convolution fusion | flops 163577856 | bytes 6815744 | tf_op jit(solution)/shard_map/bst,bsc->cst/dot_general | solution.py:130
  123.5 2.0 multiply_bitcast_fusion
  125.5 3.8 %copy.60 = f32[64,64,64]{2,1,0:T(8,128)} copy(f32[64,64,64]{0,2,1:T(8,128)} %multiply_bitcast_fusion) | data formatting | bytes 2097152 | tf_op jit(solution)/shard_map/mul | solution.py:136
  130.6 1.9 collective-permute-start.37
  132.5 6.9 %collective-permute-done.40 = f32[8,64,64]{2,1,0:T(8,128)S(1)} collective-permute-done((f32[8,64,64]{2,1,0:T(8,128)S(1)}, f32[8,64,64]{2,1,0:T(8,128)S(1)}, u32[]{:S(2)}, u32[]{:S(2)}) %collective-permute-start.40) | collective-permute-done | bytes 131104 | tf_op jit(solution)/shard_map/ppermute | solution.py:71
  140.4 6.2 %collective-permute-done.21 = bf16[64,16,256]{2,1,0:T(8,128)(2,1)} collective-permute-done((bf16[64,16,256]{2,1,0:T(8,128)(2,1)}, bf16[64,16,256]{2,1,0:T(8,128)(2,1)}, u32[]{:S(2)}, u32[]{:S(2)}) %collective-permute-start.21) | collective-permute-done | bytes 524320 | tf_op jit(solution)/shard_map/ppermute | solution.py:100
  157.4 3.9 %collective-permute-done.23 = f32[16,16,256]{2,0,1:T(8,128)S(1)} collective-permute-done((f32[16,16,256]{2,0,1:T(8,128)S(1)}, f32[16,16,256]{2,0,1:T(8,128)S(1)}, u32[]{:S(2)}, u32[]{:S(2)}) %collective-permute-start.23) | collective-permute-done | bytes 262176 | tf_op jit(solution)/shard_map/ppermute | solution.py:71
  164.3 2.7 %collective-permute-done.38 = f32[8,64,64]{2,1,0:T(8,128)S(1)} collective-permute-done((f32[8,64,64]{2,1,0:T(8,128)S(1)}, f32[8,64,64]{2,1,0:T(8,128)S(1)}, u32[]{:S(2)}, u32[]{:S(2)}) %collective-permute-start.38) | collective-permute-done | bytes 131104 | tf_op jit(solution)/shard_map/ppermute | solution.py:71
  169.9 4.3 %collective-permute-done.27 = f32[16,16,256]{2,0,1:T(8,128)S(1)} collective-permute-done((f32[16,16,256]{2,0,1:T(8,128)S(1)}, f32[16,16,256]{2,0,1:T(8,128)S(1)}, u32[]{:S(2)}, u32[]{:S(2)}) %collective-permute-start.27) | collective-permute-done | bytes 262176 | tf_op jit(solution)/shard_map/ppermute | solution.py:71
  174.7 3.5 %collective-permute-done.24 = f32[16,16,256]{2,0,1:T(8,128)S(1)} collective-permute-done((f32[16,16,256]{2,0,1:T(8,128)S(1)}, f32[16,16,256]{2,0,1:T(8,128)S(1)}, u32[]{:S(2)}, u32[]{:S(2)}) %collective-permute-start.24) | collective-permute-done | bytes 262176 | tf_op jit(solution)/shard_map/ppermute | solution.py:71
  186.5 2.9 %collective-permute-done.25 = f32[16,16,256]{2,0,1:T(8,128)S(1)} collective-permute-done((f32[16,16,256]{2,0,1:T(8,128)}, f32[16,16,256]{2,0,1:T(8,128)S(1)}, u32[]{:S(2)}, u32[]{:S(2)}) %collective-permute-start.25) | collective-permute-done | bytes 262176 | tf_op jit(solution)/shard_map/ppermute | solution.py:71
  189.4 1.8 collective-permute-done.28
  195.0 1.8 collective-permute-done.35
  200.1 4.5 %add_convert_fusion = bf16[16,256,256]{2,1,0:T(8,128)(2,1)} fusion(bf16[16,256,256]{2,1,0:T(8,128)(2,1)} %bitcast.225, bf16[256,16,256]{2,0,1:T(8,128)(2,1)} %copy-done.3, bf16[256,16,256]{2,1,0:T(8,128)(2,1)S(1)} %bitcast.222), kind=kOutput, calls=%fused_computation.14 | convolution fusion | flops 540016640 | bytes 8388608 | tf_op jit(solution)/shard_map/obt,ibo->bit/dot_general | solution.py:140
  (175 shorter events, 88.6 us)
Async XLA Ops:
  2.6 53.5 %collective-permute-start.4 = (bf16[320,256]{1,0:T(8,128)(2,1)}, bf16[320,256]{1,0:T(8,128)(2,1)}, u32[]{:S(2)}, u32[]{:S(2)}) collective-permute-start(bf16[320,256]{1,0:T(8,128)(2,1)} %bitcast.3), channel_id=1, source_target_pairs={{0,8},{4,0},{12,4},{20,12},{28,20},{24,28},{16,24},{8,16},{1,9},{5... | collective-permute-start | bytes 491528 | tf_op jit(solution)/shard_map/ppermute | solution.py:88
  5.7 36.6 %collective-permute-start = (bf16[320,256]{1,0:T(8,128)(2,1)}, bf16[320,256]{1,0:T(8,128)(2,1)}, u32[]{:S(2)}, u32[]{:S(2)}) collective-permute-start(bf16[320,256]{1,0:T(8,128)(2,1)} %bitcast.3), channel_id=1, source_target_pairs={{0,4},{4,12},{12,20},{20,28},{28,24},{24,16},{16,8},{8,0},{1,5},{5... | collective-permute-start | bytes 491528 | tf_op jit(solution)/shard_map/ppermute | solution.py:88
  8.5 31.1 %collective-permute-start.7 = (bf16[320,256]{1,0:T(8,128)(2,1)}, bf16[320,256]{1,0:T(8,128)(2,1)}, u32[]{:S(2)}, u32[]{:S(2)}) collective-permute-start(bf16[320,256]{1,0:T(8,128)(2,1)} %get-tuple-element.4), channel_id=1, source_target_pairs={{0,4},{4,12},{12,20},{20,28},{28,24},{24,16},{16,8},{8,0},{1,5},{5... | collective-permute-start | bytes 491528 | tf_op jit(solution)/shard_map/ppermute | solution.py:88
  10.5 45.7 %collective-permute-start.10 = (bf16[320,256]{1,0:T(8,128)(2,1)}, bf16[320,256]{1,0:T(8,128)(2,1)}, u32[]{:S(2)}, u32[]{:S(2)}) collective-permute-start(bf16[320,256]{1,0:T(8,128)(2,1)} %get-tuple-element.4), channel_id=1, source_target_pairs={{0,8},{4,0},{12,4},{20,12},{28,20},{24,28},{16,24},{8,16},{1,9},{5... | collective-permute-start | bytes 491528 | tf_op jit(solution)/shard_map/ppermute | solution.py:88
  16.6 58.8 %collective-permute-start.16 = (bf16[16,64,256]{2,1,0:T(8,128)(2,1)}, bf16[16,64,256]{2,1,0:T(8,128)(2,1)}, u32[]{:S(2)}, u32[]{:S(2)}) collective-permute-start(bf16[16,64,256]{2,1,0:T(8,128)(2,1)} %get-tuple-element.42), channel_id=1, source_target_pairs={{0,3},{1,0},{2,1},{3,2},{4,7},{5,4},{6,5},{7,6},{8,11},{9,8},{10,9... | collective-permute-start | bytes 1572872 | tf_op jit(solution)/shard_map/ppermute | solution.py:100
  39.6 36.4 %collective-permute-start.15 = (bf16[16,64,256]{2,1,0:T(8,128)(2,1)}, bf16[16,64,256]{2,1,0:T(8,128)(2,1)S(1)}, u32[]{:S(2)}, u32[]{:S(2)}) collective-permute-start(bf16[16,64,256]{2,1,0:T(8,128)(2,1)} %get-tuple-element.43), channel_id=1, source_target_pairs={{0,2},{1,3},{2,0},{3,1},{4,6},{5,7},{6,4},{7,5},{8,10},{9,11},{10,... | collective-permute-start | bytes 1572872 | tf_op jit(solution)/shard_map/ppermute | solution.py:100
  56.2 19.9 %collective-permute-start.14 = (bf16[16,64,256]{2,1,0:T(8,128)(2,1)S(1)}, bf16[16,64,256]{2,1,0:T(8,128)(2,1)S(1)}, u32[]{:S(2)}, u32[]{:S(2)}) collective-permute-start(bf16[16,64,256]{2,1,0:T(8,128)(2,1)S(1)} %copy-done.13), channel_id=1, source_target_pairs={{0,1},{1,2},{2,3},{3,0},{4,5},{5,6},{6,7},{7,4},{8,9},{9,10},{10,1... | collective-permute-start | bytes 1572872 | tf_op jit(solution)/shard_map/ppermute | solution.py:100
  56.2 12.1 %collective-permute-start.5 = (bf16[320,256]{1,0:T(8,128)(2,1)}, bf16[320,256]{1,0:T(8,128)(2,1)S(1)}, u32[]{:S(2)}, u32[]{:S(2)}) collective-permute-start(bf16[320,256]{1,0:T(8,128)(2,1)} %collective-permute-done.4), channel_id=1, source_target_pairs={{0,8},{4,0},{12,4},{20,12},{28,20},{24,28},{16,24},{8,16},{1,9},{5... | collective-permute-start | bytes 491528 | tf_op jit(solution)/shard_map/ppermute | solution.py:88
  84.7 25.6 %collective-permute-start.18 = (bf16[16,64,256]{2,1,0:T(8,128)(2,1)}, bf16[16,64,256]{2,1,0:T(8,128)(2,1)}, u32[]{:S(2)}, u32[]{:S(2)}) collective-permute-start(bf16[16,64,256]{2,1,0:T(8,128)(2,1)} %get-tuple-element.55), channel_id=1, source_target_pairs={{0,2},{1,3},{2,0},{3,1},{4,6},{5,7},{6,4},{7,5},{8,10},{9,11},{10,... | collective-permute-start | bytes 1572872 | tf_op jit(solution)/shard_map/ppermute | solution.py:100
  86.1 24.3 %collective-permute-start.17 = (bf16[16,64,256]{2,1,0:T(8,128)(2,1)}, bf16[16,64,256]{2,1,0:T(8,128)(2,1)}, u32[]{:S(2)}, u32[]{:S(2)}) collective-permute-start(bf16[16,64,256]{2,1,0:T(8,128)(2,1)} %get-tuple-element.56), channel_id=1, source_target_pairs={{0,1},{1,2},{2,3},{3,0},{4,5},{5,6},{6,7},{7,4},{8,9},{9,10},{10,1... | collective-permute-start | bytes 1572872 | tf_op jit(solution)/shard_map/ppermute | solution.py:100
  122.7 17.8 %collective-permute-start.22 = (bf16[64,16,256]{2,1,0:T(8,128)(2,1)}, bf16[64,16,256]{2,1,0:T(8,128)(2,1)}, u32[]{:S(2)}, u32[]{:S(2)}) collective-permute-start(bf16[64,16,256]{2,1,0:T(8,128)(2,1)} %get-tuple-element.30), channel_id=1, source_target_pairs={{0,3},{1,0},{2,1},{3,2},{4,7},{5,4},{6,5},{7,6},{8,11},{9,8},{10,9... | collective-permute-start | bytes 1572872 | tf_op jit(solution)/shard_map/ppermute | solution.py:100
  122.7 23.9 %collective-permute-start.21 = (bf16[64,16,256]{2,1,0:T(8,128)(2,1)}, bf16[64,16,256]{2,1,0:T(8,128)(2,1)}, u32[]{:S(2)}, u32[]{:S(2)}) collective-permute-start(bf16[64,16,256]{2,1,0:T(8,128)(2,1)} %get-tuple-element.31), channel_id=1, source_target_pairs={{0,2},{1,3},{2,0},{3,1},{4,6},{5,7},{6,4},{7,5},{8,10},{9,11},{10,... | collective-permute-start | bytes 1572872 | tf_op jit(solution)/shard_map/ppermute | solution.py:100
  123.2 24.3 %collective-permute-start.20 = (bf16[64,16,256]{2,1,0:T(8,128)(2,1)S(1)}, bf16[64,16,256]{2,1,0:T(8,128)(2,1)}, u32[]{:S(2)}, u32[]{:S(2)}) collective-permute-start(bf16[64,16,256]{2,1,0:T(8,128)(2,1)S(1)} %get-tuple-element.32), channel_id=1, source_target_pairs={{0,1},{1,2},{2,3},{3,0},{4,5},{5,6},{6,7},{7,4},{8,9},{9,10},{10,1... | collective-permute-start | bytes 1572872 | tf_op jit(solution)/shard_map/ppermute | solution.py:100
  130.6 23.6 %collective-permute-start.37 = (f32[8,64,64]{2,1,0:T(8,128)S(1)}, f32[8,64,64]{2,1,0:T(8,128)S(1)}, u32[]{:S(2)}, u32[]{:S(2)}) collective-permute-start(f32[8,64,64]{2,1,0:T(8,128)S(1)} %get-tuple-element.11), channel_id=1, source_target_pairs={{0,4},{4,12},{12,20},{20,28},{28,24},{24,16},{16,8},{8,0},{1,5},{5... | collective-permute-start | bytes 393224 | tf_op jit(solution)/shard_map/ppermute | solution.py:71
  140.3 13.9 %collective-permute-start.41 = (f32[8,64,64]{2,1,0:T(8,128)S(1)}, f32[8,64,64]{2,1,0:T(8,128)S(1)}, u32[]{:S(2)}, u32[]{:S(2)}) collective-permute-start(f32[8,64,64]{2,1,0:T(8,128)S(1)} %bitcast_add_fusion.2), channel_id=1, source_target_pairs={{0,8},{4,0},{12,4},{20,12},{28,20},{24,28},{16,24},{8,16},{1,9},{5... | collective-permute-start | bytes 393224 | tf_op jit(solution)/shard_map/ppermute | solution.py:71
  156.8 11.8 %collective-permute-start.42 = (f32[8,64,64]{2,1,0:T(8,128)S(1)}, f32[8,64,64]{2,1,0:T(8,128)S(1)}, u32[]{:S(2)}, u32[]{:S(2)}) collective-permute-start(f32[8,64,64]{2,1,0:T(8,128)S(1)} %get-tuple-element.10), channel_id=1, source_target_pairs={{0,8},{4,0},{12,4},{20,12},{28,20},{24,28},{16,24},{8,16},{1,9},{5... | collective-permute-start | bytes 393224 | tf_op jit(solution)/shard_map/ppermute | solution.py:71
  157.2 17.1 %collective-permute-start.27 = (f32[16,16,256]{2,0,1:T(8,128)S(1)}, f32[16,16,256]{2,0,1:T(8,128)S(1)}, u32[]{:S(2)}, u32[]{:S(2)}) collective-permute-start(f32[16,16,256]{2,0,1:T(8,128)S(1)} %get-tuple-element.18), channel_id=1, source_target_pairs={{0,8},{4,0},{12,4},{20,12},{28,20},{24,28},{16,24},{8,16},{1,9},{5... | collective-permute-start | bytes 786440 | tf_op jit(solution)/shard_map/ppermute | solution.py:71
  161.3 19.3 %collective-permute-start.30 = (f32[16,16,256]{2,0,1:T(8,128)S(1)}, f32[16,16,256]{2,0,1:T(8,128)S(1)}, u32[]{:S(2)}, u32[]{:S(2)}) collective-permute-start(f32[16,16,256]{2,0,1:T(8,128)S(1)} %get-tuple-element.23), channel_id=1, source_target_pairs={{0,4},{4,12},{12,20},{20,28},{28,24},{24,16},{16,8},{8,0},{1,5},{5... | collective-permute-start | bytes 786440 | tf_op jit(solution)/shard_map/ppermute | solution.py:71
  163.1 15.1 %collective-permute-start.24 = (f32[16,16,256]{2,0,1:T(8,128)S(1)}, f32[16,16,256]{2,0,1:T(8,128)S(1)}, u32[]{:S(2)}, u32[]{:S(2)}) collective-permute-start(f32[16,16,256]{2,0,1:T(8,128)S(1)} %bitcast_add_fusion.16), channel_id=1, source_target_pairs={{0,4},{4,12},{12,20},{20,28},{28,24},{24,16},{16,8},{8,0},{1,5},{5... | collective-permute-start | bytes 786440 | tf_op jit(solution)/shard_map/ppermute | solution.py:71
  167.0 14.1 %collective-permute-start.34 = (f32[16,16,256]{2,0,1:T(8,128)S(1)}, f32[16,16,256]{2,0,1:T(8,128)S(1)}, u32[]{:S(2)}, u32[]{:S(2)}) collective-permute-start(f32[16,16,256]{2,0,1:T(8,128)S(1)} %bitcast_add_fusion.8), channel_id=1, source_target_pairs={{0,8},{4,0},{12,4},{20,12},{28,20},{24,28},{16,24},{8,16},{1,9},{5... | collective-permute-start | bytes 786440 | tf_op jit(solution)/shard_map/ppermute | solution.py:71
  168.8 15.1 %collective-permute-start.39 = (f32[8,64,64]{2,1,0:T(8,128)S(1)}, f32[8,64,64]{2,1,0:T(8,128)S(1)}, u32[]{:S(2)}, u32[]{:S(2)}) collective-permute-start(f32[8,64,64]{2,1,0:T(8,128)S(1)} %get-tuple-element.7), channel_id=1, source_target_pairs={{0,4},{4,12},{12,20},{20,28},{28,24},{24,16},{16,8},{8,0},{1,5},{5... | collective-permute-start | bytes 393224 | tf_op jit(solution)/shard_map/ppermute | solution.py:71
  181.8 13.2 %collective-permute-start.31 = (f32[16,16,256]{2,0,1:T(8,128)}, f32[16,16,256]{2,0,1:T(8,128)S(1)}, u32[]{:S(2)}, u32[]{:S(2)}) collective-permute-start(f32[16,16,256]{2,0,1:T(8,128)} %get-tuple-element.21), channel_id=1, source_target_pairs={{0,4},{4,12},{12,20},{20,28},{28,24},{24,16},{16,8},{8,0},{1,5},{5... | collective-permute-start | bytes 786440 | tf_op jit(solution)/shard_map/ppermute | solution.py:71
  183.8 13.1 %collective-permute-start.35 = (f32[16,16,256]{2,0,1:T(8,128)S(1)}, f32[16,16,256]{2,0,1:T(8,128)}, u32[]{:S(2)}, u32[]{:S(2)}) collective-permute-start(f32[16,16,256]{2,0,1:T(8,128)S(1)} %get-tuple-element.22), channel_id=1, source_target_pairs={{0,8},{4,0},{12,4},{20,12},{28,20},{24,28},{16,24},{8,16},{1,9},{5... | collective-permute-start | bytes 786440 | tf_op jit(solution)/shard_map/ppermute | solution.py:71
  192.4 12.2 %collective-permute-start.26 = (f32[16,16,256]{2,0,1:T(8,128)S(1)}, f32[16,16,256]{2,0,1:T(8,128)S(1)}, u32[]{:S(2)}, u32[]{:S(2)}) collective-permute-start(f32[16,16,256]{2,0,1:T(8,128)S(1)} %get-tuple-element.13), channel_id=1, source_target_pairs={{0,4},{4,12},{12,20},{20,28},{28,24},{24,16},{16,8},{8,0},{1,5},{5... | collective-permute-start | bytes 786440 | tf_op jit(solution)/shard_map/ppermute | solution.py:71
  (36 other events, 393.3 us)
